TPU v7x, 32 devices: a whole 2x2x4 slice. The times are simulated.
32 devices in a mesh: space: 4 (over z), dp: 8 (over y, x, core).
Axes of the slice: x: 2, y: 2, z: 4, core: 2. Of those that a mesh axis runs over, the one named last changes fastest.
Arguments:
- features: bfloat16 [8, 12, 128, 320], P('dp', 'space'), may hold values from -6 to 6
- cotangent: bfloat16 [8, 12, 128, 320], P('dp', 'space'), may hold values from -6 to 6
- norm_gain: float32 [320], replicated, may hold values from 0.1 to 1.9
- norm_bias: float32 [320], replicated, may hold values from -0.5 to 0.5
- weight: bfloat16 [2880, 320], P('dp'), may hold values from -0.109375 to 0.109375
- moment_one: float32 [2880, 320], P('dp'), may hold values from -332.55374 to 332.55374
- moment_two: float32 [2880, 320], P('dp'), may hold values from 768 to 6144
- heights: int32 [8], P('dp'), may hold values from 6 to 12, as said below
- widths: int32 [8], P('dp'), may hold values from 64 to 128, as said below
Outputs:
- block_out: bfloat16 [8, 12, 128, 320], P('dp', 'space')
- input_grad: bfloat16 [8, 12, 128, 320], P('dp', 'space')
- weight_grad: float32 [2880, 320], P('dp')
- adam_update: float32 [2880, 320], P('dp')
Inputs may be any that keep to these rules, and one draw needn't show every extreme that they name: Image i occupies canvas rows 0 to heights[i] - 1; some image has all 12 rows. Image i occupies canvas columns 0 to widths[i] - 1; some image has all 128 columns.
All inputs are finite; a program needn't handle non-finite values.
Results may differ from a plain program's by a relative error of at most 0.017.
Values may be sent and summed in bfloat16 or wider, within the bound.
No kernel may reach another device: no remote copies, remote signals or barrier semaphores. Data moves between devices by JAX's collectives and lax.ppermute only.
A program may use at most 64 MiB of HBM per device.

v0:
```python
import jax
import jax.numpy as jnp
from jax import lax
from jax.sharding import PartitionSpec as P

GROUPS = 32


def with_halo(cells, sides, width):
    for axis, dim in sides:
        count = lax.axis_size(axis)
        ends = count - 1
        head = lax.slice_in_dim(cells, 0, width, axis=dim)
        tail = lax.slice_in_dim(cells, cells.shape[dim] - width, cells.shape[dim], axis=dim)
        cells = jnp.concatenate(
            [
                lax.ppermute(tail, axis, [(i, (i + 1) % count) for i in range(ends)]),
                cells,
                lax.ppermute(head, axis, [((i + 1) % count, i) for i in range(ends)]),
            ],
            axis=dim,
        )
    return cells


def group_sum(values, groups):
    height_dev, width_dev, channels = values.shape
    return values.reshape(height_dev, width_dev, groups, channels // groups).sum(axis=(0, 1, 3))


def spread_groups(statistic, channels):
    return jnp.repeat(statistic, channels // statistic.shape[0])


def pad_columns(padded_rows):
    return jnp.pad(padded_rows, ((0, 0), (1, 1), (0, 0)))


def local(
    features, cotangent, norm_gain, norm_bias, weight, moment_one, moment_two, heights, widths
):
    latent = features[0]
    height_dev, width_dev, channels = latent.shape
    row_ids = lax.axis_index("space") * height_dev + jnp.arange(height_dev, dtype=jnp.int32)
    inside = (
        (row_ids < heights[0])[:, None]
        & (jnp.arange(width_dev, dtype=jnp.int32) < widths[0])[None, :]
    ).astype(jnp.float32)[..., None]
    cell_count = (heights[0] * widths[0] * (channels // GROUPS)).astype(jnp.float32)
    gathered = lax.all_gather(weight, "dp", axis=0, tiled=True)
    tap_weights = gathered.reshape(9, channels, channels)
    values = latent.astype(jnp.float32) * inside
    group_total, squares = lax.psum(
        (group_sum(values, GROUPS), group_sum(values * values, GROUPS)), "space"
    )
    center = group_total / cell_count
    spread = squares / cell_count - center * center
    inverse = lax.rsqrt(spread + 1e-05)
    normed = (values - spread_groups(center, channels)) * spread_groups(inverse, channels) * inside
    before = normed * norm_gain + norm_bias
    activated = (jax.nn.silu(before) * inside).astype(jnp.bfloat16)
    act_pad = pad_columns(with_halo(activated, (("space", 0),), 1))
    output = jnp.zeros((height_dev * width_dev, channels), jnp.float32)
    for row_off in range(3):
        for col_off in range(3):
            window = act_pad[row_off : row_off + height_dev, col_off : col_off + width_dev].reshape(
                -1, channels
            )
            output = output + jnp.dot(
                window, tap_weights[row_off * 3 + col_off], preferred_element_type=jnp.float32
            )
    block_out = (output.reshape(height_dev, width_dev, channels) * inside).astype(jnp.bfloat16)
    masked = cotangent[0] * inside.astype(jnp.bfloat16)
    cot_pad = pad_columns(with_halo(masked, (("space", 0),), 1))
    flat_cot = masked.reshape(-1, channels)
    upstream = jnp.zeros((height_dev * width_dev, channels), jnp.float32)
    tap_grads = []
    for row_off in range(3):
        for col_off in range(3):
            tap_index = row_off * 3 + col_off
            window = act_pad[row_off : row_off + height_dev, col_off : col_off + width_dev].reshape(
                -1, channels
            )
            tap_grads.append(
                lax.dot_general(
                    window, flat_cot, (((0,), (0,)), ((), ())), preferred_element_type=jnp.float32
                )
            )
            cot_window = cot_pad[
                2 - row_off : 2 - row_off + height_dev, 2 - col_off : 2 - col_off + width_dev
            ].reshape(-1, channels)
            upstream = upstream + lax.dot_general(
                cot_window,
                tap_weights[tap_index],
                (((1,), (1,)), ((), ())),
                preferred_element_type=jnp.float32,
            )
    weight_terms = jnp.stack(tap_grads).reshape(9 * channels, channels)
    gate_sig = jax.nn.sigmoid(before)
    silu_slope = gate_sig * (1.0 + before * (1.0 - gate_sig))
    scaled = upstream.reshape(height_dev, width_dev, channels) * silu_slope * inside * norm_gain
    local_first = group_sum(scaled, GROUPS)
    local_second = group_sum(scaled * normed, GROUPS)
    grad_piece = lax.psum_scatter(weight_terms, "dp", scatter_dimension=0, tiled=True)
    sum_first, sum_second = lax.psum((local_first, local_second), "space")
    grad_piece = lax.psum(grad_piece.astype(jnp.bfloat16), "space").astype(jnp.float32)
    first = sum_first / cell_count
    second = sum_second / cell_count
    input_grad = (
        spread_groups(inverse, channels)
        * (scaled - spread_groups(first, channels) - normed * spread_groups(second, channels))
        * inside
    ).astype(jnp.bfloat16)
    first_new = 0.9 * moment_one + 0.1 * grad_piece
    second_new = 0.999 * moment_two + 0.001 * grad_piece * grad_piece
    adam_update = first_new / (1.0 - 0.9**10) / (jnp.sqrt(second_new / (1.0 - 0.999**10)) + 1e-08)
    return (block_out[None], input_grad[None], grad_piece, adam_update)


def solution(mesh):
    placed = (
        P("dp", "space", None, None),
        P("dp", "space", None, None),
        P(),
        P(),
        P("dp", None),
        P("dp", None),
        P("dp", None),
        P("dp"),
        P("dp"),
    )
    return jax.shard_map(
        local,
        mesh=mesh,
        in_specs=placed,
        out_specs=(
            P("dp", "space", None, None),
            P("dp", "space", None, None),
            P("dp", None),
            P("dp", None),
        ),
        check_vma=False,
    )
```

profile of v0, /device:TPU:0, one launch (start us, length us, event | category | flops | bytes accessed | tf_op | source)
XLA Modules:
  0.0 207.1 jit_solution(10719719046943289507)
XLA Ops:
  11.0 13.5 %all-reduce.4 = (f32[32]{0:T(128)S(1)}, f32[32]{0:T(128)S(1)}) all-reduce(f32[32]{0:T(128)S(1)} %reduce_sum.51, f32[32]{0:T(128)S(1)} %reduce_sum.54), channel_id=1, replica_groups=mesh['space'=4,'dp'=8] {'space'}, use_global_device_ids=true, to_apply=%region_2.0 | all-reduce | flops 64 | bytes 512 | tf_op jit(solution)/shard_map/psum | solution.py:53
  24.9 1.3 multiply_convert_fusion.4
  26.2 1.3 collective-permute-start
  27.5 1.3 collective-permute-start.1
  29.8 1.2 dynamic-slice
  31.7 2.1 %collective-permute-done.1 = bf16[1,128,320]{1,2,0:T(8,128)(2,1)S(1)} collective-permute-done((bf16[1,128,320]{1,2,0:T(8,128)(2,1)S(1)}, bf16[1,128,320]{1,2,0:T(8,128)(2,1)S(1)}, u32[]{:S(2)}, u32[]{:S(2)}) %collective-permute-start.1) | collective-permute-done | bytes 81952 | tf_op jit(solution)/shard_map/ppermute | solution.py:19
  38.7 1.3 fusion.6
  40.0 1.2 fusion.5
  44.5 5.6 %copy.68 = f32[2880,320]{0,1:T(8,128)} copy(f32[2880,320]{1,0:T(8,128)} %bitcast.48) | data formatting | bytes 7372800 | tf_op jit(solution)/shard_map/reshape | solution.py:98
  50.2 80.3 %all-reduce.9 = bf16[2880,320]{0,1:T(8,128)(2,1)S(1)} all-reduce(f32[2880,320]{0,1:T(8,128)} %copy.68), channel_id=2, replica_groups=mesh['space'=4,'dp'=8] {'dp'}, use_global_device_ids=true, to_apply=%region_12.13.clone | all-reduce | flops 921600 | bytes 5529600
  132.6 2.7 %collective-permute-start.2 = (bf16[1,128,320]{1,2,0:T(8,128)(2,1)}, bf16[1,128,320]{1,2,0:T(8,128)(2,1)S(1)}, u32[]{:S(2)}, u32[]{:S(2)}) collective-permute-start(bf16[1,128,320]{1,2,0:T(8,128)(2,1)} %get-tuple-element.30), channel_id=1, source_target_pairs={{0,8},{8,16},{16,24},{1,9},{9,17},{17,25},{2,10},{10,18},{18,26},{... | collective-permute-start | bytes 245768 | tf_op jit(solution)/shard_map/ppermute | solution.py:17
  135.2 1.5 collective-permute-start.3
  136.9 1.2 copy.60
  140.4 1.2 copy.43
  149.0 1.9 copy.57
  156.3 8.3 %all-reduce.8.cloned.1.call-done = bf16[360,320]{0,1:T(8,128)(2,1)} async-done(((bf16[360,320]{0,1:T(8,128)(2,1)}), bf16[360,320]{0,1:T(8,128)(2,1)}) %all-reduce.8.cloned.1.call-update) | async-done | bytes 230416 | tf_op jit(solution)/shard_map/psum | solution.py:106
  164.5 2.5 %fusion.17 = (f32[360,320]{0,1:T(8,128)}, f32[360,320]{0,1:T(8,128)}) fusion(f32[360,320]{0,1:T(8,128)} %param.15, f32[360,320]{0,1:T(8,128)} %param.14, bf16[360,320]{0,1:T(8,128)(2,1)} %all-reduce.8.cloned.1.call-done), kind=kLoop, calls=%fused_computation.47 | loop fusion | flops 1382400 | bytes 2073600 | tf_op jit(solution)/shard_map/div | solution.py:116
  167.0 3.9 %copy.44 = bf16[8,360,320]{1,0,2:T(8,128)(2,1)} copy(bf16[8,360,320]{1,2,0:T(8,128)(2,1)} %all-gather.3.cloned.1.call-done) | data formatting | bytes 3686400 | tf_op jit(solution)/shard_map/all_gather | solution.py:50
  170.9 3.4 %reshape.284 = bf16[2880,320]{0,1:T(8,128)(2,1)S(1)} reshape(bf16[8,360,320]{1,0,2:T(8,128)(2,1)} %copy.44) | data formatting | bytes 3686400
  174.7 1.3 fusion.50
  179.6 1.4 fusion.63
  181.0 1.5 convolution_add_fusion.8
  186.7 10.8 %all-reduce.3 = (f32[32]{0:T(128)S(1)}, f32[32]{0:T(128)S(1)}) all-reduce(f32[32]{0:T(128)S(1)} %reduce_sum.75, f32[32]{0:T(128)S(1)} %reduce_sum.72), channel_id=1, replica_groups=mesh['space'=4,'dp'=8] {'space'}, use_global_device_ids=true, to_apply=%region_11.12 | all-reduce | flops 64 | bytes 512 | tf_op jit(solution)/shard_map/psum | solution.py:105
  198.4 1.3 multiply_convert_fusion.1
  (126 shorter events, 37.3 us)
Async XLA Ops:
  8.0 156.5 %all-reduce.8.cloned.1.call-start = ((), (), s32[]{:S(2)}) async-start(), calls=%async_computation | async-start | bytes 491520 | tf_op jit(solution)/shard_map/psum | solution.py:106
  26.2 5.5 %collective-permute-start = (bf16[1,128,320]{1,2,0:T(8,128)(2,1)S(1)}, bf16[1,128,320]{1,2,0:T(8,128)(2,1)S(1)}, u32[]{:S(2)}, u32[]{:S(2)}) collective-permute-start(bf16[1,128,320]{1,2,0:T(8,128)(2,1)S(1)} %get-tuple-element.34), channel_id=1, source_target_pairs={{0,8},{8,16},{16,24},{1,9},{9,17},{17,25},{2,10},{10,18},{18,26},{... | collective-permute-start | bytes 245768 | tf_op jit(solution)/shard_map/ppermute | solution.py:17
  27.5 6.3 %collective-permute-start.1 = (bf16[1,128,320]{1,2,0:T(8,128)(2,1)S(1)}, bf16[1,128,320]{1,2,0:T(8,128)(2,1)S(1)}, u32[]{:S(2)}, u32[]{:S(2)}) collective-permute-start(bf16[1,128,320]{1,2,0:T(8,128)(2,1)S(1)} %get-tuple-element.35), channel_id=1, source_target_pairs={{8,0},{16,8},{24,16},{9,1},{17,9},{25,17},{10,2},{18,10},{26,18},{... | collective-permute-start | bytes 245768 | tf_op jit(solution)/shard_map/ppermute | solution.py:19
  31.7 6.0 %copy-start.12 = (bf16[1,128,320]{1,2,0:T(8,128)(2,1)}, bf16[1,128,320]{1,2,0:T(8,128)(2,1)S(1)}, u32[]{:S(2)}) copy-start(bf16[1,128,320]{1,2,0:T(8,128)(2,1)S(1)} %collective-permute-done) | copy-start | bytes 245764
  33.8 8.5 %copy-start.14 = (bf16[1,128,320]{1,2,0:T(8,128)(2,1)}, bf16[1,128,320]{1,2,0:T(8,128)(2,1)S(1)}, u32[]{:S(2)}) copy-start(bf16[1,128,320]{1,2,0:T(8,128)(2,1)S(1)} %collective-permute-done.1) | copy-start | bytes 245764
  34.2 4.5 %copy-start = (bf16[1,3,128,320]{2,3,1,0:T(8,128)(2,1)S(1)}, bf16[1,3,128,320]{2,3,1,0:T(8,128)(2,1)}, u32[]{:S(2)}) copy-start(bf16[1,3,128,320]{2,3,1,0:T(8,128)(2,1)} %param.9) | copy-start | bytes 737284
  34.2 4.5 %copy-start.10 = (bf16[1,3,128,320]{2,3,1,0:T(8,128)(2,1)S(1)}, bf16[1,3,128,320]{2,3,1,0:T(8,128)(2,1)}, u32[]{:S(2)}) copy-start(bf16[1,3,128,320]{2,3,1,0:T(8,128)(2,1)} %param.10) | copy-start | bytes 737284
  34.2 4.5 %copy-start.19 = (f32[320]{0:T(512)S(1)}, f32[320]{0:T(512)}, u32[]{:S(2)}) copy-start(f32[320]{0:T(512)} %param.12) | copy-start | bytes 3844
  34.2 4.5 %copy-start.20 = (f32[320]{0:T(512)S(1)}, f32[320]{0:T(512)}, u32[]{:S(2)}) copy-start(f32[320]{0:T(512)} %param.11) | copy-start | bytes 3844
  131.3 35.7 %all-gather.3.cloned.1.call-start = ((), (), s32[]{:S(2)}) async-start(), calls=%async_computation.1 | async-start | bytes 2211840 | tf_op jit(solution)/shard_map/all_gather | solution.py:50
  132.6 14.1 %collective-permute-start.2 = (bf16[1,128,320]{1,2,0:T(8,128)(2,1)}, bf16[1,128,320]{1,2,0:T(8,128)(2,1)S(1)}, u32[]{:S(2)}, u32[]{:S(2)}) collective-permute-start(bf16[1,128,320]{1,2,0:T(8,128)(2,1)} %get-tuple-element.30), channel_id=1, source_target_pairs={{0,8},{8,16},{16,24},{1,9},{9,17},{17,25},{2,10},{10,18},{18,26},{... | collective-permute-start | bytes 245768 | tf_op jit(solution)/shard_map/ppermute | solution.py:17
  135.2 11.4 %collective-permute-start.3 = (bf16[1,128,320]{1,2,0:T(8,128)(2,1)}, bf16[1,128,320]{1,2,0:T(8,128)(2,1)S(1)}, u32[]{:S(2)}, u32[]{:S(2)}) collective-permute-start(bf16[1,128,320]{1,2,0:T(8,128)(2,1)} %get-tuple-element.31), channel_id=1, source_target_pairs={{8,0},{16,8},{24,16},{9,1},{17,9},{25,17},{10,2},{18,10},{26,18},{... | collective-permute-start | bytes 245768 | tf_op jit(solution)/shard_map/ppermute | solution.py:19
  139.3 2.3 %copy-start.13 = (bf16[1,128,320]{1,2,0:T(8,128)(2,1)S(1)}, bf16[1,128,320]{1,2,0:T(8,128)(2,1)}, u32[]{:S(2)}) copy-start(bf16[1,128,320]{1,2,0:T(8,128)(2,1)} %copy-done.12) | copy-start | bytes 245764
  139.3 2.3 %copy-start.15 = (bf16[1,128,320]{1,2,0:T(8,128)(2,1)S(1)}, bf16[1,128,320]{1,2,0:T(8,128)(2,1)}, u32[]{:S(2)}) copy-start(bf16[1,128,320]{1,2,0:T(8,128)(2,1)} %copy-done.14) | copy-start | bytes 245764
  140.4 2.2 %copy-start.11 = (bf16[3,128,320]{1,2,0:T(8,128)(2,1)S(1)}, bf16[3,128,320]{1,2,0:T(8,128)(2,1)}, u32[]{:S(2)}) copy-start(bf16[3,128,320]{1,2,0:T(8,128)(2,1)} %get-tuple-element.26) | copy-start | bytes 737284
  174.3 1.7 copy-start.7
  174.3 2.1 %copy-start.3 = (bf16[3,128,320]{2,1,0:T(8,128)(2,1)S(1)}, bf16[3,128,320]{2,1,0:T(8,128)(2,1)}, u32[]{:S(2)}) copy-start(bf16[3,128,320]{2,1,0:T(8,128)(2,1)} %copy.45) | copy-start | bytes 737284
  174.7 2.2 %copy-start.2 = (bf16[3,128,320]{2,1,0:T(8,128)(2,1)S(1)}, bf16[3,128,320]{2,1,0:T(8,128)(2,1)}, u32[]{:S(2)}) copy-start(bf16[3,128,320]{2,1,0:T(8,128)(2,1)} %copy.46) | copy-start | bytes 737284
  176.0 1.1 copy-start.1
  176.8 1.1 copy-start.16
  179.6 2.9 %copy-start.9 = (bf16[3,128,320]{2,1,0:T(8,128)(2,1)S(1)}, bf16[3,128,320]{2,1,0:T(8,128)(2,1)}, u32[]{:S(2)}) copy-start(bf16[3,128,320]{2,1,0:T(8,128)(2,1)} %copy.58) | copy-start | bytes 737284
  179.6 3.3 %copy-start.8 = (bf16[3,128,320]{2,1,0:T(8,128)(2,1)S(1)}, bf16[3,128,320]{2,1,0:T(8,128)(2,1)}, u32[]{:S(2)}) copy-start(bf16[3,128,320]{2,1,0:T(8,128)(2,1)} %copy.59) | copy-start | bytes 737284
  184.4 1.1 copy-start.17
  184.4 1.1 copy-start.18
  (3 other events, 2.9 us)
Sparse Core Ops, SparseCore 0:
  131.4 33.0 all-reduce.7
Sparse Core Ops, SparseCore 1:
  133.7 24.6 all-gather.2
where the time goes:
time: 208 us; the launch traced here: 207 us
  blocking collectives  105 us (50%)
  local copies, waits for them, and re-layouts  36.4 us (18%)
  matrix products  20.9 us (10%)
  between operations  18 us (9%)
  waiting for transfers between devices  10.9 us (5%)
  other arithmetic  9.44 us (5%)
  starting transfers between devices  6.8 us (3%)
    unnamed x1, blocking collectives  80.3 us
    psum x1, blocking collectives, local(): lax.psum((group_sum(values, GROUPS), group_sum(values * values, GROUPS)),...  13.5 us
    psum x1, blocking collectives, local(): sum_first, sum_second = lax.psum((local_first, local_second), 'space')  10.8 us
    dot_general x9, matrix products, local(): lax.dot_general(window, flat_cot, (((0,), (0,)), ((), ())), preferred_ele...  10.3 us
    slice x9, local copies, waits for them, and re-layouts, local(): cot_pad[2 - row_off:2 - row_off + height_dev, 2 - col_off:2 - col_off + w...  8.48 us
    psum x1, waiting for transfers between devices, local(): lax.psum(grad_piece.astype(jnp.bfloat16), 'space').astype(jnp.float32)  8.25 us
    slice x9, local copies, waits for them, and re-layouts, local(): act_pad[row_off:row_off + height_dev, col_off:col_off + width_dev]  7.27 us
    unnamed x45, local copies, waits for them, and re-layouts  6.36 us
  transfers between devices with their start and end apart: 6, of which 2 were waited for; matrix products, arithmetic and copies ran while one was open for 12% of the time, Pallas kernels for 0%

commit v1 on v0

--- a/solution.py
+++ b/solution.py
@@ -21,6 +21,18 @@
             axis=dim,
         )
     return cells
+
+
+def space_sum(parts, axis):
+    count = lax.axis_size(axis)
+    if count & (count - 1):
+        return lax.psum(parts, axis)
+    step = 1
+    while step < count:
+        pairs = [(i, i ^ step) for i in range(count)]
+        parts = tuple(p + q for p, q in zip(parts, lax.ppermute(parts, axis, pairs)))
+        step *= 2
+    return parts
 
 
 def group_sum(values, groups):
@@ -50,7 +62,7 @@
     gathered = lax.all_gather(weight, "dp", axis=0, tiled=True)
     tap_weights = gathered.reshape(9, channels, channels)
     values = latent.astype(jnp.float32) * inside
-    group_total, squares = lax.psum(
+    group_total, squares = space_sum(
         (group_sum(values, GROUPS), group_sum(values * values, GROUPS)), "space"
     )
     center = group_total / cell_count
@@ -101,9 +113,15 @@
     scaled = upstream.reshape(height_dev, width_dev, channels) * silu_slope * inside * norm_gain
     local_first = group_sum(scaled, GROUPS)
     local_second = group_sum(scaled * normed, GROUPS)
-    grad_piece = lax.psum_scatter(weight_terms, "dp", scatter_dimension=0, tiled=True)
-    sum_first, sum_second = lax.psum((local_first, local_second), "space")
-    grad_piece = lax.psum(grad_piece.astype(jnp.bfloat16), "space").astype(jnp.float32)
+    dp_size = lax.axis_size("dp")
+    grad_piece = lax.psum_scatter(
+        weight_terms.astype(jnp.bfloat16).reshape(dp_size, -1, channels),
+        "dp",
+        scatter_dimension=0,
+        tiled=False,
+    )
+    sum_first, sum_second = space_sum((local_first, local_second), "space")
+    grad_piece = lax.psum(grad_piece, "space").astype(jnp.float32)
     first = sum_first / cell_count
     second = sum_second / cell_count
     input_grad = (

time: 208 us -> 192 us (0.923)
  blocking collectives: 105 us -> 0 us
  waiting for transfers between devices: 10.9 us -> 89.9 us
  starting transfers between devices: 6.8 us -> 24 us
  local copies, waits for them, and re-layouts: 36.4 us -> 31.8 us
  between operations: 18 us -> 15.6 us
    unnamed x1 -> x0, blocking collectives: 80.3 us -> none
    reduce_scatter x0 -> x1, waiting for transfers between devices: none -> 38.9 us  [local(): lax.psum_scatter(weight_terms.astype(jnp.bfloat16).reshape(dp_size, -1, c...]
    all_gather x1, waiting for transfers between devices: 0.01 us -> 27 us  [local(): gathered = lax.all_gather(weight, 'dp', axis=0, tiled=True)]
    psum x2 -> x0, blocking collectives: 24.3 us -> none  [the longest x1 13.5 us: local(): lax.psum((group_sum(values, GROUPS), group_sum(values * values, GROUPS)),...]
    ppermute x0 -> x8, starting transfers between devices: none -> 14.4 us  [space_sum(): lax.ppermute(parts, axis, pairs)]
    ppermute x0 -> x8, waiting for transfers between devices: none -> 7.28 us  [space_sum(): lax.ppermute(parts, axis, pairs)]
    ppermute x2, waiting for transfers between devices: 2.15 us -> 8.87 us  [with_halo(): lax.ppermute(head, axis, [((i + 1) % count, i) for i in range(ends)])]
    reshape x1 -> x0, local copies, waits for them, and re-layouts: 5.63 us -> none  [local(): weight_terms = jnp.stack(tap_grads).reshape(9 * channels, channels)]
  transfers between devices with their start and end apart: 6 -> 15, of which waited for: 2 -> 9; matrix products, arithmetic and copies ran while one was open for 12% -> 12% of each run, Pallas kernels for 0% -> 0%
where the time goes in v1:
time: 192 us
  waiting for transfers between devices  89.9 us (47%)
  local copies, waits for them, and re-layouts  31.8 us (17%)
  starting transfers between devices  24 us (12%)
  matrix products  20.2 us (11%)
  between operations  15.6 us (8%)
  other arithmetic  10.2 us (5%)
    reduce_scatter x1, waiting for transfers between devices, local(): lax.psum_scatter(weight_terms.astype(jnp.bfloat16).reshape(dp_size, -1, c...  38.9 us
    all_gather x1, waiting for transfers between devices, local(): gathered = lax.all_gather(weight, 'dp', axis=0, tiled=True)  27 us
    ppermute x8, starting transfers between devices, space_sum(): lax.ppermute(parts, axis, pairs)  14.4 us
    dot_general x9, matrix products, local(): lax.dot_general(window, flat_cot, (((0,), (0,)), ((), ())), preferred_ele...  9.52 us
    ppermute x2, waiting for transfers between devices, with_halo(): lax.ppermute(head, axis, [((i + 1) % count, i) for i in range(ends)])  8.87 us
    slice x9, local copies, waits for them, and re-layouts, local(): cot_pad[2 - row_off:2 - row_off + height_dev, 2 - col_off:2 - col_off + w...  8.5 us
    ppermute x8, waiting for transfers between devices, space_sum(): lax.ppermute(parts, axis, pairs)  7.28 us
    slice x9, local copies, waits for them, and re-layouts, local(): act_pad[row_off:row_off + height_dev, col_off:col_off + width_dev]  7.13 us
  transfers between devices with their start and end apart: 15, of which 9 were waited for; matrix products, arithmetic and copies ran while one was open for 12% of the time, Pallas kernels for 0%

profile of v1, /device:TPU:0, one launch (start us, length us, event | category | flops | bytes accessed | tf_op | source)
XLA Modules:
  0.0 191.6 jit_solution(13779045567825138440)
XLA Ops:
  10.0 3.1 %collective-permute-start = (f32[32]{0:T(128)S(1)}, f32[32]{0:T(128)S(1)}, u32[]{:S(2)}, u32[]{:S(2)}) collective-permute-start(f32[32]{0:T(128)S(1)} %reduce_sum.51), channel_id=1, source_target_pairs={{0,8},{8,0},{16,24},{24,16},{1,9},{9,1},{17,25},{25,17},{2,10},{10... | collective-permute-start | bytes 392 | tf_op jit(solution)/shard_map/ppermute | solution.py:33
  14.6 3.0 %collective-permute-start.1 = (f32[32]{0:T(128)S(1)}, f32[32]{0:T(128)S(1)}, u32[]{:S(2)}, u32[]{:S(2)}) collective-permute-start(f32[32]{0:T(128)S(1)} %add.163), channel_id=1, source_target_pairs={{0,16},{8,24},{16,0},{24,8},{1,17},{9,25},{17,1},{25,9},{2,18},{10... | collective-permute-start | bytes 392 | tf_op jit(solution)/shard_map/ppermute | solution.py:33
  17.6 1.9 collective-permute-start.3
  19.5 2.6 %collective-permute-done.3 = f32[32]{0:T(128)S(1)} collective-permute-done((f32[32]{0:T(128)S(1)}, f32[32]{0:T(128)S(1)}, u32[]{:S(2)}, u32[]{:S(2)}) %collective-permute-start.3) | collective-permute-done | bytes 160 | tf_op jit(solution)/shard_map/ppermute | solution.py:33
  23.7 3.5 %collective-permute-start.4 = (bf16[1,128,320]{1,2,0:T(8,128)(2,1)S(1)}, bf16[1,128,320]{1,2,0:T(8,128)(2,1)S(1)}, u32[]{:S(2)}, u32[]{:S(2)}) collective-permute-start(bf16[1,128,320]{1,2,0:T(8,128)(2,1)S(1)} %get-tuple-element.30), channel_id=1, source_target_pairs={{0,8},{8,16},{16,24},{1,9},{9,17},{17,25},{2,10},{10,18},{18,26},{... | collective-permute-start | bytes 245768 | tf_op jit(solution)/shard_map/ppermute | solution.py:17
  29.5 4.1 %collective-permute-done.5 = bf16[1,128,320]{1,2,0:T(8,128)(2,1)S(1)} collective-permute-done((bf16[1,128,320]{1,2,0:T(8,128)(2,1)S(1)}, bf16[1,128,320]{1,2,0:T(8,128)(2,1)S(1)}, u32[]{:S(2)}, u32[]{:S(2)}) %collective-permute-start.5) | collective-permute-done | bytes 81952 | tf_op jit(solution)/shard_map/ppermute | solution.py:19
  43.6 4.2 %copy.68 = bf16[8,360,320]{1,2,0:T(8,128)(2,1)} copy(bf16[8,360,320]{2,1,0:T(8,128)(2,1)} %bitcast.48) | data formatting | bytes 3686400 | tf_op jit(solution)/shard_map/convert_element_type | solution.py:118
  47.8 38.9 %reduce-scatter.2.cloned.1.call-done = bf16[1,360,320]{1,2,0:T(8,128)(2,1)} async-done(((bf16[8,360,320]{1,2,0:T(8,128)(2,1)}), bf16[1,360,320]{1,2,0:T(8,128)(2,1)}) %reduce-scatter.2.cloned.1.call-update) | async-done | bytes 230416 | tf_op jit(solution)/shard_map/reduce_scatter | solution.py:117
  87.5 3.4 %collective-permute-start.6 = (bf16[1,128,320]{1,2,0:T(8,128)(2,1)S(1)}, bf16[1,128,320]{1,2,0:T(8,128)(2,1)S(1)}, u32[]{:S(2)}, u32[]{:S(2)}) collective-permute-start(bf16[1,128,320]{1,2,0:T(8,128)(2,1)S(1)} %get-tuple-element.26), channel_id=1, source_target_pairs={{0,8},{8,16},{16,24},{1,9},{9,17},{17,25},{2,10},{10,18},{18,26},{... | collective-permute-start | bytes 245768 | tf_op jit(solution)/shard_map/ppermute | solution.py:17
  93.8 4.8 %collective-permute-done.7 = bf16[1,128,320]{1,2,0:T(8,128)(2,1)S(1)} collective-permute-done((bf16[1,128,320]{1,2,0:T(8,128)(2,1)S(1)}, bf16[1,128,320]{1,2,0:T(8,128)(2,1)S(1)}, u32[]{:S(2)}, u32[]{:S(2)}) %collective-permute-start.7) | collective-permute-done | bytes 81952 | tf_op jit(solution)/shard_map/ppermute | solution.py:19
  100.9 1.7 pad_maximum_fusion
  102.6 1.8 copy.57
  117.1 7.1 %all-reduce.4.cloned.1.call-done = bf16[360,320]{0,1:T(8,128)(2,1)} async-done(((bf16[360,320]{0,1:T(8,128)(2,1)}), bf16[360,320]{0,1:T(8,128)(2,1)}) %all-reduce.4.cloned.1.call-update) | async-done | bytes 230416 | tf_op jit(solution)/shard_map/psum | solution.py:124
  124.2 2.3 %fusion.35 = (f32[360,320]{0,1:T(8,128)}, f32[360,320]{0,1:T(8,128)}) fusion(f32[360,320]{0,1:T(8,128)S(1)} %copy-done.11, f32[360,320]{0,1:T(8,128)} %param.14, bf16[360,320]{0,1:T(8,128)(2,1)} %all-reduce.4.cloned.1.call-done), kind=kLoop, calls=%fused_computation.65 | loop fusion | flops 1382400 | bytes 2073600 | tf_op jit(solution)/shard_map/div | solution.py:134
  126.5 27.0 %all-gather.3.cloned.1.call-done = bf16[8,360,320]{1,2,0:T(8,128)(2,1)} async-done(((bf16[1,360,320]{1,2,0:T(8,128)(2,1)}), bf16[8,360,320]{1,2,0:T(8,128)(2,1)}) %all-gather.3.cloned.1.call-update) | async-done | bytes 1843216 | tf_op jit(solution)/shard_map/all_gather | solution.py:62
  153.5 4.0 %copy.44 = bf16[8,360,320]{1,0,2:T(8,128)(2,1)} copy(bf16[8,360,320]{1,2,0:T(8,128)(2,1)} %all-gather.3.cloned.1.call-done) | data formatting | bytes 3686400 | tf_op jit(solution)/shard_map/all_gather | solution.py:62
  157.4 3.4 %reshape.284 = bf16[2880,320]{0,1:T(8,128)(2,1)S(1)} reshape(bf16[8,360,320]{1,0,2:T(8,128)(2,1)} %copy.44) | data formatting | bytes 3686400
  161.2 1.3 fusion.68
  166.1 1.4 fusion.81
  167.5 1.5 convolution_add_fusion.8
  173.0 1.6 collective-permute-start.8
  176.6 2.4 %collective-permute-start.9 = (f32[32]{0:T(128)S(1)}, f32[32]{0:T(128)S(1)}, u32[]{:S(2)}, u32[]{:S(2)}) collective-permute-start(f32[32]{0:T(128)S(1)} %add.198), channel_id=1, source_target_pairs={{0,16},{8,24},{16,0},{24,8},{1,17},{9,25},{17,1},{25,9},{2,18},{10... | collective-permute-start | bytes 392 | tf_op jit(solution)/shard_map/ppermute | solution.py:33
  179.0 1.8 collective-permute-start.11
  181.0 2.4 %collective-permute-done.11 = f32[32]{0:T(128)S(1)} collective-permute-done((f32[32]{0:T(128)S(1)}, f32[32]{0:T(128)S(1)}, u32[]{:S(2)}, u32[]{:S(2)}) %collective-permute-start.11) | collective-permute-done | bytes 160 | tf_op jit(solution)/shard_map/ppermute | solution.py:33
  (140 shorter events, 47.0 us)
Async XLA Ops:
  7.2 79.6 %reduce-scatter.2.cloned.1.call-start = ((), (), s32[]{:S(2)}) async-start(), calls=%async_computation.1 | async-start | bytes 2211840 | tf_op jit(solution)/shard_map/reduce_scatter | solution.py:117
  10.0 4.6 %collective-permute-start = (f32[32]{0:T(128)S(1)}, f32[32]{0:T(128)S(1)}, u32[]{:S(2)}, u32[]{:S(2)}) collective-permute-start(f32[32]{0:T(128)S(1)} %reduce_sum.51), channel_id=1, source_target_pairs={{0,8},{8,0},{16,24},{24,16},{1,9},{9,1},{17,25},{25,17},{2,10},{10... | collective-permute-start | bytes 392 | tf_op jit(solution)/shard_map/ppermute | solution.py:33
  13.3 4.3 %collective-permute-start.2 = (f32[32]{0:T(128)S(1)}, f32[32]{0:T(128)S(1)}, u32[]{:S(2)}, u32[]{:S(2)}) collective-permute-start(f32[32]{0:T(128)S(1)} %reduce_sum.54), channel_id=1, source_target_pairs={{0,8},{8,0},{16,24},{24,16},{1,9},{9,1},{17,25},{25,17},{2,10},{10... | collective-permute-start | bytes 392 | tf_op jit(solution)/shard_map/ppermute | solution.py:33
  14.6 4.9 %collective-permute-start.1 = (f32[32]{0:T(128)S(1)}, f32[32]{0:T(128)S(1)}, u32[]{:S(2)}, u32[]{:S(2)}) collective-permute-start(f32[32]{0:T(128)S(1)} %add.163), channel_id=1, source_target_pairs={{0,16},{8,24},{16,0},{24,8},{1,17},{9,25},{17,1},{25,9},{2,18},{10... | collective-permute-start | bytes 392 | tf_op jit(solution)/shard_map/ppermute | solution.py:33
  17.6 4.4 %collective-permute-start.3 = (f32[32]{0:T(128)S(1)}, f32[32]{0:T(128)S(1)}, u32[]{:S(2)}, u32[]{:S(2)}) collective-permute-start(f32[32]{0:T(128)S(1)} %add.165), channel_id=1, source_target_pairs={{0,16},{8,24},{16,0},{24,8},{1,17},{9,25},{17,1},{25,9},{2,18},{10... | collective-permute-start | bytes 392 | tf_op jit(solution)/shard_map/ppermute | solution.py:33
  23.7 5.8 %collective-permute-start.4 = (bf16[1,128,320]{1,2,0:T(8,128)(2,1)S(1)}, bf16[1,128,320]{1,2,0:T(8,128)(2,1)S(1)}, u32[]{:S(2)}, u32[]{:S(2)}) collective-permute-start(bf16[1,128,320]{1,2,0:T(8,128)(2,1)S(1)} %get-tuple-element.30), channel_id=1, source_target_pairs={{0,8},{8,16},{16,24},{1,9},{9,17},{17,25},{2,10},{10,18},{18,26},{... | collective-permute-start | bytes 245768 | tf_op jit(solution)/shard_map/ppermute | solution.py:17
  27.2 6.3 %collective-permute-start.5 = (bf16[1,128,320]{1,2,0:T(8,128)(2,1)S(1)}, bf16[1,128,320]{1,2,0:T(8,128)(2,1)S(1)}, u32[]{:S(2)}, u32[]{:S(2)}) collective-permute-start(bf16[1,128,320]{1,2,0:T(8,128)(2,1)S(1)} %get-tuple-element.31), channel_id=1, source_target_pairs={{8,0},{16,8},{24,16},{9,1},{17,9},{25,17},{10,2},{18,10},{26,18},{... | collective-permute-start | bytes 245768 | tf_op jit(solution)/shard_map/ppermute | solution.py:19
  34.0 4.2 %copy-start = (bf16[1,3,128,320]{2,3,1,0:T(8,128)(2,1)S(1)}, bf16[1,3,128,320]{2,3,1,0:T(8,128)(2,1)}, u32[]{:S(2)}) copy-start(bf16[1,3,128,320]{2,3,1,0:T(8,128)(2,1)} %param.9) | copy-start | bytes 737284
  34.0 4.2 %copy-start.10 = (bf16[1,3,128,320]{2,3,1,0:T(8,128)(2,1)S(1)}, bf16[1,3,128,320]{2,3,1,0:T(8,128)(2,1)}, u32[]{:S(2)}) copy-start(bf16[1,3,128,320]{2,3,1,0:T(8,128)(2,1)} %param.10) | copy-start | bytes 737284
  34.0 4.1 %copy-start.17 = (f32[320]{0:T(512)S(1)}, f32[320]{0:T(512)}, u32[]{:S(2)}) copy-start(f32[320]{0:T(512)} %param.12) | copy-start | bytes 3844
  34.0 4.1 %copy-start.18 = (f32[320]{0:T(512)S(1)}, f32[320]{0:T(512)}, u32[]{:S(2)}) copy-start(f32[320]{0:T(512)} %param.11) | copy-start | bytes 3844
  47.8 76.4 %all-reduce.4.cloned.1.call-start = ((), (), s32[]{:S(2)}) async-start(), calls=%async_computation.2 | async-start | bytes 491520 | tf_op jit(solution)/shard_map/psum | solution.py:124
  86.8 66.7 %all-gather.3.cloned.1.call-start = ((), (), s32[]{:S(2)}) async-start(), calls=%async_computation.3 | async-start | bytes 2211840 | tf_op jit(solution)/shard_map/all_gather | solution.py:62
  87.5 6.3 %collective-permute-start.6 = (bf16[1,128,320]{1,2,0:T(8,128)(2,1)S(1)}, bf16[1,128,320]{1,2,0:T(8,128)(2,1)S(1)}, u32[]{:S(2)}, u32[]{:S(2)}) collective-permute-start(bf16[1,128,320]{1,2,0:T(8,128)(2,1)S(1)} %get-tuple-element.26), channel_id=1, source_target_pairs={{0,8},{8,16},{16,24},{1,9},{9,17},{17,25},{2,10},{10,18},{18,26},{... | collective-permute-start | bytes 245768 | tf_op jit(solution)/shard_map/ppermute | solution.py:17
  90.9 7.7 %collective-permute-start.7 = (bf16[1,128,320]{1,2,0:T(8,128)(2,1)S(1)}, bf16[1,128,320]{1,2,0:T(8,128)(2,1)S(1)}, u32[]{:S(2)}, u32[]{:S(2)}) collective-permute-start(bf16[1,128,320]{1,2,0:T(8,128)(2,1)S(1)} %get-tuple-element.27), channel_id=1, source_target_pairs={{8,0},{16,8},{24,16},{9,1},{17,9},{25,17},{10,2},{18,10},{26,18},{... | collective-permute-start | bytes 245768 | tf_op jit(solution)/shard_map/ppermute | solution.py:19
  93.8 4.8 %copy-start.14 = (bf16[1,128,320]{1,2,0:T(8,128)(2,1)}, bf16[1,128,320]{1,2,0:T(8,128)(2,1)S(1)}, u32[]{:S(2)}) copy-start(bf16[1,128,320]{1,2,0:T(8,128)(2,1)S(1)} %collective-permute-done.6) | copy-start | bytes 245764
  113.0 11.2 %copy-start.11 = (f32[360,320]{0,1:T(8,128)S(1)}, f32[360,320]{0,1:T(8,128)}, u32[]{:S(2)}) copy-start(f32[360,320]{0,1:T(8,128)} %param.15) | copy-start | bytes 1382404
  161.2 2.1 %copy-start.7 = (bf16[3,128,320]{2,1,0:T(8,128)(2,1)S(1)}, bf16[3,128,320]{2,1,0:T(8,128)(2,1)}, u32[]{:S(2)}) copy-start(bf16[3,128,320]{2,1,0:T(8,128)(2,1)} %copy.46) | copy-start | bytes 737284
  166.1 2.9 %copy-start.5 = (bf16[3,128,320]{2,1,0:T(8,128)(2,1)S(1)}, bf16[3,128,320]{2,1,0:T(8,128)(2,1)}, u32[]{:S(2)}) copy-start(bf16[3,128,320]{2,1,0:T(8,128)(2,1)} %copy.58) | copy-start | bytes 737284
  166.1 3.3 %copy-start.4 = (bf16[3,128,320]{2,1,0:T(8,128)(2,1)S(1)}, bf16[3,128,320]{2,1,0:T(8,128)(2,1)}, u32[]{:S(2)}) copy-start(bf16[3,128,320]{2,1,0:T(8,128)(2,1)} %copy.59) | copy-start | bytes 737284
  173.0 3.6 %collective-permute-start.8 = (f32[32]{0:T(128)S(1)}, f32[32]{0:T(128)S(1)}, u32[]{:S(2)}, u32[]{:S(2)}) collective-permute-start(f32[32]{0:T(128)S(1)} %reduce_sum.72), channel_id=1, source_target_pairs={{0,8},{8,0},{16,24},{24,16},{1,9},{9,1},{17,25},{25,17},{2,10},{10... | collective-permute-start | bytes 392 | tf_op jit(solution)/shard_map/ppermute | solution.py:33
  174.7 4.3 %collective-permute-start.10 = (f32[32]{0:T(128)S(1)}, f32[32]{0:T(128)S(1)}, u32[]{:S(2)}, u32[]{:S(2)}) collective-permute-start(f32[32]{0:T(128)S(1)} %reduce_sum.75), channel_id=1, source_target_pairs={{0,8},{8,0},{16,24},{24,16},{1,9},{9,1},{17,25},{25,17},{2,10},{10... | collective-permute-start | bytes 392 | tf_op jit(solution)/shard_map/ppermute | solution.py:33
  176.6 4.4 %collective-permute-start.9 = (f32[32]{0:T(128)S(1)}, f32[32]{0:T(128)S(1)}, u32[]{:S(2)}, u32[]{:S(2)}) collective-permute-start(f32[32]{0:T(128)S(1)} %add.198), channel_id=1, source_target_pairs={{0,16},{8,24},{16,0},{24,8},{1,17},{9,25},{17,1},{25,9},{2,18},{10... | collective-permute-start | bytes 392 | tf_op jit(solution)/shard_map/ppermute | solution.py:33
  179.0 4.4 %collective-permute-start.11 = (f32[32]{0:T(128)S(1)}, f32[32]{0:T(128)S(1)}, u32[]{:S(2)}, u32[]{:S(2)}) collective-permute-start(f32[32]{0:T(128)S(1)} %add.200), channel_id=1, source_target_pairs={{0,16},{8,24},{16,0},{24,8},{1,17},{9,25},{17,1},{25,9},{2,18},{10... | collective-permute-start | bytes 392 | tf_op jit(solution)/shard_map/ppermute | solution.py:33
  (10 other events, 11.7 us)
Sparse Core Ops, SparseCore 0:
  47.9 38.8 reduce-scatter.1
  89.2 34.9 all-reduce.3
  126.1 27.3 all-gather.2

commit v2 on v1

--- a/solution.py
+++ b/solution.py
@@ -33,6 +33,45 @@
         parts = tuple(p + q for p, q in zip(parts, lax.ppermute(parts, axis, pairs)))
         step *= 2
     return parts
+
+
+def halving_scatter(partial, axis):
+    count = lax.axis_size(axis)
+    rows, channels = partial.shape[0] // count, partial.shape[1]
+    if count & (count - 1):
+        summed = lax.psum_scatter(
+            partial.astype(jnp.bfloat16).reshape(count, rows, channels),
+            axis,
+            scatter_dimension=0,
+            tiled=False,
+        )
+        return summed.astype(jnp.float32)
+    index = lax.axis_index(axis)
+    held = partial.reshape(count, rows, channels)
+    step = 1
+    while step < count:
+        bit = (index // step) % 2
+        paired = held.reshape(-1, 2, rows, channels)
+        keep = lax.dynamic_index_in_dim(paired, bit, axis=1, keepdims=False)
+        send = lax.dynamic_index_in_dim(paired, 1 - bit, axis=1, keepdims=False)
+        pairs = [(i, i ^ step) for i in range(count)]
+        got = lax.ppermute(send.astype(jnp.bfloat16), axis, pairs)
+        held = keep + got.astype(jnp.float32)
+        step *= 2
+    return held[0]
+
+
+def replicated_sum(value, axis):
+    count = lax.axis_size(axis)
+    if count & (count - 1):
+        return lax.psum(value.astype(jnp.bfloat16), axis).astype(jnp.float32)
+    step = 1
+    while step < count:
+        mine = value.astype(jnp.bfloat16)
+        pairs = [(i, i ^ step) for i in range(count)]
+        value = mine.astype(jnp.float32) + lax.ppermute(mine, axis, pairs).astype(jnp.float32)
+        step *= 2
+    return value
 
 
 def group_sum(values, groups):
@@ -113,15 +152,9 @@
     scaled = upstream.reshape(height_dev, width_dev, channels) * silu_slope * inside * norm_gain
     local_first = group_sum(scaled, GROUPS)
     local_second = group_sum(scaled * normed, GROUPS)
-    dp_size = lax.axis_size("dp")
-    grad_piece = lax.psum_scatter(
-        weight_terms.astype(jnp.bfloat16).reshape(dp_size, -1, channels),
-        "dp",
-        scatter_dimension=0,
-        tiled=False,
-    )
+    grad_piece = halving_scatter(weight_terms, "dp")
     sum_first, sum_second = space_sum((local_first, local_second), "space")
-    grad_piece = lax.psum(grad_piece, "space").astype(jnp.float32)
+    grad_piece = replicated_sum(grad_piece, "space")
     first = sum_first / cell_count
     second = sum_second / cell_count
     input_grad = (

time: 192 us -> 143 us (0.74)
  waiting for transfers between devices: 89.9 us -> 25.3 us
  other arithmetic: 10.2 us -> 17.1 us
  starting transfers between devices: 24 us -> 30.3 us
  local copies, waits for them, and re-layouts: 31.8 us -> 37.7 us
  matrix products: 20.2 us -> 15.3 us
    reduce_scatter x1 -> x0, waiting for transfers between devices: 38.9 us -> none  [local(): lax.psum_scatter(weight_terms.astype(jnp.bfloat16).reshape(dp_size, -1, c...]
    all_gather x1, waiting for transfers between devices: 27 us -> 0.01 us  [local(): gathered = lax.all_gather(weight, 'dp', axis=0, tiled=True)]
    ppermute x0 -> x5, waiting for transfers between devices: none -> 15.4 us  [the longest x3 10.2 us: halving_scatter(): got = lax.ppermute(send.astype(jnp.bfloat16), axis, pairs)]
    psum x1 -> x0, waiting for transfers between devices: 7.13 us -> none  [local(): grad_piece = lax.psum(grad_piece, 'space').astype(jnp.float32)]
    ppermute x0 -> x5, starting transfers between devices: none -> 7.01 us  [the longest x2 4.02 us: replicated_sum(): lax.ppermute(mine, axis, pairs).astype(jnp.float32)]
    dot_general x9, matrix products: 9.52 us -> 3.19 us  [local(): lax.dot_general(window, flat_cot, (((0,), (0,)), ((), ())), preferred_ele...]
    ppermute x2, waiting for transfers between devices: 8.87 us -> 4.03 us  [with_halo(): lax.ppermute(head, axis, [((i + 1) % count, i) for i in range(ends)])]
    unnamed x40 -> x63, local copies, waits for them, and re-layouts: 4.78 us -> 9.24 us
  transfers between devices with their start and end apart: 15 -> 18, of which waited for: 9 -> 8; matrix products, arithmetic and copies ran while one was open for 12% -> 24% of each run, Pallas kernels for 0% -> 0%
where the time goes in v2:
time: 143 us; the launch traced here: 142 us
  local copies, waits for them, and re-layouts  37.7 us (26%)
  starting transfers between devices  30.3 us (21%)
  waiting for transfers between devices  25.3 us (18%)
  other arithmetic  17.1 us (12%)
  between operations  16.2 us (11%)
  matrix products  15.3 us (11%)
    ppermute x8, starting transfers between devices, space_sum(): lax.ppermute(parts, axis, pairs)  13.6 us
    ppermute x3, waiting for transfers between devices, halving_scatter(): got = lax.ppermute(send.astype(jnp.bfloat16), axis, pairs)  10.2 us
    unnamed x63, local copies, waits for them, and re-layouts  9.24 us
    slice x9, local copies, waits for them, and re-layouts, local(): cot_pad[2 - row_off:2 - row_off + height_dev, 2 - col_off:2 - col_off + w...  7.48 us
    dot_general x9, matrix products, local(): lax.dot_general(cot_window, tap_weights[tap_index], (((1,), (1,)), ((), (...  6.96 us
    ppermute x2, starting transfers between devices, with_halo(): lax.ppermute(tail, axis, [(i, (i + 1) % count) for i in range(ends)])  6.87 us
    ppermute x8, waiting for transfers between devices, space_sum(): lax.ppermute(parts, axis, pairs)  5.86 us
    slice x9, local copies, waits for them, and re-layouts, local(): act_pad[row_off:row_off + height_dev, col_off:col_off + width_dev]  5.62 us
  transfers between devices with their start and end apart: 18, of which 8 were waited for; matrix products, arithmetic and copies ran while one was open for 24% of the time, Pallas kernels for 0%

profile of v2, /device:TPU:0, one launch (start us, length us, event | category | flops | bytes accessed | tf_op | source)
XLA Modules:
  0.0 141.9 jit_solution(9379928919204207706)
XLA Ops:
  10.0 3.1 %collective-permute-start = (f32[32]{0:T(128)S(1)}, f32[32]{0:T(128)S(1)}, u32[]{:S(2)}, u32[]{:S(2)}) collective-permute-start(f32[32]{0:T(128)S(1)} %reduce_sum.51), channel_id=1, source_target_pairs={{0,8},{8,0},{16,24},{24,16},{1,9},{9,1},{17,25},{25,17},{2,10},{10... | collective-permute-start | bytes 392 | tf_op jit(solution)/shard_map/ppermute | solution.py:33
  14.6 3.0 %collective-permute-start.1 = (f32[32]{0:T(128)S(1)}, f32[32]{0:T(128)S(1)}, u32[]{:S(2)}, u32[]{:S(2)}) collective-permute-start(f32[32]{0:T(128)S(1)} %add.211), channel_id=1, source_target_pairs={{0,16},{8,24},{16,0},{24,8},{1,17},{9,25},{17,1},{25,9},{2,18},{10... | collective-permute-start | bytes 392 | tf_op jit(solution)/shard_map/ppermute | solution.py:33
  17.6 1.9 %collective-permute-start.3 = (f32[32]{0:T(128)S(1)}, f32[32]{0:T(128)S(1)}, u32[]{:S(2)}, u32[]{:S(2)}) collective-permute-start(f32[32]{0:T(128)S(1)} %add.213), channel_id=1, source_target_pairs={{0,16},{8,24},{16,0},{24,8},{1,17},{9,25},{17,1},{25,9},{2,18},{10... | collective-permute-start | bytes 392 | tf_op jit(solution)/shard_map/ppermute | solution.py:33
  19.5 2.6 %collective-permute-done.3 = f32[32]{0:T(128)S(1)} collective-permute-done((f32[32]{0:T(128)S(1)}, f32[32]{0:T(128)S(1)}, u32[]{:S(2)}, u32[]{:S(2)}) %collective-permute-start.3) | collective-permute-done | bytes 160 | tf_op jit(solution)/shard_map/ppermute | solution.py:33
  23.8 3.5 %collective-permute-start.4 = (bf16[1,128,320]{1,2,0:T(8,128)(2,1)S(1)}, bf16[1,128,320]{1,2,0:T(8,128)(2,1)S(1)}, u32[]{:S(2)}, u32[]{:S(2)}) collective-permute-start(bf16[1,128,320]{1,2,0:T(8,128)(2,1)S(1)} %get-tuple-element.30), channel_id=1, source_target_pairs={{0,8},{8,16},{16,24},{1,9},{9,17},{17,25},{2,10},{10,18},{18,26},{... | collective-permute-start | bytes 245768 | tf_op jit(solution)/shard_map/ppermute | solution.py:17
  29.6 4.0 %collective-permute-done.5 = bf16[1,128,320]{1,2,0:T(8,128)(2,1)S(1)} collective-permute-done((bf16[1,128,320]{1,2,0:T(8,128)(2,1)S(1)}, bf16[1,128,320]{1,2,0:T(8,128)(2,1)S(1)}, u32[]{:S(2)}, u32[]{:S(2)}) %collective-permute-start.5) | collective-permute-done | bytes 81952 | tf_op jit(solution)/shard_map/ppermute | solution.py:19
  37.3 2.0 %copy-done.2 = f32[9,320,320]{2,1,0:T(8,128)} copy-done((f32[9,320,320]{2,1,0:T(8,128)}, f32[9,320,320]{2,1,0:T(8,128)S(1)}, u32[]{:S(2)}) %copy-start.2) | copy-done | bytes 3686424
  41.0 1.8 %constant_dynamic-slice_fusion.1 = f32[4,1,360,320]{3,2,1,0:T(8,128)S(1)} fusion(f32[4,2,360,320]{3,2,1,0:T(8,128)} %bitcast.153, s32[]{:T(128)S(6)} %select_n.45), kind=kLoop, calls=%fused_computation.133 | loop fusion | bytes 3686404 | tf_op jit(solution)/shard_map/jit(dynamic_index_in_dim)/dynamic_slice | solution.py:55
  42.8 1.8 %copy.68 = f32[4,1,360,320]{2,3,0,1:T(8,128)} copy(f32[4,1,360,320]{3,2,1,0:T(8,128)S(1)} %constant_dynamic-slice_fusion.1) | data formatting | bytes 3686400 | tf_op jit(solution)/shard_map/jit(dynamic_index_in_dim)/dynamic_slice | solution.py:55
  44.6 2.0 %bitcast_add_fusion = f32[4,360,320]{1,2,0:T(8,128)S(1)} fusion(f32[4,1,360,320]{2,3,0,1:T(8,128)} %copy.68, bf16[4,360,320]{1,2,0:T(8,128)(2,1)} %collective-permute-done.12), kind=kLoop, calls=%fused_computation.2 | loop fusion | flops 921600 | bytes 4608000 | tf_op jit(solution)/shard_map/add | solution.py:59
  49.6 3.4 %collective-permute-start.6 = (bf16[1,128,320]{1,2,0:T(8,128)(2,1)}, bf16[1,128,320]{1,2,0:T(8,128)(2,1)}, u32[]{:S(2)}, u32[]{:S(2)}) collective-permute-start(bf16[1,128,320]{1,2,0:T(8,128)(2,1)} %get-tuple-element.26), channel_id=1, source_target_pairs={{0,8},{8,16},{16,24},{1,9},{9,17},{17,25},{2,10},{10,18},{18,26},{... | collective-permute-start | bytes 245768 | tf_op jit(solution)/shard_map/ppermute | solution.py:17
  53.0 1.5 %collective-permute-start.7 = (bf16[1,128,320]{1,2,0:T(8,128)(2,1)}, bf16[1,128,320]{1,2,0:T(8,128)(2,1)}, u32[]{:S(2)}, u32[]{:S(2)}) collective-permute-start(bf16[1,128,320]{1,2,0:T(8,128)(2,1)} %get-tuple-element.27), channel_id=1, source_target_pairs={{8,0},{16,8},{24,16},{9,1},{17,9},{25,17},{10,2},{18,10},{26,18},{... | collective-permute-start | bytes 245768 | tf_op jit(solution)/shard_map/ppermute | solution.py:19
  56.2 6.9 %collective-permute-done.13 = bf16[2,360,320]{1,2,0:T(8,128)(2,1)} collective-permute-done((bf16[2,360,320]{1,2,0:T(8,128)(2,1)}, bf16[2,360,320]{1,2,0:T(8,128)(2,1)}, u32[]{:S(2)}, u32[]{:S(2)}) %collective-permute-start.13) | collective-permute-done | bytes 460832 | tf_op jit(solution)/shard_map/ppermute | solution.py:58
  65.2 1.5 %collective-permute-start.14 = (bf16[1,360,320]{1,2,0:T(8,128)(2,1)S(1)}, bf16[1,360,320]{1,2,0:T(8,128)(2,1)}, u32[]{:S(2)}, u32[]{:S(2)}) collective-permute-start(bf16[1,360,320]{1,2,0:T(8,128)(2,1)S(1)} %dynamic-slice_convert_fusion.1), channel_id=1, source_target_pairs={{0,4},{1,5},{2,6},{3,7},{4,0},{5,1},{6,2},{7,3},{8,12},{9,13},{10,... | collective-permute-start | bytes 691208 | tf_op jit(solution)/shard_map/ppermute | solution.py:58
  70.2 3.3 %collective-permute-done.14 = bf16[1,360,320]{1,2,0:T(8,128)(2,1)} collective-permute-done((bf16[1,360,320]{1,2,0:T(8,128)(2,1)S(1)}, bf16[1,360,320]{1,2,0:T(8,128)(2,1)}, u32[]{:S(2)}, u32[]{:S(2)}) %collective-permute-start.14) | collective-permute-done | bytes 230432 | tf_op jit(solution)/shard_map/ppermute | solution.py:58
  74.5 1.6 %collective-permute-start.15 = (bf16[360,320]{0,1:T(8,128)(2,1)S(1)}, bf16[360,320]{0,1:T(8,128)(2,1)}, u32[]{:S(2)}, u32[]{:S(2)}) collective-permute-start(bf16[360,320]{0,1:T(8,128)(2,1)S(1)} %fusion.32), channel_id=1, source_target_pairs={{0,8},{8,0},{16,24},{24,16},{1,9},{9,1},{17,25},{25,17},{2,10},{10... | collective-permute-start | bytes 691208 | tf_op jit(solution)/shard_map/ppermute | solution.py:72
  85.5 2.5 %collective-permute-start.16 = (bf16[360,320]{0,1:T(8,128)(2,1)S(1)}, bf16[360,320]{0,1:T(8,128)(2,1)}, u32[]{:S(2)}, u32[]{:S(2)}) collective-permute-start(bf16[360,320]{0,1:T(8,128)(2,1)S(1)} %add_convert_fusion), channel_id=1, source_target_pairs={{0,16},{8,24},{16,0},{24,8},{1,17},{9,25},{17,1},{25,9},{2,18},{10... | collective-permute-start | bytes 691208 | tf_op jit(solution)/shard_map/ppermute | solution.py:72
  93.7 5.2 %collective-permute-done.16 = bf16[360,320]{0,1:T(8,128)(2,1)} collective-permute-done((bf16[360,320]{0,1:T(8,128)(2,1)S(1)}, bf16[360,320]{0,1:T(8,128)(2,1)}, u32[]{:S(2)}, u32[]{:S(2)}) %collective-permute-start.16) | collective-permute-done | bytes 230432 | tf_op jit(solution)/shard_map/ppermute | solution.py:72
  98.9 2.4 %fusion.17 = (f32[360,320]{0,1:T(8,128)}, f32[360,320]{0,1:T(8,128)}) fusion(f32[360,320]{0,1:T(8,128)S(1)} %copy-done.23, f32[360,320]{0,1:T(8,128)} %param.14, bf16[360,320]{0,1:T(8,128)(2,1)} %collective-permute-done.16, bf16[360,320]{0,1:T(8,128)(2,1)S(1)} %add_convert_fusion), kind=kLoop, calls=%fused_computation.51 | loop fusion | flops 1612800 | bytes 2304000 | tf_op jit(solution)/shard_map/div | solution.py:167
  101.3 4.0 %copy.44 = bf16[8,360,320]{1,0,2:T(8,128)(2,1)} copy(bf16[8,360,320]{1,2,0:T(8,128)(2,1)} %all-gather.3.cloned.1.call-done) | data formatting | bytes 3686400 | tf_op jit(solution)/shard_map/all_gather | solution.py:101
  105.3 3.4 %reshape.294 = bf16[2880,320]{0,1:T(8,128)(2,1)S(1)} reshape(bf16[8,360,320]{1,0,2:T(8,128)(2,1)} %copy.44) | data formatting | bytes 3686400
  116.9 1.5 %convolution_add_fusion.8 = f32[384,320]{0,1:T(8,128)S(1)} fusion(f32[384,320]{0,1:T(8,128)S(1)} %fusion.65, bf16[384,320]{1,0:T(8,128)(2,1)} %bitcast.163, bf16[2880,320]{0,1:T(8,128)(2,1)S(1)} %reshape.294), kind=kOutput, calls=%fused_computation.32 | convolution fusion | flops 78766080 | bytes 1474560 | tf_op jit(solution)/shard_map/dot_general | solution.py:143
  124.4 2.1 %collective-permute-start.10 = (f32[32]{0:T(128)S(1)}, f32[32]{0:T(128)S(1)}, u32[]{:S(2)}, u32[]{:S(2)}) collective-permute-start(f32[32]{0:T(128)S(1)} %reduce_sum.75), channel_id=1, source_target_pairs={{0,8},{8,0},{16,24},{24,16},{1,9},{9,1},{17,25},{25,17},{2,10},{10... | collective-permute-start | bytes 392 | tf_op jit(solution)/shard_map/ppermute | solution.py:33
  129.0 2.2 %collective-permute-start.11 = (f32[32]{0:T(128)S(1)}, f32[32]{0:T(128)S(1)}, u32[]{:S(2)}, u32[]{:S(2)}) collective-permute-start(f32[32]{0:T(128)S(1)} %add.248), channel_id=1, source_target_pairs={{0,16},{8,24},{16,0},{24,8},{1,17},{9,25},{17,1},{25,9},{2,18},{10... | collective-permute-start | bytes 392 | tf_op jit(solution)/shard_map/ppermute | solution.py:33
  (175 shorter events, 58.6 us)
Async XLA Ops:
  7.2 94.1 %all-gather.3.cloned.1.call-start = ((), (), s32[]{:S(2)}) async-start(), calls=%async_computation | async-start | bytes 2211840 | tf_op jit(solution)/shard_map/all_gather | solution.py:101
  8.5 11.0 %copy-start.29 = (pred[3]{0:T(512)(128)(4,1)}, pred[3]{0:T(512)(128)(4,1)S(1)}, u32[]{:S(2)}) copy-start(pred[3]{0:T(512)(128)(4,1)S(1)} %add_compare_fusion) | copy-start | bytes 13
  10.0 4.6 %collective-permute-start = (f32[32]{0:T(128)S(1)}, f32[32]{0:T(128)S(1)}, u32[]{:S(2)}, u32[]{:S(2)}) collective-permute-start(f32[32]{0:T(128)S(1)} %reduce_sum.51), channel_id=1, source_target_pairs={{0,8},{8,0},{16,24},{24,16},{1,9},{9,1},{17,25},{25,17},{2,10},{10... | collective-permute-start | bytes 392 | tf_op jit(solution)/shard_map/ppermute | solution.py:33
  13.3 4.3 %collective-permute-start.2 = (f32[32]{0:T(128)S(1)}, f32[32]{0:T(128)S(1)}, u32[]{:S(2)}, u32[]{:S(2)}) collective-permute-start(f32[32]{0:T(128)S(1)} %reduce_sum.54), channel_id=1, source_target_pairs={{0,8},{8,0},{16,24},{24,16},{1,9},{9,1},{17,25},{25,17},{2,10},{10... | collective-permute-start | bytes 392 | tf_op jit(solution)/shard_map/ppermute | solution.py:33
  14.6 4.9 %collective-permute-start.1 = (f32[32]{0:T(128)S(1)}, f32[32]{0:T(128)S(1)}, u32[]{:S(2)}, u32[]{:S(2)}) collective-permute-start(f32[32]{0:T(128)S(1)} %add.211), channel_id=1, source_target_pairs={{0,16},{8,24},{16,0},{24,8},{1,17},{9,25},{17,1},{25,9},{2,18},{10... | collective-permute-start | bytes 392 | tf_op jit(solution)/shard_map/ppermute | solution.py:33
  17.6 4.4 %collective-permute-start.3 = (f32[32]{0:T(128)S(1)}, f32[32]{0:T(128)S(1)}, u32[]{:S(2)}, u32[]{:S(2)}) collective-permute-start(f32[32]{0:T(128)S(1)} %add.213), channel_id=1, source_target_pairs={{0,16},{8,24},{16,0},{24,8},{1,17},{9,25},{17,1},{25,9},{2,18},{10... | collective-permute-start | bytes 392 | tf_op jit(solution)/shard_map/ppermute | solution.py:33
  23.8 5.8 %collective-permute-start.4 = (bf16[1,128,320]{1,2,0:T(8,128)(2,1)S(1)}, bf16[1,128,320]{1,2,0:T(8,128)(2,1)S(1)}, u32[]{:S(2)}, u32[]{:S(2)}) collective-permute-start(bf16[1,128,320]{1,2,0:T(8,128)(2,1)S(1)} %get-tuple-element.30), channel_id=1, source_target_pairs={{0,8},{8,16},{16,24},{1,9},{9,17},{17,25},{2,10},{10,18},{18,26},{... | collective-permute-start | bytes 245768 | tf_op jit(solution)/shard_map/ppermute | solution.py:17
  27.3 6.3 %collective-permute-start.5 = (bf16[1,128,320]{1,2,0:T(8,128)(2,1)S(1)}, bf16[1,128,320]{1,2,0:T(8,128)(2,1)S(1)}, u32[]{:S(2)}, u32[]{:S(2)}) collective-permute-start(bf16[1,128,320]{1,2,0:T(8,128)(2,1)S(1)} %get-tuple-element.31), channel_id=1, source_target_pairs={{8,0},{16,8},{24,16},{9,1},{17,9},{25,17},{10,2},{18,10},{26,18},{... | collective-permute-start | bytes 245768 | tf_op jit(solution)/shard_map/ppermute | solution.py:19
  40.9 3.7 %collective-permute-start.12 = (bf16[4,360,320]{1,2,0:T(8,128)(2,1)}, bf16[4,360,320]{1,2,0:T(8,128)(2,1)}, u32[]{:S(2)}, u32[]{:S(2)}) collective-permute-start(bf16[4,360,320]{1,2,0:T(8,128)(2,1)} %bitcast.120), channel_id=1, source_target_pairs={{0,1},{1,0},{2,3},{3,2},{4,5},{5,4},{6,7},{7,6},{8,9},{9,8},{10,11... | collective-permute-start | bytes 2764808 | tf_op jit(solution)/shard_map/ppermute | solution.py:58
  44.6 9.9 %copy-start.18 = (bf16[1,3,128,320]{2,3,1,0:T(8,128)(2,1)S(1)}, bf16[1,3,128,320]{2,3,1,0:T(8,128)(2,1)}, u32[]{:S(2)}) copy-start(bf16[1,3,128,320]{2,3,1,0:T(8,128)(2,1)} %param.10) | copy-start | bytes 737284
  47.5 15.6 %collective-permute-start.13 = (bf16[2,360,320]{1,2,0:T(8,128)(2,1)}, bf16[2,360,320]{1,2,0:T(8,128)(2,1)}, u32[]{:S(2)}, u32[]{:S(2)}) collective-permute-start(bf16[2,360,320]{1,2,0:T(8,128)(2,1)} %fusion.18), channel_id=1, source_target_pairs={{0,2},{1,3},{2,0},{3,1},{4,6},{5,7},{6,4},{7,5},{8,10},{9,11},{10,... | collective-permute-start | bytes 1382408 | tf_op jit(solution)/shard_map/ppermute | solution.py:58
  49.6 19.2 %collective-permute-start.6 = (bf16[1,128,320]{1,2,0:T(8,128)(2,1)}, bf16[1,128,320]{1,2,0:T(8,128)(2,1)}, u32[]{:S(2)}, u32[]{:S(2)}) collective-permute-start(bf16[1,128,320]{1,2,0:T(8,128)(2,1)} %get-tuple-element.26), channel_id=1, source_target_pairs={{0,8},{8,16},{16,24},{1,9},{9,17},{17,25},{2,10},{10,18},{18,26},{... | collective-permute-start | bytes 245768 | tf_op jit(solution)/shard_map/ppermute | solution.py:17
  53.0 15.8 %collective-permute-start.7 = (bf16[1,128,320]{1,2,0:T(8,128)(2,1)}, bf16[1,128,320]{1,2,0:T(8,128)(2,1)}, u32[]{:S(2)}, u32[]{:S(2)}) collective-permute-start(bf16[1,128,320]{1,2,0:T(8,128)(2,1)} %get-tuple-element.27), channel_id=1, source_target_pairs={{8,0},{16,8},{24,16},{9,1},{17,9},{25,17},{10,2},{18,10},{26,18},{... | collective-permute-start | bytes 245768 | tf_op jit(solution)/shard_map/ppermute | solution.py:19
  55.4 12.2 %copy-start.1 = (bf16[1,3,128,320]{2,3,1,0:T(8,128)(2,1)S(1)}, bf16[1,3,128,320]{2,3,1,0:T(8,128)(2,1)}, u32[]{:S(2)}) copy-start(bf16[1,3,128,320]{2,3,1,0:T(8,128)(2,1)} %param.9) | copy-start | bytes 737284
  55.4 11.3 %copy-start.6 = (bf16[1,3,128,320]{3,2,1,0:T(8,128)(2,1)S(1)}, bf16[1,3,128,320]{3,2,1,0:T(8,128)(2,1)}, u32[]{:S(2)}) copy-start(bf16[1,3,128,320]{3,2,1,0:T(8,128)(2,1)} %copy.60) | copy-start | bytes 737284
  65.2 8.3 %collective-permute-start.14 = (bf16[1,360,320]{1,2,0:T(8,128)(2,1)S(1)}, bf16[1,360,320]{1,2,0:T(8,128)(2,1)}, u32[]{:S(2)}, u32[]{:S(2)}) collective-permute-start(bf16[1,360,320]{1,2,0:T(8,128)(2,1)S(1)} %dynamic-slice_convert_fusion.1), channel_id=1, source_target_pairs={{0,4},{1,5},{2,6},{3,7},{4,0},{5,1},{6,2},{7,3},{8,12},{9,13},{10,... | collective-permute-start | bytes 691208 | tf_op jit(solution)/shard_map/ppermute | solution.py:58
  74.5 10.0 %collective-permute-start.15 = (bf16[360,320]{0,1:T(8,128)(2,1)S(1)}, bf16[360,320]{0,1:T(8,128)(2,1)}, u32[]{:S(2)}, u32[]{:S(2)}) collective-permute-start(bf16[360,320]{0,1:T(8,128)(2,1)S(1)} %fusion.32), channel_id=1, source_target_pairs={{0,8},{8,0},{16,24},{24,16},{1,9},{9,1},{17,25},{25,17},{2,10},{10... | collective-permute-start | bytes 691208 | tf_op jit(solution)/shard_map/ppermute | solution.py:72
  85.5 13.4 %collective-permute-start.16 = (bf16[360,320]{0,1:T(8,128)(2,1)S(1)}, bf16[360,320]{0,1:T(8,128)(2,1)}, u32[]{:S(2)}, u32[]{:S(2)}) collective-permute-start(bf16[360,320]{0,1:T(8,128)(2,1)S(1)} %add_convert_fusion), channel_id=1, source_target_pairs={{0,16},{8,24},{16,0},{24,8},{1,17},{9,25},{17,1},{25,9},{2,18},{10... | collective-permute-start | bytes 691208 | tf_op jit(solution)/shard_map/ppermute | solution.py:72
  88.7 10.2 %copy-start.23 = (f32[360,320]{0,1:T(8,128)S(1)}, f32[360,320]{0,1:T(8,128)}, u32[]{:S(2)}) copy-start(f32[360,320]{0,1:T(8,128)} %param.15) | copy-start | bytes 1382404
  123.8 10.0 %copy-start.5 = (f32[1,3,128,320]{2,3,1,0:T(8,128)S(1)}, f32[1,3,128,320]{2,3,1,0:T(8,128)}, u32[]{:S(2)}) copy-start(f32[1,3,128,320]{2,3,1,0:T(8,128)} %copy.55) | copy-start | bytes 1474564
  124.1 3.6 %collective-permute-start.8 = (f32[32]{0:T(128)S(1)}, f32[32]{0:T(128)S(1)}, u32[]{:S(2)}, u32[]{:S(2)}) collective-permute-start(f32[32]{0:T(128)S(1)} %reduce_sum.72), channel_id=1, source_target_pairs={{0,8},{8,0},{16,24},{24,16},{1,9},{9,1},{17,25},{25,17},{2,10},{10... | collective-permute-start | bytes 392 | tf_op jit(solution)/shard_map/ppermute | solution.py:33
  124.4 4.6 %collective-permute-start.10 = (f32[32]{0:T(128)S(1)}, f32[32]{0:T(128)S(1)}, u32[]{:S(2)}, u32[]{:S(2)}) collective-permute-start(f32[32]{0:T(128)S(1)} %reduce_sum.75), channel_id=1, source_target_pairs={{0,8},{8,0},{16,24},{24,16},{1,9},{9,1},{17,25},{25,17},{2,10},{10... | collective-permute-start | bytes 392 | tf_op jit(solution)/shard_map/ppermute | solution.py:33
  127.7 4.5 %collective-permute-start.9 = (f32[32]{0:T(128)S(1)}, f32[32]{0:T(128)S(1)}, u32[]{:S(2)}, u32[]{:S(2)}) collective-permute-start(f32[32]{0:T(128)S(1)} %add.246), channel_id=1, source_target_pairs={{0,16},{8,24},{16,0},{24,8},{1,17},{9,25},{17,1},{25,9},{2,18},{10... | collective-permute-start | bytes 392 | tf_op jit(solution)/shard_map/ppermute | solution.py:33
  129.0 4.4 %collective-permute-start.11 = (f32[32]{0:T(128)S(1)}, f32[32]{0:T(128)S(1)}, u32[]{:S(2)}, u32[]{:S(2)}) collective-permute-start(f32[32]{0:T(128)S(1)} %add.248), channel_id=1, source_target_pairs={{0,16},{8,24},{16,0},{24,8},{1,17},{9,25},{17,1},{25,9},{2,18},{10... | collective-permute-start | bytes 392 | tf_op jit(solution)/shard_map/ppermute | solution.py:33
  (24 other events, 53.6 us)
Sparse Core Ops, SparseCore 0:
  41.1 28.9 all-gather.2

commit v3 on v2

--- a/solution.py
+++ b/solution.py
@@ -25,14 +25,16 @@
 
 def space_sum(parts, axis):
     count = lax.axis_size(axis)
-    if count & (count - 1):
+    if count > 4:
         return lax.psum(parts, axis)
-    step = 1
-    while step < count:
-        pairs = [(i, i ^ step) for i in range(count)]
-        parts = tuple(p + q for p, q in zip(parts, lax.ppermute(parts, axis, pairs)))
-        step *= 2
-    return parts
+    joined = jnp.stack(parts)
+    shifted = [
+        lax.ppermute(joined, axis, [(i, (i + shift) % count) for i in range(count)])
+        for shift in range(1, count)
+    ]
+    for got in shifted:
+        joined = joined + got
+    return tuple(joined)
 
 
 def halving_scatter(partial, axis):
@@ -111,42 +113,32 @@
     before = normed * norm_gain + norm_bias
     activated = (jax.nn.silu(before) * inside).astype(jnp.bfloat16)
     act_pad = pad_columns(with_halo(activated, (("space", 0),), 1))
-    output = jnp.zeros((height_dev * width_dev, channels), jnp.float32)
-    for row_off in range(3):
-        for col_off in range(3):
-            window = act_pad[row_off : row_off + height_dev, col_off : col_off + width_dev].reshape(
-                -1, channels
-            )
-            output = output + jnp.dot(
-                window, tap_weights[row_off * 3 + col_off], preferred_element_type=jnp.float32
-            )
+    act_cols = jnp.concatenate(
+        [
+            act_pad[row_off : row_off + height_dev, col_off : col_off + width_dev]
+            for row_off in range(3)
+            for col_off in range(3)
+        ],
+        axis=-1,
+    ).reshape(height_dev * width_dev, 9 * channels)
+    output = jnp.dot(act_cols, gathered, preferred_element_type=jnp.float32)
     block_out = (output.reshape(height_dev, width_dev, channels) * inside).astype(jnp.bfloat16)
     masked = cotangent[0] * inside.astype(jnp.bfloat16)
     cot_pad = pad_columns(with_halo(masked, (("space", 0),), 1))
     flat_cot = masked.reshape(-1, channels)
-    upstream = jnp.zeros((height_dev * width_dev, channels), jnp.float32)
-    tap_grads = []
-    for row_off in range(3):
-        for col_off in range(3):
-            tap_index = row_off * 3 + col_off
-            window = act_pad[row_off : row_off + height_dev, col_off : col_off + width_dev].reshape(
-                -1, channels
-            )
-            tap_grads.append(
-                lax.dot_general(
-                    window, flat_cot, (((0,), (0,)), ((), ())), preferred_element_type=jnp.float32
-                )
-            )
-            cot_window = cot_pad[
-                2 - row_off : 2 - row_off + height_dev, 2 - col_off : 2 - col_off + width_dev
-            ].reshape(-1, channels)
-            upstream = upstream + lax.dot_general(
-                cot_window,
-                tap_weights[tap_index],
-                (((1,), (1,)), ((), ())),
-                preferred_element_type=jnp.float32,
-            )
-    weight_terms = jnp.stack(tap_grads).reshape(9 * channels, channels)
+    weight_terms = lax.dot_general(
+        act_cols, flat_cot, (((0,), (0,)), ((), ())), preferred_element_type=jnp.float32
+    )
+    cot_cols = jnp.concatenate(
+        [
+            cot_pad[2 - row_off : 2 - row_off + height_dev, 2 - col_off : 2 - col_off + width_dev]
+            for row_off in range(3)
+            for col_off in range(3)
+        ],
+        axis=-1,
+    ).reshape(height_dev * width_dev, 9 * channels)
+    flipped = tap_weights.transpose(0, 2, 1).reshape(9 * channels, channels)
+    upstream = jnp.dot(cot_cols, flipped, preferred_element_type=jnp.float32)
     gate_sig = jax.nn.sigmoid(before)
     silu_slope = gate_sig * (1.0 + before * (1.0 - gate_sig))
     scaled = upstream.reshape(height_dev, width_dev, channels) * silu_slope * inside * norm_gain

time: 143 us -> 136 us (0.951)
  waiting for transfers between devices: 25.3 us -> 41.8 us
  local copies, waits for them, and re-layouts: 37.7 us -> 28.4 us
  matrix products: 15.3 us -> 8.34 us
  other arithmetic: 17.1 us -> 11.4 us
    slice x18 -> x0, local copies, waits for them, and re-layouts: 13.1 us -> none  [the longest x9 7.48 us: local(): cot_pad[2 - row_off:2 - row_off + height_dev, 2 - col_off:2 - col_off + w...]
    ppermute x3, waiting for transfers between devices: 10.2 us -> 20.1 us  [halving_scatter(): got = lax.ppermute(send.astype(jnp.bfloat16), axis, pairs)]
    dot_general x27 -> x3, matrix products: 15.3 us -> 8.34 us  [the longest x1 3.77 us: local(): upstream = jnp.dot(cot_cols, flipped, preferred_element_type=jnp.float32)]
    all_gather x1, waiting for transfers between devices: 0.01 us -> 6.2 us  [local(): gathered = lax.all_gather(weight, 'dp', axis=0, tiled=True)]
    ppermute x2, waiting for transfers between devices: 4.03 us -> 0.06 us  [with_halo(): lax.ppermute(head, axis, [((i + 1) % count, i) for i in range(ends)])]
    dynamic_slice x3 -> x0, local copies, waits for them, and re-layouts: 3.74 us -> none  [the longest x2 3.62 us: halving_scatter(): keep = lax.dynamic_index_in_dim(paired, bit, axis=1, keepdims=False)]
    concatenate x0 -> x3, local copies, waits for them, and re-layouts: none -> 3.66 us  [the longest x2 2.93 us: local(): jnp.concatenate([act_pad[row_off:row_off + height_dev, col_off:col_off +...]
    convert_element_type x3 -> x0, other arithmetic: 3.31 us -> none  [the longest x1 1.28 us: local(): input_grad = (spread_groups(inverse, channels) * (scaled - spread_groups(...]
  transfers between devices with their start and end apart: 18 -> 16, of which waited for: 8 -> 10; matrix products, arithmetic and copies ran while one was open for 24% -> 16% of each run, Pallas kernels for 0% -> 0%
where the time goes in v3:
time: 136 us; the launch traced here: 135 us
  waiting for transfers between devices  41.8 us (31%)
  starting transfers between devices  29.7 us (22%)
  local copies, waits for them, and re-layouts  28.4 us (21%)
  between operations  15.8 us (12%)
  other arithmetic  11.4 us (8%)
  matrix products  8.34 us (6%)
    ppermute x3, waiting for transfers between devices, halving_scatter(): got = lax.ppermute(send.astype(jnp.bfloat16), axis, pairs)  20.1 us
    unnamed x34, local copies, waits for them, and re-layouts  12.3 us
    ppermute x6, starting transfers between devices, space_sum(): lax.ppermute(joined, axis, [(i, (i + shift) % count) for i in range(count)])  10.6 us
    ppermute x2, starting transfers between devices, with_halo(): lax.ppermute(tail, axis, [(i, (i + 1) % count) for i in range(ends)])  9.74 us
    ppermute x2, waiting for transfers between devices, replicated_sum(): lax.ppermute(mine, axis, pairs).astype(jnp.float32)  7.4 us
    all_gather x1, waiting for transfers between devices, local(): gathered = lax.all_gather(weight, 'dp', axis=0, tiled=True)  6.2 us
    all_gather x2, local copies, waits for them, and re-layouts, local(): gathered = lax.all_gather(weight, 'dp', axis=0, tiled=True)  5.43 us
    ppermute x6, waiting for transfers between devices, space_sum(): lax.ppermute(joined, axis, [(i, (i + shift) % count) for i in range(count)])  4.27 us
  transfers between devices with their start and end apart: 16, of which 10 were waited for; matrix products, arithmetic and copies ran while one was open for 16% of the time, Pallas kernels for 0%

profile of v3, /device:TPU:0, one launch (start us, length us, event | category | flops | bytes accessed | tf_op | source)
XLA Modules:
  0.0 135.3 jit_solution(5435813915890611269)
XLA Ops:
  10.9 5.1 %collective-permute-start.2 = (f32[2,32]{1,0:T(2,128)S(1)}, f32[2,32]{1,0:T(2,128)S(1)}, u32[]{:S(2)}, u32[]{:S(2)}) collective-permute-start(f32[2,32]{1,0:T(2,128)S(1)} %pad_maximum_fusion.4), channel_id=1, source_target_pairs={{0,24},{8,0},{16,8},{24,16},{1,25},{9,1},{17,9},{25,17},{2,26},{10... | collective-permute-start | bytes 776 | tf_op jit(solution)/shard_map/ppermute | solution.py:32
  19.3 5.0 %collective-permute-start.5 = (bf16[1,128,320]{1,2,0:T(8,128)(2,1)S(1)}, bf16[1,128,320]{1,2,0:T(8,128)(2,1)S(1)}, u32[]{:S(2)}, u32[]{:S(2)}) collective-permute-start(bf16[1,128,320]{1,2,0:T(8,128)(2,1)S(1)} %get-tuple-element.14), channel_id=1, source_target_pairs={{0,8},{8,16},{16,24},{1,9},{9,17},{17,25},{2,10},{10,18},{18,26},{... | collective-permute-start | bytes 245768 | tf_op jit(solution)/shard_map/ppermute | solution.py:17
  24.8 1.6 %collective-permute-done.5 = bf16[1,128,320]{1,2,0:T(8,128)(2,1)S(1)} collective-permute-done((bf16[1,128,320]{1,2,0:T(8,128)(2,1)S(1)}, bf16[1,128,320]{1,2,0:T(8,128)(2,1)S(1)}, u32[]{:S(2)}, u32[]{:S(2)}) %collective-permute-start.5) | collective-permute-done | bytes 81952 | tf_op jit(solution)/shard_map/ppermute | solution.py:17
  33.8 6.2 %all-gather.3.cloned.1.call-done = bf16[8,360,320]{1,2,0:T(8,128)(2,1)} async-done(((bf16[1,360,320]{1,2,0:T(8,128)(2,1)}), bf16[8,360,320]{1,2,0:T(8,128)(2,1)}) %all-gather.3.cloned.1.call-update) | async-done | bytes 1843216 | tf_op jit(solution)/shard_map/all_gather | solution.py:103
  40.0 3.0 %copy.25 = bf16[8,360,320]{2,1,0:T(8,128)(2,1)S(1)} copy(bf16[8,360,320]{1,2,0:T(8,128)(2,1)} %all-gather.3.cloned.1.call-done) | data formatting | bytes 3686400 | tf_op jit(solution)/shard_map/all_gather | solution.py:103
  43.0 2.5 %copy.26 = bf16[9,320,320]{2,1,0:T(8,128)(2,1)} copy(bf16[9,320,320]{1,2,0:T(8,128)(2,1)S(1)} %bitcast.104) | data formatting | bytes 3686400 | tf_op jit(solution)/shard_map/transpose | solution.py:140
  45.5 3.8 %fusion.38 = (f32[320]{0:T(512)S(1)}, f32[320]{0:T(512)S(1)}, f32[3,128,320]{1,2,0:T(8,128)S(1)}) fusion(f32[320]{0:T(512)S(1)} %mul.171, f32[320]{0:T(512)S(1)} %sub.46, f32[3,128]{1,0:T(4,128)S(1)} %get-tuple-element.21, bf16[1,3,128,320]{2,3,1,0:T(8,128)(2,1)S(1)} %copy-done.6, f32[320]{0:T(512)S(1)} %copy-done.9, f32[320]{0:T(512)S(1)} %copy-done.10, ...), kind=kOutput, calls=%fused_computation.90 | convolution fusion | flops 710245760 | bytes 4801536 | tf_op jit(solution)/shard_map/dot_general | solution.py:141
  49.7 3.4 %collective-permute-start.9 = (f32[2,32]{1,0:T(2,128)S(1)}, f32[2,32]{1,0:T(2,128)S(1)}, u32[]{:S(2)}, u32[]{:S(2)}) collective-permute-start(f32[2,32]{1,0:T(2,128)S(1)} %pad_maximum_fusion.5), channel_id=1, source_target_pairs={{0,24},{8,0},{16,8},{24,16},{1,25},{9,1},{17,9},{25,17},{2,26},{10... | collective-permute-start | bytes 776 | tf_op jit(solution)/shard_map/ppermute | solution.py:32
  54.4 3.2 %collective-permute-done.8 = f32[2,32]{1,0:T(2,128)S(1)} collective-permute-done((f32[2,32]{1,0:T(2,128)S(1)}, f32[2,32]{1,0:T(2,128)S(1)}, u32[]{:S(2)}, u32[]{:S(2)}) %collective-permute-start.8) | collective-permute-done | bytes 288 | tf_op jit(solution)/shard_map/ppermute | solution.py:32
  61.3 4.7 %collective-permute-start.3 = (bf16[1,128,320]{1,2,0:T(8,128)(2,1)S(1)}, bf16[1,128,320]{1,2,0:T(8,128)(2,1)S(1)}, u32[]{:S(2)}, u32[]{:S(2)}) collective-permute-start(bf16[1,128,320]{1,2,0:T(8,128)(2,1)S(1)} %get-tuple-element.16), channel_id=1, source_target_pairs={{0,8},{8,16},{16,24},{1,9},{9,17},{17,25},{2,10},{10,18},{18,26},{... | collective-permute-start | bytes 245768 | tf_op jit(solution)/shard_map/ppermute | solution.py:17
  66.3 1.6 %collective-permute-done.3 = bf16[1,128,320]{1,2,0:T(8,128)(2,1)S(1)} collective-permute-done((bf16[1,128,320]{1,2,0:T(8,128)(2,1)S(1)}, bf16[1,128,320]{1,2,0:T(8,128)(2,1)S(1)}, u32[]{:S(2)}, u32[]{:S(2)}) %collective-permute-start.3) | collective-permute-done | bytes 81952 | tf_op jit(solution)/shard_map/ppermute | solution.py:17
  69.1 2.8 %copy.28 = bf16[3,128,2880]{2,1,0:T(8,128)(2,1)} copy(bf16[3,128,2880]{1,2,0:T(8,128)(2,1)S(1)} %slice_dynamic-update-slice_fusion.6) | data formatting | bytes 4423680 | tf_op jit(solution)/shard_map/concatenate | solution.py:116
  71.9 3.0 %copy.29 = bf16[2880,384]{1,0:T(8,128)(2,1)S(1)} copy(bf16[2880,384]{0,1:T(8,128)(2,1)} %bitcast.103) | data formatting | bytes 4423680 | tf_op jit(solution)/shard_map/dot_general | solution.py:129
  76.1 1.8 %copy-done = f32[4,2,360,320]{2,3,1,0:T(8,128)} copy-done((f32[4,2,360,320]{2,3,1,0:T(8,128)}, f32[4,2,360,320]{2,3,1,0:T(8,128)S(1)}, u32[]{:S(2)}) %copy-start) | copy-done | bytes 3686424
  78.2 2.5 %collective-permute-done.10 = bf16[4,360,320]{1,2,0:T(8,128)(2,1)S(1)} collective-permute-done((bf16[4,360,320]{1,2,0:T(8,128)(2,1)S(1)}, bf16[4,360,320]{1,2,0:T(8,128)(2,1)S(1)}, u32[]{:S(2)}, u32[]{:S(2)}) %collective-permute-start.10) | collective-permute-done | bytes 921632 | tf_op jit(solution)/shard_map/ppermute | solution.py:60
  80.7 1.7 %bitcast_add_fusion = f32[4,360,320]{1,2,0:T(8,128)S(1)} fusion(bf16[4,360,320]{1,2,0:T(8,128)(2,1)S(1)} %collective-permute-done.10, f32[4,2,360,320]{2,3,1,0:T(8,128)} %copy-done, s32[]{:T(128)S(6)} %select_n.45), kind=kLoop, calls=%fused_computation.2 | loop fusion | flops 921600 | bytes 4608004 | tf_op jit(solution)/shard_map/add | solution.py:61
  83.8 1.5 %collective-permute-start.11 = (bf16[2,360,320]{1,2,0:T(8,128)(2,1)S(1)}, bf16[2,360,320]{1,2,0:T(8,128)(2,1)S(1)}, u32[]{:S(2)}, u32[]{:S(2)}) collective-permute-start(bf16[2,360,320]{1,2,0:T(8,128)(2,1)S(1)} %fusion.28), channel_id=1, source_target_pairs={{0,2},{1,3},{2,0},{3,1},{4,6},{5,7},{6,4},{7,5},{8,10},{9,11},{10,... | collective-permute-start | bytes 1382408 | tf_op jit(solution)/shard_map/ppermute | solution.py:60
  85.3 11.8 %collective-permute-done.11 = bf16[2,360,320]{1,2,0:T(8,128)(2,1)S(1)} collective-permute-done((bf16[2,360,320]{1,2,0:T(8,128)(2,1)S(1)}, bf16[2,360,320]{1,2,0:T(8,128)(2,1)S(1)}, u32[]{:S(2)}, u32[]{:S(2)}) %collective-permute-start.11) | collective-permute-done | bytes 460832 | tf_op jit(solution)/shard_map/ppermute | solution.py:60
  99.9 5.8 %collective-permute-done.12 = bf16[1,360,320]{1,2,0:T(8,128)(2,1)S(1)} collective-permute-done((bf16[1,360,320]{1,2,0:T(8,128)(2,1)S(1)}, bf16[1,360,320]{1,2,0:T(8,128)(2,1)S(1)}, u32[]{:S(2)}, u32[]{:S(2)}) %collective-permute-start.12) | collective-permute-done | bytes 230432 | tf_op jit(solution)/shard_map/ppermute | solution.py:60
  105.7 2.4 %collective-permute-start.13 = (bf16[360,320]{0,1:T(8,128)(2,1)S(1)}, bf16[360,320]{0,1:T(8,128)(2,1)S(1)}, u32[]{:S(2)}, u32[]{:S(2)}) collective-permute-start(bf16[360,320]{0,1:T(8,128)(2,1)S(1)} %fusion.29), channel_id=1, source_target_pairs={{0,8},{8,0},{16,24},{24,16},{1,9},{9,1},{17,25},{25,17},{2,10},{10... | collective-permute-start | bytes 691208 | tf_op jit(solution)/shard_map/ppermute | solution.py:74
  108.2 2.5 %copy.24 = bf16[8,360,320]{1,0,2:T(8,128)(2,1)} copy(bf16[8,360,320]{1,2,0:T(8,128)(2,1)S(1)} %copy-done.1) | data formatting | bytes 3686400 | tf_op jit(solution)/shard_map/all_gather | solution.py:103
  110.7 4.5 %reshape.149 = bf16[2880,320,1]{0,1,2:T(8,128)(2,1)} reshape(bf16[8,360,320]{1,0,2:T(8,128)(2,1)} %copy.24) | data formatting | bytes 3686400
  116.5 3.3 %fusion.4 = bf16[1,3,128,320]{2,3,1,0:T(8,128)(2,1)} fusion(bf16[2880,320,1]{0,1,2:T(8,128)(2,1)} %reshape.149, bf16[3,128,2880]{1,2,0:T(8,128)(2,1)S(1)} %copy-done.4, f32[3,128]{1,0:T(4,128)S(1)} %get-tuple-element.21), kind=kOutput, calls=%fused_computation.10 | convolution fusion | flops 708034560 | bytes 4302336 | tf_op jit(solution)/shard_map/dot_general | solution.py:124
  119.8 7.4 %collective-permute-done.14 = bf16[360,320]{0,1:T(8,128)(2,1)S(1)} collective-permute-done((bf16[360,320]{0,1:T(8,128)(2,1)S(1)}, bf16[360,320]{0,1:T(8,128)(2,1)S(1)}, u32[]{:S(2)}, u32[]{:S(2)}) %collective-permute-start.14) | collective-permute-done | bytes 230432 | tf_op jit(solution)/shard_map/ppermute | solution.py:74
  (100 shorter events, 28.6 us)
Async XLA Ops:
  7.2 32.8 %all-gather.3.cloned.1.call-start = ((), (), s32[]{:S(2)}) async-start(), calls=%async_computation | async-start | bytes 2211840 | tf_op jit(solution)/shard_map/all_gather | solution.py:103
  9.3 20.7 %copy-start.5 = (bf16[1,3,128,320]{2,3,1,0:T(8,128)(2,1)S(1)}, bf16[1,3,128,320]{2,3,1,0:T(8,128)(2,1)}, u32[]{:S(2)}) copy-start(bf16[1,3,128,320]{2,3,1,0:T(8,128)(2,1)} %param.10) | copy-start | bytes 737284
  10.9 13.4 %collective-permute-start.2 = (f32[2,32]{1,0:T(2,128)S(1)}, f32[2,32]{1,0:T(2,128)S(1)}, u32[]{:S(2)}, u32[]{:S(2)}) collective-permute-start(f32[2,32]{1,0:T(2,128)S(1)} %pad_maximum_fusion.4), channel_id=1, source_target_pairs={{0,24},{8,0},{16,8},{24,16},{1,25},{9,1},{17,9},{25,17},{2,26},{10... | collective-permute-start | bytes 776 | tf_op jit(solution)/shard_map/ppermute | solution.py:32
  16.0 8.3 %collective-permute-start.1 = (f32[2,32]{1,0:T(2,128)S(1)}, f32[2,32]{1,0:T(2,128)S(1)}, u32[]{:S(2)}, u32[]{:S(2)}) collective-permute-start(f32[2,32]{1,0:T(2,128)S(1)} %pad_maximum_fusion.4), channel_id=1, source_target_pairs={{0,16},{8,24},{16,0},{24,8},{1,17},{9,25},{17,1},{25,9},{2,18},{10... | collective-permute-start | bytes 776 | tf_op jit(solution)/shard_map/ppermute | solution.py:32
  16.1 8.3 %collective-permute-start = (f32[2,32]{1,0:T(2,128)S(1)}, f32[2,32]{1,0:T(2,128)S(1)}, u32[]{:S(2)}, u32[]{:S(2)}) collective-permute-start(f32[2,32]{1,0:T(2,128)S(1)} %pad_maximum_fusion.4), channel_id=1, source_target_pairs={{0,8},{8,16},{16,24},{24,0},{1,9},{9,17},{17,25},{25,1},{2,10},{10... | collective-permute-start | bytes 776 | tf_op jit(solution)/shard_map/ppermute | solution.py:32
  18.0 6.8 %collective-permute-start.6 = (bf16[1,128,320]{1,2,0:T(8,128)(2,1)S(1)}, bf16[1,128,320]{1,2,0:T(8,128)(2,1)S(1)}, u32[]{:S(2)}, u32[]{:S(2)}) collective-permute-start(bf16[1,128,320]{1,2,0:T(8,128)(2,1)S(1)} %get-tuple-element.15), channel_id=1, source_target_pairs={{8,0},{16,8},{24,16},{9,1},{17,9},{25,17},{10,2},{18,10},{26,18},{... | collective-permute-start | bytes 245768 | tf_op jit(solution)/shard_map/ppermute | solution.py:19
  19.3 7.1 %collective-permute-start.5 = (bf16[1,128,320]{1,2,0:T(8,128)(2,1)S(1)}, bf16[1,128,320]{1,2,0:T(8,128)(2,1)S(1)}, u32[]{:S(2)}, u32[]{:S(2)}) collective-permute-start(bf16[1,128,320]{1,2,0:T(8,128)(2,1)S(1)} %get-tuple-element.14), channel_id=1, source_target_pairs={{0,8},{8,16},{16,24},{1,9},{9,17},{17,25},{2,10},{10,18},{18,26},{... | collective-permute-start | bytes 245768 | tf_op jit(solution)/shard_map/ppermute | solution.py:17
  43.0 2.5 %copy-start.6 = (bf16[1,3,128,320]{2,3,1,0:T(8,128)(2,1)S(1)}, bf16[1,3,128,320]{2,3,1,0:T(8,128)(2,1)}, u32[]{:S(2)}) copy-start(bf16[1,3,128,320]{2,3,1,0:T(8,128)(2,1)} %param.9) | copy-start | bytes 737284
  43.0 2.5 %copy-start.9 = (f32[320]{0:T(512)S(1)}, f32[320]{0:T(512)}, u32[]{:S(2)}) copy-start(f32[320]{0:T(512)} %param.12) | copy-start | bytes 3844
  49.7 4.7 %collective-permute-start.9 = (f32[2,32]{1,0:T(2,128)S(1)}, f32[2,32]{1,0:T(2,128)S(1)}, u32[]{:S(2)}, u32[]{:S(2)}) collective-permute-start(f32[2,32]{1,0:T(2,128)S(1)} %pad_maximum_fusion.5), channel_id=1, source_target_pairs={{0,24},{8,0},{16,8},{24,16},{1,25},{9,1},{17,9},{25,17},{2,26},{10... | collective-permute-start | bytes 776 | tf_op jit(solution)/shard_map/ppermute | solution.py:32
  53.1 4.5 %collective-permute-start.8 = (f32[2,32]{1,0:T(2,128)S(1)}, f32[2,32]{1,0:T(2,128)S(1)}, u32[]{:S(2)}, u32[]{:S(2)}) collective-permute-start(f32[2,32]{1,0:T(2,128)S(1)} %pad_maximum_fusion.5), channel_id=1, source_target_pairs={{0,16},{8,24},{16,0},{24,8},{1,17},{9,25},{17,1},{25,9},{2,18},{10... | collective-permute-start | bytes 776 | tf_op jit(solution)/shard_map/ppermute | solution.py:32
  53.1 5.4 %collective-permute-start.7 = (f32[2,32]{1,0:T(2,128)S(1)}, f32[2,32]{1,0:T(2,128)S(1)}, u32[]{:S(2)}, u32[]{:S(2)}) collective-permute-start(f32[2,32]{1,0:T(2,128)S(1)} %pad_maximum_fusion.5), channel_id=1, source_target_pairs={{0,8},{8,16},{16,24},{24,0},{1,9},{9,17},{17,25},{25,1},{2,10},{10... | collective-permute-start | bytes 776 | tf_op jit(solution)/shard_map/ppermute | solution.py:32
  60.0 6.3 %collective-permute-start.4 = (bf16[1,128,320]{1,2,0:T(8,128)(2,1)S(1)}, bf16[1,128,320]{1,2,0:T(8,128)(2,1)S(1)}, u32[]{:S(2)}, u32[]{:S(2)}) collective-permute-start(bf16[1,128,320]{1,2,0:T(8,128)(2,1)S(1)} %get-tuple-element.17), channel_id=1, source_target_pairs={{8,0},{16,8},{24,16},{9,1},{17,9},{25,17},{10,2},{18,10},{26,18},{... | collective-permute-start | bytes 245768 | tf_op jit(solution)/shard_map/ppermute | solution.py:19
  61.3 6.6 %collective-permute-start.3 = (bf16[1,128,320]{1,2,0:T(8,128)(2,1)S(1)}, bf16[1,128,320]{1,2,0:T(8,128)(2,1)S(1)}, u32[]{:S(2)}, u32[]{:S(2)}) collective-permute-start(bf16[1,128,320]{1,2,0:T(8,128)(2,1)S(1)} %get-tuple-element.16), channel_id=1, source_target_pairs={{0,8},{8,16},{16,24},{1,9},{9,17},{17,25},{2,10},{10,18},{18,26},{... | collective-permute-start | bytes 245768 | tf_op jit(solution)/shard_map/ppermute | solution.py:17
  69.1 2.8 %copy-start.3 = (bf16[3,128,2880]{1,2,0:T(8,128)(2,1)}, bf16[3,128,2880]{1,2,0:T(8,128)(2,1)S(1)}, u32[]{:S(2)}) copy-start(bf16[3,128,2880]{1,2,0:T(8,128)(2,1)S(1)} %slice_dynamic-update-slice_fusion.6) | copy-start | bytes 6635524
  78.0 2.6 %collective-permute-start.10 = (bf16[4,360,320]{1,2,0:T(8,128)(2,1)S(1)}, bf16[4,360,320]{1,2,0:T(8,128)(2,1)S(1)}, u32[]{:S(2)}, u32[]{:S(2)}) collective-permute-start(bf16[4,360,320]{1,2,0:T(8,128)(2,1)S(1)} %fusion.5), channel_id=1, source_target_pairs={{0,1},{1,0},{2,3},{3,2},{4,5},{5,4},{6,7},{7,6},{8,9},{9,8},{10,11... | collective-permute-start | bytes 2764808 | tf_op jit(solution)/shard_map/ppermute | solution.py:60
  83.8 24.4 %copy-start.1 = (bf16[8,360,320]{1,2,0:T(8,128)(2,1)S(1)}, bf16[8,360,320]{1,2,0:T(8,128)(2,1)}, u32[]{:S(2)}) copy-start(bf16[8,360,320]{1,2,0:T(8,128)(2,1)} %all-gather.3.cloned.1.call-done) | copy-start | bytes 5529604
  83.8 13.3 %collective-permute-start.11 = (bf16[2,360,320]{1,2,0:T(8,128)(2,1)S(1)}, bf16[2,360,320]{1,2,0:T(8,128)(2,1)S(1)}, u32[]{:S(2)}, u32[]{:S(2)}) collective-permute-start(bf16[2,360,320]{1,2,0:T(8,128)(2,1)S(1)} %fusion.28), channel_id=1, source_target_pairs={{0,2},{1,3},{2,0},{3,1},{4,6},{5,7},{6,4},{7,5},{8,10},{9,11},{10,... | collective-permute-start | bytes 1382408 | tf_op jit(solution)/shard_map/ppermute | solution.py:60
  98.4 7.2 %collective-permute-start.12 = (bf16[1,360,320]{1,2,0:T(8,128)(2,1)S(1)}, bf16[1,360,320]{1,2,0:T(8,128)(2,1)S(1)}, u32[]{:S(2)}, u32[]{:S(2)}) collective-permute-start(bf16[1,360,320]{1,2,0:T(8,128)(2,1)S(1)} %dynamic-slice_convert_fusion.1), channel_id=1, source_target_pairs={{0,4},{1,5},{2,6},{3,7},{4,0},{5,1},{6,2},{7,3},{8,12},{9,13},{10,... | collective-permute-start | bytes 691208 | tf_op jit(solution)/shard_map/ppermute | solution.py:60
  105.7 9.4 %collective-permute-start.13 = (bf16[360,320]{0,1:T(8,128)(2,1)S(1)}, bf16[360,320]{0,1:T(8,128)(2,1)S(1)}, u32[]{:S(2)}, u32[]{:S(2)}) collective-permute-start(bf16[360,320]{0,1:T(8,128)(2,1)S(1)} %fusion.29), channel_id=1, source_target_pairs={{0,8},{8,0},{16,24},{24,16},{1,9},{9,1},{17,25},{25,17},{2,10},{10... | collective-permute-start | bytes 691208 | tf_op jit(solution)/shard_map/ppermute | solution.py:74
  110.6 5.8 %copy-start.4 = (bf16[3,128,2880]{1,2,0:T(8,128)(2,1)S(1)}, bf16[3,128,2880]{1,2,0:T(8,128)(2,1)}, u32[]{:S(2)}) copy-start(bf16[3,128,2880]{1,2,0:T(8,128)(2,1)} %copy-done.3) | copy-start | bytes 6635524
  115.2 12.0 %copy-start.7 = (f32[360,320]{0,1:T(8,128)S(1)}, f32[360,320]{0,1:T(8,128)}, u32[]{:S(2)}) copy-start(f32[360,320]{0,1:T(8,128)} %param.15) | copy-start | bytes 1382404
  115.3 12.0 %copy-start.8 = (f32[360,320]{0,1:T(8,128)S(1)}, f32[360,320]{0,1:T(8,128)}, u32[]{:S(2)}) copy-start(f32[360,320]{0,1:T(8,128)} %param.14) | copy-start | bytes 1382404
  115.3 11.9 %collective-permute-start.14 = (bf16[360,320]{0,1:T(8,128)(2,1)S(1)}, bf16[360,320]{0,1:T(8,128)(2,1)S(1)}, u32[]{:S(2)}, u32[]{:S(2)}) collective-permute-start(bf16[360,320]{0,1:T(8,128)(2,1)S(1)} %add_convert_fusion), channel_id=1, source_target_pairs={{0,16},{8,24},{16,0},{24,8},{1,17},{9,25},{17,1},{25,9},{2,18},{10... | collective-permute-start | bytes 691208 | tf_op jit(solution)/shard_map/ppermute | solution.py:74
  (3 other events, 5.7 us)
Sparse Core Ops, SparseCore 0:
  9.9 30.0 all-gather.2

commit v4 on v3

--- a/solution.py
+++ b/solution.py
@@ -101,7 +101,6 @@
     ).astype(jnp.float32)[..., None]
     cell_count = (heights[0] * widths[0] * (channels // GROUPS)).astype(jnp.float32)
     gathered = lax.all_gather(weight, "dp", axis=0, tiled=True)
-    tap_weights = gathered.reshape(9, channels, channels)
     values = latent.astype(jnp.float32) * inside
     group_total, squares = space_sum(
         (group_sum(values, GROUPS), group_sum(values * values, GROUPS)), "space"
@@ -121,14 +120,16 @@
         ],
         axis=-1,
     ).reshape(height_dev * width_dev, 9 * channels)
-    output = jnp.dot(act_cols, gathered, preferred_element_type=jnp.float32)
-    block_out = (output.reshape(height_dev, width_dev, channels) * inside).astype(jnp.bfloat16)
     masked = cotangent[0] * inside.astype(jnp.bfloat16)
     cot_pad = pad_columns(with_halo(masked, (("space", 0),), 1))
     flat_cot = masked.reshape(-1, channels)
     weight_terms = lax.dot_general(
         act_cols, flat_cot, (((0,), (0,)), ((), ())), preferred_element_type=jnp.float32
     )
+    weight_terms, gathered, cot_pad = lax.optimization_barrier((weight_terms, gathered, cot_pad))
+    output = jnp.dot(act_cols, gathered, preferred_element_type=jnp.float32)
+    block_out = (output.reshape(height_dev, width_dev, channels) * inside).astype(jnp.bfloat16)
+    tap_weights = gathered.reshape(9, channels, channels)
     cot_cols = jnp.concatenate(
         [
             cot_pad[2 - row_off : 2 - row_off + height_dev, 2 - col_off : 2 - col_off + width_dev]

time: 136 us -> 125 us (0.919)
  waiting for transfers between devices: 41.8 us -> 27.3 us
  local copies, waits for them, and re-layouts: 28.4 us -> 32.8 us
    ppermute x3, waiting for transfers between devices: 20.1 us -> 7.33 us  [halving_scatter(): got = lax.ppermute(send.astype(jnp.bfloat16), axis, pairs)]
    another operation x0 -> x1, local copies, waits for them, and re-layouts: none -> 8.12 us  [halving_scatter(): paired = held.reshape(-1, 2, rows, channels)]
    optimization_barrier x0 -> x2, local copies, waits for them, and re-layouts: none -> 6.15 us  [local(): lax.optimization_barrier((weight_terms, gathered, cot_pad))]
    unnamed x34, local copies, waits for them, and re-layouts: 12.3 us -> 6.34 us
    dynamic_slice x0 -> x2, local copies, waits for them, and re-layouts: none -> 5.57 us  [the longest x1 3.88 us: halving_scatter(): send = lax.dynamic_index_in_dim(paired, 1 - bit, axis=1, keepdims=False)]
    ppermute x2, waiting for transfers between devices: 0.06 us -> 4.47 us  [with_halo(): lax.ppermute(head, axis, [((i + 1) % count, i) for i in range(ends)])]
    ppermute x2, waiting for transfers between devices: 7.4 us -> 11.7 us  [replicated_sum(): lax.ppermute(mine, axis, pairs).astype(jnp.float32)]
    ppermute x6, waiting for transfers between devices: 4.27 us -> 0.02 us  [space_sum(): lax.ppermute(joined, axis, [(i, (i + shift) % count) for i in range(count)])]
  transfers between devices with their start and end apart: 16 -> 16, of which waited for: 10 -> 7; matrix products, arithmetic and copies ran while one was open for 16% -> 21% of each run, Pallas kernels for 0% -> 0%
where the time goes in v4:
time: 125 us
  local copies, waits for them, and re-layouts  32.8 us (26%)
  starting transfers between devices  28.7 us (23%)
  waiting for transfers between devices  27.3 us (22%)
  between operations  15.9 us (13%)
  other arithmetic  11.5 us (9%)
  matrix products  8.65 us (7%)
    ppermute x2, waiting for transfers between devices, replicated_sum(): lax.ppermute(mine, axis, pairs).astype(jnp.float32)  11.7 us
    ppermute x6, starting transfers between devices, space_sum(): lax.ppermute(joined, axis, [(i, (i + shift) % count) for i in range(count)])  10.6 us
    another operation x1, local copies, waits for them, and re-layouts, halving_scatter(): paired = held.reshape(-1, 2, rows, channels)  8.12 us
    ppermute x2, starting transfers between devices, with_halo(): lax.ppermute(tail, axis, [(i, (i + 1) % count) for i in range(ends)])  8.04 us
    ppermute x3, waiting for transfers between devices, halving_scatter(): got = lax.ppermute(send.astype(jnp.bfloat16), axis, pairs)  7.33 us
    unnamed x34, local copies, waits for them, and re-layouts  6.34 us
    optimization_barrier x2, local copies, waits for them, and re-layouts, local(): lax.optimization_barrier((weight_terms, gathered, cot_pad))  6.15 us
    ppermute x2, waiting for transfers between devices, with_halo(): lax.ppermute(head, axis, [((i + 1) % count, i) for i in range(ends)])  4.47 us
  transfers between devices with their start and end apart: 16, of which 7 were waited for; matrix products, arithmetic and copies ran while one was open for 21% of the time, Pallas kernels for 0%

profile of v4, /device:TPU:0, one launch (start us, length us, event | category | flops | bytes accessed | tf_op | source)
XLA Modules:
  0.0 124.9 jit_solution(12039003618660622113)
XLA Ops:
  10.2 4.1 %collective-permute-start.1 = (f32[2,32]{1,0:T(2,128)S(1)}, f32[2,32]{1,0:T(2,128)S(1)}, u32[]{:S(2)}, u32[]{:S(2)}) collective-permute-start(f32[2,32]{1,0:T(2,128)S(1)} %pad_maximum_fusion.2), channel_id=1, source_target_pairs={{0,16},{8,24},{16,0},{24,8},{1,17},{9,25},{17,1},{25,9},{2,18},{10... | collective-permute-start | bytes 776 | tf_op jit(solution)/shard_map/ppermute | solution.py:32
  17.4 3.5 %collective-permute-start.5 = (bf16[1,128,320]{1,2,0:T(8,128)(2,1)S(1)}, bf16[1,128,320]{1,2,0:T(8,128)(2,1)S(1)}, u32[]{:S(2)}, u32[]{:S(2)}) collective-permute-start(bf16[1,128,320]{1,2,0:T(8,128)(2,1)S(1)} %get-tuple-element.18), channel_id=1, source_target_pairs={{0,8},{8,16},{16,24},{1,9},{9,17},{17,25},{2,10},{10,18},{18,26},{... | collective-permute-start | bytes 245768 | tf_op jit(solution)/shard_map/ppermute | solution.py:17
  24.0 4.6 %collective-permute-start.3 = (bf16[1,128,320]{1,2,0:T(8,128)(2,1)S(1)}, bf16[1,128,320]{1,2,0:T(8,128)(2,1)S(1)}, u32[]{:S(2)}, u32[]{:S(2)}) collective-permute-start(bf16[1,128,320]{1,2,0:T(8,128)(2,1)S(1)} %get-tuple-element.20), channel_id=1, source_target_pairs={{0,8},{8,16},{16,24},{1,9},{9,17},{17,25},{2,10},{10,18},{18,26},{... | collective-permute-start | bytes 245768 | tf_op jit(solution)/shard_map/ppermute | solution.py:17
  30.6 4.5 %collective-permute-done.4 = bf16[1,128,320]{1,2,0:T(8,128)(2,1)S(1)} collective-permute-done((bf16[1,128,320]{1,2,0:T(8,128)(2,1)S(1)}, bf16[1,128,320]{1,2,0:T(8,128)(2,1)S(1)}, u32[]{:S(2)}, u32[]{:S(2)}) %collective-permute-start.4) | collective-permute-done | bytes 81952 | tf_op jit(solution)/shard_map/ppermute | solution.py:19
  38.0 3.1 %convolution_bitcast_fusion = f32[2880,320]{0,1:T(8,128)} fusion(bf16[3,128,2880]{1,2,0:T(8,128)(2,1)S(1)} %slice_dynamic-update-slice_fusion, bf16[3,128,320]{1,2,0:T(8,128)(2,1)S(1)} %bitcast_multiply_fusion), kind=kOutput, calls=%fused_computation | convolution fusion | flops 707788800 | bytes 6144000 | tf_op jit(solution)/shard_map/dot_general | solution.py:126
  41.1 3.6 %all-gather.3.cloned.1.call-done = bf16[8,360,320]{1,2,0:T(8,128)(2,1)} async-done(((bf16[1,360,320]{1,2,0:T(8,128)(2,1)}), bf16[8,360,320]{1,2,0:T(8,128)(2,1)}) %all-gather.3.cloned.1.call-update) | async-done | bytes 1843216 | tf_op jit(solution)/shard_map/all_gather | solution.py:103
  44.7 2.7 %copy.20 = bf16[8,360,320]{1,0,2:T(8,128)(2,1)S(1)} copy(bf16[8,360,320]{1,2,0:T(8,128)(2,1)} %all-gather.3.cloned.1.call-done) | data formatting | bytes 3686400 | tf_op jit(solution)/shard_map/all_gather | solution.py:103
  47.4 2.9 %reshape.132 = bf16[2880,320]{0,1:T(8,128)(2,1)} reshape(bf16[8,360,320]{1,0,2:T(8,128)(2,1)S(1)} %copy.20) | data formatting | bytes 3686400 | tf_op jit(solution)/shard_map/optimization_barrier | solution.py:129
  50.2 8.1 %reshape_reshape.3 = f32[4,2,360,320]{2,1,0,3:T(2,128)} reshape(f32[2880,320]{0,1:T(8,128)} %convolution_bitcast_fusion) | data formatting | bytes 7372800 | tf_op jit(solution)/shard_map/reshape;reshape | solution.py:56
  58.3 3.9 %constant_dynamic-slice_fusion = bf16[4,1,360,320]{2,1,0,3:T(2,128)(2,1)S(1)} fusion(f32[4,2,360,320]{2,1,0,3:T(2,128)} %reshape_reshape.3, s32[]{:T(128)S(6)} %select_n.46), kind=kLoop, calls=%fused_computation.77 | loop fusion | bytes 1843204 | tf_op jit(solution)/shard_map/jit(dynamic_index_in_dim)/dynamic_slice | solution.py:58
  63.6 3.3 %copy.21 = bf16[2880,320]{1,0:T(8,128)(2,1)S(1)} copy(bf16[2880,320]{0,1:T(8,128)(2,1)} %reshape.132) | data formatting | bytes 3686400 | tf_op jit(solution)/shard_map/optimization_barrier | solution.py:129
  66.9 2.5 %copy.22 = bf16[9,320,320]{2,1,0:T(8,128)(2,1)} copy(bf16[9,320,320]{1,2,0:T(8,128)(2,1)S(1)} %bitcast.104) | data formatting | bytes 3686400 | tf_op jit(solution)/shard_map/transpose | solution.py:141
  71.5 1.7 %constant_dynamic-slice_fusion.1 = f32[4,1,360,320]{2,1,0,3:T(1,128)S(1)} fusion(f32[4,2,360,320]{2,1,0,3:T(2,128)S(1)} %copy-done, s32[]{:T(128)S(6)} %select_n.45), kind=kLoop, calls=%fused_computation.78 | loop fusion | bytes 3686404 | tf_op jit(solution)/shard_map/jit(dynamic_index_in_dim)/dynamic_slice | solution.py:57
  76.1 1.5 %collective-permute-start.11 = (bf16[2,360,320]{1,2,0:T(8,128)(2,1)S(1)}, bf16[2,360,320]{1,2,0:T(8,128)(2,1)}, u32[]{:S(2)}, u32[]{:S(2)}) collective-permute-start(bf16[2,360,320]{1,2,0:T(8,128)(2,1)S(1)} %fusion.37), channel_id=1, source_target_pairs={{0,2},{1,3},{2,0},{3,1},{4,6},{5,7},{6,4},{7,5},{8,10},{9,11},{10,... | collective-permute-start | bytes 1382408 | tf_op jit(solution)/shard_map/ppermute | solution.py:60
  77.7 2.1 %fusion.45 = (f32[320]{0:T(512)S(1)}, f32[320]{0:T(512)S(1)}, f32[3,128,320]{1,2,0:T(8,128)}) fusion(f32[320]{0:T(512)S(1)} %mul.163, f32[320]{0:T(512)S(1)} %sub.46, f32[3,128]{1,0:T(4,128)S(1)} %get-tuple-element.25, bf16[1,3,128,320]{2,3,1,0:T(8,128)(2,1)S(1)} %copy-done.4, f32[320]{0:T(512)S(1)} %copy-done.8, f32[320]{0:T(512)S(1)} %copy-done.9, ...), kind=kOutput, calls=%fused_computation.92 | convolution fusion | flops 710245760 | bytes 4801536 | tf_op jit(solution)/shard_map/dot_general | solution.py:142
  80.3 2.5 %collective-permute-start.8 = (f32[2,32]{1,0:T(2,128)S(1)}, f32[2,32]{1,0:T(2,128)S(1)}, u32[]{:S(2)}, u32[]{:S(2)}) collective-permute-start(f32[2,32]{1,0:T(2,128)S(1)} %pad_maximum_fusion.3), channel_id=1, source_target_pairs={{0,16},{8,24},{16,0},{24,8},{1,17},{9,25},{17,1},{25,9},{2,18},{10... | collective-permute-start | bytes 776 | tf_op jit(solution)/shard_map/ppermute | solution.py:32
  84.8 4.9 %collective-permute-done.11 = bf16[2,360,320]{1,2,0:T(8,128)(2,1)} collective-permute-done((bf16[2,360,320]{1,2,0:T(8,128)(2,1)S(1)}, bf16[2,360,320]{1,2,0:T(8,128)(2,1)}, u32[]{:S(2)}, u32[]{:S(2)}) %collective-permute-start.11) | collective-permute-done | bytes 460832 | tf_op jit(solution)/shard_map/ppermute | solution.py:60
  92.6 3.5 %fusion.11 = bf16[1,3,128,320]{2,3,1,0:T(8,128)(2,1)} fusion(bf16[3,128,2880]{1,2,0:T(8,128)(2,1)} %copy-done.3, bf16[2880,320]{0,1:T(8,128)(2,1)S(1)} %copy-done.1, f32[3,128]{1,0:T(4,128)S(1)} %get-tuple-element.25), kind=kOutput, calls=%fused_computation.13 | convolution fusion | flops 708034560 | bytes 4302336 | tf_op jit(solution)/shard_map/dot_general | solution.py:130
  96.1 2.4 %collective-permute-done.12 = bf16[1,360,320]{1,2,0:T(8,128)(2,1)S(1)} collective-permute-done((bf16[1,360,320]{1,2,0:T(8,128)(2,1)S(1)}, bf16[1,360,320]{1,2,0:T(8,128)(2,1)S(1)}, u32[]{:S(2)}, u32[]{:S(2)}) %collective-permute-start.12) | collective-permute-done | bytes 230432 | tf_op jit(solution)/shard_map/ppermute | solution.py:60
  98.6 1.6 %collective-permute-start.13 = (bf16[360,320]{0,1:T(8,128)(2,1)S(1)}, bf16[360,320]{0,1:T(8,128)(2,1)S(1)}, u32[]{:S(2)}, u32[]{:S(2)}) collective-permute-start(bf16[360,320]{0,1:T(8,128)(2,1)S(1)} %fusion.38), channel_id=1, source_target_pairs={{0,8},{8,0},{16,24},{24,16},{1,9},{9,1},{17,25},{25,17},{2,10},{10... | collective-permute-start | bytes 691208 | tf_op jit(solution)/shard_map/ppermute | solution.py:74
  100.5 4.5 %collective-permute-done.13 = bf16[360,320]{0,1:T(8,128)(2,1)S(1)} collective-permute-done((bf16[360,320]{0,1:T(8,128)(2,1)S(1)}, bf16[360,320]{0,1:T(8,128)(2,1)S(1)}, u32[]{:S(2)}, u32[]{:S(2)}) %collective-permute-start.13) | collective-permute-done | bytes 230432 | tf_op jit(solution)/shard_map/ppermute | solution.py:74
  105.1 2.5 %collective-permute-start.14 = (bf16[360,320]{0,1:T(8,128)(2,1)S(1)}, bf16[360,320]{0,1:T(8,128)(2,1)S(1)}, u32[]{:S(2)}, u32[]{:S(2)}) collective-permute-start(bf16[360,320]{0,1:T(8,128)(2,1)S(1)} %add_convert_fusion), channel_id=1, source_target_pairs={{0,16},{8,24},{16,0},{24,8},{1,17},{9,25},{17,1},{25,9},{2,18},{10... | collective-permute-start | bytes 691208 | tf_op jit(solution)/shard_map/ppermute | solution.py:74
  107.5 2.0 %fusion.41 = bf16[1,3,128,320]{2,3,1,0:T(8,128)(2,1)} fusion(f32[320]{0:T(512)S(1)} %mul.180, f32[320]{0:T(512)S(1)} %sub.46, f32[3,128]{1,0:T(4,128)S(1)} %get-tuple-element.25, bf16[1,3,128,320]{2,3,1,0:T(8,128)(2,1)S(1)} %copy-done.4, f32[3,128,320]{1,2,0:T(8,128)} %get-tuple-element.26, f32[320]{0:T(512)S(1)} %sub.51, f32[320]{0:T(512)S(1)} %mul.163), kind=kLoop, calls=%fused_computation.74 | loop fusion | flops 1351680 | bytes 989696 | tf_op jit(solution)/shard_map/broadcast_in_dim | solution.py:161
  109.5 7.2 %collective-permute-done.14 = bf16[360,320]{0,1:T(8,128)(2,1)S(1)} collective-permute-done((bf16[360,320]{0,1:T(8,128)(2,1)S(1)}, bf16[360,320]{0,1:T(8,128)(2,1)S(1)}, u32[]{:S(2)}, u32[]{:S(2)}) %collective-permute-start.14) | collective-permute-done | bytes 230432 | tf_op jit(solution)/shard_map/ppermute | solution.py:74
  (98 shorter events, 26.1 us)
Async XLA Ops:
  7.2 37.5 %all-gather.3.cloned.1.call-start = ((), (), s32[]{:S(2)}) async-start(), calls=%async_computation | async-start | bytes 2211840 | tf_op jit(solution)/shard_map/all_gather | solution.py:103
  10.2 12.0 %collective-permute-start.1 = (f32[2,32]{1,0:T(2,128)S(1)}, f32[2,32]{1,0:T(2,128)S(1)}, u32[]{:S(2)}, u32[]{:S(2)}) collective-permute-start(f32[2,32]{1,0:T(2,128)S(1)} %pad_maximum_fusion.2), channel_id=1, source_target_pairs={{0,16},{8,24},{16,0},{24,8},{1,17},{9,25},{17,1},{25,9},{2,18},{10... | collective-permute-start | bytes 776 | tf_op jit(solution)/shard_map/ppermute | solution.py:32
  14.3 7.9 %collective-permute-start.2 = (f32[2,32]{1,0:T(2,128)S(1)}, f32[2,32]{1,0:T(2,128)S(1)}, u32[]{:S(2)}, u32[]{:S(2)}) collective-permute-start(f32[2,32]{1,0:T(2,128)S(1)} %pad_maximum_fusion.2), channel_id=1, source_target_pairs={{0,24},{8,0},{16,8},{24,16},{1,25},{9,1},{17,9},{25,17},{2,26},{10... | collective-permute-start | bytes 776 | tf_op jit(solution)/shard_map/ppermute | solution.py:32
  15.7 6.6 %collective-permute-start = (f32[2,32]{1,0:T(2,128)S(1)}, f32[2,32]{1,0:T(2,128)S(1)}, u32[]{:S(2)}, u32[]{:S(2)}) collective-permute-start(f32[2,32]{1,0:T(2,128)S(1)} %pad_maximum_fusion.2), channel_id=1, source_target_pairs={{0,8},{8,16},{16,24},{24,0},{1,9},{9,17},{17,25},{25,1},{2,10},{10... | collective-permute-start | bytes 776 | tf_op jit(solution)/shard_map/ppermute | solution.py:32
  17.4 12.7 %collective-permute-start.5 = (bf16[1,128,320]{1,2,0:T(8,128)(2,1)S(1)}, bf16[1,128,320]{1,2,0:T(8,128)(2,1)S(1)}, u32[]{:S(2)}, u32[]{:S(2)}) collective-permute-start(bf16[1,128,320]{1,2,0:T(8,128)(2,1)S(1)} %get-tuple-element.18), channel_id=1, source_target_pairs={{0,8},{8,16},{16,24},{1,9},{9,17},{17,25},{2,10},{10,18},{18,26},{... | collective-permute-start | bytes 245768 | tf_op jit(solution)/shard_map/ppermute | solution.py:17
  20.8 9.2 %collective-permute-start.6 = (bf16[1,128,320]{1,2,0:T(8,128)(2,1)S(1)}, bf16[1,128,320]{1,2,0:T(8,128)(2,1)S(1)}, u32[]{:S(2)}, u32[]{:S(2)}) collective-permute-start(bf16[1,128,320]{1,2,0:T(8,128)(2,1)S(1)} %get-tuple-element.19), channel_id=1, source_target_pairs={{8,0},{16,8},{24,16},{9,1},{17,9},{25,17},{10,2},{18,10},{26,18},{... | collective-permute-start | bytes 245768 | tf_op jit(solution)/shard_map/ppermute | solution.py:19
  24.0 6.6 %collective-permute-start.3 = (bf16[1,128,320]{1,2,0:T(8,128)(2,1)S(1)}, bf16[1,128,320]{1,2,0:T(8,128)(2,1)S(1)}, u32[]{:S(2)}, u32[]{:S(2)}) collective-permute-start(bf16[1,128,320]{1,2,0:T(8,128)(2,1)S(1)} %get-tuple-element.20), channel_id=1, source_target_pairs={{0,8},{8,16},{16,24},{1,9},{9,17},{17,25},{2,10},{10,18},{18,26},{... | collective-permute-start | bytes 245768 | tf_op jit(solution)/shard_map/ppermute | solution.py:17
  28.5 7.2 %copy-start.4 = (bf16[1,3,128,320]{2,3,1,0:T(8,128)(2,1)S(1)}, bf16[1,3,128,320]{2,3,1,0:T(8,128)(2,1)}, u32[]{:S(2)}) copy-start(bf16[1,3,128,320]{2,3,1,0:T(8,128)(2,1)} %param.9) | copy-start | bytes 737284
  28.6 7.2 %copy-start.8 = (f32[320]{0:T(512)S(1)}, f32[320]{0:T(512)}, u32[]{:S(2)}) copy-start(f32[320]{0:T(512)} %param.12) | copy-start | bytes 3844
  28.6 7.2 %copy-start.9 = (f32[320]{0:T(512)S(1)}, f32[320]{0:T(512)}, u32[]{:S(2)}) copy-start(f32[320]{0:T(512)} %param.11) | copy-start | bytes 3844
  28.6 6.5 %collective-permute-start.4 = (bf16[1,128,320]{1,2,0:T(8,128)(2,1)S(1)}, bf16[1,128,320]{1,2,0:T(8,128)(2,1)S(1)}, u32[]{:S(2)}, u32[]{:S(2)}) collective-permute-start(bf16[1,128,320]{1,2,0:T(8,128)(2,1)S(1)} %get-tuple-element.21), channel_id=1, source_target_pairs={{8,0},{16,8},{24,16},{9,1},{17,9},{25,17},{10,2},{18,10},{26,18},{... | collective-permute-start | bytes 245768 | tf_op jit(solution)/shard_map/ppermute | solution.py:19
  63.4 9.9 %collective-permute-start.10 = (bf16[4,360,320]{1,2,0:T(8,128)(2,1)}, bf16[4,360,320]{1,2,0:T(8,128)(2,1)}, u32[]{:S(2)}, u32[]{:S(2)}) collective-permute-start(bf16[4,360,320]{1,2,0:T(8,128)(2,1)} %bitcast.99), channel_id=1, source_target_pairs={{0,1},{1,0},{2,3},{3,2},{4,5},{5,4},{6,7},{7,6},{8,9},{9,8},{10,11... | collective-permute-start | bytes 2764808 | tf_op jit(solution)/shard_map/ppermute | solution.py:60
  69.4 2.1 %copy-start = (f32[4,2,360,320]{2,1,0,3:T(2,128)S(1)}, f32[4,2,360,320]{2,1,0,3:T(2,128)}, u32[]{:S(2)}) copy-start(f32[4,2,360,320]{2,1,0,3:T(2,128)} %reshape_reshape.3) | copy-start | bytes 11059204
  73.2 4.4 %copy-start.5 = (bf16[9,320,320]{2,1,0:T(8,128)(2,1)S(1)}, bf16[9,320,320]{2,1,0:T(8,128)(2,1)}, u32[]{:S(2)}) copy-start(bf16[9,320,320]{2,1,0:T(8,128)(2,1)} %copy.22) | copy-start | bytes 5529604
  76.1 13.5 %collective-permute-start.11 = (bf16[2,360,320]{1,2,0:T(8,128)(2,1)S(1)}, bf16[2,360,320]{1,2,0:T(8,128)(2,1)}, u32[]{:S(2)}, u32[]{:S(2)}) collective-permute-start(bf16[2,360,320]{1,2,0:T(8,128)(2,1)S(1)} %fusion.37), channel_id=1, source_target_pairs={{0,2},{1,3},{2,0},{3,1},{4,6},{5,7},{6,4},{7,5},{8,10},{9,11},{10,... | collective-permute-start | bytes 1382408 | tf_op jit(solution)/shard_map/ppermute | solution.py:60
  79.8 12.8 %copy-start.1 = (bf16[2880,320]{0,1:T(8,128)(2,1)S(1)}, bf16[2880,320]{0,1:T(8,128)(2,1)}, u32[]{:S(2)}) copy-start(bf16[2880,320]{0,1:T(8,128)(2,1)} %reshape.132) | copy-start | bytes 5529604
  80.3 19.9 %collective-permute-start.8 = (f32[2,32]{1,0:T(2,128)S(1)}, f32[2,32]{1,0:T(2,128)S(1)}, u32[]{:S(2)}, u32[]{:S(2)}) collective-permute-start(f32[2,32]{1,0:T(2,128)S(1)} %pad_maximum_fusion.3), channel_id=1, source_target_pairs={{0,16},{8,24},{16,0},{24,8},{1,17},{9,25},{17,1},{25,9},{2,18},{10... | collective-permute-start | bytes 776 | tf_op jit(solution)/shard_map/ppermute | solution.py:32
  82.7 17.4 %collective-permute-start.9 = (f32[2,32]{1,0:T(2,128)S(1)}, f32[2,32]{1,0:T(2,128)S(1)}, u32[]{:S(2)}, u32[]{:S(2)}) collective-permute-start(f32[2,32]{1,0:T(2,128)S(1)} %pad_maximum_fusion.3), channel_id=1, source_target_pairs={{0,24},{8,0},{16,8},{24,16},{1,25},{9,1},{17,9},{25,17},{2,26},{10... | collective-permute-start | bytes 776 | tf_op jit(solution)/shard_map/ppermute | solution.py:32
  84.2 16.0 %collective-permute-start.7 = (f32[2,32]{1,0:T(2,128)S(1)}, f32[2,32]{1,0:T(2,128)S(1)}, u32[]{:S(2)}, u32[]{:S(2)}) collective-permute-start(f32[2,32]{1,0:T(2,128)S(1)} %pad_maximum_fusion.3), channel_id=1, source_target_pairs={{0,8},{8,16},{16,24},{24,0},{1,9},{9,17},{17,25},{25,1},{2,10},{10... | collective-permute-start | bytes 776 | tf_op jit(solution)/shard_map/ppermute | solution.py:32
  91.2 7.3 %collective-permute-start.12 = (bf16[1,360,320]{1,2,0:T(8,128)(2,1)S(1)}, bf16[1,360,320]{1,2,0:T(8,128)(2,1)S(1)}, u32[]{:S(2)}, u32[]{:S(2)}) collective-permute-start(bf16[1,360,320]{1,2,0:T(8,128)(2,1)S(1)} %dynamic-slice_convert_fusion.1), channel_id=1, source_target_pairs={{0,4},{1,5},{2,6},{3,7},{4,0},{5,1},{6,2},{7,3},{8,12},{9,13},{10,... | collective-permute-start | bytes 691208 | tf_op jit(solution)/shard_map/ppermute | solution.py:60
  96.1 20.6 %copy-start.6 = (f32[360,320]{0,1:T(8,128)S(1)}, f32[360,320]{0,1:T(8,128)}, u32[]{:S(2)}) copy-start(f32[360,320]{0,1:T(8,128)} %param.15) | copy-start | bytes 1382404
  96.1 20.6 %copy-start.7 = (f32[360,320]{0,1:T(8,128)S(1)}, f32[360,320]{0,1:T(8,128)}, u32[]{:S(2)}) copy-start(f32[360,320]{0,1:T(8,128)} %param.14) | copy-start | bytes 1382404
  98.6 6.4 %collective-permute-start.13 = (bf16[360,320]{0,1:T(8,128)(2,1)S(1)}, bf16[360,320]{0,1:T(8,128)(2,1)S(1)}, u32[]{:S(2)}, u32[]{:S(2)}) collective-permute-start(bf16[360,320]{0,1:T(8,128)(2,1)S(1)} %fusion.38), channel_id=1, source_target_pairs={{0,8},{8,0},{16,24},{24,16},{1,9},{9,1},{17,25},{25,17},{2,10},{10... | collective-permute-start | bytes 691208 | tf_op jit(solution)/shard_map/ppermute | solution.py:74
  105.1 11.7 %collective-permute-start.14 = (bf16[360,320]{0,1:T(8,128)(2,1)S(1)}, bf16[360,320]{0,1:T(8,128)(2,1)S(1)}, u32[]{:S(2)}, u32[]{:S(2)}) collective-permute-start(bf16[360,320]{0,1:T(8,128)(2,1)S(1)} %add_convert_fusion), channel_id=1, source_target_pairs={{0,16},{8,24},{16,0},{24,8},{1,17},{9,25},{17,1},{25,9},{2,18},{10... | collective-permute-start | bytes 691208 | tf_op jit(solution)/shard_map/ppermute | solution.py:74
  (2 other events, 2.7 us)
Sparse Core Ops, SparseCore 0:
  16.5 28.1 all-gather.2

commit v5 on v4

--- a/solution.py
+++ b/solution.py
@@ -1,6 +1,7 @@
 import jax
 import jax.numpy as jnp
 from jax import lax
+from jax.experimental.layout import Layout, with_layout_constraint
 from jax.sharding import PartitionSpec as P
 
 GROUPS = 32
@@ -37,6 +38,10 @@
     return tuple(joined)
 
 
+def row_major(value):
+    return with_layout_constraint(value, Layout(major_to_minor=tuple(range(value.ndim))))
+
+
 def halving_scatter(partial, axis):
     count = lax.axis_size(axis)
     rows, channels = partial.shape[0] // count, partial.shape[1]
@@ -54,11 +59,11 @@
     while step < count:
         bit = (index // step) % 2
         paired = held.reshape(-1, 2, rows, channels)
-        keep = lax.dynamic_index_in_dim(paired, bit, axis=1, keepdims=False)
-        send = lax.dynamic_index_in_dim(paired, 1 - bit, axis=1, keepdims=False)
+        keep = row_major(lax.dynamic_index_in_dim(paired, bit, axis=1, keepdims=False))
+        send = row_major(lax.dynamic_index_in_dim(paired, 1 - bit, axis=1, keepdims=False))
         pairs = [(i, i ^ step) for i in range(count)]
         got = lax.ppermute(send.astype(jnp.bfloat16), axis, pairs)
-        held = keep + got.astype(jnp.float32)
+        held = row_major(keep + got.astype(jnp.float32))
         step *= 2
     return held[0]
 
@@ -126,6 +131,7 @@
     weight_terms = lax.dot_general(
         act_cols, flat_cot, (((0,), (0,)), ((), ())), preferred_element_type=jnp.float32
     )
+    weight_terms = row_major(weight_terms)
     weight_terms, gathered, cot_pad = lax.optimization_barrier((weight_terms, gathered, cot_pad))
     output = jnp.dot(act_cols, gathered, preferred_element_type=jnp.float32)
     block_out = (output.reshape(height_dev, width_dev, channels) * inside).astype(jnp.bfloat16)

time: 125 us -> 124 us (level)
  other arithmetic: 11.5 us -> 8.99 us
  starting transfers between devices: 28.7 us -> 30.2 us
    unnamed x34 -> x37, local copies, waits for them, and re-layouts: 6.34 us -> 15 us
    another operation x1 -> x0, local copies, waits for them, and re-layouts: 8.12 us -> none  [halving_scatter(): paired = held.reshape(-1, 2, rows, channels)]
    dynamic_slice x2 -> x0, local copies, waits for them, and re-layouts: 5.57 us -> none  [the longest x1 3.88 us: halving_scatter(): send = lax.dynamic_index_in_dim(paired, 1 - bit, axis=1, keepdims=False)]
    ppermute x2, waiting for transfers between devices: 4.47 us -> 0.07 us  [with_halo(): lax.ppermute(head, axis, [((i + 1) % count, i) for i in range(ends)])]
    ppermute x2, waiting for transfers between devices: 11.7 us -> 14.7 us  [replicated_sum(): lax.ppermute(mine, axis, pairs).astype(jnp.float32)]
    convert_element_type x2 -> x5, local copies, waits for them, and re-layouts: 0.09 us -> 2.85 us  [halving_scatter(): got = lax.ppermute(send.astype(jnp.bfloat16), axis, pairs)]
    ppermute x0 -> x2, local copies, waits for them, and re-layouts: none -> 2.05 us  [halving_scatter(): got = lax.ppermute(send.astype(jnp.bfloat16), axis, pairs)]
    dot_general x1, matrix products: 2.13 us -> 3.77 us  [local(): upstream = jnp.dot(cot_cols, flipped, preferred_element_type=jnp.float32)]
  transfers between devices with their start and end apart: 16 -> 16, of which waited for: 7 -> 7; matrix products, arithmetic and copies ran while one was open for 21% -> 19% of each run, Pallas kernels for 0% -> 0%
where the time goes in v5:
time: 124 us
  local copies, waits for them, and re-layouts  33.2 us (27%)
  starting transfers between devices  30.2 us (24%)
  waiting for transfers between devices  26.6 us (21%)
  between operations  15.9 us (13%)
  matrix products  9.15 us (7%)
  other arithmetic  8.99 us (7%)
    unnamed x37, local copies, waits for them, and re-layouts  15 us
    ppermute x2, waiting for transfers between devices, replicated_sum(): lax.ppermute(mine, axis, pairs).astype(jnp.float32)  14.7 us
    ppermute x6, starting transfers between devices, space_sum(): lax.ppermute(joined, axis, [(i, (i + shift) % count) for i in range(count)])  10.6 us
    ppermute x2, starting transfers between devices, with_halo(): lax.ppermute(tail, axis, [(i, (i + 1) % count) for i in range(ends)])  9.56 us
    ppermute x3, waiting for transfers between devices, halving_scatter(): got = lax.ppermute(send.astype(jnp.bfloat16), axis, pairs)  7.96 us
    optimization_barrier x2, local copies, waits for them, and re-layouts, local(): lax.optimization_barrier((weight_terms, gathered, cot_pad))  5.98 us
    ppermute x2, starting transfers between devices, replicated_sum(): lax.ppermute(mine, axis, pairs).astype(jnp.float32)  4.03 us
    dot_general x1, matrix products, local(): upstream = jnp.dot(cot_cols, flipped, preferred_element_type=jnp.float32)  3.77 us
  transfers between devices with their start and end apart: 16, of which 7 were waited for; matrix products, arithmetic and copies ran while one was open for 19% of the time, Pallas kernels for 0%

profile of v5, /device:TPU:0, one launch (start us, length us, event | category | flops | bytes accessed | tf_op | source)
XLA Modules:
  0.0 124.0 jit_solution(11651369387194514509)
XLA Ops:
  10.3 5.1 %collective-permute-start.2 = (f32[2,32]{1,0:T(2,128)S(1)}, f32[2,32]{1,0:T(2,128)S(1)}, u32[]{:S(2)}, u32[]{:S(2)}) collective-permute-start(f32[2,32]{1,0:T(2,128)S(1)} %pad_maximum_fusion.2), channel_id=1, source_target_pairs={{0,24},{8,0},{16,8},{24,16},{1,25},{9,1},{17,9},{25,17},{2,26},{10... | collective-permute-start | bytes 776 | tf_op jit(solution)/shard_map/ppermute | solution.py:33
  18.8 5.0 %collective-permute-start.5 = (bf16[1,128,320]{1,2,0:T(8,128)(2,1)S(1)}, bf16[1,128,320]{1,2,0:T(8,128)(2,1)S(1)}, u32[]{:S(2)}, u32[]{:S(2)}) collective-permute-start(bf16[1,128,320]{1,2,0:T(8,128)(2,1)S(1)} %get-tuple-element.34), channel_id=1, source_target_pairs={{0,8},{8,16},{16,24},{1,9},{9,17},{17,25},{2,10},{10,18},{18,26},{... | collective-permute-start | bytes 245768 | tf_op jit(solution)/shard_map/ppermute | solution.py:18
  23.9 2.1 %copy.63 = f32[360,320]{1,0:T(8,128)} copy(f32[360,320]{0,1:T(8,128)} %param.15) | data formatting | bytes 921600 | tf_op args[6]
  29.1 4.6 %collective-permute-start.3 = (bf16[1,128,320]{1,2,0:T(8,128)(2,1)S(1)}, bf16[1,128,320]{1,2,0:T(8,128)(2,1)S(1)}, u32[]{:S(2)}, u32[]{:S(2)}) collective-permute-start(bf16[1,128,320]{1,2,0:T(8,128)(2,1)S(1)} %get-tuple-element.36), channel_id=1, source_target_pairs={{0,8},{8,16},{16,24},{1,9},{9,17},{17,25},{2,10},{10,18},{18,26},{... | collective-permute-start | bytes 245768 | tf_op jit(solution)/shard_map/ppermute | solution.py:18
  34.1 1.6 %collective-permute-done.3 = bf16[1,128,320]{1,2,0:T(8,128)(2,1)S(1)} collective-permute-done((bf16[1,128,320]{1,2,0:T(8,128)(2,1)S(1)}, bf16[1,128,320]{1,2,0:T(8,128)(2,1)S(1)}, u32[]{:S(2)}, u32[]{:S(2)}) %collective-permute-start.3) | collective-permute-done | bytes 81952 | tf_op jit(solution)/shard_map/ppermute | solution.py:18
  38.6 3.5 %convolution_bitcast_fusion = f32[2880,320]{1,0:T(8,128)} fusion(bf16[3,128,2880]{1,2,0:T(8,128)(2,1)S(1)} %slice_dynamic-update-slice_fusion, bf16[3,128,320]{1,2,0:T(8,128)(2,1)S(1)} %bitcast_multiply_fusion), kind=kOutput, calls=%fused_computation | convolution fusion | flops 707788800 | bytes 6144000 | tf_op jit(solution)/shard_map/dot_general | solution.py:131
  42.1 2.3 %all-gather.3.cloned.1.call-done = bf16[8,360,320]{1,2,0:T(8,128)(2,1)} async-done(((bf16[1,360,320]{1,2,0:T(8,128)(2,1)}), bf16[8,360,320]{1,2,0:T(8,128)(2,1)}) %all-gather.3.cloned.1.call-update) | async-done | bytes 1843216 | tf_op jit(solution)/shard_map/all_gather | solution.py:108
  44.4 2.7 %copy.50 = bf16[8,360,320]{1,0,2:T(8,128)(2,1)S(1)} copy(bf16[8,360,320]{1,2,0:T(8,128)(2,1)} %all-gather.3.cloned.1.call-done) | data formatting | bytes 3686400 | tf_op jit(solution)/shard_map/all_gather | solution.py:108
  47.1 2.7 %reshape.128 = bf16[2880,320]{0,1:T(8,128)(2,1)} reshape(bf16[8,360,320]{1,0,2:T(8,128)(2,1)S(1)} %copy.50) | data formatting | bytes 3686400 | tf_op jit(solution)/shard_map/optimization_barrier | solution.py:135
  54.0 3.3 %copy.51 = bf16[2880,320]{1,0:T(8,128)(2,1)S(1)} copy(bf16[2880,320]{0,1:T(8,128)(2,1)} %reshape.128) | data formatting | bytes 3686400 | tf_op jit(solution)/shard_map/optimization_barrier | solution.py:135
  57.3 2.5 %copy.52 = bf16[9,320,320]{2,1,0:T(8,128)(2,1)} copy(bf16[9,320,320]{1,2,0:T(8,128)(2,1)S(1)} %bitcast.112) | data formatting | bytes 3686400 | tf_op jit(solution)/shard_map/transpose | solution.py:147
  59.8 1.7 %bitcast_convert_fusion = bf16[4,360,320]{2,1,0:T(8,128)(2,1)S(1)} fusion(f32[4,2,360,320]{3,2,1,0:T(8,128)} %bitcast.110, s32[]{:T(128)S(6)} %select_n.46), kind=kLoop, calls=%fused_computation.3 | loop fusion | bytes 1843204 | tf_op jit(solution)/shard_map/convert_element_type | solution.py:65
  66.5 1.8 %bitcast_add_fusion = f32[4,360,320]{2,1,0:T(8,128)S(1)} fusion(bf16[4,360,320]{2,1,0:T(8,128)(2,1)S(1)} %copy.57, f32[4,2,360,320]{3,2,1,0:T(8,128)} %bitcast.111, s32[]{:T(128)S(6)} %select_n.45), kind=kLoop, calls=%fused_computation.4 | loop fusion | flops 921600 | bytes 4608004 | tf_op jit(solution)/shard_map/add | solution.py:66
  70.0 1.5 %collective-permute-start.11 = (bf16[2,360,320]{1,2,0:T(8,128)(2,1)S(1)}, bf16[2,360,320]{1,2,0:T(8,128)(2,1)}, u32[]{:S(2)}, u32[]{:S(2)}) collective-permute-start(bf16[2,360,320]{1,2,0:T(8,128)(2,1)S(1)} %copy.60), channel_id=1, source_target_pairs={{0,2},{1,3},{2,0},{3,1},{4,6},{5,7},{6,4},{7,5},{8,10},{9,11},{10,... | collective-permute-start | bytes 1382408 | tf_op jit(solution)/shard_map/ppermute | solution.py:65
  71.6 3.8 %fusion.43 = (f32[320]{0:T(512)S(1)}, f32[320]{0:T(512)S(1)}, f32[3,128,320]{1,2,0:T(8,128)S(1)}) fusion(f32[320]{0:T(512)S(1)} %mul.163, f32[320]{0:T(512)S(1)} %sub.46, f32[3,128]{1,0:T(4,128)S(1)} %get-tuple-element.41, bf16[1,3,128,320]{2,3,1,0:T(8,128)(2,1)S(1)} %copy-done.4, f32[320]{0:T(512)S(1)} %copy-done.8, f32[320]{0:T(512)S(1)} %copy-done.9, ...), kind=kOutput, calls=%fused_computation.88 | convolution fusion | flops 710245760 | bytes 4801536 | tf_op jit(solution)/shard_map/dot_general | solution.py:148
  75.8 3.4 %collective-permute-start.9 = (f32[2,32]{1,0:T(2,128)S(1)}, f32[2,32]{1,0:T(2,128)S(1)}, u32[]{:S(2)}, u32[]{:S(2)}) collective-permute-start(f32[2,32]{1,0:T(2,128)S(1)} %pad_maximum_fusion.3), channel_id=1, source_target_pairs={{0,24},{8,0},{16,8},{24,16},{1,25},{9,1},{17,9},{25,17},{2,26},{10... | collective-permute-start | bytes 776 | tf_op jit(solution)/shard_map/ppermute | solution.py:33
  80.3 3.3 %collective-permute-done.11 = bf16[2,360,320]{1,2,0:T(8,128)(2,1)} collective-permute-done((bf16[2,360,320]{1,2,0:T(8,128)(2,1)S(1)}, bf16[2,360,320]{1,2,0:T(8,128)(2,1)}, u32[]{:S(2)}, u32[]{:S(2)}) %collective-permute-start.11) | collective-permute-done | bytes 460832 | tf_op jit(solution)/shard_map/ppermute | solution.py:65
  84.9 1.5 %bitcast_add_fusion.1 = f32[2,360,320]{2,1,0:T(8,128)S(1)} fusion(bf16[2,360,320]{2,1,0:T(8,128)(2,1)S(1)} %copy.61, f32[2,2,360,320]{3,2,1,0:T(8,128)} %bitcast.114, s32[]{:T(128)S(6)} %select_n.49), kind=kLoop, calls=%fused_computation.15 | loop fusion | flops 460800 | bytes 2304004 | tf_op jit(solution)/shard_map/add | solution.py:66
  87.9 1.8 %fusion.11 = bf16[1,3,128,320]{2,3,1,0:T(8,128)(2,1)} fusion(bf16[3,128,2880]{1,2,0:T(8,128)(2,1)S(1)} %copy-done.3, bf16[2880,320]{0,1:T(8,128)(2,1)S(1)} %copy-done, f32[3,128]{1,0:T(4,128)S(1)} %get-tuple-element.41), kind=kOutput, calls=%fused_computation.13 | convolution fusion | flops 708034560 | bytes 4302336 | tf_op jit(solution)/shard_map/dot_general | solution.py:136
  89.8 4.7 %collective-permute-done.12 = bf16[1,360,320]{2,1,0:T(8,128)(2,1)S(1)} collective-permute-done((bf16[1,360,320]{2,1,0:T(8,128)(2,1)S(1)}, bf16[1,360,320]{2,1,0:T(8,128)(2,1)S(1)}, u32[]{:S(2)}, u32[]{:S(2)}) %collective-permute-start.12) | collective-permute-done | bytes 230432 | tf_op jit(solution)/shard_map/ppermute | solution.py:65
  94.5 1.6 %collective-permute-start.13 = (bf16[360,320]{1,0:T(8,128)(2,1)S(1)}, bf16[360,320]{1,0:T(8,128)(2,1)S(1)}, u32[]{:S(2)}, u32[]{:S(2)}) collective-permute-start(bf16[360,320]{1,0:T(8,128)(2,1)S(1)} %fusion.36), channel_id=1, source_target_pairs={{0,8},{8,0},{16,24},{24,16},{1,9},{9,1},{17,25},{25,17},{2,10},{10... | collective-permute-start | bytes 691208 | tf_op jit(solution)/shard_map/ppermute | solution.py:79
  96.5 5.1 %collective-permute-done.13 = bf16[360,320]{1,0:T(8,128)(2,1)S(1)} collective-permute-done((bf16[360,320]{1,0:T(8,128)(2,1)S(1)}, bf16[360,320]{1,0:T(8,128)(2,1)S(1)}, u32[]{:S(2)}, u32[]{:S(2)}) %collective-permute-start.13) | collective-permute-done | bytes 230432 | tf_op jit(solution)/shard_map/ppermute | solution.py:79
  101.7 2.5 %collective-permute-start.14 = (bf16[360,320]{1,0:T(8,128)(2,1)S(1)}, bf16[360,320]{1,0:T(8,128)(2,1)S(1)}, u32[]{:S(2)}, u32[]{:S(2)}) collective-permute-start(bf16[360,320]{1,0:T(8,128)(2,1)S(1)} %add_convert_fusion), channel_id=1, source_target_pairs={{0,16},{8,24},{16,0},{24,8},{1,17},{9,25},{17,1},{25,9},{2,18},{10... | collective-permute-start | bytes 691208 | tf_op jit(solution)/shard_map/ppermute | solution.py:79
  105.1 9.6 %collective-permute-done.14 = bf16[360,320]{1,0:T(8,128)(2,1)S(1)} collective-permute-done((bf16[360,320]{1,0:T(8,128)(2,1)S(1)}, bf16[360,320]{1,0:T(8,128)(2,1)S(1)}, u32[]{:S(2)}, u32[]{:S(2)}) %collective-permute-start.14) | collective-permute-done | bytes 230432 | tf_op jit(solution)/shard_map/ppermute | solution.py:79
  (103 shorter events, 30.4 us)
Async XLA Ops:
  7.2 20.3 %copy-start.4 = (bf16[1,3,128,320]{2,3,1,0:T(8,128)(2,1)S(1)}, bf16[1,3,128,320]{2,3,1,0:T(8,128)(2,1)}, u32[]{:S(2)}) copy-start(bf16[1,3,128,320]{2,3,1,0:T(8,128)(2,1)} %param.9) | copy-start | bytes 737284
  7.2 18.8 %copy-start.7 = (f32[360,320]{0,1:T(8,128)S(1)}, f32[360,320]{0,1:T(8,128)}, u32[]{:S(2)}) copy-start(f32[360,320]{0,1:T(8,128)} %param.14) | copy-start | bytes 1382404
  7.2 20.3 %copy-start.8 = (f32[320]{0:T(512)S(1)}, f32[320]{0:T(512)}, u32[]{:S(2)}) copy-start(f32[320]{0:T(512)} %param.12) | copy-start | bytes 3844
  7.2 20.3 %copy-start.9 = (f32[320]{0:T(512)S(1)}, f32[320]{0:T(512)}, u32[]{:S(2)}) copy-start(f32[320]{0:T(512)} %param.11) | copy-start | bytes 3844
  7.2 37.2 %all-gather.3.cloned.1.call-start = ((), (), s32[]{:S(2)}) async-start(), calls=%async_computation | async-start | bytes 2211840 | tf_op jit(solution)/shard_map/all_gather | solution.py:108
  10.3 16.7 %collective-permute-start.2 = (f32[2,32]{1,0:T(2,128)S(1)}, f32[2,32]{1,0:T(2,128)S(1)}, u32[]{:S(2)}, u32[]{:S(2)}) collective-permute-start(f32[2,32]{1,0:T(2,128)S(1)} %pad_maximum_fusion.2), channel_id=1, source_target_pairs={{0,24},{8,0},{16,8},{24,16},{1,25},{9,1},{17,9},{25,17},{2,26},{10... | collective-permute-start | bytes 776 | tf_op jit(solution)/shard_map/ppermute | solution.py:33
  15.4 11.6 %collective-permute-start.1 = (f32[2,32]{1,0:T(2,128)S(1)}, f32[2,32]{1,0:T(2,128)S(1)}, u32[]{:S(2)}, u32[]{:S(2)}) collective-permute-start(f32[2,32]{1,0:T(2,128)S(1)} %pad_maximum_fusion.2), channel_id=1, source_target_pairs={{0,16},{8,24},{16,0},{24,8},{1,17},{9,25},{17,1},{25,9},{2,18},{10... | collective-permute-start | bytes 776 | tf_op jit(solution)/shard_map/ppermute | solution.py:33
  15.4 11.6 %collective-permute-start = (f32[2,32]{1,0:T(2,128)S(1)}, f32[2,32]{1,0:T(2,128)S(1)}, u32[]{:S(2)}, u32[]{:S(2)}) collective-permute-start(f32[2,32]{1,0:T(2,128)S(1)} %pad_maximum_fusion.2), channel_id=1, source_target_pairs={{0,8},{8,16},{16,24},{24,0},{1,9},{9,17},{17,25},{25,1},{2,10},{10... | collective-permute-start | bytes 776 | tf_op jit(solution)/shard_map/ppermute | solution.py:33
  17.5 16.2 %collective-permute-start.6 = (bf16[1,128,320]{1,2,0:T(8,128)(2,1)S(1)}, bf16[1,128,320]{1,2,0:T(8,128)(2,1)S(1)}, u32[]{:S(2)}, u32[]{:S(2)}) collective-permute-start(bf16[1,128,320]{1,2,0:T(8,128)(2,1)S(1)} %get-tuple-element.35), channel_id=1, source_target_pairs={{8,0},{16,8},{24,16},{9,1},{17,9},{25,17},{10,2},{18,10},{26,18},{... | collective-permute-start | bytes 245768 | tf_op jit(solution)/shard_map/ppermute | solution.py:20
  18.8 14.9 %collective-permute-start.5 = (bf16[1,128,320]{1,2,0:T(8,128)(2,1)S(1)}, bf16[1,128,320]{1,2,0:T(8,128)(2,1)S(1)}, u32[]{:S(2)}, u32[]{:S(2)}) collective-permute-start(bf16[1,128,320]{1,2,0:T(8,128)(2,1)S(1)} %get-tuple-element.34), channel_id=1, source_target_pairs={{0,8},{8,16},{16,24},{1,9},{9,17},{17,25},{2,10},{10,18},{18,26},{... | collective-permute-start | bytes 245768 | tf_op jit(solution)/shard_map/ppermute | solution.py:18
  27.8 6.3 %collective-permute-start.4 = (bf16[1,128,320]{1,2,0:T(8,128)(2,1)S(1)}, bf16[1,128,320]{1,2,0:T(8,128)(2,1)S(1)}, u32[]{:S(2)}, u32[]{:S(2)}) collective-permute-start(bf16[1,128,320]{1,2,0:T(8,128)(2,1)S(1)} %get-tuple-element.37), channel_id=1, source_target_pairs={{8,0},{16,8},{24,16},{9,1},{17,9},{25,17},{10,2},{18,10},{26,18},{... | collective-permute-start | bytes 245768 | tf_op jit(solution)/shard_map/ppermute | solution.py:20
  29.1 6.6 %collective-permute-start.3 = (bf16[1,128,320]{1,2,0:T(8,128)(2,1)S(1)}, bf16[1,128,320]{1,2,0:T(8,128)(2,1)S(1)}, u32[]{:S(2)}, u32[]{:S(2)}) collective-permute-start(bf16[1,128,320]{1,2,0:T(8,128)(2,1)S(1)} %get-tuple-element.36), channel_id=1, source_target_pairs={{0,8},{8,16},{16,24},{1,9},{9,17},{17,25},{2,10},{10,18},{18,26},{... | collective-permute-start | bytes 245768 | tf_op jit(solution)/shard_map/ppermute | solution.py:18
  62.3 3.5 %collective-permute-start.10 = (bf16[4,360,320]{1,2,0:T(8,128)(2,1)S(1)}, bf16[4,360,320]{1,2,0:T(8,128)(2,1)S(1)}, u32[]{:S(2)}, u32[]{:S(2)}) collective-permute-start(bf16[4,360,320]{1,2,0:T(8,128)(2,1)S(1)} %copy.56), channel_id=1, source_target_pairs={{0,1},{1,0},{2,3},{3,2},{4,5},{5,4},{6,7},{7,6},{8,9},{9,8},{10,11... | collective-permute-start | bytes 2764808 | tf_op jit(solution)/shard_map/ppermute | solution.py:65
  70.0 13.5 %collective-permute-start.11 = (bf16[2,360,320]{1,2,0:T(8,128)(2,1)S(1)}, bf16[2,360,320]{1,2,0:T(8,128)(2,1)}, u32[]{:S(2)}, u32[]{:S(2)}) collective-permute-start(bf16[2,360,320]{1,2,0:T(8,128)(2,1)S(1)} %copy.60), channel_id=1, source_target_pairs={{0,2},{1,3},{2,0},{3,1},{4,6},{5,7},{6,4},{7,5},{8,10},{9,11},{10,... | collective-permute-start | bytes 1382408 | tf_op jit(solution)/shard_map/ppermute | solution.py:65
  75.5 12.5 %copy-start = (bf16[2880,320]{0,1:T(8,128)(2,1)S(1)}, bf16[2880,320]{0,1:T(8,128)(2,1)}, u32[]{:S(2)}) copy-start(bf16[2880,320]{0,1:T(8,128)(2,1)} %reshape.128) | copy-start | bytes 5529604
  75.8 20.3 %collective-permute-start.9 = (f32[2,32]{1,0:T(2,128)S(1)}, f32[2,32]{1,0:T(2,128)S(1)}, u32[]{:S(2)}, u32[]{:S(2)}) collective-permute-start(f32[2,32]{1,0:T(2,128)S(1)} %pad_maximum_fusion.3), channel_id=1, source_target_pairs={{0,24},{8,0},{16,8},{24,16},{1,25},{9,1},{17,9},{25,17},{2,26},{10... | collective-permute-start | bytes 776 | tf_op jit(solution)/shard_map/ppermute | solution.py:33
  79.2 16.9 %collective-permute-start.8 = (f32[2,32]{1,0:T(2,128)S(1)}, f32[2,32]{1,0:T(2,128)S(1)}, u32[]{:S(2)}, u32[]{:S(2)}) collective-permute-start(f32[2,32]{1,0:T(2,128)S(1)} %pad_maximum_fusion.3), channel_id=1, source_target_pairs={{0,16},{8,24},{16,0},{24,8},{1,17},{9,25},{17,1},{25,9},{2,18},{10... | collective-permute-start | bytes 776 | tf_op jit(solution)/shard_map/ppermute | solution.py:33
  79.2 16.9 %collective-permute-start.7 = (f32[2,32]{1,0:T(2,128)S(1)}, f32[2,32]{1,0:T(2,128)S(1)}, u32[]{:S(2)}, u32[]{:S(2)}) collective-permute-start(f32[2,32]{1,0:T(2,128)S(1)} %pad_maximum_fusion.3), channel_id=1, source_target_pairs={{0,8},{8,16},{16,24},{24,0},{1,9},{9,17},{17,25},{25,1},{2,10},{10... | collective-permute-start | bytes 776 | tf_op jit(solution)/shard_map/ppermute | solution.py:33
  84.9 3.0 %copy-start.3 = (bf16[3,128,2880]{1,2,0:T(8,128)(2,1)S(1)}, bf16[3,128,2880]{1,2,0:T(8,128)(2,1)}, u32[]{:S(2)}) copy-start(bf16[3,128,2880]{1,2,0:T(8,128)(2,1)} %copy-done.2) | copy-start | bytes 6635524
  86.5 8.0 %collective-permute-start.12 = (bf16[1,360,320]{2,1,0:T(8,128)(2,1)S(1)}, bf16[1,360,320]{2,1,0:T(8,128)(2,1)S(1)}, u32[]{:S(2)}, u32[]{:S(2)}) collective-permute-start(bf16[1,360,320]{2,1,0:T(8,128)(2,1)S(1)} %dynamic-slice_convert_fusion), channel_id=1, source_target_pairs={{0,4},{1,5},{2,6},{3,7},{4,0},{5,1},{6,2},{7,3},{8,12},{9,13},{10,... | collective-permute-start | bytes 691208 | tf_op jit(solution)/shard_map/ppermute | solution.py:65
  89.8 24.9 %copy-start.5 = (f32[360,320]{1,0:T(8,128)S(1)}, f32[360,320]{1,0:T(8,128)}, u32[]{:S(2)}) copy-start(f32[360,320]{1,0:T(8,128)} %copy.63) | copy-start | bytes 1382404
  89.8 24.9 %copy-start.6 = (f32[360,320]{1,0:T(8,128)S(1)}, f32[360,320]{1,0:T(8,128)}, u32[]{:S(2)}) copy-start(f32[360,320]{1,0:T(8,128)} %copy.62) | copy-start | bytes 1382404
  94.5 7.1 %collective-permute-start.13 = (bf16[360,320]{1,0:T(8,128)(2,1)S(1)}, bf16[360,320]{1,0:T(8,128)(2,1)S(1)}, u32[]{:S(2)}, u32[]{:S(2)}) collective-permute-start(bf16[360,320]{1,0:T(8,128)(2,1)S(1)} %fusion.36), channel_id=1, source_target_pairs={{0,8},{8,0},{16,24},{24,16},{1,9},{9,1},{17,25},{25,17},{2,10},{10... | collective-permute-start | bytes 691208 | tf_op jit(solution)/shard_map/ppermute | solution.py:79
  101.7 13.0 %collective-permute-start.14 = (bf16[360,320]{1,0:T(8,128)(2,1)S(1)}, bf16[360,320]{1,0:T(8,128)(2,1)S(1)}, u32[]{:S(2)}, u32[]{:S(2)}) collective-permute-start(bf16[360,320]{1,0:T(8,128)(2,1)S(1)} %add_convert_fusion), channel_id=1, source_target_pairs={{0,16},{8,24},{16,0},{24,8},{1,17},{9,25},{17,1},{25,9},{2,18},{10... | collective-permute-start | bytes 691208 | tf_op jit(solution)/shard_map/ppermute | solution.py:79
  (2 other events, 2.8 us)
Sparse Core Ops, SparseCore 0:
  16.6 27.7 all-gather.2

commit v6 on v5

--- a/solution.py
+++ b/solution.py
@@ -42,7 +42,7 @@
     return with_layout_constraint(value, Layout(major_to_minor=tuple(range(value.ndim))))
 
 
-def halving_scatter(partial, axis):
+def halving_scatter(partial, axis, companions):
     count = lax.axis_size(axis)
     rows, channels = partial.shape[0] // count, partial.shape[1]
     if count & (count - 1):
@@ -52,7 +52,7 @@
             scatter_dimension=0,
             tiled=False,
         )
-        return summed.astype(jnp.float32)
+        return summed.astype(jnp.float32), companions
     index = lax.axis_index(axis)
     held = partial.reshape(count, rows, channels)
     step = 1
@@ -64,8 +64,10 @@
         pairs = [(i, i ^ step) for i in range(count)]
         got = lax.ppermute(send.astype(jnp.bfloat16), axis, pairs)
         held = row_major(keep + got.astype(jnp.float32))
+        if step == 1:
+            held, companions = lax.optimization_barrier((held, companions))
         step *= 2
-    return held[0]
+    return held[0], companions
 
 
 def replicated_sum(value, axis):
@@ -105,7 +107,7 @@
         & (jnp.arange(width_dev, dtype=jnp.int32) < widths[0])[None, :]
     ).astype(jnp.float32)[..., None]
     cell_count = (heights[0] * widths[0] * (channels // GROUPS)).astype(jnp.float32)
-    gathered = lax.all_gather(weight, "dp", axis=0, tiled=True)
+    gathered = row_major(lax.all_gather(row_major(weight), "dp", axis=0, tiled=True))
     values = latent.astype(jnp.float32) * inside
     group_total, squares = space_sum(
         (group_sum(values, GROUPS), group_sum(values * values, GROUPS)), "space"
@@ -132,7 +134,7 @@
         act_cols, flat_cot, (((0,), (0,)), ((), ())), preferred_element_type=jnp.float32
     )
     weight_terms = row_major(weight_terms)
-    weight_terms, gathered, cot_pad = lax.optimization_barrier((weight_terms, gathered, cot_pad))
+    grad_piece, (gathered, cot_pad) = halving_scatter(weight_terms, "dp", (gathered, cot_pad))
     output = jnp.dot(act_cols, gathered, preferred_element_type=jnp.float32)
     block_out = (output.reshape(height_dev, width_dev, channels) * inside).astype(jnp.bfloat16)
     tap_weights = gathered.reshape(9, channels, channels)
@@ -151,7 +153,6 @@
     scaled = upstream.reshape(height_dev, width_dev, channels) * silu_slope * inside * norm_gain
     local_first = group_sum(scaled, GROUPS)
     local_second = group_sum(scaled * normed, GROUPS)
-    grad_piece = halving_scatter(weight_terms, "dp")
     sum_first, sum_second = space_sum((local_first, local_second), "space")
     grad_piece = replicated_sum(grad_piece, "space")
     first = sum_first / cell_count

time: 124 us -> 114 us (0.919)
  local copies, waits for them, and re-layouts: 33.2 us -> 21.8 us
  other arithmetic: 8.99 us -> 11.5 us
  matrix products: 9.15 us -> 7.2 us
    optimization_barrier x2 -> x0, local copies, waits for them, and re-layouts: 5.98 us -> none  [local(): lax.optimization_barrier((weight_terms, gathered, cot_pad))]
    unnamed x37 -> x39, local copies, waits for them, and re-layouts: 15 us -> 9.07 us
    ppermute x6, waiting for transfers between devices: 0.02 us -> 4.33 us  [space_sum(): lax.ppermute(joined, axis, [(i, (i + shift) % count) for i in range(count)])]
    transpose x1 -> x0, local copies, waits for them, and re-layouts: 2.55 us -> none  [local(): flipped = tap_weights.transpose(0, 2, 1).reshape(9 * channels, channels)]
    reshape x0 -> x1, local copies, waits for them, and re-layouts: none -> 2.47 us  [local(): tap_weights = gathered.reshape(9, channels, channels)]
    all_gather x1, waiting for transfers between devices: 2.29 us -> 0.01 us  [local(): lax.all_gather(row_major(weight), 'dp', axis=0, tiled=True)]
    dot_general x1, matrix products: 3.54 us -> 1.52 us  [local(): lax.dot_general(act_cols, flat_cot, (((0,), (0,)), ((), ())), preferred_e...]
    ppermute x3, waiting for transfers between devices: 7.96 us -> 6.25 us  [halving_scatter(): got = lax.ppermute(send.astype(jnp.bfloat16), axis, pairs)]
  transfers between devices with their start and end apart: 16 -> 16, of which waited for: 7 -> 9; matrix products, arithmetic and copies ran while one was open for 19% -> 21% of each run, Pallas kernels for 0% -> 0%
where the time goes in v6:
time: 114 us; the launch traced here: 113 us
  starting transfers between devices  31.1 us (27%)
  waiting for transfers between devices  25.9 us (23%)
  local copies, waits for them, and re-layouts  21.8 us (19%)
  between operations  15.9 us (14%)
  other arithmetic  11.5 us (10%)
  matrix products  7.2 us (6%)
    ppermute x2, waiting for transfers between devices, replicated_sum(): lax.ppermute(mine, axis, pairs).astype(jnp.float32)  14.1 us
    ppermute x6, starting transfers between devices, space_sum(): lax.ppermute(joined, axis, [(i, (i + shift) % count) for i in range(count)])  11.8 us
    ppermute x2, starting transfers between devices, with_halo(): lax.ppermute(tail, axis, [(i, (i + 1) % count) for i in range(ends)])  9.47 us
    unnamed x39, local copies, waits for them, and re-layouts  9.07 us
    ppermute x3, waiting for transfers between devices, halving_scatter(): got = lax.ppermute(send.astype(jnp.bfloat16), axis, pairs)  6.25 us
    add x2, other arithmetic, halving_scatter(): held = row_major(keep + got.astype(jnp.float32))  4.76 us
    ppermute x6, waiting for transfers between devices, space_sum(): lax.ppermute(joined, axis, [(i, (i + shift) % count) for i in range(count)])  4.33 us
    ppermute x2, starting transfers between devices, replicated_sum(): lax.ppermute(mine, axis, pairs).astype(jnp.float32)  4.13 us
  transfers between devices with their start and end apart: 16, of which 9 were waited for; matrix products, arithmetic and copies ran while one was open for 21% of the time, Pallas kernels for 0%

profile of v6, /device:TPU:0, one launch (start us, length us, event | category | flops | bytes accessed | tf_op | source)
XLA Modules:
  0.0 113.5 jit_solution(2625010795951970194)
XLA Ops:
  10.2 5.1 %collective-permute-start.2 = (f32[2,32]{1,0:T(2,128)S(1)}, f32[2,32]{1,0:T(2,128)S(1)}, u32[]{:S(2)}, u32[]{:S(2)}) collective-permute-start(f32[2,32]{1,0:T(2,128)S(1)} %pad_maximum_fusion.2), channel_id=1, source_target_pairs={{0,24},{8,0},{16,8},{24,16},{1,25},{9,1},{17,9},{25,17},{2,26},{10... | collective-permute-start | bytes 776 | tf_op jit(solution)/shard_map/ppermute | solution.py:33
  16.6 3.2 %collective-permute-done.1 = f32[2,32]{1,0:T(2,128)S(1)} collective-permute-done((f32[2,32]{1,0:T(2,128)S(1)}, f32[2,32]{1,0:T(2,128)S(1)}, u32[]{:S(2)}, u32[]{:S(2)}) %collective-permute-start.1) | collective-permute-done | bytes 288 | tf_op jit(solution)/shard_map/ppermute | solution.py:33
  23.8 4.6 %collective-permute-start.3 = (bf16[1,128,320]{1,2,0:T(8,128)(2,1)S(1)}, bf16[1,128,320]{1,2,0:T(8,128)(2,1)S(1)}, u32[]{:S(2)}, u32[]{:S(2)}) collective-permute-start(bf16[1,128,320]{1,2,0:T(8,128)(2,1)S(1)} %get-tuple-element.36), channel_id=1, source_target_pairs={{0,8},{8,16},{16,24},{1,9},{9,17},{17,25},{2,10},{10,18},{18,26},{... | collective-permute-start | bytes 245768 | tf_op jit(solution)/shard_map/ppermute | solution.py:18
  31.9 1.5 %fusion.46 = f32[2880,320,1]{1,0,2:T(8,128)S(1)} fusion(bf16[3,128,2880]{1,2,0:T(8,128)(2,1)S(1)} %slice_dynamic-update-slice_fusion, bf16[3,128,320]{1,2,0:T(8,128)(2,1)S(1)} %bitcast_multiply_fusion), kind=kOutput, calls=%fused_computation.90 | convolution fusion | flops 707788800 | bytes 6144000 | tf_op jit(solution)/shard_map/dot_general | solution.py:133
  33.5 2.0 %copy-done = f32[2880,320,1]{1,0,2:T(8,128)} copy-done((f32[2880,320,1]{1,0,2:T(8,128)}, f32[2880,320,1]{1,0,2:T(8,128)S(1)}, u32[]{:S(2)}) %copy-start) | copy-done | bytes 3686424
  35.6 1.4 %copy.56 = bf16[4,360,320]{1,2,0:T(8,128)(2,1)} copy(bf16[4,360,320]{2,1,0:T(8,128)(2,1)S(1)} %bitcast_convert_fusion) | data formatting | bytes 1843200 | tf_op jit(solution)/shard_map/convert_element_type | solution.py:65
  38.3 4.9 %collective-permute-start.6 = (bf16[1,128,320]{1,2,0:T(8,128)(2,1)S(1)}, bf16[1,128,320]{1,2,0:T(8,128)(2,1)S(1)}, u32[]{:S(2)}, u32[]{:S(2)}) collective-permute-start(bf16[1,128,320]{1,2,0:T(8,128)(2,1)S(1)} %get-tuple-element.34), channel_id=1, source_target_pairs={{0,8},{8,16},{16,24},{1,9},{9,17},{17,25},{2,10},{10,18},{18,26},{... | collective-permute-start | bytes 245768 | tf_op jit(solution)/shard_map/ppermute | solution.py:18
  46.7 3.3 %bitcast_add_fusion = f32[4,360,320]{2,1,0:T(8,128)} fusion(bf16[4,360,320]{2,1,0:T(8,128)(2,1)S(1)} %copy.57, f32[4,2,360,320]{3,2,1,0:T(8,128)} %bitcast.110, s32[]{:T(128)S(6)} %select_n.45), kind=kLoop, calls=%fused_computation.3 | loop fusion | flops 921600 | bytes 4608004 | tf_op jit(solution)/shard_map/add | solution.py:66
  50.0 3.0 %copy.60 = bf16[8,360,320]{2,1,0:T(8,128)(2,1)S(1)} copy(bf16[8,360,320]{1,2,0:T(8,128)(2,1)} %all-gather.3.cloned.1.call-done) | data formatting | bytes 3686400 | tf_op jit(solution)/shard_map/all_gather | solution.py:110
  54.2 1.4 %copy-done.8 = bf16[3,128,2880]{1,2,0:T(8,128)(2,1)} copy-done((bf16[3,128,2880]{1,2,0:T(8,128)(2,1)}, bf16[3,128,2880]{1,2,0:T(8,128)(2,1)S(1)}, u32[]{:S(2)}) %copy-start.8) | copy-done | bytes 2211864
  55.6 2.5 %copy.62 = bf16[9,320,320]{1,2,0:T(8,128)(2,1)} copy(bf16[9,320,320]{2,1,0:T(8,128)(2,1)S(1)} %bitcast.111) | data formatting | bytes 3686400 | tf_op jit(solution)/shard_map/reshape | solution.py:140
  60.4 1.5 %collective-permute-start.11 = (bf16[2,360,320]{1,2,0:T(8,128)(2,1)}, bf16[2,360,320]{1,2,0:T(8,128)(2,1)}, u32[]{:S(2)}, u32[]{:S(2)}) collective-permute-start(bf16[2,360,320]{1,2,0:T(8,128)(2,1)} %copy.66), channel_id=1, source_target_pairs={{0,2},{1,3},{2,0},{3,1},{4,6},{5,7},{6,4},{7,5},{8,10},{9,11},{10,... | collective-permute-start | bytes 1382408 | tf_op jit(solution)/shard_map/ppermute | solution.py:65
  61.9 3.8 %fusion.43 = (f32[320]{0:T(512)S(1)}, f32[320]{0:T(512)S(1)}, f32[3,128,320]{1,2,0:T(8,128)S(1)}) fusion(f32[320]{0:T(512)S(1)} %mul.163, f32[320]{0:T(512)S(1)} %sub.46, f32[3,128]{1,0:T(4,128)S(1)} %get-tuple-element.41, bf16[1,3,128,320]{2,3,1,0:T(8,128)(2,1)S(1)} %copy-done.3, f32[320]{0:T(512)S(1)} %copy-done.9, f32[320]{0:T(512)S(1)} %copy-done.10, ...), kind=kOutput, calls=%fused_computation.87 | convolution fusion | flops 710245760 | bytes 4801536 | tf_op jit(solution)/shard_map/dot_general | solution.py:150
  66.1 3.4 %collective-permute-start.10 = (f32[2,32]{1,0:T(2,128)S(1)}, f32[2,32]{1,0:T(2,128)S(1)}, u32[]{:S(2)}, u32[]{:S(2)}) collective-permute-start(f32[2,32]{1,0:T(2,128)S(1)} %pad_maximum_fusion.3), channel_id=1, source_target_pairs={{0,24},{8,0},{16,8},{24,16},{1,25},{9,1},{17,9},{25,17},{2,26},{10... | collective-permute-start | bytes 776 | tf_op jit(solution)/shard_map/ppermute | solution.py:33
  70.1 1.7 %collective-permute-start.8 = (f32[2,32]{1,0:T(2,128)S(1)}, f32[2,32]{1,0:T(2,128)S(1)}, u32[]{:S(2)}, u32[]{:S(2)}) collective-permute-start(f32[2,32]{1,0:T(2,128)S(1)} %pad_maximum_fusion.3), channel_id=1, source_target_pairs={{0,8},{8,16},{16,24},{24,0},{1,9},{9,17},{17,25},{25,1},{2,10},{10... | collective-permute-start | bytes 776 | tf_op jit(solution)/shard_map/ppermute | solution.py:33
  71.8 2.0 %collective-permute-done.11 = bf16[2,360,320]{1,2,0:T(8,128)(2,1)} collective-permute-done((bf16[2,360,320]{1,2,0:T(8,128)(2,1)}, bf16[2,360,320]{1,2,0:T(8,128)(2,1)}, u32[]{:S(2)}, u32[]{:S(2)}) %collective-permute-start.11) | collective-permute-done | bytes 460832 | tf_op jit(solution)/shard_map/ppermute | solution.py:65
  75.2 1.5 %bitcast_add_fusion.1 = f32[2,360,320]{2,1,0:T(8,128)S(1)} fusion(bf16[2,360,320]{2,1,0:T(8,128)(2,1)S(1)} %copy.67, f32[2,2,360,320]{3,2,1,0:T(8,128)} %bitcast.114, s32[]{:T(128)S(6)} %select_n.49), kind=kLoop, calls=%fused_computation.14 | loop fusion | flops 460800 | bytes 2304004 | tf_op jit(solution)/shard_map/add | solution.py:66
  76.7 1.6 %collective-permute-start.12 = (bf16[1,360,320]{2,1,0:T(8,128)(2,1)S(1)}, bf16[1,360,320]{2,1,0:T(8,128)(2,1)S(1)}, u32[]{:S(2)}, u32[]{:S(2)}) collective-permute-start(bf16[1,360,320]{2,1,0:T(8,128)(2,1)S(1)} %dynamic-slice_convert_fusion), channel_id=1, source_target_pairs={{0,4},{1,5},{2,6},{3,7},{4,0},{5,1},{6,2},{7,3},{8,12},{9,13},{10,... | collective-permute-start | bytes 691208 | tf_op jit(solution)/shard_map/ppermute | solution.py:65
  78.3 1.9 %fusion.11 = bf16[1,3,128,320]{2,3,1,0:T(8,128)(2,1)} fusion(bf16[3,128,2880]{1,2,0:T(8,128)(2,1)S(1)} %copy-done.2, bf16[2880,320]{1,0:T(8,128)(2,1)S(1)} %bitcast.112, f32[3,128]{1,0:T(4,128)S(1)} %get-tuple-element.41), kind=kOutput, calls=%fused_computation.12 | convolution fusion | flops 708034560 | bytes 4302336 | tf_op jit(solution)/shard_map/dot_general | solution.py:138
  80.2 4.3 %collective-permute-done.12 = bf16[1,360,320]{2,1,0:T(8,128)(2,1)S(1)} collective-permute-done((bf16[1,360,320]{2,1,0:T(8,128)(2,1)S(1)}, bf16[1,360,320]{2,1,0:T(8,128)(2,1)S(1)}, u32[]{:S(2)}, u32[]{:S(2)}) %collective-permute-start.12) | collective-permute-done | bytes 230432 | tf_op jit(solution)/shard_map/ppermute | solution.py:65
  84.6 1.9 %collective-permute-start.13 = (bf16[360,320]{1,0:T(8,128)(2,1)S(1)}, bf16[360,320]{1,0:T(8,128)(2,1)S(1)}, u32[]{:S(2)}, u32[]{:S(2)}) collective-permute-start(bf16[360,320]{1,0:T(8,128)(2,1)S(1)} %fusion.36), channel_id=1, source_target_pairs={{0,8},{8,0},{16,24},{24,16},{1,9},{9,1},{17,25},{25,17},{2,10},{10... | collective-permute-start | bytes 691208 | tf_op jit(solution)/shard_map/ppermute | solution.py:81
  86.9 4.5 %collective-permute-done.13 = bf16[360,320]{1,0:T(8,128)(2,1)S(1)} collective-permute-done((bf16[360,320]{1,0:T(8,128)(2,1)S(1)}, bf16[360,320]{1,0:T(8,128)(2,1)S(1)}, u32[]{:S(2)}, u32[]{:S(2)}) %collective-permute-start.13) | collective-permute-done | bytes 230432 | tf_op jit(solution)/shard_map/ppermute | solution.py:81
  91.5 2.2 %collective-permute-start.14 = (bf16[360,320]{1,0:T(8,128)(2,1)S(1)}, bf16[360,320]{1,0:T(8,128)(2,1)S(1)}, u32[]{:S(2)}, u32[]{:S(2)}) collective-permute-start(bf16[360,320]{1,0:T(8,128)(2,1)S(1)} %add_convert_fusion), channel_id=1, source_target_pairs={{0,16},{8,24},{16,0},{24,8},{1,17},{9,25},{17,1},{25,9},{2,18},{10... | collective-permute-start | bytes 691208 | tf_op jit(solution)/shard_map/ppermute | solution.py:81
  94.6 9.6 %collective-permute-done.14 = bf16[360,320]{1,0:T(8,128)(2,1)S(1)} collective-permute-done((bf16[360,320]{1,0:T(8,128)(2,1)S(1)}, bf16[360,320]{1,0:T(8,128)(2,1)S(1)}, u32[]{:S(2)}, u32[]{:S(2)}) %collective-permute-start.14) | collective-permute-done | bytes 230432 | tf_op jit(solution)/shard_map/ppermute | solution.py:81
  (103 shorter events, 25.0 us)
Async XLA Ops:
  7.2 42.8 %all-gather.3.cloned.1.call-start = ((), (), s32[]{:S(2)}) async-start(), calls=%async_computation | async-start | bytes 2211840 | tf_op jit(solution)/shard_map/all_gather | solution.py:110
  10.2 6.4 %collective-permute-start.2 = (f32[2,32]{1,0:T(2,128)S(1)}, f32[2,32]{1,0:T(2,128)S(1)}, u32[]{:S(2)}, u32[]{:S(2)}) collective-permute-start(f32[2,32]{1,0:T(2,128)S(1)} %pad_maximum_fusion.2), channel_id=1, source_target_pairs={{0,24},{8,0},{16,8},{24,16},{1,25},{9,1},{17,9},{25,17},{2,26},{10... | collective-permute-start | bytes 776 | tf_op jit(solution)/shard_map/ppermute | solution.py:33
  15.3 4.5 %collective-permute-start.1 = (f32[2,32]{1,0:T(2,128)S(1)}, f32[2,32]{1,0:T(2,128)S(1)}, u32[]{:S(2)}, u32[]{:S(2)}) collective-permute-start(f32[2,32]{1,0:T(2,128)S(1)} %pad_maximum_fusion.2), channel_id=1, source_target_pairs={{0,16},{8,24},{16,0},{24,8},{1,17},{9,25},{17,1},{25,9},{2,18},{10... | collective-permute-start | bytes 776 | tf_op jit(solution)/shard_map/ppermute | solution.py:33
  15.3 5.4 %collective-permute-start = (f32[2,32]{1,0:T(2,128)S(1)}, f32[2,32]{1,0:T(2,128)S(1)}, u32[]{:S(2)}, u32[]{:S(2)}) collective-permute-start(f32[2,32]{1,0:T(2,128)S(1)} %pad_maximum_fusion.2), channel_id=1, source_target_pairs={{0,8},{8,16},{16,24},{24,0},{1,9},{9,17},{17,25},{25,1},{2,10},{10... | collective-permute-start | bytes 776 | tf_op jit(solution)/shard_map/ppermute | solution.py:33
  21.1 10.0 %copy-start.3 = (bf16[1,3,128,320]{2,3,1,0:T(8,128)(2,1)S(1)}, bf16[1,3,128,320]{2,3,1,0:T(8,128)(2,1)}, u32[]{:S(2)}) copy-start(bf16[1,3,128,320]{2,3,1,0:T(8,128)(2,1)} %param.9) | copy-start | bytes 737284
  21.1 10.0 %copy-start.9 = (f32[320]{0:T(512)S(1)}, f32[320]{0:T(512)}, u32[]{:S(2)}) copy-start(f32[320]{0:T(512)} %param.12) | copy-start | bytes 3844
  21.1 10.0 %copy-start.10 = (f32[320]{0:T(512)S(1)}, f32[320]{0:T(512)}, u32[]{:S(2)}) copy-start(f32[320]{0:T(512)} %param.11) | copy-start | bytes 3844
  22.5 6.8 %collective-permute-start.4 = (bf16[1,128,320]{1,2,0:T(8,128)(2,1)S(1)}, bf16[1,128,320]{1,2,0:T(8,128)(2,1)S(1)}, u32[]{:S(2)}, u32[]{:S(2)}) collective-permute-start(bf16[1,128,320]{1,2,0:T(8,128)(2,1)S(1)} %get-tuple-element.37), channel_id=1, source_target_pairs={{8,0},{16,8},{24,16},{9,1},{17,9},{25,17},{10,2},{18,10},{26,18},{... | collective-permute-start | bytes 245768 | tf_op jit(solution)/shard_map/ppermute | solution.py:20
  23.8 6.6 %collective-permute-start.3 = (bf16[1,128,320]{1,2,0:T(8,128)(2,1)S(1)}, bf16[1,128,320]{1,2,0:T(8,128)(2,1)S(1)}, u32[]{:S(2)}, u32[]{:S(2)}) collective-permute-start(bf16[1,128,320]{1,2,0:T(8,128)(2,1)S(1)} %get-tuple-element.36), channel_id=1, source_target_pairs={{0,8},{8,16},{16,24},{1,9},{9,17},{17,25},{2,10},{10,18},{18,26},{... | collective-permute-start | bytes 245768 | tf_op jit(solution)/shard_map/ppermute | solution.py:18
  35.5 7.8 %copy-start.6 = (f32[360,320]{0,1:T(8,128)S(1)}, f32[360,320]{0,1:T(8,128)}, u32[]{:S(2)}) copy-start(f32[360,320]{0,1:T(8,128)} %param.15) | copy-start | bytes 1382404
  35.6 8.8 %copy-start.7 = (f32[360,320]{0,1:T(8,128)S(1)}, f32[360,320]{0,1:T(8,128)}, u32[]{:S(2)}) copy-start(f32[360,320]{0,1:T(8,128)} %param.14) | copy-start | bytes 1382404
  37.0 9.0 %collective-permute-start.5 = (bf16[4,360,320]{1,2,0:T(8,128)(2,1)}, bf16[4,360,320]{1,2,0:T(8,128)(2,1)S(1)}, u32[]{:S(2)}, u32[]{:S(2)}) collective-permute-start(bf16[4,360,320]{1,2,0:T(8,128)(2,1)} %copy.56), channel_id=1, source_target_pairs={{0,1},{1,0},{2,3},{3,2},{4,5},{5,4},{6,7},{7,6},{8,9},{9,8},{10,11... | collective-permute-start | bytes 2764808 | tf_op jit(solution)/shard_map/ppermute | solution.py:65
  37.0 8.4 %collective-permute-start.7 = (bf16[1,128,320]{1,2,0:T(8,128)(2,1)S(1)}, bf16[1,128,320]{1,2,0:T(8,128)(2,1)S(1)}, u32[]{:S(2)}, u32[]{:S(2)}) collective-permute-start(bf16[1,128,320]{1,2,0:T(8,128)(2,1)S(1)} %get-tuple-element.35), channel_id=1, source_target_pairs={{8,0},{16,8},{24,16},{9,1},{17,9},{25,17},{10,2},{18,10},{26,18},{... | collective-permute-start | bytes 245768 | tf_op jit(solution)/shard_map/ppermute | solution.py:20
  38.3 7.3 %collective-permute-start.6 = (bf16[1,128,320]{1,2,0:T(8,128)(2,1)S(1)}, bf16[1,128,320]{1,2,0:T(8,128)(2,1)S(1)}, u32[]{:S(2)}, u32[]{:S(2)}) collective-permute-start(bf16[1,128,320]{1,2,0:T(8,128)(2,1)S(1)} %get-tuple-element.34), channel_id=1, source_target_pairs={{0,8},{8,16},{16,24},{1,9},{9,17},{17,25},{2,10},{10,18},{18,26},{... | collective-permute-start | bytes 245768 | tf_op jit(solution)/shard_map/ppermute | solution.py:18
  60.4 13.5 %collective-permute-start.11 = (bf16[2,360,320]{1,2,0:T(8,128)(2,1)}, bf16[2,360,320]{1,2,0:T(8,128)(2,1)}, u32[]{:S(2)}, u32[]{:S(2)}) collective-permute-start(bf16[2,360,320]{1,2,0:T(8,128)(2,1)} %copy.66), channel_id=1, source_target_pairs={{0,2},{1,3},{2,0},{3,1},{4,6},{5,7},{6,4},{7,5},{8,10},{9,11},{10,... | collective-permute-start | bytes 1382408 | tf_op jit(solution)/shard_map/ppermute | solution.py:65
  66.1 20.4 %collective-permute-start.10 = (f32[2,32]{1,0:T(2,128)S(1)}, f32[2,32]{1,0:T(2,128)S(1)}, u32[]{:S(2)}, u32[]{:S(2)}) collective-permute-start(f32[2,32]{1,0:T(2,128)S(1)} %pad_maximum_fusion.3), channel_id=1, source_target_pairs={{0,24},{8,0},{16,8},{24,16},{1,25},{9,1},{17,9},{25,17},{2,26},{10... | collective-permute-start | bytes 776 | tf_op jit(solution)/shard_map/ppermute | solution.py:33
  69.5 16.9 %collective-permute-start.9 = (f32[2,32]{1,0:T(2,128)S(1)}, f32[2,32]{1,0:T(2,128)S(1)}, u32[]{:S(2)}, u32[]{:S(2)}) collective-permute-start(f32[2,32]{1,0:T(2,128)S(1)} %pad_maximum_fusion.3), channel_id=1, source_target_pairs={{0,16},{8,24},{16,0},{24,8},{1,17},{9,25},{17,1},{25,9},{2,18},{10... | collective-permute-start | bytes 776 | tf_op jit(solution)/shard_map/ppermute | solution.py:33
  70.1 16.4 %collective-permute-start.8 = (f32[2,32]{1,0:T(2,128)S(1)}, f32[2,32]{1,0:T(2,128)S(1)}, u32[]{:S(2)}, u32[]{:S(2)}) collective-permute-start(f32[2,32]{1,0:T(2,128)S(1)} %pad_maximum_fusion.3), channel_id=1, source_target_pairs={{0,8},{8,16},{16,24},{24,0},{1,9},{9,17},{17,25},{25,1},{2,10},{10... | collective-permute-start | bytes 776 | tf_op jit(solution)/shard_map/ppermute | solution.py:33
  75.2 3.1 %copy-start.2 = (bf16[3,128,2880]{1,2,0:T(8,128)(2,1)S(1)}, bf16[3,128,2880]{1,2,0:T(8,128)(2,1)}, u32[]{:S(2)}) copy-start(bf16[3,128,2880]{1,2,0:T(8,128)(2,1)} %copy-done.1) | copy-start | bytes 6635524
  76.7 7.8 %collective-permute-start.12 = (bf16[1,360,320]{2,1,0:T(8,128)(2,1)S(1)}, bf16[1,360,320]{2,1,0:T(8,128)(2,1)S(1)}, u32[]{:S(2)}, u32[]{:S(2)}) collective-permute-start(bf16[1,360,320]{2,1,0:T(8,128)(2,1)S(1)} %dynamic-slice_convert_fusion), channel_id=1, source_target_pairs={{0,4},{1,5},{2,6},{3,7},{4,0},{5,1},{6,2},{7,3},{8,12},{9,13},{10,... | collective-permute-start | bytes 691208 | tf_op jit(solution)/shard_map/ppermute | solution.py:65
  80.2 24.0 %copy-start.4 = (f32[360,320]{1,0:T(8,128)S(1)}, f32[360,320]{1,0:T(8,128)}, u32[]{:S(2)}) copy-start(f32[360,320]{1,0:T(8,128)} %copy.69) | copy-start | bytes 1382404
  80.2 24.0 %copy-start.5 = (f32[360,320]{1,0:T(8,128)S(1)}, f32[360,320]{1,0:T(8,128)}, u32[]{:S(2)}) copy-start(f32[360,320]{1,0:T(8,128)} %copy.68) | copy-start | bytes 1382404
  84.6 6.8 %collective-permute-start.13 = (bf16[360,320]{1,0:T(8,128)(2,1)S(1)}, bf16[360,320]{1,0:T(8,128)(2,1)S(1)}, u32[]{:S(2)}, u32[]{:S(2)}) collective-permute-start(bf16[360,320]{1,0:T(8,128)(2,1)S(1)} %fusion.36), channel_id=1, source_target_pairs={{0,8},{8,0},{16,24},{24,16},{1,9},{9,1},{17,25},{25,17},{2,10},{10... | collective-permute-start | bytes 691208 | tf_op jit(solution)/shard_map/ppermute | solution.py:81
  91.5 12.7 %collective-permute-start.14 = (bf16[360,320]{1,0:T(8,128)(2,1)S(1)}, bf16[360,320]{1,0:T(8,128)(2,1)S(1)}, u32[]{:S(2)}, u32[]{:S(2)}) collective-permute-start(bf16[360,320]{1,0:T(8,128)(2,1)S(1)} %add_convert_fusion), channel_id=1, source_target_pairs={{0,16},{8,24},{16,0},{24,8},{1,17},{9,25},{17,1},{25,9},{2,18},{10... | collective-permute-start | bytes 691208 | tf_op jit(solution)/shard_map/ppermute | solution.py:81
  (3 other events, 4.9 us)
Sparse Core Ops, SparseCore 0:
  16.5 27.7 all-gather.2

commit v7 on v6

--- a/solution.py
+++ b/solution.py
@@ -67,7 +67,18 @@
         if step == 1:
             held, companions = lax.optimization_barrier((held, companions))
         step *= 2
-    return held[0], companions
+        if step < count <= 4 * step:
+            break
+    if step == count:
+        return held[0], companions
+    spots = count // step
+    own = index // step
+    total = lax.dynamic_index_in_dim(held, own, keepdims=False)
+    for shift in range(1, spots):
+        send = lax.dynamic_index_in_dim(held, own ^ shift, keepdims=False)
+        pairs = [(i, i ^ (shift * step)) for i in range(count)]
+        total = total + lax.ppermute(send.astype(jnp.bfloat16), axis, pairs).astype(jnp.float32)
+    return total, companions
 
 
 def replicated_sum(value, axis):
@@ -154,7 +165,9 @@
     local_first = group_sum(scaled, GROUPS)
     local_second = group_sum(scaled * normed, GROUPS)
     sum_first, sum_second = space_sum((local_first, local_second), "space")
-    grad_piece = replicated_sum(grad_piece, "space")
+    grad_piece = with_layout_constraint(
+        replicated_sum(grad_piece, "space"), Layout(major_to_minor=(1, 0))
+    )
     first = sum_first / cell_count
     second = sum_second / cell_count
     input_grad = (

time: 114 us -> 116 us (1.018)
  matrix products: 7.2 us -> 9.45 us
  waiting for transfers between devices: 25.9 us -> 28 us
  other arithmetic: 11.5 us -> 9.76 us
    ppermute x3 -> x1, waiting for transfers between devices: 6.25 us -> 0.01 us  [halving_scatter(): got = lax.ppermute(send.astype(jnp.bfloat16), axis, pairs)]
    ppermute x0 -> x3, waiting for transfers between devices: none -> 4.53 us  [halving_scatter(): lax.ppermute(send.astype(jnp.bfloat16), axis, pairs).astype(jnp.float32)]
    unnamed x39 -> x35, local copies, waits for them, and re-layouts: 9.07 us -> 5 us
    ppermute x0 -> x3, starting transfers between devices: none -> 3.55 us  [halving_scatter(): lax.ppermute(send.astype(jnp.bfloat16), axis, pairs).astype(jnp.float32)]
    ppermute x3 -> x1, starting transfers between devices: 3.08 us -> 0.01 us  [halving_scatter(): got = lax.ppermute(send.astype(jnp.bfloat16), axis, pairs)]
    add x2 -> x1, other arithmetic: 4.76 us -> 2.15 us  [halving_scatter(): held = row_major(keep + got.astype(jnp.float32))]
    convert_element_type x5 -> x2, local copies, waits for them, and re-layouts: 3.86 us -> 1.51 us  [halving_scatter(): got = lax.ppermute(send.astype(jnp.bfloat16), axis, pairs)]
    reshape x1, local copies, waits for them, and re-layouts: 2.47 us -> 4.26 us  [local(): tap_weights = gathered.reshape(9, channels, channels)]
  transfers between devices with their start and end apart: 16 -> 17, of which waited for: 9 -> 12; matrix products, arithmetic and copies ran while one was open for 21% -> 17% of each run, Pallas kernels for 0% -> 0%
where the time goes in v7:
time: 116 us
  starting transfers between devices  31.4 us (27%)
  waiting for transfers between devices  28 us (24%)
  local copies, waits for them, and re-layouts  21.4 us (18%)
  between operations  15.8 us (14%)
  other arithmetic  9.76 us (8%)
  matrix products  9.45 us (8%)
    ppermute x2, waiting for transfers between devices, replicated_sum(): lax.ppermute(mine, axis, pairs).astype(jnp.float32)  15.5 us
    ppermute x6, starting transfers between devices, space_sum(): lax.ppermute(joined, axis, [(i, (i + shift) % count) for i in range(count)])  11.8 us
    ppermute x2, starting transfers between devices, with_halo(): lax.ppermute(tail, axis, [(i, (i + 1) % count) for i in range(ends)])  9.47 us
    unnamed x35, local copies, waits for them, and re-layouts  5 us
    ppermute x6, waiting for transfers between devices, space_sum(): lax.ppermute(joined, axis, [(i, (i + shift) % count) for i in range(count)])  4.62 us
    ppermute x3, waiting for transfers between devices, halving_scatter(): lax.ppermute(send.astype(jnp.bfloat16), axis, pairs).astype(jnp.float32)  4.53 us
    dot_general x1, matrix products, local(): upstream = jnp.dot(cot_cols, flipped, preferred_element_type=jnp.float32)  4.4 us
    reshape x1, local copies, waits for them, and re-layouts, local(): tap_weights = gathered.reshape(9, channels, channels)  4.26 us
  transfers between devices with their start and end apart: 17, of which 12 were waited for; matrix products, arithmetic and copies ran while one was open for 17% of the time, Pallas kernels for 0%

profile of v7, /device:TPU:0, one launch (start us, length us, event | category | flops | bytes accessed | tf_op | source)
XLA Modules:
  0.0 115.8 jit_solution(16169920930194060142)
XLA Ops:
  10.2 5.1 %collective-permute-start.2 = (f32[2,32]{1,0:T(2,128)S(1)}, f32[2,32]{1,0:T(2,128)S(1)}, u32[]{:S(2)}, u32[]{:S(2)}) collective-permute-start(f32[2,32]{1,0:T(2,128)S(1)} %pad_maximum_fusion.2), channel_id=1, source_target_pairs={{0,24},{8,0},{16,8},{24,16},{1,25},{9,1},{17,9},{25,17},{2,26},{10... | collective-permute-start | bytes 776 | tf_op jit(solution)/shard_map/ppermute | solution.py:33
  16.6 3.2 %collective-permute-done.1 = f32[2,32]{1,0:T(2,128)S(1)} collective-permute-done((f32[2,32]{1,0:T(2,128)S(1)}, f32[2,32]{1,0:T(2,128)S(1)}, u32[]{:S(2)}, u32[]{:S(2)}) %collective-permute-start.1) | collective-permute-done | bytes 288 | tf_op jit(solution)/shard_map/ppermute | solution.py:33
  23.8 4.6 %collective-permute-start.3 = (bf16[1,128,320]{1,2,0:T(8,128)(2,1)S(1)}, bf16[1,128,320]{1,2,0:T(8,128)(2,1)S(1)}, u32[]{:S(2)}, u32[]{:S(2)}) collective-permute-start(bf16[1,128,320]{1,2,0:T(8,128)(2,1)S(1)} %get-tuple-element.23), channel_id=1, source_target_pairs={{0,8},{8,16},{16,24},{1,9},{9,17},{17,25},{2,10},{10,18},{18,26},{... | collective-permute-start | bytes 245768 | tf_op jit(solution)/shard_map/ppermute | solution.py:18
  31.9 1.5 %fusion.51 = f32[2880,320,1]{1,0,2:T(8,128)S(1)} fusion(bf16[3,128,2880]{1,2,0:T(8,128)(2,1)S(1)} %slice_dynamic-update-slice_fusion, bf16[3,128,320]{1,2,0:T(8,128)(2,1)S(1)} %bitcast_multiply_fusion), kind=kOutput, calls=%fused_computation.96 | convolution fusion | flops 707788800 | bytes 6144000 | tf_op jit(solution)/shard_map/dot_general | solution.py:144
  33.5 2.0 %copy-done = f32[2880,320,1]{1,0,2:T(8,128)} copy-done((f32[2880,320,1]{1,0,2:T(8,128)}, f32[2880,320,1]{1,0,2:T(8,128)S(1)}, u32[]{:S(2)}) %copy-start) | copy-done | bytes 3686424
  35.6 1.4 %copy.48 = bf16[4,360,320]{1,2,0:T(8,128)(2,1)} copy(bf16[4,360,320]{2,1,0:T(8,128)(2,1)S(1)} %bitcast_convert_fusion) | data formatting | bytes 1843200 | tf_op jit(solution)/shard_map/convert_element_type | solution.py:65
  38.3 4.9 %collective-permute-start.6 = (bf16[1,128,320]{1,2,0:T(8,128)(2,1)S(1)}, bf16[1,128,320]{1,2,0:T(8,128)(2,1)S(1)}, u32[]{:S(2)}, u32[]{:S(2)}) collective-permute-start(bf16[1,128,320]{1,2,0:T(8,128)(2,1)S(1)} %get-tuple-element.21), channel_id=1, source_target_pairs={{0,8},{8,16},{16,24},{1,9},{9,17},{17,25},{2,10},{10,18},{18,26},{... | collective-permute-start | bytes 245768 | tf_op jit(solution)/shard_map/ppermute | solution.py:18
  46.0 1.4 %copy.49 = bf16[4,360,320]{2,1,0:T(8,128)(2,1)} copy(bf16[4,360,320]{1,2,0:T(8,128)(2,1)S(1)} %collective-permute-done.5) | data formatting | bytes 1843200 | tf_op jit(solution)/shard_map/ppermute | solution.py:65
  47.4 2.1 %bitcast_add_fusion = f32[4,360,320]{2,1,0:T(8,128)S(1)} fusion(bf16[4,360,320]{2,1,0:T(8,128)(2,1)} %copy.49, f32[4,2,360,320]{3,2,1,0:T(8,128)} %bitcast.113, s32[]{:T(128)S(6)} %select_n.33), kind=kLoop, calls=%fused_computation.3 | loop fusion | flops 921600 | bytes 4608004 | tf_op jit(solution)/shard_map/add | solution.py:66
  49.6 4.1 %copy.52 = bf16[8,360,320]{2,1,0:T(8,128)(2,1)} copy(bf16[8,360,320]{1,2,0:T(8,128)(2,1)} %all-gather.3.cloned.1.call-done) | data formatting | bytes 3686400 | tf_op jit(solution)/shard_map/all_gather | solution.py:121
  54.9 1.3 %copy-done.8 = bf16[3,128,2880]{1,2,0:T(8,128)(2,1)} copy-done((bf16[3,128,2880]{1,2,0:T(8,128)(2,1)}, bf16[3,128,2880]{1,2,0:T(8,128)(2,1)S(1)}, u32[]{:S(2)}) %copy-start.8) | copy-done | bytes 2211864
  56.3 4.3 %copy.54 = bf16[9,320,320]{1,2,0:T(8,128)(2,1)} copy(bf16[9,320,320]{2,1,0:T(8,128)(2,1)} %bitcast.114) | data formatting | bytes 3686400 | tf_op jit(solution)/shard_map/reshape | solution.py:151
  60.5 4.4 %fusion.48 = (f32[320]{0:T(512)S(1)}, f32[320]{0:T(512)S(1)}, f32[3,128,320]{1,2,0:T(8,128)}) fusion(f32[320]{0:T(512)S(1)} %mul.163, f32[320]{0:T(512)S(1)} %sub.37, f32[3,128]{1,0:T(4,128)S(1)} %get-tuple-element.28, bf16[1,3,128,320]{2,3,1,0:T(8,128)(2,1)S(1)} %copy-done.3, f32[320]{0:T(512)S(1)} %copy-done.9, f32[320]{0:T(512)S(1)} %copy-done.10, ...), kind=kOutput, calls=%fused_computation.93 | convolution fusion | flops 710245760 | bytes 4801536 | tf_op jit(solution)/shard_map/dot_general | solution.py:161
  65.4 3.4 %collective-permute-start.10 = (f32[2,32]{1,0:T(2,128)S(1)}, f32[2,32]{1,0:T(2,128)S(1)}, u32[]{:S(2)}, u32[]{:S(2)}) collective-permute-start(f32[2,32]{1,0:T(2,128)S(1)} %pad_maximum_fusion.3), channel_id=1, source_target_pairs={{0,24},{8,0},{16,8},{24,16},{1,25},{9,1},{17,9},{25,17},{2,26},{10... | collective-permute-start | bytes 776 | tf_op jit(solution)/shard_map/ppermute | solution.py:33
  69.4 1.4 %copy.57 = bf16[4,360,320]{1,2,0:T(8,128)(2,1)} copy(f32[4,360,320]{2,1,0:T(8,128)S(1)} %bitcast_add_fusion) | data formatting | bytes 2764800 | tf_op jit(solution)/shard_map/optimization_barrier | solution.py:68
  73.1 2.5 %collective-permute-start.13 = (bf16[360,320]{0,1:T(8,128)(2,1)S(1)}, bf16[360,320]{0,1:T(8,128)(2,1)S(1)}, u32[]{:S(2)}, u32[]{:S(2)}) collective-permute-start(bf16[360,320]{0,1:T(8,128)(2,1)S(1)} %get-tuple-element.19), channel_id=1, source_target_pairs={{0,6},{1,7},{2,4},{3,5},{4,2},{5,3},{6,0},{7,1},{8,14},{9,15},{10,... | collective-permute-start | bytes 691208 | tf_op jit(solution)/shard_map/ppermute | solution.py:80
  76.6 3.5 %fusion.11 = bf16[1,3,128,320]{2,3,1,0:T(8,128)(2,1)} fusion(bf16[3,128,2880]{1,2,0:T(8,128)(2,1)} %copy-done.2, bf16[2880,320]{1,0:T(8,128)(2,1)S(1)} %bitcast.115, f32[3,128]{1,0:T(4,128)S(1)} %get-tuple-element.28), kind=kOutput, calls=%fused_computation.12 | convolution fusion | flops 708034560 | bytes 4302336 | tf_op jit(solution)/shard_map/dot_general | solution.py:149
  80.2 2.8 %collective-permute-done.13 = bf16[360,320]{0,1:T(8,128)(2,1)S(1)} collective-permute-done((bf16[360,320]{0,1:T(8,128)(2,1)S(1)}, bf16[360,320]{0,1:T(8,128)(2,1)S(1)}, u32[]{:S(2)}, u32[]{:S(2)}) %collective-permute-start.13) | collective-permute-done | bytes 230432 | tf_op jit(solution)/shard_map/ppermute | solution.py:80
  83.0 1.7 %collective-permute-start.8 = (f32[2,32]{1,0:T(2,128)S(1)}, f32[2,32]{1,0:T(2,128)S(1)}, u32[]{:S(2)}, u32[]{:S(2)}) collective-permute-start(f32[2,32]{1,0:T(2,128)S(1)} %pad_maximum_fusion.3), channel_id=1, source_target_pairs={{0,8},{8,16},{16,24},{24,0},{1,9},{9,17},{17,25},{25,1},{2,10},{10... | collective-permute-start | bytes 776 | tf_op jit(solution)/shard_map/ppermute | solution.py:33
  84.7 1.6 %collective-permute-done.12 = bf16[360,320]{0,1:T(8,128)(2,1)S(1)} collective-permute-done((bf16[360,320]{0,1:T(8,128)(2,1)S(1)}, bf16[360,320]{0,1:T(8,128)(2,1)S(1)}, u32[]{:S(2)}, u32[]{:S(2)}) %collective-permute-start.12) | collective-permute-done | bytes 230432 | tf_op jit(solution)/shard_map/ppermute | solution.py:80
  86.6 1.5 %collective-permute-start.14 = (bf16[360,320]{0,1:T(8,128)(2,1)S(1)}, bf16[360,320]{0,1:T(8,128)(2,1)S(1)}, u32[]{:S(2)}, u32[]{:S(2)}) collective-permute-start(bf16[360,320]{0,1:T(8,128)(2,1)S(1)} %fusion.38), channel_id=1, source_target_pairs={{0,8},{8,0},{16,24},{24,16},{1,9},{9,1},{17,25},{25,17},{2,10},{10... | collective-permute-start | bytes 691208 | tf_op jit(solution)/shard_map/ppermute | solution.py:92
  88.7 5.7 %collective-permute-done.14 = bf16[360,320]{0,1:T(8,128)(2,1)S(1)} collective-permute-done((bf16[360,320]{0,1:T(8,128)(2,1)S(1)}, bf16[360,320]{0,1:T(8,128)(2,1)S(1)}, u32[]{:S(2)}, u32[]{:S(2)}) %collective-permute-start.14) | collective-permute-done | bytes 230432 | tf_op jit(solution)/shard_map/ppermute | solution.py:92
  94.5 2.4 %collective-permute-start.15 = (bf16[360,320]{0,1:T(8,128)(2,1)S(1)}, bf16[360,320]{0,1:T(8,128)(2,1)S(1)}, u32[]{:S(2)}, u32[]{:S(2)}) collective-permute-start(bf16[360,320]{0,1:T(8,128)(2,1)S(1)} %add_convert_fusion), channel_id=1, source_target_pairs={{0,16},{8,24},{16,0},{24,8},{1,17},{9,25},{17,1},{25,9},{2,18},{10... | collective-permute-start | bytes 691208 | tf_op jit(solution)/shard_map/ppermute | solution.py:92
  97.9 9.8 %collective-permute-done.15 = bf16[360,320]{0,1:T(8,128)(2,1)S(1)} collective-permute-done((bf16[360,320]{0,1:T(8,128)(2,1)S(1)}, bf16[360,320]{0,1:T(8,128)(2,1)S(1)}, u32[]{:S(2)}, u32[]{:S(2)}) %collective-permute-start.15) | collective-permute-done | bytes 230432 | tf_op jit(solution)/shard_map/ppermute | solution.py:92
  (100 shorter events, 23.2 us)
Async XLA Ops:
  7.2 42.4 %all-gather.3.cloned.1.call-start = ((), (), s32[]{:S(2)}) async-start(), calls=%async_computation | async-start | bytes 2211840 | tf_op jit(solution)/shard_map/all_gather | solution.py:121
  10.2 6.4 %collective-permute-start.2 = (f32[2,32]{1,0:T(2,128)S(1)}, f32[2,32]{1,0:T(2,128)S(1)}, u32[]{:S(2)}, u32[]{:S(2)}) collective-permute-start(f32[2,32]{1,0:T(2,128)S(1)} %pad_maximum_fusion.2), channel_id=1, source_target_pairs={{0,24},{8,0},{16,8},{24,16},{1,25},{9,1},{17,9},{25,17},{2,26},{10... | collective-permute-start | bytes 776 | tf_op jit(solution)/shard_map/ppermute | solution.py:33
  15.3 4.5 %collective-permute-start.1 = (f32[2,32]{1,0:T(2,128)S(1)}, f32[2,32]{1,0:T(2,128)S(1)}, u32[]{:S(2)}, u32[]{:S(2)}) collective-permute-start(f32[2,32]{1,0:T(2,128)S(1)} %pad_maximum_fusion.2), channel_id=1, source_target_pairs={{0,16},{8,24},{16,0},{24,8},{1,17},{9,25},{17,1},{25,9},{2,18},{10... | collective-permute-start | bytes 776 | tf_op jit(solution)/shard_map/ppermute | solution.py:33
  15.3 5.4 %collective-permute-start = (f32[2,32]{1,0:T(2,128)S(1)}, f32[2,32]{1,0:T(2,128)S(1)}, u32[]{:S(2)}, u32[]{:S(2)}) collective-permute-start(f32[2,32]{1,0:T(2,128)S(1)} %pad_maximum_fusion.2), channel_id=1, source_target_pairs={{0,8},{8,16},{16,24},{24,0},{1,9},{9,17},{17,25},{25,1},{2,10},{10... | collective-permute-start | bytes 776 | tf_op jit(solution)/shard_map/ppermute | solution.py:33
  21.1 10.0 %copy-start.3 = (bf16[1,3,128,320]{2,3,1,0:T(8,128)(2,1)S(1)}, bf16[1,3,128,320]{2,3,1,0:T(8,128)(2,1)}, u32[]{:S(2)}) copy-start(bf16[1,3,128,320]{2,3,1,0:T(8,128)(2,1)} %param.9) | copy-start | bytes 737284
  21.1 10.0 %copy-start.9 = (f32[320]{0:T(512)S(1)}, f32[320]{0:T(512)}, u32[]{:S(2)}) copy-start(f32[320]{0:T(512)} %param.12) | copy-start | bytes 3844
  21.1 10.0 %copy-start.10 = (f32[320]{0:T(512)S(1)}, f32[320]{0:T(512)}, u32[]{:S(2)}) copy-start(f32[320]{0:T(512)} %param.11) | copy-start | bytes 3844
  22.5 6.8 %collective-permute-start.4 = (bf16[1,128,320]{1,2,0:T(8,128)(2,1)S(1)}, bf16[1,128,320]{1,2,0:T(8,128)(2,1)S(1)}, u32[]{:S(2)}, u32[]{:S(2)}) collective-permute-start(bf16[1,128,320]{1,2,0:T(8,128)(2,1)S(1)} %get-tuple-element.24), channel_id=1, source_target_pairs={{8,0},{16,8},{24,16},{9,1},{17,9},{25,17},{10,2},{18,10},{26,18},{... | collective-permute-start | bytes 245768 | tf_op jit(solution)/shard_map/ppermute | solution.py:20
  23.8 6.6 %collective-permute-start.3 = (bf16[1,128,320]{1,2,0:T(8,128)(2,1)S(1)}, bf16[1,128,320]{1,2,0:T(8,128)(2,1)S(1)}, u32[]{:S(2)}, u32[]{:S(2)}) collective-permute-start(bf16[1,128,320]{1,2,0:T(8,128)(2,1)S(1)} %get-tuple-element.23), channel_id=1, source_target_pairs={{0,8},{8,16},{16,24},{1,9},{9,17},{17,25},{2,10},{10,18},{18,26},{... | collective-permute-start | bytes 245768 | tf_op jit(solution)/shard_map/ppermute | solution.py:18
  37.0 9.0 %collective-permute-start.5 = (bf16[4,360,320]{1,2,0:T(8,128)(2,1)}, bf16[4,360,320]{1,2,0:T(8,128)(2,1)S(1)}, u32[]{:S(2)}, u32[]{:S(2)}) collective-permute-start(bf16[4,360,320]{1,2,0:T(8,128)(2,1)} %copy.48), channel_id=1, source_target_pairs={{0,1},{1,0},{2,3},{3,2},{4,5},{5,4},{6,7},{7,6},{8,9},{9,8},{10,11... | collective-permute-start | bytes 2764808 | tf_op jit(solution)/shard_map/ppermute | solution.py:65
  37.0 7.4 %collective-permute-start.7 = (bf16[1,128,320]{1,2,0:T(8,128)(2,1)S(1)}, bf16[1,128,320]{1,2,0:T(8,128)(2,1)S(1)}, u32[]{:S(2)}, u32[]{:S(2)}) collective-permute-start(bf16[1,128,320]{1,2,0:T(8,128)(2,1)S(1)} %get-tuple-element.22), channel_id=1, source_target_pairs={{8,0},{16,8},{24,16},{9,1},{17,9},{25,17},{10,2},{18,10},{26,18},{... | collective-permute-start | bytes 245768 | tf_op jit(solution)/shard_map/ppermute | solution.py:20
  38.3 7.3 %collective-permute-start.6 = (bf16[1,128,320]{1,2,0:T(8,128)(2,1)S(1)}, bf16[1,128,320]{1,2,0:T(8,128)(2,1)S(1)}, u32[]{:S(2)}, u32[]{:S(2)}) collective-permute-start(bf16[1,128,320]{1,2,0:T(8,128)(2,1)S(1)} %get-tuple-element.21), channel_id=1, source_target_pairs={{0,8},{8,16},{16,24},{1,9},{9,17},{17,25},{2,10},{10,18},{18,26},{... | collective-permute-start | bytes 245768 | tf_op jit(solution)/shard_map/ppermute | solution.py:18
  65.4 22.7 %collective-permute-start.10 = (f32[2,32]{1,0:T(2,128)S(1)}, f32[2,32]{1,0:T(2,128)S(1)}, u32[]{:S(2)}, u32[]{:S(2)}) collective-permute-start(f32[2,32]{1,0:T(2,128)S(1)} %pad_maximum_fusion.3), channel_id=1, source_target_pairs={{0,24},{8,0},{16,8},{24,16},{1,25},{9,1},{17,9},{25,17},{2,26},{10... | collective-permute-start | bytes 776 | tf_op jit(solution)/shard_map/ppermute | solution.py:33
  68.8 19.3 %collective-permute-start.9 = (f32[2,32]{1,0:T(2,128)S(1)}, f32[2,32]{1,0:T(2,128)S(1)}, u32[]{:S(2)}, u32[]{:S(2)}) collective-permute-start(f32[2,32]{1,0:T(2,128)S(1)} %pad_maximum_fusion.3), channel_id=1, source_target_pairs={{0,16},{8,24},{16,0},{24,8},{1,17},{9,25},{17,1},{25,9},{2,18},{10... | collective-permute-start | bytes 776 | tf_op jit(solution)/shard_map/ppermute | solution.py:33
  73.1 9.9 %collective-permute-start.13 = (bf16[360,320]{0,1:T(8,128)(2,1)S(1)}, bf16[360,320]{0,1:T(8,128)(2,1)S(1)}, u32[]{:S(2)}, u32[]{:S(2)}) collective-permute-start(bf16[360,320]{0,1:T(8,128)(2,1)S(1)} %get-tuple-element.19), channel_id=1, source_target_pairs={{0,6},{1,7},{2,4},{3,5},{4,2},{5,3},{6,0},{7,1},{8,14},{9,15},{10,... | collective-permute-start | bytes 691208 | tf_op jit(solution)/shard_map/ppermute | solution.py:80
  75.6 10.7 %collective-permute-start.12 = (bf16[360,320]{0,1:T(8,128)(2,1)S(1)}, bf16[360,320]{0,1:T(8,128)(2,1)S(1)}, u32[]{:S(2)}, u32[]{:S(2)}) collective-permute-start(bf16[360,320]{0,1:T(8,128)(2,1)S(1)} %get-tuple-element.20), channel_id=1, source_target_pairs={{0,4},{1,5},{2,6},{3,7},{4,0},{5,1},{6,2},{7,3},{8,12},{9,13},{10,... | collective-permute-start | bytes 691208 | tf_op jit(solution)/shard_map/ppermute | solution.py:80
  76.1 10.3 %copy-start.4 = (f32[1,360,320]{1,2,0:T(8,128)S(1)}, f32[1,360,320]{1,2,0:T(8,128)}, u32[]{:S(2)}) copy-start(f32[1,360,320]{1,2,0:T(8,128)} %copy.56) | copy-start | bytes 1382404
  76.1 10.3 %collective-permute-start.11 = (bf16[360,320]{0,1:T(8,128)(2,1)S(1)}, bf16[360,320]{0,1:T(8,128)(2,1)S(1)}, u32[]{:S(2)}, u32[]{:S(2)}) collective-permute-start(bf16[360,320]{0,1:T(8,128)(2,1)S(1)} %get-tuple-element.18), channel_id=1, source_target_pairs={{0,2},{1,3},{2,0},{3,1},{4,6},{5,7},{6,4},{7,5},{8,10},{9,11},{10,... | collective-permute-start | bytes 691208 | tf_op jit(solution)/shard_map/ppermute | solution.py:80
  80.2 16.7 %copy-start.7 = (f32[3,128,320]{1,2,0:T(8,128)S(1)}, f32[3,128,320]{1,2,0:T(8,128)}, u32[]{:S(2)}) copy-start(f32[3,128,320]{1,2,0:T(8,128)} %get-tuple-element.29) | copy-start | bytes 1474564
  80.2 27.5 %copy-start.5 = (f32[360,320]{0,1:T(8,128)S(1)}, f32[360,320]{0,1:T(8,128)}, u32[]{:S(2)}) copy-start(f32[360,320]{0,1:T(8,128)} %param.15) | copy-start | bytes 1382404
  80.2 27.5 %copy-start.6 = (f32[360,320]{0,1:T(8,128)S(1)}, f32[360,320]{0,1:T(8,128)}, u32[]{:S(2)}) copy-start(f32[360,320]{0,1:T(8,128)} %param.14) | copy-start | bytes 1382404
  83.0 5.4 %collective-permute-start.8 = (f32[2,32]{1,0:T(2,128)S(1)}, f32[2,32]{1,0:T(2,128)S(1)}, u32[]{:S(2)}, u32[]{:S(2)}) collective-permute-start(f32[2,32]{1,0:T(2,128)S(1)} %pad_maximum_fusion.3), channel_id=1, source_target_pairs={{0,8},{8,16},{16,24},{24,0},{1,9},{9,17},{17,25},{25,1},{2,10},{10... | collective-permute-start | bytes 776 | tf_op jit(solution)/shard_map/ppermute | solution.py:33
  86.6 7.8 %collective-permute-start.14 = (bf16[360,320]{0,1:T(8,128)(2,1)S(1)}, bf16[360,320]{0,1:T(8,128)(2,1)S(1)}, u32[]{:S(2)}, u32[]{:S(2)}) collective-permute-start(bf16[360,320]{0,1:T(8,128)(2,1)S(1)} %fusion.38), channel_id=1, source_target_pairs={{0,8},{8,0},{16,24},{24,16},{1,9},{9,1},{17,25},{25,17},{2,10},{10... | collective-permute-start | bytes 691208 | tf_op jit(solution)/shard_map/ppermute | solution.py:92
  94.5 13.1 %collective-permute-start.15 = (bf16[360,320]{0,1:T(8,128)(2,1)S(1)}, bf16[360,320]{0,1:T(8,128)(2,1)S(1)}, u32[]{:S(2)}, u32[]{:S(2)}) collective-permute-start(bf16[360,320]{0,1:T(8,128)(2,1)S(1)} %add_convert_fusion), channel_id=1, source_target_pairs={{0,16},{8,24},{16,0},{24,8},{1,17},{9,25},{17,1},{25,9},{2,18},{10... | collective-permute-start | bytes 691208 | tf_op jit(solution)/shard_map/ppermute | solution.py:92
  (4 other events, 10.7 us)
Sparse Core Ops, SparseCore 0:
  16.5 27.7 all-gather.2

commit v8 on v7

--- a/solution.py
+++ b/solution.py
@@ -64,13 +64,11 @@
         pairs = [(i, i ^ step) for i in range(count)]
         got = lax.ppermute(send.astype(jnp.bfloat16), axis, pairs)
         held = row_major(keep + got.astype(jnp.float32))
-        if step == 1:
-            held, companions = lax.optimization_barrier((held, companions))
         step *= 2
         if step < count <= 4 * step:
             break
     if step == count:
-        return held[0], companions
+        return lax.optimization_barrier((held[0], companions))
     spots = count // step
     own = index // step
     total = lax.dynamic_index_in_dim(held, own, keepdims=False)
@@ -78,7 +76,7 @@
         send = lax.dynamic_index_in_dim(held, own ^ shift, keepdims=False)
         pairs = [(i, i ^ (shift * step)) for i in range(count)]
         total = total + lax.ppermute(send.astype(jnp.bfloat16), axis, pairs).astype(jnp.float32)
-    return total, companions
+    return lax.optimization_barrier((total, companions))
 
 
 def replicated_sum(value, axis):

time: 116 us -> 112 us (0.966)
  other arithmetic: 9.76 us -> 13.6 us
  starting transfers between devices: 31.4 us -> 28.4 us
  local copies, waits for them, and re-layouts: 21.4 us -> 18.9 us
  waiting for transfers between devices: 28 us -> 25.6 us
    unnamed x35 -> x38, local copies, waits for them, and re-layouts: 5 us -> 7.6 us
    ppermute x6, starting transfers between devices: 11.8 us -> 9.42 us  [space_sum(): lax.ppermute(joined, axis, [(i, (i + shift) % count) for i in range(count)])]
    ppermute x2, waiting for transfers between devices: 15.5 us -> 13.5 us  [replicated_sum(): lax.ppermute(mine, axis, pairs).astype(jnp.float32)]
    reshape x1, local copies, waits for them, and re-layouts: 4.26 us -> 2.48 us  [local(): tap_weights = gathered.reshape(9, channels, channels)]
    ppermute x3, waiting for transfers between devices: 4.53 us -> 5.99 us  [halving_scatter(): lax.ppermute(send.astype(jnp.bfloat16), axis, pairs).astype(jnp.float32)]
    optimization_barrier x1 -> x0, local copies, waits for them, and re-layouts: 1.41 us -> none  [halving_scatter(): held, companions = lax.optimization_barrier((held, companions))]
    add x0 -> x1, other arithmetic: none -> 1.29 us  [halving_scatter(): total + lax.ppermute(send.astype(jnp.bfloat16), axis, pairs).astype(jnp.f...]
    convert_element_type x1 -> x0, local copies, waits for them, and re-layouts: 1.25 us -> none  [halving_scatter(): send.astype(jnp.bfloat16)]
  transfers between devices with their start and end apart: 17 -> 17, of which waited for: 12 -> 10; matrix products, arithmetic and copies ran while one was open for 17% -> 21% of each run, Pallas kernels for 0% -> 0%
where the time goes in v8:
time: 112 us
  starting transfers between devices  28.4 us (25%)
  waiting for transfers between devices  25.6 us (23%)
  local copies, waits for them, and re-layouts  18.9 us (17%)
  between operations  15.8 us (14%)
  other arithmetic  13.6 us (12%)
  matrix products  9.45 us (8%)
    ppermute x2, waiting for transfers between devices, replicated_sum(): lax.ppermute(mine, axis, pairs).astype(jnp.float32)  13.5 us
    ppermute x2, starting transfers between devices, with_halo(): lax.ppermute(tail, axis, [(i, (i + 1) % count) for i in range(ends)])  10.1 us
    ppermute x6, starting transfers between devices, space_sum(): lax.ppermute(joined, axis, [(i, (i + shift) % count) for i in range(count)])  9.42 us
    unnamed x38, local copies, waits for them, and re-layouts  7.6 us
    ppermute x3, waiting for transfers between devices, halving_scatter(): lax.ppermute(send.astype(jnp.bfloat16), axis, pairs).astype(jnp.float32)  5.99 us
    ppermute x6, waiting for transfers between devices, space_sum(): lax.ppermute(joined, axis, [(i, (i + shift) % count) for i in range(count)])  4.96 us
    dot_general x1, matrix products, local(): upstream = jnp.dot(cot_cols, flipped, preferred_element_type=jnp.float32)  4.4 us
    dot_general x1, matrix products, local(): output = jnp.dot(act_cols, gathered, preferred_element_type=jnp.float32)  3.53 us
  transfers between devices with their start and end apart: 17, of which 10 were waited for; matrix products, arithmetic and copies ran while one was open for 21% of the time, Pallas kernels for 0%

profile of v8, /device:TPU:0, one launch (start us, length us, event | category | flops | bytes accessed | tf_op | source)
XLA Modules:
  0.0 111.7 jit_solution(8547884376293675641)
XLA Ops:
  10.2 5.1 %collective-permute-start.2 = (f32[2,32]{1,0:T(2,128)S(1)}, f32[2,32]{1,0:T(2,128)S(1)}, u32[]{:S(2)}, u32[]{:S(2)}) collective-permute-start(f32[2,32]{1,0:T(2,128)S(1)} %pad_maximum_fusion.2), channel_id=1, source_target_pairs={{0,24},{8,0},{16,8},{24,16},{1,25},{9,1},{17,9},{25,17},{2,26},{10... | collective-permute-start | bytes 776 | tf_op jit(solution)/shard_map/ppermute | solution.py:33
  16.6 3.2 %collective-permute-done.1 = f32[2,32]{1,0:T(2,128)S(1)} collective-permute-done((f32[2,32]{1,0:T(2,128)S(1)}, f32[2,32]{1,0:T(2,128)S(1)}, u32[]{:S(2)}, u32[]{:S(2)}) %collective-permute-start.1) | collective-permute-done | bytes 288 | tf_op jit(solution)/shard_map/ppermute | solution.py:33
  21.1 1.3 %multiply_convert_fusion = bf16[3,128,320]{1,2,0:T(8,128)(2,1)S(1)} fusion(bf16[1,3,128,320]{2,3,1,0:T(8,128)(2,1)} %param.9, f32[320]{0:T(512)} %param.12, f32[320]{0:T(512)} %param.11, f32[320]{0:T(512)S(1)} %mul.163, f32[320]{0:T(512)S(1)} %sub.37, f32[3,128]{1,0:T(4,128)S(1)} %get-tuple-element.28), kind=kLoop, calls=%fused_computation.47 | loop fusion | flops 1597440 | bytes 498176 | tf_op jit(solution)/shard_map/convert_element_type | solution.py:129
  22.5 1.3 %collective-permute-start.4 = (bf16[1,128,320]{1,2,0:T(8,128)(2,1)S(1)}, bf16[1,128,320]{1,2,0:T(8,128)(2,1)S(1)}, u32[]{:S(2)}, u32[]{:S(2)}) collective-permute-start(bf16[1,128,320]{1,2,0:T(8,128)(2,1)S(1)} %get-tuple-element.24), channel_id=1, source_target_pairs={{8,0},{16,8},{24,16},{9,1},{17,9},{25,17},{10,2},{18,10},{26,18},{... | collective-permute-start | bytes 245768 | tf_op jit(solution)/shard_map/ppermute | solution.py:20
  23.8 4.6 %collective-permute-start.3 = (bf16[1,128,320]{1,2,0:T(8,128)(2,1)S(1)}, bf16[1,128,320]{1,2,0:T(8,128)(2,1)S(1)}, u32[]{:S(2)}, u32[]{:S(2)}) collective-permute-start(bf16[1,128,320]{1,2,0:T(8,128)(2,1)S(1)} %get-tuple-element.23), channel_id=1, source_target_pairs={{0,8},{8,16},{16,24},{1,9},{9,17},{17,25},{2,10},{10,18},{18,26},{... | collective-permute-start | bytes 245768 | tf_op jit(solution)/shard_map/ppermute | solution.py:18
  31.9 1.5 %fusion.47 = f32[2880,320,1]{1,0,2:T(8,128)S(1)} fusion(bf16[3,128,2880]{1,2,0:T(8,128)(2,1)S(1)} %slice_dynamic-update-slice_fusion, bf16[3,128,320]{1,2,0:T(8,128)(2,1)S(1)} %bitcast_multiply_fusion), kind=kOutput, calls=%fused_computation.95 | convolution fusion | flops 707788800 | bytes 6144000 | tf_op jit(solution)/shard_map/dot_general | solution.py:142
  33.5 2.0 %copy-done = f32[2880,320,1]{1,0,2:T(8,128)} copy-done((f32[2880,320,1]{1,0,2:T(8,128)}, f32[2880,320,1]{1,0,2:T(8,128)S(1)}, u32[]{:S(2)}) %copy-start) | copy-done | bytes 3686424
  38.4 5.5 %collective-permute-start.9 = (bf16[1,128,320]{1,2,0:T(8,128)(2,1)}, bf16[1,128,320]{1,2,0:T(8,128)(2,1)}, u32[]{:S(2)}, u32[]{:S(2)}) collective-permute-start(bf16[1,128,320]{1,2,0:T(8,128)(2,1)} %get-tuple-element.21), channel_id=1, source_target_pairs={{0,8},{8,16},{16,24},{1,9},{9,17},{17,25},{2,10},{10,18},{18,26},{... | collective-permute-start | bytes 245768 | tf_op jit(solution)/shard_map/ppermute | solution.py:18
  44.7 1.8 %bitcast_add_fusion = f32[4,360,320]{2,1,0:T(8,128)S(1)} fusion(bf16[4,360,320]{2,1,0:T(8,128)(2,1)S(1)} %copy.49, f32[4,2,360,320]{3,2,1,0:T(8,128)} %bitcast.114, s32[]{:T(128)S(6)} %select_n.33), kind=kLoop, calls=%fused_computation.3 | loop fusion | flops 921600 | bytes 4608004 | tf_op jit(solution)/shard_map/add | solution.py:66
  47.5 2.5 %collective-permute-start.8 = (bf16[360,320]{0,1:T(8,128)(2,1)}, bf16[360,320]{0,1:T(8,128)(2,1)S(1)}, u32[]{:S(2)}, u32[]{:S(2)}) collective-permute-start(bf16[360,320]{0,1:T(8,128)(2,1)} %bitcast.119), channel_id=1, source_target_pairs={{0,6},{1,7},{2,4},{3,5},{4,2},{5,3},{6,0},{7,1},{8,14},{9,15},{10,... | collective-permute-start | bytes 691208 | tf_op jit(solution)/shard_map/ppermute | solution.py:78
  52.7 1.3 %select_maximum_fusion = bf16[5,130,320]{1,2,0:T(8,128)(2,1)S(1)} fusion(bf16[1,128,320]{1,2,0:T(8,128)(2,1)} %collective-permute-done.10, bf16[3,128,320]{1,2,0:T(8,128)(2,1)S(1)} %copy-done.5, bf16[1,128,320]{1,2,0:T(8,128)(2,1)} %collective-permute-done.9), kind=kLoop, calls=%fused_computation.13 | loop fusion | flops 2496000 | bytes 825600 | tf_op jit(solution)/shard_map/concatenate | solution.py:16
  57.5 4.6 %collective-permute-done.7 = bf16[360,320]{0,1:T(8,128)(2,1)} collective-permute-done((bf16[360,320]{0,1:T(8,128)(2,1)}, bf16[360,320]{0,1:T(8,128)(2,1)}, u32[]{:S(2)}, u32[]{:S(2)}) %collective-permute-start.7) | collective-permute-done | bytes 230432 | tf_op jit(solution)/shard_map/ppermute | solution.py:78
  62.2 1.3 %fusion.37 = bf16[360,320]{0,1:T(8,128)(2,1)S(1)} fusion(f32[1,360,320]{1,2,0:T(8,128)S(1)} %copy.50, bf16[360,320]{0,1:T(8,128)(2,1)} %copy-done.7, bf16[360,320]{0,1:T(8,128)(2,1)} %collective-permute-done.7, bf16[360,320]{0,1:T(8,128)(2,1)} %collective-permute-done.6), kind=kLoop, calls=%fused_computation.44 | loop fusion | flops 806400 | bytes 1382400 | tf_op jit(solution)/shard_map/add | solution.py:78
  63.5 3.0 %copy.56 = bf16[8,360,320]{2,1,0:T(8,128)(2,1)S(1)} copy(bf16[8,360,320]{1,2,0:T(8,128)(2,1)} %all-gather.3.cloned.1.call-done) | data formatting | bytes 3686400 | tf_op jit(solution)/shard_map/all_gather | solution.py:119
  67.7 1.4 %copy-done.8 = bf16[3,128,2880]{1,2,0:T(8,128)(2,1)} copy-done((bf16[3,128,2880]{1,2,0:T(8,128)(2,1)}, bf16[3,128,2880]{1,2,0:T(8,128)(2,1)S(1)}, u32[]{:S(2)}) %copy-start.8) | copy-done | bytes 2211864
  69.1 2.5 %copy.58 = bf16[9,320,320]{1,2,0:T(8,128)(2,1)} copy(bf16[9,320,320]{2,1,0:T(8,128)(2,1)S(1)} %bitcast.115) | data formatting | bytes 3686400 | tf_op jit(solution)/shard_map/reshape | solution.py:149
  71.5 4.4 %fusion.44 = (f32[320]{0:T(512)S(1)}, f32[320]{0:T(512)S(1)}, f32[3,128,320]{1,2,0:T(8,128)}) fusion(f32[320]{0:T(512)S(1)} %mul.163, f32[320]{0:T(512)S(1)} %sub.37, f32[3,128]{1,0:T(4,128)S(1)} %get-tuple-element.28, bf16[1,3,128,320]{2,3,1,0:T(8,128)(2,1)S(1)} %copy-done.3, f32[320]{0:T(512)S(1)} %copy-done.9, f32[320]{0:T(512)S(1)} %copy-done.10, ...), kind=kOutput, calls=%fused_computation.92 | convolution fusion | flops 710245760 | bytes 4801536 | tf_op jit(solution)/shard_map/dot_general | solution.py:159
  76.8 2.3 %collective-permute-start.12 = (f32[2,32]{1,0:T(2,128)S(1)}, f32[2,32]{1,0:T(2,128)S(1)}, u32[]{:S(2)}, u32[]{:S(2)}) collective-permute-start(f32[2,32]{1,0:T(2,128)S(1)} %pad_maximum_fusion.3), channel_id=1, source_target_pairs={{0,16},{8,24},{16,0},{24,8},{1,17},{9,25},{17,1},{25,9},{2,18},{10... | collective-permute-start | bytes 776 | tf_op jit(solution)/shard_map/ppermute | solution.py:33
  79.7 3.5 %fusion.11 = bf16[1,3,128,320]{2,3,1,0:T(8,128)(2,1)} fusion(bf16[3,128,2880]{1,2,0:T(8,128)(2,1)} %copy-done.1, bf16[2880,320]{1,0:T(8,128)(2,1)S(1)} %bitcast.116, f32[3,128]{1,0:T(4,128)S(1)} %get-tuple-element.28), kind=kOutput, calls=%fused_computation.12 | convolution fusion | flops 708034560 | bytes 4302336 | tf_op jit(solution)/shard_map/dot_general | solution.py:147
  84.9 5.3 %collective-permute-done.14 = bf16[360,320]{0,1:T(8,128)(2,1)S(1)} collective-permute-done((bf16[360,320]{0,1:T(8,128)(2,1)S(1)}, bf16[360,320]{0,1:T(8,128)(2,1)S(1)}, u32[]{:S(2)}, u32[]{:S(2)}) %collective-permute-start.14) | collective-permute-done | bytes 230432 | tf_op jit(solution)/shard_map/ppermute | solution.py:90
  90.3 2.1 %collective-permute-start.15 = (bf16[360,320]{0,1:T(8,128)(2,1)S(1)}, bf16[360,320]{0,1:T(8,128)(2,1)S(1)}, u32[]{:S(2)}, u32[]{:S(2)}) collective-permute-start(bf16[360,320]{0,1:T(8,128)(2,1)S(1)} %add_convert_fusion), channel_id=1, source_target_pairs={{0,16},{8,24},{16,0},{24,8},{1,17},{9,25},{17,1},{25,9},{2,18},{10... | collective-permute-start | bytes 691208 | tf_op jit(solution)/shard_map/ppermute | solution.py:90
  92.4 2.0 %fusion.40 = bf16[1,3,128,320]{2,3,1,0:T(8,128)(2,1)} fusion(f32[320]{0:T(512)S(1)} %mul.180, f32[320]{0:T(512)S(1)} %sub.37, f32[3,128]{1,0:T(4,128)S(1)} %get-tuple-element.28, bf16[1,3,128,320]{2,3,1,0:T(8,128)(2,1)S(1)} %copy-done.3, f32[3,128,320]{1,2,0:T(8,128)} %get-tuple-element.29, f32[320]{0:T(512)S(1)} %sub.44, f32[320]{0:T(512)S(1)} %mul.163), kind=kLoop, calls=%fused_computation.72 | loop fusion | flops 1351680 | bytes 989696 | tf_op jit(solution)/shard_map/broadcast_in_dim | solution.py:179
  94.3 8.2 %collective-permute-done.15 = bf16[360,320]{0,1:T(8,128)(2,1)S(1)} collective-permute-done((bf16[360,320]{0,1:T(8,128)(2,1)S(1)}, bf16[360,320]{0,1:T(8,128)(2,1)S(1)}, u32[]{:S(2)}, u32[]{:S(2)}) %collective-permute-start.15) | collective-permute-done | bytes 230432 | tf_op jit(solution)/shard_map/ppermute | solution.py:90
  102.5 2.3 %fusion.35 = (f32[360,320]{0,1:T(8,128)}, f32[360,320]{0,1:T(8,128)}) fusion(f32[360,320]{0,1:T(8,128)S(1)} %copy-done.6, f32[360,320]{0,1:T(8,128)} %param.14, bf16[360,320]{0,1:T(8,128)(2,1)S(1)} %collective-permute-done.15, bf16[360,320]{0,1:T(8,128)(2,1)S(1)} %add_convert_fusion), kind=kLoop, calls=%fused_computation.41 | loop fusion | flops 1612800 | bytes 2304000 | tf_op jit(solution)/shard_map/div | solution.py:178
  (102 shorter events, 23.0 us)
Async XLA Ops:
  7.2 56.3 %all-gather.3.cloned.1.call-start = ((), (), s32[]{:S(2)}) async-start(), calls=%async_computation | async-start | bytes 2211840 | tf_op jit(solution)/shard_map/all_gather | solution.py:119
  10.2 6.4 %collective-permute-start.2 = (f32[2,32]{1,0:T(2,128)S(1)}, f32[2,32]{1,0:T(2,128)S(1)}, u32[]{:S(2)}, u32[]{:S(2)}) collective-permute-start(f32[2,32]{1,0:T(2,128)S(1)} %pad_maximum_fusion.2), channel_id=1, source_target_pairs={{0,24},{8,0},{16,8},{24,16},{1,25},{9,1},{17,9},{25,17},{2,26},{10... | collective-permute-start | bytes 776 | tf_op jit(solution)/shard_map/ppermute | solution.py:33
  15.3 4.5 %collective-permute-start.1 = (f32[2,32]{1,0:T(2,128)S(1)}, f32[2,32]{1,0:T(2,128)S(1)}, u32[]{:S(2)}, u32[]{:S(2)}) collective-permute-start(f32[2,32]{1,0:T(2,128)S(1)} %pad_maximum_fusion.2), channel_id=1, source_target_pairs={{0,16},{8,24},{16,0},{24,8},{1,17},{9,25},{17,1},{25,9},{2,18},{10... | collective-permute-start | bytes 776 | tf_op jit(solution)/shard_map/ppermute | solution.py:33
  15.3 5.4 %collective-permute-start = (f32[2,32]{1,0:T(2,128)S(1)}, f32[2,32]{1,0:T(2,128)S(1)}, u32[]{:S(2)}, u32[]{:S(2)}) collective-permute-start(f32[2,32]{1,0:T(2,128)S(1)} %pad_maximum_fusion.2), channel_id=1, source_target_pairs={{0,8},{8,16},{16,24},{24,0},{1,9},{9,17},{17,25},{25,1},{2,10},{10... | collective-permute-start | bytes 776 | tf_op jit(solution)/shard_map/ppermute | solution.py:33
  21.1 10.0 %copy-start.2 = (bf16[1,3,128,320]{2,3,1,0:T(8,128)(2,1)S(1)}, bf16[1,3,128,320]{2,3,1,0:T(8,128)(2,1)}, u32[]{:S(2)}) copy-start(bf16[1,3,128,320]{2,3,1,0:T(8,128)(2,1)} %param.9) | copy-start | bytes 737284
  21.1 10.0 %copy-start.9 = (f32[320]{0:T(512)S(1)}, f32[320]{0:T(512)}, u32[]{:S(2)}) copy-start(f32[320]{0:T(512)} %param.12) | copy-start | bytes 3844
  21.1 10.0 %copy-start.10 = (f32[320]{0:T(512)S(1)}, f32[320]{0:T(512)}, u32[]{:S(2)}) copy-start(f32[320]{0:T(512)} %param.11) | copy-start | bytes 3844
  22.5 6.9 %collective-permute-start.4 = (bf16[1,128,320]{1,2,0:T(8,128)(2,1)S(1)}, bf16[1,128,320]{1,2,0:T(8,128)(2,1)S(1)}, u32[]{:S(2)}, u32[]{:S(2)}) collective-permute-start(bf16[1,128,320]{1,2,0:T(8,128)(2,1)S(1)} %get-tuple-element.24), channel_id=1, source_target_pairs={{8,0},{16,8},{24,16},{9,1},{17,9},{25,17},{10,2},{18,10},{26,18},{... | collective-permute-start | bytes 245768 | tf_op jit(solution)/shard_map/ppermute | solution.py:20
  23.8 6.6 %collective-permute-start.3 = (bf16[1,128,320]{1,2,0:T(8,128)(2,1)S(1)}, bf16[1,128,320]{1,2,0:T(8,128)(2,1)S(1)}, u32[]{:S(2)}, u32[]{:S(2)}) collective-permute-start(bf16[1,128,320]{1,2,0:T(8,128)(2,1)S(1)} %get-tuple-element.23), channel_id=1, source_target_pairs={{0,8},{8,16},{16,24},{1,9},{9,17},{17,25},{2,10},{10,18},{18,26},{... | collective-permute-start | bytes 245768 | tf_op jit(solution)/shard_map/ppermute | solution.py:18
  29.3 7.1 %copy-start.4 = (bf16[3,128,320]{1,2,0:T(8,128)(2,1)}, bf16[3,128,320]{1,2,0:T(8,128)(2,1)S(1)}, u32[]{:S(2)}) copy-start(bf16[3,128,320]{1,2,0:T(8,128)(2,1)S(1)} %bitcast_multiply_fusion) | copy-start | bytes 737284
  36.3 7.6 %collective-permute-start.5 = (bf16[4,360,320]{1,2,0:T(8,128)(2,1)S(1)}, bf16[4,360,320]{1,2,0:T(8,128)(2,1)S(1)}, u32[]{:S(2)}, u32[]{:S(2)}) collective-permute-start(bf16[4,360,320]{1,2,0:T(8,128)(2,1)S(1)} %copy.48), channel_id=1, source_target_pairs={{0,1},{1,0},{2,3},{3,2},{4,5},{5,4},{6,7},{7,6},{8,9},{9,8},{10,11... | collective-permute-start | bytes 2764808 | tf_op jit(solution)/shard_map/ppermute | solution.py:65
  37.1 15.6 %collective-permute-start.10 = (bf16[1,128,320]{1,2,0:T(8,128)(2,1)}, bf16[1,128,320]{1,2,0:T(8,128)(2,1)}, u32[]{:S(2)}, u32[]{:S(2)}) collective-permute-start(bf16[1,128,320]{1,2,0:T(8,128)(2,1)} %get-tuple-element.22), channel_id=1, source_target_pairs={{8,0},{16,8},{24,16},{9,1},{17,9},{25,17},{10,2},{18,10},{26,18},{... | collective-permute-start | bytes 245768 | tf_op jit(solution)/shard_map/ppermute | solution.py:20
  38.4 14.3 %collective-permute-start.9 = (bf16[1,128,320]{1,2,0:T(8,128)(2,1)}, bf16[1,128,320]{1,2,0:T(8,128)(2,1)}, u32[]{:S(2)}, u32[]{:S(2)}) collective-permute-start(bf16[1,128,320]{1,2,0:T(8,128)(2,1)} %get-tuple-element.21), channel_id=1, source_target_pairs={{0,8},{8,16},{16,24},{1,9},{9,17},{17,25},{2,10},{10,18},{18,26},{... | collective-permute-start | bytes 245768 | tf_op jit(solution)/shard_map/ppermute | solution.py:18
  46.5 6.2 %copy-start.5 = (bf16[3,128,320]{1,2,0:T(8,128)(2,1)S(1)}, bf16[3,128,320]{1,2,0:T(8,128)(2,1)}, u32[]{:S(2)}) copy-start(bf16[3,128,320]{1,2,0:T(8,128)(2,1)} %copy-done.4) | copy-start | bytes 737284
  47.5 9.9 %collective-permute-start.8 = (bf16[360,320]{0,1:T(8,128)(2,1)}, bf16[360,320]{0,1:T(8,128)(2,1)S(1)}, u32[]{:S(2)}, u32[]{:S(2)}) collective-permute-start(bf16[360,320]{0,1:T(8,128)(2,1)} %bitcast.119), channel_id=1, source_target_pairs={{0,6},{1,7},{2,4},{3,5},{4,2},{5,3},{6,0},{7,1},{8,14},{9,15},{10,... | collective-permute-start | bytes 691208 | tf_op jit(solution)/shard_map/ppermute | solution.py:78
  50.8 11.2 %collective-permute-start.7 = (bf16[360,320]{0,1:T(8,128)(2,1)}, bf16[360,320]{0,1:T(8,128)(2,1)}, u32[]{:S(2)}, u32[]{:S(2)}) collective-permute-start(bf16[360,320]{0,1:T(8,128)(2,1)} %bitcast.99), channel_id=1, source_target_pairs={{0,4},{1,5},{2,6},{3,7},{4,0},{5,1},{6,2},{7,3},{8,12},{9,13},{10,... | collective-permute-start | bytes 691208 | tf_op jit(solution)/shard_map/ppermute | solution.py:78
  52.2 10.0 %collective-permute-start.6 = (bf16[360,320]{0,1:T(8,128)(2,1)}, bf16[360,320]{0,1:T(8,128)(2,1)}, u32[]{:S(2)}, u32[]{:S(2)}) collective-permute-start(bf16[360,320]{0,1:T(8,128)(2,1)} %bitcast.100), channel_id=1, source_target_pairs={{0,2},{1,3},{2,0},{3,1},{4,6},{5,7},{6,4},{7,5},{8,10},{9,11},{10,... | collective-permute-start | bytes 691208 | tf_op jit(solution)/shard_map/ppermute | solution.py:78
  57.4 4.6 %copy-start.7 = (bf16[360,320]{0,1:T(8,128)(2,1)}, bf16[360,320]{0,1:T(8,128)(2,1)S(1)}, u32[]{:S(2)}) copy-start(bf16[360,320]{0,1:T(8,128)(2,1)S(1)} %collective-permute-done.8) | copy-start | bytes 691204
  76.4 26.1 %copy-start.6 = (f32[360,320]{0,1:T(8,128)S(1)}, f32[360,320]{0,1:T(8,128)}, u32[]{:S(2)}) copy-start(f32[360,320]{0,1:T(8,128)} %param.15) | copy-start | bytes 1382404
  76.4 7.4 %collective-permute-start.13 = (f32[2,32]{1,0:T(2,128)S(1)}, f32[2,32]{1,0:T(2,128)S(1)}, u32[]{:S(2)}, u32[]{:S(2)}) collective-permute-start(f32[2,32]{1,0:T(2,128)S(1)} %pad_maximum_fusion.3), channel_id=1, source_target_pairs={{0,24},{8,0},{16,8},{24,16},{1,25},{9,1},{17,9},{25,17},{2,26},{10... | collective-permute-start | bytes 776 | tf_op jit(solution)/shard_map/ppermute | solution.py:33
  76.8 7.0 %collective-permute-start.12 = (f32[2,32]{1,0:T(2,128)S(1)}, f32[2,32]{1,0:T(2,128)S(1)}, u32[]{:S(2)}, u32[]{:S(2)}) collective-permute-start(f32[2,32]{1,0:T(2,128)S(1)} %pad_maximum_fusion.3), channel_id=1, source_target_pairs={{0,16},{8,24},{16,0},{24,8},{1,17},{9,25},{17,1},{25,9},{2,18},{10... | collective-permute-start | bytes 776 | tf_op jit(solution)/shard_map/ppermute | solution.py:33
  79.1 5.4 %collective-permute-start.11 = (f32[2,32]{1,0:T(2,128)S(1)}, f32[2,32]{1,0:T(2,128)S(1)}, u32[]{:S(2)}, u32[]{:S(2)}) collective-permute-start(f32[2,32]{1,0:T(2,128)S(1)} %pad_maximum_fusion.3), channel_id=1, source_target_pairs={{0,8},{8,16},{16,24},{24,0},{1,9},{9,17},{17,25},{25,1},{2,10},{10... | collective-permute-start | bytes 776 | tf_op jit(solution)/shard_map/ppermute | solution.py:33
  83.3 6.9 %collective-permute-start.14 = (bf16[360,320]{0,1:T(8,128)(2,1)S(1)}, bf16[360,320]{0,1:T(8,128)(2,1)S(1)}, u32[]{:S(2)}, u32[]{:S(2)}) collective-permute-start(bf16[360,320]{0,1:T(8,128)(2,1)S(1)} %fusion.37), channel_id=1, source_target_pairs={{0,8},{8,0},{16,24},{24,16},{1,9},{9,1},{17,25},{25,17},{2,10},{10... | collective-permute-start | bytes 691208 | tf_op jit(solution)/shard_map/ppermute | solution.py:90
  90.3 12.2 %collective-permute-start.15 = (bf16[360,320]{0,1:T(8,128)(2,1)S(1)}, bf16[360,320]{0,1:T(8,128)(2,1)S(1)}, u32[]{:S(2)}, u32[]{:S(2)}) collective-permute-start(bf16[360,320]{0,1:T(8,128)(2,1)S(1)} %add_convert_fusion), channel_id=1, source_target_pairs={{0,16},{8,24},{16,0},{24,8},{1,17},{9,25},{17,1},{25,9},{2,18},{10... | collective-permute-start | bytes 691208 | tf_op jit(solution)/shard_map/ppermute | solution.py:90
  (4 other events, 7.4 us)
Sparse Core Ops, SparseCore 0:
  16.5 27.7 all-gather.2

commit v9 on v7

--- a/solution.py
+++ b/solution.py
@@ -64,8 +64,6 @@
         pairs = [(i, i ^ step) for i in range(count)]
         got = lax.ppermute(send.astype(jnp.bfloat16), axis, pairs)
         held = row_major(keep + got.astype(jnp.float32))
-        if step == 1:
-            held, companions = lax.optimization_barrier((held, companions))
         step *= 2
         if step < count <= 4 * step:
             break
@@ -81,17 +79,20 @@
     return total, companions
 
 
-def replicated_sum(value, axis):
+def replicated_sum(value, axis, companions):
     count = lax.axis_size(axis)
     if count & (count - 1):
-        return lax.psum(value.astype(jnp.bfloat16), axis).astype(jnp.float32)
+        value, companions = lax.optimization_barrier((value, companions))
+        return lax.psum(value.astype(jnp.bfloat16), axis).astype(jnp.float32), companions
     step = 1
     while step < count:
         mine = value.astype(jnp.bfloat16)
         pairs = [(i, i ^ step) for i in range(count)]
         value = mine.astype(jnp.float32) + lax.ppermute(mine, axis, pairs).astype(jnp.float32)
+        if step == 1:
+            value, companions = lax.optimization_barrier((value, companions))
         step *= 2
-    return value
+    return value, companions
 
 
 def group_sum(values, groups):
@@ -145,7 +146,8 @@
         act_cols, flat_cot, (((0,), (0,)), ((), ())), preferred_element_type=jnp.float32
     )
     weight_terms = row_major(weight_terms)
-    grad_piece, (gathered, cot_pad) = halving_scatter(weight_terms, "dp", (gathered, cot_pad))
+    grad_piece, companions = halving_scatter(weight_terms, "dp", (gathered, cot_pad))
+    grad_piece, (gathered, cot_pad) = replicated_sum(grad_piece, "space", companions)
     output = jnp.dot(act_cols, gathered, preferred_element_type=jnp.float32)
     block_out = (output.reshape(height_dev, width_dev, channels) * inside).astype(jnp.bfloat16)
     tap_weights = gathered.reshape(9, channels, channels)
@@ -165,9 +167,7 @@
     local_first = group_sum(scaled, GROUPS)
     local_second = group_sum(scaled * normed, GROUPS)
     sum_first, sum_second = space_sum((local_first, local_second), "space")
-    grad_piece = with_layout_constraint(
-        replicated_sum(grad_piece, "space"), Layout(major_to_minor=(1, 0))
-    )
+    grad_piece = with_layout_constraint(grad_piece, Layout(major_to_minor=(1, 0)))
     first = sum_first / cell_count
     second = sum_second / cell_count
     input_grad = (

time: 116 us -> 111 us (0.957)
  local copies, waits for them, and re-layouts: 21.4 us -> 16.4 us
  other arithmetic: 9.76 us -> 12.4 us
  starting transfers between devices: 31.4 us -> 29.7 us
    ppermute x2, waiting for transfers between devices: 15.5 us -> 7.78 us  [replicated_sum(): lax.ppermute(mine, axis, pairs).astype(jnp.float32)]
    ppermute x3, waiting for transfers between devices: 4.53 us -> 9.13 us  [halving_scatter(): lax.ppermute(send.astype(jnp.bfloat16), axis, pairs).astype(jnp.float32)]
    unnamed x35 -> x36, local copies, waits for them, and re-layouts: 5 us -> 7.58 us
    ppermute x1, waiting for transfers between devices: 0.01 us -> 2.51 us  [halving_scatter(): got = lax.ppermute(send.astype(jnp.bfloat16), axis, pairs)]
    ppermute x6, starting transfers between devices: 11.8 us -> 9.98 us  [space_sum(): lax.ppermute(joined, axis, [(i, (i + shift) % count) for i in range(count)])]
    reshape x1, local copies, waits for them, and re-layouts: 4.26 us -> 2.47 us  [local(): tap_weights = gathered.reshape(9, channels, channels)]
    optimization_barrier x1 -> x0, local copies, waits for them, and re-layouts: 1.41 us -> none  [halving_scatter(): held, companions = lax.optimization_barrier((held, companions))]
    convert_element_type x1 -> x0, local copies, waits for them, and re-layouts: 1.25 us -> none  [halving_scatter(): send.astype(jnp.bfloat16)]
  transfers between devices with their start and end apart: 17 -> 17, of which waited for: 12 -> 10; matrix products, arithmetic and copies ran while one was open for 17% -> 18% of each run, Pallas kernels for 0% -> 0%
where the time goes in v9:
time: 111 us
  starting transfers between devices  29.7 us (27%)
  waiting for transfers between devices  26.9 us (24%)
  local copies, waits for them, and re-layouts  16.4 us (15%)
  between operations  15.9 us (14%)
  other arithmetic  12.4 us (11%)
  matrix products  9.45 us (9%)
    ppermute x6, starting transfers between devices, space_sum(): lax.ppermute(joined, axis, [(i, (i + shift) % count) for i in range(count)])  9.98 us
    ppermute x3, waiting for transfers between devices, halving_scatter(): lax.ppermute(send.astype(jnp.bfloat16), axis, pairs).astype(jnp.float32)  9.13 us
    ppermute x2, starting transfers between devices, with_halo(): lax.ppermute(tail, axis, [(i, (i + 1) % count) for i in range(ends)])  9.1 us
    ppermute x2, waiting for transfers between devices, replicated_sum(): lax.ppermute(mine, axis, pairs).astype(jnp.float32)  7.78 us
    unnamed x36, local copies, waits for them, and re-layouts  7.58 us
    ppermute x2, starting transfers between devices, replicated_sum(): lax.ppermute(mine, axis, pairs).astype(jnp.float32)  4.44 us
    dot_general x1, matrix products, local(): upstream = jnp.dot(cot_cols, flipped, preferred_element_type=jnp.float32)  4.4 us
    ppermute x6, waiting for transfers between devices, space_sum(): lax.ppermute(joined, axis, [(i, (i + shift) % count) for i in range(count)])  4.33 us
  transfers between devices with their start and end apart: 17, of which 10 were waited for; matrix products, arithmetic and copies ran while one was open for 18% of the time, Pallas kernels for 0%

profile of v9, /device:TPU:0, one launch (start us, length us, event | category | flops | bytes accessed | tf_op | source)
XLA Modules:
  0.0 110.7 jit_solution(17073555405632866834)
XLA Ops:
  10.2 5.1 %collective-permute-start.2 = (f32[2,32]{1,0:T(2,128)S(1)}, f32[2,32]{1,0:T(2,128)S(1)}, u32[]{:S(2)}, u32[]{:S(2)}) collective-permute-start(f32[2,32]{1,0:T(2,128)S(1)} %pad_maximum_fusion.2), channel_id=1, source_target_pairs={{0,24},{8,0},{16,8},{24,16},{1,25},{9,1},{17,9},{25,17},{2,26},{10... | collective-permute-start | bytes 776 | tf_op jit(solution)/shard_map/ppermute | solution.py:33
  16.6 3.2 %collective-permute-done.1 = f32[2,32]{1,0:T(2,128)S(1)} collective-permute-done((f32[2,32]{1,0:T(2,128)S(1)}, f32[2,32]{1,0:T(2,128)S(1)}, u32[]{:S(2)}, u32[]{:S(2)}) %collective-permute-start.1) | collective-permute-done | bytes 288 | tf_op jit(solution)/shard_map/ppermute | solution.py:33
  21.1 1.3 %multiply_convert_fusion = bf16[3,128,320]{1,2,0:T(8,128)(2,1)S(1)} fusion(bf16[1,3,128,320]{2,3,1,0:T(8,128)(2,1)} %param.9, f32[320]{0:T(512)} %param.12, f32[320]{0:T(512)} %param.11, f32[320]{0:T(512)S(1)} %mul.163, f32[320]{0:T(512)S(1)} %sub.37, f32[3,128]{1,0:T(4,128)S(1)} %get-tuple-element.28), kind=kLoop, calls=%fused_computation.48 | loop fusion | flops 1597440 | bytes 498176 | tf_op jit(solution)/shard_map/convert_element_type | solution.py:132
  23.8 4.6 %collective-permute-start.3 = (bf16[1,128,320]{1,2,0:T(8,128)(2,1)S(1)}, bf16[1,128,320]{1,2,0:T(8,128)(2,1)S(1)}, u32[]{:S(2)}, u32[]{:S(2)}) collective-permute-start(bf16[1,128,320]{1,2,0:T(8,128)(2,1)S(1)} %get-tuple-element.23), channel_id=1, source_target_pairs={{0,8},{8,16},{16,24},{1,9},{9,17},{17,25},{2,10},{10,18},{18,26},{... | collective-permute-start | bytes 245768 | tf_op jit(solution)/shard_map/ppermute | solution.py:18
  31.9 1.5 %fusion.48 = f32[2880,320,1]{1,0,2:T(8,128)S(1)} fusion(bf16[3,128,2880]{1,2,0:T(8,128)(2,1)S(1)} %slice_dynamic-update-slice_fusion, bf16[3,128,320]{1,2,0:T(8,128)(2,1)S(1)} %bitcast_multiply_fusion), kind=kOutput, calls=%fused_computation.96 | convolution fusion | flops 707788800 | bytes 6144000 | tf_op jit(solution)/shard_map/dot_general | solution.py:145
  33.5 2.0 %copy-done = f32[2880,320,1]{1,0,2:T(8,128)} copy-done((f32[2880,320,1]{1,0,2:T(8,128)}, f32[2880,320,1]{1,0,2:T(8,128)S(1)}, u32[]{:S(2)}) %copy-start) | copy-done | bytes 3686424
  36.4 2.5 %collective-permute-done.5 = bf16[4,360,320]{1,2,0:T(8,128)(2,1)S(1)} collective-permute-done((bf16[4,360,320]{1,2,0:T(8,128)(2,1)S(1)}, bf16[4,360,320]{1,2,0:T(8,128)(2,1)S(1)}, u32[]{:S(2)}, u32[]{:S(2)}) %collective-permute-start.5) | collective-permute-done | bytes 921632 | tf_op jit(solution)/shard_map/ppermute | solution.py:65
  39.7 1.8 %bitcast_add_fusion = f32[4,360,320]{2,1,0:T(8,128)S(1)} fusion(bf16[4,360,320]{2,1,0:T(8,128)(2,1)S(1)} %copy.49, f32[4,2,360,320]{3,2,1,0:T(8,128)} %bitcast.116, s32[]{:T(128)S(6)} %select_n.33), kind=kLoop, calls=%fused_computation.3 | loop fusion | flops 921600 | bytes 4608004 | tf_op jit(solution)/shard_map/add | solution.py:66
  42.5 2.5 %collective-permute-start.8 = (bf16[360,320]{0,1:T(8,128)(2,1)}, bf16[360,320]{0,1:T(8,128)(2,1)S(1)}, u32[]{:S(2)}, u32[]{:S(2)}) collective-permute-start(bf16[360,320]{0,1:T(8,128)(2,1)} %bitcast.100), channel_id=1, source_target_pairs={{0,6},{1,7},{2,4},{3,5},{4,2},{5,3},{6,0},{7,1},{8,14},{9,15},{10,... | collective-permute-start | bytes 691208 | tf_op jit(solution)/shard_map/ppermute | solution.py:78
  48.0 4.5 %collective-permute-done.8 = bf16[360,320]{0,1:T(8,128)(2,1)S(1)} collective-permute-done((bf16[360,320]{0,1:T(8,128)(2,1)}, bf16[360,320]{0,1:T(8,128)(2,1)S(1)}, u32[]{:S(2)}, u32[]{:S(2)}) %collective-permute-start.8) | collective-permute-done | bytes 230432 | tf_op jit(solution)/shard_map/ppermute | solution.py:78
  52.5 4.4 %collective-permute-done.7 = bf16[360,320]{0,1:T(8,128)(2,1)S(1)} collective-permute-done((bf16[360,320]{0,1:T(8,128)(2,1)}, bf16[360,320]{0,1:T(8,128)(2,1)S(1)}, u32[]{:S(2)}, u32[]{:S(2)}) %collective-permute-start.7) | collective-permute-done | bytes 230432 | tf_op jit(solution)/shard_map/ppermute | solution.py:78
  58.2 2.4 %collective-permute-start.9 = (bf16[360,320]{0,1:T(8,128)(2,1)S(1)}, bf16[360,320]{0,1:T(8,128)(2,1)S(1)}, u32[]{:S(2)}, u32[]{:S(2)}) collective-permute-start(bf16[360,320]{0,1:T(8,128)(2,1)S(1)} %fusion.38), channel_id=1, source_target_pairs={{0,8},{8,0},{16,24},{24,16},{1,9},{9,1},{17,25},{25,17},{2,10},{10... | collective-permute-start | bytes 691208 | tf_op jit(solution)/shard_map/ppermute | solution.py:91
  61.9 4.6 %collective-permute-start.10 = (bf16[1,128,320]{1,2,0:T(8,128)(2,1)S(1)}, bf16[1,128,320]{1,2,0:T(8,128)(2,1)S(1)}, u32[]{:S(2)}, u32[]{:S(2)}) collective-permute-start(bf16[1,128,320]{1,2,0:T(8,128)(2,1)S(1)} %get-tuple-element.21), channel_id=1, source_target_pairs={{0,8},{8,16},{16,24},{1,9},{9,17},{17,25},{2,10},{10,18},{18,26},{... | collective-permute-start | bytes 245768 | tf_op jit(solution)/shard_map/ppermute | solution.py:18
  66.5 2.1 %collective-permute-done.11 = bf16[1,128,320]{1,2,0:T(8,128)(2,1)S(1)} collective-permute-done((bf16[1,128,320]{1,2,0:T(8,128)(2,1)S(1)}, bf16[1,128,320]{1,2,0:T(8,128)(2,1)S(1)}, u32[]{:S(2)}, u32[]{:S(2)}) %collective-permute-start.11) | collective-permute-done | bytes 81952 | tf_op jit(solution)/shard_map/ppermute | solution.py:20
  69.1 3.0 %copy.56 = bf16[8,360,320]{2,1,0:T(8,128)(2,1)S(1)} copy(bf16[8,360,320]{1,2,0:T(8,128)(2,1)} %all-gather.3.cloned.1.call-done) | data formatting | bytes 3686400 | tf_op jit(solution)/shard_map/all_gather | solution.py:122
  73.3 1.4 %copy-done.7 = bf16[3,128,2880]{1,2,0:T(8,128)(2,1)} copy-done((bf16[3,128,2880]{1,2,0:T(8,128)(2,1)}, bf16[3,128,2880]{1,2,0:T(8,128)(2,1)S(1)}, u32[]{:S(2)}) %copy-start.7) | copy-done | bytes 2211864
  74.7 2.5 %copy.58 = bf16[9,320,320]{1,2,0:T(8,128)(2,1)} copy(bf16[9,320,320]{2,1,0:T(8,128)(2,1)S(1)} %bitcast.117) | data formatting | bytes 3686400 | tf_op jit(solution)/shard_map/reshape | solution.py:153
  77.1 4.4 %fusion.45 = (f32[320]{0:T(512)S(1)}, f32[320]{0:T(512)S(1)}, f32[3,128,320]{1,2,0:T(8,128)}) fusion(f32[320]{0:T(512)S(1)} %mul.163, f32[320]{0:T(512)S(1)} %sub.37, f32[3,128]{1,0:T(4,128)S(1)} %get-tuple-element.28, bf16[1,3,128,320]{2,3,1,0:T(8,128)(2,1)S(1)} %copy-done.3, f32[320]{0:T(512)S(1)} %copy-done.8, f32[320]{0:T(512)S(1)} %copy-done.9, ...), kind=kOutput, calls=%fused_computation.93 | convolution fusion | flops 710245760 | bytes 4801536 | tf_op jit(solution)/shard_map/dot_general | solution.py:163
  82.0 2.9 %collective-permute-start.14 = (f32[2,32]{1,0:T(2,128)S(1)}, f32[2,32]{1,0:T(2,128)S(1)}, u32[]{:S(2)}, u32[]{:S(2)}) collective-permute-start(f32[2,32]{1,0:T(2,128)S(1)} %pad_maximum_fusion.3), channel_id=1, source_target_pairs={{0,24},{8,0},{16,8},{24,16},{1,25},{9,1},{17,9},{25,17},{2,26},{10... | collective-permute-start | bytes 776 | tf_op jit(solution)/shard_map/ppermute | solution.py:33
  85.9 3.5 %fusion.11 = bf16[1,3,128,320]{2,3,1,0:T(8,128)(2,1)} fusion(bf16[3,128,2880]{1,2,0:T(8,128)(2,1)} %copy-done.1, bf16[2880,320]{1,0:T(8,128)(2,1)S(1)} %bitcast.118, f32[3,128]{1,0:T(4,128)S(1)} %get-tuple-element.28), kind=kOutput, calls=%fused_computation.12 | convolution fusion | flops 708034560 | bytes 4302336 | tf_op jit(solution)/shard_map/dot_general | solution.py:151
  89.4 2.0 %collective-permute-start.15 = (bf16[360,320]{0,1:T(8,128)(2,1)S(1)}, bf16[360,320]{0,1:T(8,128)(2,1)S(1)}, u32[]{:S(2)}, u32[]{:S(2)}) collective-permute-start(bf16[360,320]{0,1:T(8,128)(2,1)S(1)} %convert_add_fusion.1), channel_id=1, source_target_pairs={{0,16},{8,24},{16,0},{24,8},{1,17},{9,25},{17,1},{25,9},{2,18},{10... | collective-permute-start | bytes 691208 | tf_op jit(solution)/shard_map/ppermute | solution.py:91
  91.8 2.0 %fusion.41 = bf16[1,3,128,320]{2,3,1,0:T(8,128)(2,1)} fusion(f32[320]{0:T(512)S(1)} %mul.180, f32[320]{0:T(512)S(1)} %sub.37, f32[3,128]{1,0:T(4,128)S(1)} %get-tuple-element.28, bf16[1,3,128,320]{2,3,1,0:T(8,128)(2,1)S(1)} %copy-done.3, f32[3,128,320]{1,2,0:T(8,128)} %get-tuple-element.29, f32[320]{0:T(512)S(1)} %sub.44, f32[320]{0:T(512)S(1)} %mul.163), kind=kLoop, calls=%fused_computation.73 | loop fusion | flops 1351680 | bytes 989696 | tf_op jit(solution)/shard_map/broadcast_in_dim | solution.py:181
  93.8 7.8 %collective-permute-done.15 = bf16[360,320]{0,1:T(8,128)(2,1)S(1)} collective-permute-done((bf16[360,320]{0,1:T(8,128)(2,1)S(1)}, bf16[360,320]{0,1:T(8,128)(2,1)S(1)}, u32[]{:S(2)}, u32[]{:S(2)}) %collective-permute-start.15) | collective-permute-done | bytes 230432 | tf_op jit(solution)/shard_map/ppermute | solution.py:91
  101.6 2.3 %fusion.35 = (f32[360,320]{0,1:T(8,128)}, f32[360,320]{0,1:T(8,128)}) fusion(f32[360,320]{0,1:T(8,128)S(1)} %copy-done.6, f32[360,320]{0,1:T(8,128)} %param.14, bf16[360,320]{0,1:T(8,128)(2,1)S(1)} %collective-permute-done.15, bf16[360,320]{0,1:T(8,128)(2,1)S(1)} %convert_add_fusion.1), kind=kLoop, calls=%fused_computation.41 | loop fusion | flops 1612800 | bytes 2304000 | tf_op jit(solution)/shard_map/div | solution.py:180
  (100 shorter events, 20.6 us)
Async XLA Ops:
  7.2 61.9 %all-gather.3.cloned.1.call-start = ((), (), s32[]{:S(2)}) async-start(), calls=%async_computation | async-start | bytes 2211840 | tf_op jit(solution)/shard_map/all_gather | solution.py:122
  10.2 6.4 %collective-permute-start.2 = (f32[2,32]{1,0:T(2,128)S(1)}, f32[2,32]{1,0:T(2,128)S(1)}, u32[]{:S(2)}, u32[]{:S(2)}) collective-permute-start(f32[2,32]{1,0:T(2,128)S(1)} %pad_maximum_fusion.2), channel_id=1, source_target_pairs={{0,24},{8,0},{16,8},{24,16},{1,25},{9,1},{17,9},{25,17},{2,26},{10... | collective-permute-start | bytes 776 | tf_op jit(solution)/shard_map/ppermute | solution.py:33
  15.3 4.5 %collective-permute-start.1 = (f32[2,32]{1,0:T(2,128)S(1)}, f32[2,32]{1,0:T(2,128)S(1)}, u32[]{:S(2)}, u32[]{:S(2)}) collective-permute-start(f32[2,32]{1,0:T(2,128)S(1)} %pad_maximum_fusion.2), channel_id=1, source_target_pairs={{0,16},{8,24},{16,0},{24,8},{1,17},{9,25},{17,1},{25,9},{2,18},{10... | collective-permute-start | bytes 776 | tf_op jit(solution)/shard_map/ppermute | solution.py:33
  15.3 5.4 %collective-permute-start = (f32[2,32]{1,0:T(2,128)S(1)}, f32[2,32]{1,0:T(2,128)S(1)}, u32[]{:S(2)}, u32[]{:S(2)}) collective-permute-start(f32[2,32]{1,0:T(2,128)S(1)} %pad_maximum_fusion.2), channel_id=1, source_target_pairs={{0,8},{8,16},{16,24},{24,0},{1,9},{9,17},{17,25},{25,1},{2,10},{10... | collective-permute-start | bytes 776 | tf_op jit(solution)/shard_map/ppermute | solution.py:33
  21.1 10.0 %copy-start.2 = (bf16[1,3,128,320]{2,3,1,0:T(8,128)(2,1)S(1)}, bf16[1,3,128,320]{2,3,1,0:T(8,128)(2,1)}, u32[]{:S(2)}) copy-start(bf16[1,3,128,320]{2,3,1,0:T(8,128)(2,1)} %param.9) | copy-start | bytes 737284
  21.1 10.0 %copy-start.8 = (f32[320]{0:T(512)S(1)}, f32[320]{0:T(512)}, u32[]{:S(2)}) copy-start(f32[320]{0:T(512)} %param.12) | copy-start | bytes 3844
  21.1 10.0 %copy-start.9 = (f32[320]{0:T(512)S(1)}, f32[320]{0:T(512)}, u32[]{:S(2)}) copy-start(f32[320]{0:T(512)} %param.11) | copy-start | bytes 3844
  22.5 6.9 %collective-permute-start.4 = (bf16[1,128,320]{1,2,0:T(8,128)(2,1)S(1)}, bf16[1,128,320]{1,2,0:T(8,128)(2,1)S(1)}, u32[]{:S(2)}, u32[]{:S(2)}) collective-permute-start(bf16[1,128,320]{1,2,0:T(8,128)(2,1)S(1)} %get-tuple-element.24), channel_id=1, source_target_pairs={{8,0},{16,8},{24,16},{9,1},{17,9},{25,17},{10,2},{18,10},{26,18},{... | collective-permute-start | bytes 245768 | tf_op jit(solution)/shard_map/ppermute | solution.py:20
  23.8 6.6 %collective-permute-start.3 = (bf16[1,128,320]{1,2,0:T(8,128)(2,1)S(1)}, bf16[1,128,320]{1,2,0:T(8,128)(2,1)S(1)}, u32[]{:S(2)}, u32[]{:S(2)}) collective-permute-start(bf16[1,128,320]{1,2,0:T(8,128)(2,1)S(1)} %get-tuple-element.23), channel_id=1, source_target_pairs={{0,8},{8,16},{16,24},{1,9},{9,17},{17,25},{2,10},{10,18},{18,26},{... | collective-permute-start | bytes 245768 | tf_op jit(solution)/shard_map/ppermute | solution.py:18
  29.3 2.6 %copy-start.4 = (bf16[3,128,320]{1,2,0:T(8,128)(2,1)}, bf16[3,128,320]{1,2,0:T(8,128)(2,1)S(1)}, u32[]{:S(2)}) copy-start(bf16[3,128,320]{1,2,0:T(8,128)(2,1)S(1)} %bitcast_multiply_fusion) | copy-start | bytes 737284
  36.3 2.6 %collective-permute-start.5 = (bf16[4,360,320]{1,2,0:T(8,128)(2,1)S(1)}, bf16[4,360,320]{1,2,0:T(8,128)(2,1)S(1)}, u32[]{:S(2)}, u32[]{:S(2)}) collective-permute-start(bf16[4,360,320]{1,2,0:T(8,128)(2,1)S(1)} %copy.48), channel_id=1, source_target_pairs={{0,1},{1,0},{2,3},{3,2},{4,5},{5,4},{6,7},{7,6},{8,9},{9,8},{10,11... | collective-permute-start | bytes 2764808 | tf_op jit(solution)/shard_map/ppermute | solution.py:65
  42.5 10.0 %collective-permute-start.8 = (bf16[360,320]{0,1:T(8,128)(2,1)}, bf16[360,320]{0,1:T(8,128)(2,1)S(1)}, u32[]{:S(2)}, u32[]{:S(2)}) collective-permute-start(bf16[360,320]{0,1:T(8,128)(2,1)} %bitcast.100), channel_id=1, source_target_pairs={{0,6},{1,7},{2,4},{3,5},{4,2},{5,3},{6,0},{7,1},{8,14},{9,15},{10,... | collective-permute-start | bytes 691208 | tf_op jit(solution)/shard_map/ppermute | solution.py:78
  45.0 15.6 %copy-start.5 = (bf16[3,128,320]{1,2,0:T(8,128)(2,1)S(1)}, bf16[3,128,320]{1,2,0:T(8,128)(2,1)}, u32[]{:S(2)}) copy-start(bf16[3,128,320]{1,2,0:T(8,128)(2,1)} %copy-done.4) | copy-start | bytes 737284
  45.9 11.0 %collective-permute-start.7 = (bf16[360,320]{0,1:T(8,128)(2,1)}, bf16[360,320]{0,1:T(8,128)(2,1)S(1)}, u32[]{:S(2)}, u32[]{:S(2)}) collective-permute-start(bf16[360,320]{0,1:T(8,128)(2,1)} %bitcast.121), channel_id=1, source_target_pairs={{0,4},{1,5},{2,6},{3,7},{4,0},{5,1},{6,2},{7,3},{8,12},{9,13},{10,... | collective-permute-start | bytes 691208 | tf_op jit(solution)/shard_map/ppermute | solution.py:78
  47.2 9.9 %collective-permute-start.6 = (bf16[360,320]{0,1:T(8,128)(2,1)}, bf16[360,320]{0,1:T(8,128)(2,1)}, u32[]{:S(2)}, u32[]{:S(2)}) collective-permute-start(bf16[360,320]{0,1:T(8,128)(2,1)} %bitcast.102), channel_id=1, source_target_pairs={{0,2},{1,3},{2,0},{3,1},{4,6},{5,7},{6,4},{7,5},{8,10},{9,11},{10,... | collective-permute-start | bytes 691208 | tf_op jit(solution)/shard_map/ppermute | solution.py:78
  58.2 10.8 %collective-permute-start.9 = (bf16[360,320]{0,1:T(8,128)(2,1)S(1)}, bf16[360,320]{0,1:T(8,128)(2,1)S(1)}, u32[]{:S(2)}, u32[]{:S(2)}) collective-permute-start(bf16[360,320]{0,1:T(8,128)(2,1)S(1)} %fusion.38), channel_id=1, source_target_pairs={{0,8},{8,0},{16,24},{24,16},{1,9},{9,1},{17,25},{25,17},{2,10},{10... | collective-permute-start | bytes 691208 | tf_op jit(solution)/shard_map/ppermute | solution.py:91
  60.6 8.0 %collective-permute-start.11 = (bf16[1,128,320]{1,2,0:T(8,128)(2,1)S(1)}, bf16[1,128,320]{1,2,0:T(8,128)(2,1)S(1)}, u32[]{:S(2)}, u32[]{:S(2)}) collective-permute-start(bf16[1,128,320]{1,2,0:T(8,128)(2,1)S(1)} %get-tuple-element.22), channel_id=1, source_target_pairs={{8,0},{16,8},{24,16},{9,1},{17,9},{25,17},{10,2},{18,10},{26,18},{... | collective-permute-start | bytes 245768 | tf_op jit(solution)/shard_map/ppermute | solution.py:20
  61.9 6.7 %collective-permute-start.10 = (bf16[1,128,320]{1,2,0:T(8,128)(2,1)S(1)}, bf16[1,128,320]{1,2,0:T(8,128)(2,1)S(1)}, u32[]{:S(2)}, u32[]{:S(2)}) collective-permute-start(bf16[1,128,320]{1,2,0:T(8,128)(2,1)S(1)} %get-tuple-element.21), channel_id=1, source_target_pairs={{0,8},{8,16},{16,24},{1,9},{9,17},{17,25},{2,10},{10,18},{18,26},{... | collective-permute-start | bytes 245768 | tf_op jit(solution)/shard_map/ppermute | solution.py:18
  74.7 2.5 %copy-start.3 = (bf16[1,3,128,320]{2,3,1,0:T(8,128)(2,1)S(1)}, bf16[1,3,128,320]{2,3,1,0:T(8,128)(2,1)}, u32[]{:S(2)}) copy-start(bf16[1,3,128,320]{2,3,1,0:T(8,128)(2,1)} %param.9) | copy-start | bytes 737284
  82.0 19.6 %copy-start.6 = (f32[360,320]{0,1:T(8,128)S(1)}, f32[360,320]{0,1:T(8,128)}, u32[]{:S(2)}) copy-start(f32[360,320]{0,1:T(8,128)} %param.15) | copy-start | bytes 1382404
  82.0 9.4 %collective-permute-start.14 = (f32[2,32]{1,0:T(2,128)S(1)}, f32[2,32]{1,0:T(2,128)S(1)}, u32[]{:S(2)}, u32[]{:S(2)}) collective-permute-start(f32[2,32]{1,0:T(2,128)S(1)} %pad_maximum_fusion.3), channel_id=1, source_target_pairs={{0,24},{8,0},{16,8},{24,16},{1,25},{9,1},{17,9},{25,17},{2,26},{10... | collective-permute-start | bytes 776 | tf_op jit(solution)/shard_map/ppermute | solution.py:33
  84.9 6.5 %collective-permute-start.13 = (f32[2,32]{1,0:T(2,128)S(1)}, f32[2,32]{1,0:T(2,128)S(1)}, u32[]{:S(2)}, u32[]{:S(2)}) collective-permute-start(f32[2,32]{1,0:T(2,128)S(1)} %pad_maximum_fusion.3), channel_id=1, source_target_pairs={{0,16},{8,24},{16,0},{24,8},{1,17},{9,25},{17,1},{25,9},{2,18},{10... | collective-permute-start | bytes 776 | tf_op jit(solution)/shard_map/ppermute | solution.py:33
  85.8 5.6 %collective-permute-start.12 = (f32[2,32]{1,0:T(2,128)S(1)}, f32[2,32]{1,0:T(2,128)S(1)}, u32[]{:S(2)}, u32[]{:S(2)}) collective-permute-start(f32[2,32]{1,0:T(2,128)S(1)} %pad_maximum_fusion.3), channel_id=1, source_target_pairs={{0,8},{8,16},{16,24},{24,0},{1,9},{9,17},{17,25},{25,1},{2,10},{10... | collective-permute-start | bytes 776 | tf_op jit(solution)/shard_map/ppermute | solution.py:33
  89.4 12.2 %collective-permute-start.15 = (bf16[360,320]{0,1:T(8,128)(2,1)S(1)}, bf16[360,320]{0,1:T(8,128)(2,1)S(1)}, u32[]{:S(2)}, u32[]{:S(2)}) collective-permute-start(bf16[360,320]{0,1:T(8,128)(2,1)S(1)} %convert_add_fusion.1), channel_id=1, source_target_pairs={{0,16},{8,24},{16,0},{24,8},{1,17},{9,25},{17,1},{25,9},{2,18},{10... | collective-permute-start | bytes 691208 | tf_op jit(solution)/shard_map/ppermute | solution.py:91
  (3 other events, 4.9 us)
Sparse Core Ops, SparseCore 0:
  16.5 27.7 all-gather.2

commit v10 on v9

--- a/solution.py
+++ b/solution.py
@@ -64,6 +64,8 @@
         pairs = [(i, i ^ step) for i in range(count)]
         got = lax.ppermute(send.astype(jnp.bfloat16), axis, pairs)
         held = row_major(keep + got.astype(jnp.float32))
+        if step == 1:
+            held, companions = lax.optimization_barrier((held, companions))
         step *= 2
         if step < count <= 4 * step:
             break
@@ -146,8 +148,8 @@
         act_cols, flat_cot, (((0,), (0,)), ((), ())), preferred_element_type=jnp.float32
     )
     weight_terms = row_major(weight_terms)
-    grad_piece, companions = halving_scatter(weight_terms, "dp", (gathered, cot_pad))
-    grad_piece, (gathered, cot_pad) = replicated_sum(grad_piece, "space", companions)
+    grad_piece, gathered = halving_scatter(weight_terms, "dp", gathered)
+    grad_piece, (gathered, cot_pad) = replicated_sum(grad_piece, "space", (gathered, cot_pad))
     output = jnp.dot(act_cols, gathered, preferred_element_type=jnp.float32)
     block_out = (output.reshape(height_dev, width_dev, channels) * inside).astype(jnp.bfloat16)
     tap_weights = gathered.reshape(9, channels, channels)

time: 111 us -> 116 us (1.045)
  waiting for transfers between devices: 26.9 us -> 31.4 us
    all_gather x1, waiting for transfers between devices: 0.02 us -> 2.78 us  [local(): lax.all_gather(row_major(weight), 'dp', axis=0, tiled=True)]
    unnamed x36 -> x35, local copies, waits for them, and re-layouts: 7.58 us -> 4.98 us
    ppermute x3, waiting for transfers between devices: 9.13 us -> 10.8 us  [halving_scatter(): lax.ppermute(send.astype(jnp.bfloat16), axis, pairs).astype(jnp.float32)]
  transfers between devices with their start and end apart: 17 -> 17, of which waited for: 10 -> 11; matrix products, arithmetic and copies ran while one was open for 18% -> 13% of each run, Pallas kernels for 0% -> 0%
where the time goes in v10:
time: 116 us; the launch traced here: 115 us
  waiting for transfers between devices  31.4 us (27%)
  starting transfers between devices  29.9 us (26%)
  local copies, waits for them, and re-layouts  16.4 us (14%)
  between operations  15.9 us (14%)
  other arithmetic  12.5 us (11%)
  matrix products  9.45 us (8%)
    ppermute x3, waiting for transfers between devices, halving_scatter(): lax.ppermute(send.astype(jnp.bfloat16), axis, pairs).astype(jnp.float32)  10.8 us
    ppermute x6, starting transfers between devices, space_sum(): lax.ppermute(joined, axis, [(i, (i + shift) % count) for i in range(count)])  10.7 us
    ppermute x2, starting transfers between devices, with_halo(): lax.ppermute(tail, axis, [(i, (i + 1) % count) for i in range(ends)])  9.1 us
    ppermute x2, waiting for transfers between devices, replicated_sum(): lax.ppermute(mine, axis, pairs).astype(jnp.float32)  7.6 us
    unnamed x35, local copies, waits for them, and re-layouts  4.98 us
    dot_general x1, matrix products, local(): upstream = jnp.dot(cot_cols, flipped, preferred_element_type=jnp.float32)  4.4 us
    ppermute x6, waiting for transfers between devices, space_sum(): lax.ppermute(joined, axis, [(i, (i + shift) % count) for i in range(count)])  4.33 us
    all_gather x1, local copies, waits for them, and re-layouts, local(): lax.all_gather(row_major(weight), 'dp', axis=0, tiled=True)  4.06 us
  transfers between devices with their start and end apart: 17, of which 11 were waited for; matrix products, arithmetic and copies ran while one was open for 13% of the time, Pallas kernels for 0%

profile of v10, /device:TPU:0, one launch (start us, length us, event | category | flops | bytes accessed | tf_op | source)
XLA Modules:
  0.0 115.4 jit_solution(3609611145293216476)
XLA Ops:
  10.2 5.1 %collective-permute-start.2 = (f32[2,32]{1,0:T(2,128)S(1)}, f32[2,32]{1,0:T(2,128)S(1)}, u32[]{:S(2)}, u32[]{:S(2)}) collective-permute-start(f32[2,32]{1,0:T(2,128)S(1)} %pad_maximum_fusion.2), channel_id=1, source_target_pairs={{0,24},{8,0},{16,8},{24,16},{1,25},{9,1},{17,9},{25,17},{2,26},{10... | collective-permute-start | bytes 776 | tf_op jit(solution)/shard_map/ppermute | solution.py:33
  16.6 3.2 %collective-permute-done.1 = f32[2,32]{1,0:T(2,128)S(1)} collective-permute-done((f32[2,32]{1,0:T(2,128)S(1)}, f32[2,32]{1,0:T(2,128)S(1)}, u32[]{:S(2)}, u32[]{:S(2)}) %collective-permute-start.1) | collective-permute-done | bytes 288 | tf_op jit(solution)/shard_map/ppermute | solution.py:33
  23.8 4.6 %collective-permute-start.3 = (bf16[1,128,320]{1,2,0:T(8,128)(2,1)S(1)}, bf16[1,128,320]{1,2,0:T(8,128)(2,1)S(1)}, u32[]{:S(2)}, u32[]{:S(2)}) collective-permute-start(bf16[1,128,320]{1,2,0:T(8,128)(2,1)S(1)} %get-tuple-element.27), channel_id=1, source_target_pairs={{0,8},{8,16},{16,24},{1,9},{9,17},{17,25},{2,10},{10,18},{18,26},{... | collective-permute-start | bytes 245768 | tf_op jit(solution)/shard_map/ppermute | solution.py:18
  31.9 1.5 %fusion.51 = f32[2880,320,1]{1,0,2:T(8,128)S(1)} fusion(bf16[3,128,2880]{1,2,0:T(8,128)(2,1)S(1)} %slice_dynamic-update-slice_fusion, bf16[3,128,320]{1,2,0:T(8,128)(2,1)S(1)} %bitcast_multiply_fusion), kind=kOutput, calls=%fused_computation.96 | convolution fusion | flops 707788800 | bytes 6144000 | tf_op jit(solution)/shard_map/dot_general | solution.py:147
  33.5 2.0 %copy-done = f32[2880,320,1]{1,0,2:T(8,128)} copy-done((f32[2880,320,1]{1,0,2:T(8,128)}, f32[2880,320,1]{1,0,2:T(8,128)S(1)}, u32[]{:S(2)}) %copy-start) | copy-done | bytes 3686424
  36.5 2.5 %collective-permute-done.5 = bf16[4,360,320]{1,2,0:T(8,128)(2,1)S(1)} collective-permute-done((bf16[4,360,320]{1,2,0:T(8,128)(2,1)S(1)}, bf16[4,360,320]{1,2,0:T(8,128)(2,1)S(1)}, u32[]{:S(2)}, u32[]{:S(2)}) %collective-permute-start.5) | collective-permute-done | bytes 921632 | tf_op jit(solution)/shard_map/ppermute | solution.py:65
  39.7 1.8 %bitcast_add_fusion = f32[4,360,320]{2,1,0:T(8,128)S(1)} fusion(bf16[4,360,320]{2,1,0:T(8,128)(2,1)S(1)} %copy.49, f32[4,2,360,320]{3,2,1,0:T(8,128)} %bitcast.113, s32[]{:T(128)S(6)} %select_n.33), kind=kLoop, calls=%fused_computation.3 | loop fusion | flops 921600 | bytes 4608004 | tf_op jit(solution)/shard_map/add | solution.py:66
  41.5 2.8 %all-gather.3.cloned.1.call-done = bf16[8,360,320]{1,2,0:T(8,128)(2,1)} async-done(((bf16[1,360,320]{1,2,0:T(8,128)(2,1)}), bf16[8,360,320]{1,2,0:T(8,128)(2,1)}) %all-gather.3.cloned.1.call-update) | async-done | bytes 1843216 | tf_op jit(solution)/shard_map/all_gather | solution.py:124
  44.3 4.1 %copy.52 = bf16[8,360,320]{2,1,0:T(8,128)(2,1)} copy(bf16[8,360,320]{1,2,0:T(8,128)(2,1)} %all-gather.3.cloned.1.call-done) | data formatting | bytes 3686400 | tf_op jit(solution)/shard_map/all_gather | solution.py:124
  50.0 1.5 %collective-permute-start.8 = (bf16[360,320]{0,1:T(8,128)(2,1)}, bf16[360,320]{0,1:T(8,128)(2,1)S(1)}, u32[]{:S(2)}, u32[]{:S(2)}) collective-permute-start(bf16[360,320]{0,1:T(8,128)(2,1)} %get-tuple-element.23), channel_id=1, source_target_pairs={{0,6},{1,7},{2,4},{3,5},{4,2},{5,3},{6,0},{7,1},{8,14},{9,15},{10,... | collective-permute-start | bytes 691208 | tf_op jit(solution)/shard_map/ppermute | solution.py:80
  51.5 1.5 %collective-permute-start.7 = (bf16[360,320]{0,1:T(8,128)(2,1)}, bf16[360,320]{0,1:T(8,128)(2,1)S(1)}, u32[]{:S(2)}, u32[]{:S(2)}) collective-permute-start(bf16[360,320]{0,1:T(8,128)(2,1)} %get-tuple-element.24), channel_id=1, source_target_pairs={{0,4},{1,5},{2,6},{3,7},{4,0},{5,1},{6,2},{7,3},{8,12},{9,13},{10,... | collective-permute-start | bytes 691208 | tf_op jit(solution)/shard_map/ppermute | solution.py:80
  53.8 6.2 %collective-permute-done.8 = bf16[360,320]{0,1:T(8,128)(2,1)S(1)} collective-permute-done((bf16[360,320]{0,1:T(8,128)(2,1)}, bf16[360,320]{0,1:T(8,128)(2,1)S(1)}, u32[]{:S(2)}, u32[]{:S(2)}) %collective-permute-start.8) | collective-permute-done | bytes 230432 | tf_op jit(solution)/shard_map/ppermute | solution.py:80
  60.0 4.6 %collective-permute-done.7 = bf16[360,320]{0,1:T(8,128)(2,1)S(1)} collective-permute-done((bf16[360,320]{0,1:T(8,128)(2,1)}, bf16[360,320]{0,1:T(8,128)(2,1)S(1)}, u32[]{:S(2)}, u32[]{:S(2)}) %collective-permute-start.7) | collective-permute-done | bytes 230432 | tf_op jit(solution)/shard_map/ppermute | solution.py:80
  65.7 1.6 %collective-permute-start.9 = (bf16[360,320]{0,1:T(8,128)(2,1)S(1)}, bf16[360,320]{0,1:T(8,128)(2,1)S(1)}, u32[]{:S(2)}, u32[]{:S(2)}) collective-permute-start(bf16[360,320]{0,1:T(8,128)(2,1)S(1)} %fusion.38), channel_id=1, source_target_pairs={{0,8},{8,0},{16,24},{24,16},{1,9},{9,1},{17,25},{25,17},{2,10},{10... | collective-permute-start | bytes 691208 | tf_op jit(solution)/shard_map/ppermute | solution.py:93
  68.5 4.6 %collective-permute-start.10 = (bf16[1,128,320]{1,2,0:T(8,128)(2,1)S(1)}, bf16[1,128,320]{1,2,0:T(8,128)(2,1)S(1)}, u32[]{:S(2)}, u32[]{:S(2)}) collective-permute-start(bf16[1,128,320]{1,2,0:T(8,128)(2,1)S(1)} %get-tuple-element.25), channel_id=1, source_target_pairs={{0,8},{8,16},{16,24},{1,9},{9,17},{17,25},{2,10},{10,18},{18,26},{... | collective-permute-start | bytes 245768 | tf_op jit(solution)/shard_map/ppermute | solution.py:18
  73.1 2.3 %collective-permute-done.11 = bf16[1,128,320]{1,2,0:T(8,128)(2,1)S(1)} collective-permute-done((bf16[1,128,320]{1,2,0:T(8,128)(2,1)S(1)}, bf16[1,128,320]{1,2,0:T(8,128)(2,1)S(1)}, u32[]{:S(2)}, u32[]{:S(2)}) %collective-permute-start.11) | collective-permute-done | bytes 81952 | tf_op jit(solution)/shard_map/ppermute | solution.py:20
  78.5 2.5 %copy.58 = bf16[9,320,320]{1,2,0:T(8,128)(2,1)} copy(bf16[9,320,320]{2,1,0:T(8,128)(2,1)S(1)} %bitcast.114) | data formatting | bytes 3686400 | tf_op jit(solution)/shard_map/reshape | solution.py:155
  81.0 4.4 %fusion.48 = (f32[320]{0:T(512)S(1)}, f32[320]{0:T(512)S(1)}, f32[3,128,320]{1,2,0:T(8,128)}) fusion(f32[320]{0:T(512)S(1)} %mul.163, f32[320]{0:T(512)S(1)} %sub.37, f32[3,128]{1,0:T(4,128)S(1)} %get-tuple-element.32, bf16[1,3,128,320]{2,3,1,0:T(8,128)(2,1)S(1)} %copy-done.4, f32[320]{0:T(512)S(1)} %copy-done.9, f32[320]{0:T(512)S(1)} %copy-done.10, ...), kind=kOutput, calls=%fused_computation.93 | convolution fusion | flops 710245760 | bytes 4801536 | tf_op jit(solution)/shard_map/dot_general | solution.py:165
  85.8 4.0 %collective-permute-start.14 = (f32[2,32]{1,0:T(2,128)S(1)}, f32[2,32]{1,0:T(2,128)S(1)}, u32[]{:S(2)}, u32[]{:S(2)}) collective-permute-start(f32[2,32]{1,0:T(2,128)S(1)} %pad_maximum_fusion.3), channel_id=1, source_target_pairs={{0,24},{8,0},{16,8},{24,16},{1,25},{9,1},{17,9},{25,17},{2,26},{10... | collective-permute-start | bytes 776 | tf_op jit(solution)/shard_map/ppermute | solution.py:33
  90.5 3.5 %fusion.11 = bf16[1,3,128,320]{2,3,1,0:T(8,128)(2,1)} fusion(bf16[3,128,2880]{1,2,0:T(8,128)(2,1)} %copy-done.2, bf16[2880,320]{1,0:T(8,128)(2,1)S(1)} %bitcast.115, f32[3,128]{1,0:T(4,128)S(1)} %get-tuple-element.32), kind=kOutput, calls=%fused_computation.12 | convolution fusion | flops 708034560 | bytes 4302336 | tf_op jit(solution)/shard_map/dot_general | solution.py:153
  94.0 2.3 %collective-permute-start.15 = (bf16[360,320]{0,1:T(8,128)(2,1)S(1)}, bf16[360,320]{0,1:T(8,128)(2,1)S(1)}, u32[]{:S(2)}, u32[]{:S(2)}) collective-permute-start(bf16[360,320]{0,1:T(8,128)(2,1)S(1)} %convert_add_fusion.1), channel_id=1, source_target_pairs={{0,16},{8,24},{16,0},{24,8},{1,17},{9,25},{17,1},{25,9},{2,18},{10... | collective-permute-start | bytes 691208 | tf_op jit(solution)/shard_map/ppermute | solution.py:93
  96.7 2.0 %fusion.44 = bf16[1,3,128,320]{2,3,1,0:T(8,128)(2,1)} fusion(f32[320]{0:T(512)S(1)} %mul.180, f32[320]{0:T(512)S(1)} %sub.37, f32[3,128]{1,0:T(4,128)S(1)} %get-tuple-element.32, bf16[1,3,128,320]{2,3,1,0:T(8,128)(2,1)S(1)} %copy-done.4, f32[3,128,320]{1,2,0:T(8,128)} %get-tuple-element.33, f32[320]{0:T(512)S(1)} %sub.44, f32[320]{0:T(512)S(1)} %mul.163), kind=kLoop, calls=%fused_computation.76 | loop fusion | flops 1351680 | bytes 989696 | tf_op jit(solution)/shard_map/broadcast_in_dim | solution.py:183
  98.7 7.6 %collective-permute-done.15 = bf16[360,320]{0,1:T(8,128)(2,1)S(1)} collective-permute-done((bf16[360,320]{0,1:T(8,128)(2,1)S(1)}, bf16[360,320]{0,1:T(8,128)(2,1)S(1)}, u32[]{:S(2)}, u32[]{:S(2)}) %collective-permute-start.15) | collective-permute-done | bytes 230432 | tf_op jit(solution)/shard_map/ppermute | solution.py:93
  106.3 2.3 %fusion.35 = (f32[360,320]{0,1:T(8,128)}, f32[360,320]{0,1:T(8,128)}) fusion(f32[360,320]{0,1:T(8,128)S(1)} %copy-done.7, f32[360,320]{0,1:T(8,128)} %param.14, bf16[360,320]{0,1:T(8,128)(2,1)S(1)} %collective-permute-done.15, bf16[360,320]{0,1:T(8,128)(2,1)S(1)} %convert_add_fusion.1), kind=kLoop, calls=%fused_computation.41 | loop fusion | flops 1612800 | bytes 2304000 | tf_op jit(solution)/shard_map/div | solution.py:182
  (100 shorter events, 21.3 us)
Async XLA Ops:
  7.2 37.2 %all-gather.3.cloned.1.call-start = ((), (), s32[]{:S(2)}) async-start(), calls=%async_computation | async-start | bytes 2211840 | tf_op jit(solution)/shard_map/all_gather | solution.py:124
  10.2 6.4 %collective-permute-start.2 = (f32[2,32]{1,0:T(2,128)S(1)}, f32[2,32]{1,0:T(2,128)S(1)}, u32[]{:S(2)}, u32[]{:S(2)}) collective-permute-start(f32[2,32]{1,0:T(2,128)S(1)} %pad_maximum_fusion.2), channel_id=1, source_target_pairs={{0,24},{8,0},{16,8},{24,16},{1,25},{9,1},{17,9},{25,17},{2,26},{10... | collective-permute-start | bytes 776 | tf_op jit(solution)/shard_map/ppermute | solution.py:33
  15.3 4.5 %collective-permute-start.1 = (f32[2,32]{1,0:T(2,128)S(1)}, f32[2,32]{1,0:T(2,128)S(1)}, u32[]{:S(2)}, u32[]{:S(2)}) collective-permute-start(f32[2,32]{1,0:T(2,128)S(1)} %pad_maximum_fusion.2), channel_id=1, source_target_pairs={{0,16},{8,24},{16,0},{24,8},{1,17},{9,25},{17,1},{25,9},{2,18},{10... | collective-permute-start | bytes 776 | tf_op jit(solution)/shard_map/ppermute | solution.py:33
  15.3 5.4 %collective-permute-start = (f32[2,32]{1,0:T(2,128)S(1)}, f32[2,32]{1,0:T(2,128)S(1)}, u32[]{:S(2)}, u32[]{:S(2)}) collective-permute-start(f32[2,32]{1,0:T(2,128)S(1)} %pad_maximum_fusion.2), channel_id=1, source_target_pairs={{0,8},{8,16},{16,24},{24,0},{1,9},{9,17},{17,25},{25,1},{2,10},{10... | collective-permute-start | bytes 776 | tf_op jit(solution)/shard_map/ppermute | solution.py:33
  21.1 10.0 %copy-start.3 = (bf16[1,3,128,320]{2,3,1,0:T(8,128)(2,1)S(1)}, bf16[1,3,128,320]{2,3,1,0:T(8,128)(2,1)}, u32[]{:S(2)}) copy-start(bf16[1,3,128,320]{2,3,1,0:T(8,128)(2,1)} %param.9) | copy-start | bytes 737284
  21.1 10.0 %copy-start.9 = (f32[320]{0:T(512)S(1)}, f32[320]{0:T(512)}, u32[]{:S(2)}) copy-start(f32[320]{0:T(512)} %param.12) | copy-start | bytes 3844
  21.1 10.0 %copy-start.10 = (f32[320]{0:T(512)S(1)}, f32[320]{0:T(512)}, u32[]{:S(2)}) copy-start(f32[320]{0:T(512)} %param.11) | copy-start | bytes 3844
  22.5 6.9 %collective-permute-start.4 = (bf16[1,128,320]{1,2,0:T(8,128)(2,1)S(1)}, bf16[1,128,320]{1,2,0:T(8,128)(2,1)S(1)}, u32[]{:S(2)}, u32[]{:S(2)}) collective-permute-start(bf16[1,128,320]{1,2,0:T(8,128)(2,1)S(1)} %get-tuple-element.28), channel_id=1, source_target_pairs={{8,0},{16,8},{24,16},{9,1},{17,9},{25,17},{10,2},{18,10},{26,18},{... | collective-permute-start | bytes 245768 | tf_op jit(solution)/shard_map/ppermute | solution.py:20
  23.8 6.6 %collective-permute-start.3 = (bf16[1,128,320]{1,2,0:T(8,128)(2,1)S(1)}, bf16[1,128,320]{1,2,0:T(8,128)(2,1)S(1)}, u32[]{:S(2)}, u32[]{:S(2)}) collective-permute-start(bf16[1,128,320]{1,2,0:T(8,128)(2,1)S(1)} %get-tuple-element.27), channel_id=1, source_target_pairs={{0,8},{8,16},{16,24},{1,9},{9,17},{17,25},{2,10},{10,18},{18,26},{... | collective-permute-start | bytes 245768 | tf_op jit(solution)/shard_map/ppermute | solution.py:18
  29.3 2.6 %copy-start.5 = (bf16[3,128,320]{1,2,0:T(8,128)(2,1)}, bf16[3,128,320]{1,2,0:T(8,128)(2,1)S(1)}, u32[]{:S(2)}) copy-start(bf16[3,128,320]{1,2,0:T(8,128)(2,1)S(1)} %bitcast_multiply_fusion) | copy-start | bytes 737284
  36.3 2.6 %collective-permute-start.5 = (bf16[4,360,320]{1,2,0:T(8,128)(2,1)S(1)}, bf16[4,360,320]{1,2,0:T(8,128)(2,1)S(1)}, u32[]{:S(2)}, u32[]{:S(2)}) collective-permute-start(bf16[4,360,320]{1,2,0:T(8,128)(2,1)S(1)} %copy.48), channel_id=1, source_target_pairs={{0,1},{1,0},{2,3},{3,2},{4,5},{5,4},{6,7},{7,6},{8,9},{9,8},{10,11... | collective-permute-start | bytes 2764808 | tf_op jit(solution)/shard_map/ppermute | solution.py:65
  49.1 18.1 %copy-start.6 = (bf16[3,128,320]{1,2,0:T(8,128)(2,1)S(1)}, bf16[3,128,320]{1,2,0:T(8,128)(2,1)}, u32[]{:S(2)}) copy-start(bf16[3,128,320]{1,2,0:T(8,128)(2,1)} %copy-done.5) | copy-start | bytes 737284
  50.0 9.9 %collective-permute-start.8 = (bf16[360,320]{0,1:T(8,128)(2,1)}, bf16[360,320]{0,1:T(8,128)(2,1)S(1)}, u32[]{:S(2)}, u32[]{:S(2)}) collective-permute-start(bf16[360,320]{0,1:T(8,128)(2,1)} %get-tuple-element.23), channel_id=1, source_target_pairs={{0,6},{1,7},{2,4},{3,5},{4,2},{5,3},{6,0},{7,1},{8,14},{9,15},{10,... | collective-permute-start | bytes 691208 | tf_op jit(solution)/shard_map/ppermute | solution.py:80
  51.5 13.0 %collective-permute-start.7 = (bf16[360,320]{0,1:T(8,128)(2,1)}, bf16[360,320]{0,1:T(8,128)(2,1)S(1)}, u32[]{:S(2)}, u32[]{:S(2)}) collective-permute-start(bf16[360,320]{0,1:T(8,128)(2,1)} %get-tuple-element.24), channel_id=1, source_target_pairs={{0,4},{1,5},{2,6},{3,7},{4,0},{5,1},{6,2},{7,3},{8,12},{9,13},{10,... | collective-permute-start | bytes 691208 | tf_op jit(solution)/shard_map/ppermute | solution.py:80
  53.0 11.6 %collective-permute-start.6 = (bf16[360,320]{0,1:T(8,128)(2,1)}, bf16[360,320]{0,1:T(8,128)(2,1)}, u32[]{:S(2)}, u32[]{:S(2)}) collective-permute-start(bf16[360,320]{0,1:T(8,128)(2,1)} %get-tuple-element.22), channel_id=1, source_target_pairs={{0,2},{1,3},{2,0},{3,1},{4,6},{5,7},{6,4},{7,5},{8,10},{9,11},{10,... | collective-permute-start | bytes 691208 | tf_op jit(solution)/shard_map/ppermute | solution.py:80
  65.7 10.1 %collective-permute-start.9 = (bf16[360,320]{0,1:T(8,128)(2,1)S(1)}, bf16[360,320]{0,1:T(8,128)(2,1)S(1)}, u32[]{:S(2)}, u32[]{:S(2)}) collective-permute-start(bf16[360,320]{0,1:T(8,128)(2,1)S(1)} %fusion.38), channel_id=1, source_target_pairs={{0,8},{8,0},{16,24},{24,16},{1,9},{9,1},{17,25},{25,17},{2,10},{10... | collective-permute-start | bytes 691208 | tf_op jit(solution)/shard_map/ppermute | solution.py:93
  67.2 8.2 %collective-permute-start.11 = (bf16[1,128,320]{1,2,0:T(8,128)(2,1)S(1)}, bf16[1,128,320]{1,2,0:T(8,128)(2,1)S(1)}, u32[]{:S(2)}, u32[]{:S(2)}) collective-permute-start(bf16[1,128,320]{1,2,0:T(8,128)(2,1)S(1)} %get-tuple-element.26), channel_id=1, source_target_pairs={{8,0},{16,8},{24,16},{9,1},{17,9},{25,17},{10,2},{18,10},{26,18},{... | collective-permute-start | bytes 245768 | tf_op jit(solution)/shard_map/ppermute | solution.py:20
  68.5 6.9 %collective-permute-start.10 = (bf16[1,128,320]{1,2,0:T(8,128)(2,1)S(1)}, bf16[1,128,320]{1,2,0:T(8,128)(2,1)S(1)}, u32[]{:S(2)}, u32[]{:S(2)}) collective-permute-start(bf16[1,128,320]{1,2,0:T(8,128)(2,1)S(1)} %get-tuple-element.25), channel_id=1, source_target_pairs={{0,8},{8,16},{16,24},{1,9},{9,17},{17,25},{2,10},{10,18},{18,26},{... | collective-permute-start | bytes 245768 | tf_op jit(solution)/shard_map/ppermute | solution.py:18
  75.9 2.6 %copy-start.1 = (bf16[8,360,320]{2,1,0:T(8,128)(2,1)S(1)}, bf16[8,360,320]{2,1,0:T(8,128)(2,1)}, u32[]{:S(2)}) copy-start(bf16[8,360,320]{2,1,0:T(8,128)(2,1)} %copy.52) | copy-start | bytes 5529604
  85.8 20.4 %copy-start.7 = (f32[360,320]{0,1:T(8,128)S(1)}, f32[360,320]{0,1:T(8,128)}, u32[]{:S(2)}) copy-start(f32[360,320]{0,1:T(8,128)} %param.15) | copy-start | bytes 1382404
  85.8 10.4 %collective-permute-start.14 = (f32[2,32]{1,0:T(2,128)S(1)}, f32[2,32]{1,0:T(2,128)S(1)}, u32[]{:S(2)}, u32[]{:S(2)}) collective-permute-start(f32[2,32]{1,0:T(2,128)S(1)} %pad_maximum_fusion.3), channel_id=1, source_target_pairs={{0,24},{8,0},{16,8},{24,16},{1,25},{9,1},{17,9},{25,17},{2,26},{10... | collective-permute-start | bytes 776 | tf_op jit(solution)/shard_map/ppermute | solution.py:33
  89.8 6.5 %collective-permute-start.13 = (f32[2,32]{1,0:T(2,128)S(1)}, f32[2,32]{1,0:T(2,128)S(1)}, u32[]{:S(2)}, u32[]{:S(2)}) collective-permute-start(f32[2,32]{1,0:T(2,128)S(1)} %pad_maximum_fusion.3), channel_id=1, source_target_pairs={{0,16},{8,24},{16,0},{24,8},{1,17},{9,25},{17,1},{25,9},{2,18},{10... | collective-permute-start | bytes 776 | tf_op jit(solution)/shard_map/ppermute | solution.py:33
  89.8 6.5 %collective-permute-start.12 = (f32[2,32]{1,0:T(2,128)S(1)}, f32[2,32]{1,0:T(2,128)S(1)}, u32[]{:S(2)}, u32[]{:S(2)}) collective-permute-start(f32[2,32]{1,0:T(2,128)S(1)} %pad_maximum_fusion.3), channel_id=1, source_target_pairs={{0,8},{8,16},{16,24},{24,0},{1,9},{9,17},{17,25},{25,1},{2,10},{10... | collective-permute-start | bytes 776 | tf_op jit(solution)/shard_map/ppermute | solution.py:33
  94.0 12.3 %collective-permute-start.15 = (bf16[360,320]{0,1:T(8,128)(2,1)S(1)}, bf16[360,320]{0,1:T(8,128)(2,1)S(1)}, u32[]{:S(2)}, u32[]{:S(2)}) collective-permute-start(bf16[360,320]{0,1:T(8,128)(2,1)S(1)} %convert_add_fusion.1), channel_id=1, source_target_pairs={{0,16},{8,24},{16,0},{24,8},{1,17},{9,25},{17,1},{25,9},{2,18},{10... | collective-permute-start | bytes 691208 | tf_op jit(solution)/shard_map/ppermute | solution.py:93
  (4 other events, 7.4 us)
Sparse Core Ops, SparseCore 0:
  16.5 27.7 all-gather.2

commit v11 on v9

--- a/solution.py
+++ b/solution.py
@@ -146,6 +146,7 @@
         act_cols, flat_cot, (((0,), (0,)), ((), ())), preferred_element_type=jnp.float32
     )
     weight_terms = row_major(weight_terms)
+    weight_terms, cot_pad = lax.optimization_barrier((weight_terms, cot_pad))
     grad_piece, companions = halving_scatter(weight_terms, "dp", (gathered, cot_pad))
     grad_piece, (gathered, cot_pad) = replicated_sum(grad_piece, "space", companions)
     output = jnp.dot(act_cols, gathered, preferred_element_type=jnp.float32)

time: 111 us -> 115 us (1.036)
  local copies, waits for them, and re-layouts: 16.4 us -> 21.6 us
  starting transfers between devices: 29.7 us -> 26.6 us
  waiting for transfers between devices: 26.9 us -> 28.2 us
    ppermute x2, waiting for transfers between devices: 7.78 us -> 14.7 us  [replicated_sum(): lax.ppermute(mine, axis, pairs).astype(jnp.float32)]
    ppermute x6, waiting for transfers between devices: 4.33 us -> 0.02 us  [space_sum(): lax.ppermute(joined, axis, [(i, (i + shift) % count) for i in range(count)])]
    ppermute x3, waiting for transfers between devices: 9.13 us -> 6.32 us  [halving_scatter(): lax.ppermute(send.astype(jnp.bfloat16), axis, pairs).astype(jnp.float32)]
    ppermute x2, waiting for transfers between devices: 2.1 us -> 4.47 us  [with_halo(): lax.ppermute(head, axis, [((i + 1) % count, i) for i in range(ends)])]
    ppermute x2, starting transfers between devices: 4.44 us -> 2.27 us  [replicated_sum(): lax.ppermute(mine, axis, pairs).astype(jnp.float32)]
    ppermute x2, starting transfers between devices: 9.1 us -> 7.14 us  [with_halo(): lax.ppermute(tail, axis, [(i, (i + 1) % count) for i in range(ends)])]
    unnamed x36 -> x46, local copies, waits for them, and re-layouts: 7.58 us -> 9.51 us
    dynamic_slice x2, local copies, waits for them, and re-layouts: 0.25 us -> 2.11 us  [halving_scatter(): total = lax.dynamic_index_in_dim(held, own, keepdims=False)]
  transfers between devices with their start and end apart: 17 -> 17, of which waited for: 10 -> 7; matrix products, arithmetic and copies ran while one was open for 18% -> 22% of each run, Pallas kernels for 0% -> 0%
where the time goes in v11:
time: 115 us
  waiting for transfers between devices  28.2 us (25%)
  starting transfers between devices  26.6 us (23%)
  local copies, waits for them, and re-layouts  21.6 us (19%)
  between operations  15.9 us (14%)
  other arithmetic  12.8 us (11%)
  matrix products  9.45 us (8%)
    ppermute x2, waiting for transfers between devices, replicated_sum(): lax.ppermute(mine, axis, pairs).astype(jnp.float32)  14.7 us
    ppermute x6, starting transfers between devices, space_sum(): lax.ppermute(joined, axis, [(i, (i + shift) % count) for i in range(count)])  10.9 us
    unnamed x46, local copies, waits for them, and re-layouts  9.51 us
    ppermute x2, starting transfers between devices, with_halo(): lax.ppermute(tail, axis, [(i, (i + 1) % count) for i in range(ends)])  7.14 us
    ppermute x3, waiting for transfers between devices, halving_scatter(): lax.ppermute(send.astype(jnp.bfloat16), axis, pairs).astype(jnp.float32)  6.32 us
    ppermute x2, waiting for transfers between devices, with_halo(): lax.ppermute(head, axis, [((i + 1) % count, i) for i in range(ends)])  4.47 us
    dot_general x1, matrix products, local(): upstream = jnp.dot(cot_cols, flipped, preferred_element_type=jnp.float32)  4.4 us
    dot_general x1, matrix products, local(): output = jnp.dot(act_cols, gathered, preferred_element_type=jnp.float32)  3.53 us
  transfers between devices with their start and end apart: 17, of which 7 were waited for; matrix products, arithmetic and copies ran while one was open for 22% of the time, Pallas kernels for 0%

profile of v11, /device:TPU:0, one launch (start us, length us, event | category | flops | bytes accessed | tf_op | source)
XLA Modules:
  0.0 114.7 jit_solution(2758234953735324309)
XLA Ops:
  10.2 3.1 %collective-permute-start = (f32[2,32]{1,0:T(2,128)S(1)}, f32[2,32]{1,0:T(2,128)S(1)}, u32[]{:S(2)}, u32[]{:S(2)}) collective-permute-start(f32[2,32]{1,0:T(2,128)S(1)} %pad_maximum_fusion.2), channel_id=1, source_target_pairs={{0,8},{8,16},{16,24},{24,0},{1,9},{9,17},{17,25},{25,1},{2,10},{10... | collective-permute-start | bytes 776 | tf_op jit(solution)/shard_map/ppermute | solution.py:33
  13.3 2.6 %collective-permute-start.1 = (f32[2,32]{1,0:T(2,128)S(1)}, f32[2,32]{1,0:T(2,128)S(1)}, u32[]{:S(2)}, u32[]{:S(2)}) collective-permute-start(f32[2,32]{1,0:T(2,128)S(1)} %pad_maximum_fusion.2), channel_id=1, source_target_pairs={{0,16},{8,24},{16,0},{24,8},{1,17},{9,25},{17,1},{25,9},{2,18},{10... | collective-permute-start | bytes 776 | tf_op jit(solution)/shard_map/ppermute | solution.py:33
  18.2 2.6 %collective-permute-start.5 = (bf16[1,128,320]{1,2,0:T(8,128)(2,1)S(1)}, bf16[1,128,320]{1,2,0:T(8,128)(2,1)S(1)}, u32[]{:S(2)}, u32[]{:S(2)}) collective-permute-start(bf16[1,128,320]{1,2,0:T(8,128)(2,1)S(1)} %get-tuple-element.25), channel_id=1, source_target_pairs={{0,8},{8,16},{16,24},{1,9},{9,17},{17,25},{2,10},{10,18},{18,26},{... | collective-permute-start | bytes 245768 | tf_op jit(solution)/shard_map/ppermute | solution.py:18
  23.9 4.6 %collective-permute-start.3 = (bf16[1,128,320]{1,2,0:T(8,128)(2,1)S(1)}, bf16[1,128,320]{1,2,0:T(8,128)(2,1)S(1)}, u32[]{:S(2)}, u32[]{:S(2)}) collective-permute-start(bf16[1,128,320]{1,2,0:T(8,128)(2,1)S(1)} %get-tuple-element.27), channel_id=1, source_target_pairs={{0,8},{8,16},{16,24},{1,9},{9,17},{17,25},{2,10},{10,18},{18,26},{... | collective-permute-start | bytes 245768 | tf_op jit(solution)/shard_map/ppermute | solution.py:18
  30.5 4.5 %collective-permute-done.4 = bf16[1,128,320]{1,2,0:T(8,128)(2,1)S(1)} collective-permute-done((bf16[1,128,320]{1,2,0:T(8,128)(2,1)S(1)}, bf16[1,128,320]{1,2,0:T(8,128)(2,1)S(1)}, u32[]{:S(2)}, u32[]{:S(2)}) %collective-permute-start.4) | collective-permute-done | bytes 81952 | tf_op jit(solution)/shard_map/ppermute | solution.py:20
  36.6 1.5 %convolution_bitcast_fusion = f32[2880,320]{1,0:T(8,128)S(1)} fusion(bf16[3,128,2880]{1,2,0:T(8,128)(2,1)S(1)} %slice_dynamic-update-slice_fusion, bf16[3,128,320]{1,2,0:T(8,128)(2,1)S(1)} %bitcast_multiply_fusion), kind=kOutput, calls=%fused_computation | convolution fusion | flops 707788800 | bytes 6144000 | tf_op jit(solution)/shard_map/dot_general | solution.py:145
  38.1 2.0 %copy-done = f32[2880,320]{1,0:T(8,128)} copy-done((f32[2880,320]{1,0:T(8,128)}, f32[2880,320]{1,0:T(8,128)S(1)}, u32[]{:S(2)}) %copy-start) | copy-done | bytes 3686424
  41.1 2.5 %collective-permute-done.7 = bf16[4,360,320]{1,2,0:T(8,128)(2,1)S(1)} collective-permute-done((bf16[4,360,320]{1,2,0:T(8,128)(2,1)S(1)}, bf16[4,360,320]{1,2,0:T(8,128)(2,1)S(1)}, u32[]{:S(2)}, u32[]{:S(2)}) %collective-permute-start.7) | collective-permute-done | bytes 921632 | tf_op jit(solution)/shard_map/ppermute | solution.py:65
  45.0 2.2 %bitcast_add_fusion = f32[4,360,320]{2,1,0:T(8,128)S(1)} fusion(bf16[4,360,320]{2,1,0:T(8,128)(2,1)} %copy.49, f32[4,2,360,320]{3,2,1,0:T(8,128)} %bitcast.116, s32[]{:T(128)S(6)} %select_n.33), kind=kLoop, calls=%fused_computation.4 | loop fusion | flops 921600 | bytes 4608004 | tf_op jit(solution)/shard_map/add | solution.py:66
  48.1 1.8 %copy.69 = bf16[1,360,320]{1,2,0:T(8,128)(2,1)} copy(bf16[1,360,320]{2,1,0:T(8,128)(2,1)} %get-tuple-element.24) | data formatting | bytes 460800
  49.9 2.5 %collective-permute-start.10 = (bf16[360,320]{0,1:T(8,128)(2,1)}, bf16[360,320]{0,1:T(8,128)(2,1)}, u32[]{:S(2)}, u32[]{:S(2)}) collective-permute-start(bf16[360,320]{0,1:T(8,128)(2,1)} %bitcast.121), channel_id=1, source_target_pairs={{0,6},{1,7},{2,4},{3,5},{4,2},{5,3},{6,0},{7,1},{8,14},{9,15},{10,... | collective-permute-start | bytes 691208 | tf_op jit(solution)/shard_map/ppermute | solution.py:78
  52.4 1.8 %copy.67 = bf16[1,360,320]{1,2,0:T(8,128)(2,1)} copy(bf16[1,360,320]{2,1,0:T(8,128)(2,1)} %get-tuple-element.22) | data formatting | bytes 460800
  58.2 1.8 %collective-permute-done.10 = bf16[360,320]{0,1:T(8,128)(2,1)} collective-permute-done((bf16[360,320]{0,1:T(8,128)(2,1)}, bf16[360,320]{0,1:T(8,128)(2,1)}, u32[]{:S(2)}, u32[]{:S(2)}) %collective-permute-start.10) | collective-permute-done | bytes 230432 | tf_op jit(solution)/shard_map/ppermute | solution.py:78
  59.9 4.6 %collective-permute-done.8 = bf16[360,320]{0,1:T(8,128)(2,1)} collective-permute-done((bf16[360,320]{0,1:T(8,128)(2,1)}, bf16[360,320]{0,1:T(8,128)(2,1)}, u32[]{:S(2)}, u32[]{:S(2)}) %collective-permute-start.8) | collective-permute-done | bytes 230432 | tf_op jit(solution)/shard_map/ppermute | solution.py:78
  65.9 7.1 %collective-permute-done.11 = bf16[360,320]{0,1:T(8,128)(2,1)S(1)} collective-permute-done((bf16[360,320]{0,1:T(8,128)(2,1)S(1)}, bf16[360,320]{0,1:T(8,128)(2,1)S(1)}, u32[]{:S(2)}, u32[]{:S(2)}) %collective-permute-start.11) | collective-permute-done | bytes 230432 | tf_op jit(solution)/shard_map/ppermute | solution.py:91
  73.1 3.0 %copy.56 = bf16[8,360,320]{2,1,0:T(8,128)(2,1)S(1)} copy(bf16[8,360,320]{1,2,0:T(8,128)(2,1)} %all-gather.3.cloned.1.call-done) | data formatting | bytes 3686400 | tf_op jit(solution)/shard_map/all_gather | solution.py:122
  78.8 2.5 %copy.58 = bf16[9,320,320]{1,2,0:T(8,128)(2,1)} copy(bf16[9,320,320]{2,1,0:T(8,128)(2,1)S(1)} %bitcast.117) | data formatting | bytes 3686400 | tf_op jit(solution)/shard_map/reshape | solution.py:154
  81.3 4.4 %fusion.45 = (f32[320]{0:T(512)S(1)}, f32[320]{0:T(512)S(1)}, f32[3,128,320]{1,2,0:T(8,128)}) fusion(f32[320]{0:T(512)S(1)} %copy-done.7, f32[320]{0:T(512)S(1)} %copy-done.9, f32[3,128]{1,0:T(4,128)S(1)} %copy-done.5, bf16[1,3,128,320]{2,3,1,0:T(8,128)(2,1)S(1)} %copy-done.2, f32[320]{0:T(512)S(1)} %copy-done.12, f32[320]{0:T(512)S(1)} %copy-done.14, ...), kind=kOutput, calls=%fused_computation.94 | convolution fusion | flops 710245760 | bytes 4801536 | tf_op jit(solution)/shard_map/dot_general | solution.py:164
  86.8 3.3 %collective-permute-start.14 = (f32[2,32]{1,0:T(2,128)S(1)}, f32[2,32]{1,0:T(2,128)S(1)}, u32[]{:S(2)}, u32[]{:S(2)}) collective-permute-start(f32[2,32]{1,0:T(2,128)S(1)} %pad_maximum_fusion.3), channel_id=1, source_target_pairs={{0,24},{8,0},{16,8},{24,16},{1,25},{9,1},{17,9},{25,17},{2,26},{10... | collective-permute-start | bytes 776 | tf_op jit(solution)/shard_map/ppermute | solution.py:33
  90.0 3.5 %fusion.11 = bf16[1,3,128,320]{2,3,1,0:T(8,128)(2,1)} fusion(bf16[3,128,2880]{1,2,0:T(8,128)(2,1)} %copy-done.1, bf16[2880,320]{1,0:T(8,128)(2,1)S(1)} %bitcast.118, f32[3,128]{1,0:T(4,128)S(1)} %copy-done.5), kind=kOutput, calls=%fused_computation.13 | convolution fusion | flops 708034560 | bytes 4302336 | tf_op jit(solution)/shard_map/dot_general | solution.py:152
  93.6 2.0 %collective-permute-start.15 = (bf16[360,320]{0,1:T(8,128)(2,1)S(1)}, bf16[360,320]{0,1:T(8,128)(2,1)S(1)}, u32[]{:S(2)}, u32[]{:S(2)}) collective-permute-start(bf16[360,320]{0,1:T(8,128)(2,1)S(1)} %convert_add_fusion.1), channel_id=1, source_target_pairs={{0,16},{8,24},{16,0},{24,8},{1,17},{9,25},{17,1},{25,9},{2,18},{10... | collective-permute-start | bytes 691208 | tf_op jit(solution)/shard_map/ppermute | solution.py:91
  96.0 2.0 %fusion.41 = bf16[1,3,128,320]{2,3,1,0:T(8,128)(2,1)} fusion(f32[320]{0:T(512)S(1)} %mul.180, f32[320]{0:T(512)S(1)} %copy-done.9, f32[3,128]{1,0:T(4,128)S(1)} %copy-done.5, bf16[1,3,128,320]{2,3,1,0:T(8,128)(2,1)S(1)} %copy-done.2, f32[3,128,320]{1,2,0:T(8,128)} %get-tuple-element.33, f32[320]{0:T(512)S(1)} %sub.44, f32[320]{0:T(512)S(1)} %copy-done.7), kind=kLoop, calls=%fused_computation.74 | loop fusion | flops 1351680 | bytes 989696 | tf_op jit(solution)/shard_map/broadcast_in_dim | solution.py:182
  98.0 7.6 %collective-permute-done.15 = bf16[360,320]{0,1:T(8,128)(2,1)S(1)} collective-permute-done((bf16[360,320]{0,1:T(8,128)(2,1)S(1)}, bf16[360,320]{0,1:T(8,128)(2,1)S(1)}, u32[]{:S(2)}, u32[]{:S(2)}) %collective-permute-start.15) | collective-permute-done | bytes 230432 | tf_op jit(solution)/shard_map/ppermute | solution.py:91
  105.6 2.3 %fusion.35 = (f32[360,320]{0,1:T(8,128)}, f32[360,320]{0,1:T(8,128)}) fusion(f32[360,320]{0,1:T(8,128)S(1)} %copy-done.3, f32[360,320]{0,1:T(8,128)} %param.14, bf16[360,320]{0,1:T(8,128)(2,1)S(1)} %collective-permute-done.15, bf16[360,320]{0,1:T(8,128)(2,1)S(1)} %convert_add_fusion.1), kind=kLoop, calls=%fused_computation.42 | loop fusion | flops 1612800 | bytes 2304000 | tf_op jit(solution)/shard_map/div | solution.py:181
  (110 shorter events, 23.2 us)
Async XLA Ops:
  7.2 66.0 %all-gather.3.cloned.1.call-start = ((), (), s32[]{:S(2)}) async-start(), calls=%async_computation | async-start | bytes 2211840 | tf_op jit(solution)/shard_map/all_gather | solution.py:122
  8.6 27.1 %copy-start.4 = (f32[3,128]{1,0:T(4,128)}, f32[3,128]{1,0:T(4,128)S(1)}, u32[]{:S(2)}) copy-start(f32[3,128]{1,0:T(4,128)S(1)} %get-tuple-element.32) | copy-start | bytes 4612
  10.2 11.9 %collective-permute-start = (f32[2,32]{1,0:T(2,128)S(1)}, f32[2,32]{1,0:T(2,128)S(1)}, u32[]{:S(2)}, u32[]{:S(2)}) collective-permute-start(f32[2,32]{1,0:T(2,128)S(1)} %pad_maximum_fusion.2), channel_id=1, source_target_pairs={{0,8},{8,16},{16,24},{24,0},{1,9},{9,17},{17,25},{25,1},{2,10},{10... | collective-permute-start | bytes 776 | tf_op jit(solution)/shard_map/ppermute | solution.py:33
  13.3 8.9 %collective-permute-start.1 = (f32[2,32]{1,0:T(2,128)S(1)}, f32[2,32]{1,0:T(2,128)S(1)}, u32[]{:S(2)}, u32[]{:S(2)}) collective-permute-start(f32[2,32]{1,0:T(2,128)S(1)} %pad_maximum_fusion.2), channel_id=1, source_target_pairs={{0,16},{8,24},{16,0},{24,8},{1,17},{9,25},{17,1},{25,9},{2,18},{10... | collective-permute-start | bytes 776 | tf_op jit(solution)/shard_map/ppermute | solution.py:33
  15.9 6.3 %collective-permute-start.2 = (f32[2,32]{1,0:T(2,128)S(1)}, f32[2,32]{1,0:T(2,128)S(1)}, u32[]{:S(2)}, u32[]{:S(2)}) collective-permute-start(f32[2,32]{1,0:T(2,128)S(1)} %pad_maximum_fusion.2), channel_id=1, source_target_pairs={{0,24},{8,0},{16,8},{24,16},{1,25},{9,1},{17,9},{25,17},{2,26},{10... | collective-permute-start | bytes 776 | tf_op jit(solution)/shard_map/ppermute | solution.py:33
  18.2 11.7 %collective-permute-start.5 = (bf16[1,128,320]{1,2,0:T(8,128)(2,1)S(1)}, bf16[1,128,320]{1,2,0:T(8,128)(2,1)S(1)}, u32[]{:S(2)}, u32[]{:S(2)}) collective-permute-start(bf16[1,128,320]{1,2,0:T(8,128)(2,1)S(1)} %get-tuple-element.25), channel_id=1, source_target_pairs={{0,8},{8,16},{16,24},{1,9},{9,17},{17,25},{2,10},{10,18},{18,26},{... | collective-permute-start | bytes 245768 | tf_op jit(solution)/shard_map/ppermute | solution.py:18
  20.8 9.1 %collective-permute-start.6 = (bf16[1,128,320]{1,2,0:T(8,128)(2,1)S(1)}, bf16[1,128,320]{1,2,0:T(8,128)(2,1)S(1)}, u32[]{:S(2)}, u32[]{:S(2)}) collective-permute-start(bf16[1,128,320]{1,2,0:T(8,128)(2,1)S(1)} %get-tuple-element.26), channel_id=1, source_target_pairs={{8,0},{16,8},{24,16},{9,1},{17,9},{25,17},{10,2},{18,10},{26,18},{... | collective-permute-start | bytes 245768 | tf_op jit(solution)/shard_map/ppermute | solution.py:20
  22.4 13.3 %copy-start.6 = (f32[320]{0:T(512)}, f32[320]{0:T(512)S(1)}, u32[]{:S(2)}) copy-start(f32[320]{0:T(512)S(1)} %mul.163) | copy-start | bytes 3844
  22.6 13.1 %copy-start.8 = (f32[320]{0:T(512)}, f32[320]{0:T(512)S(1)}, u32[]{:S(2)}) copy-start(f32[320]{0:T(512)S(1)} %sub.37) | copy-start | bytes 3844
  23.9 6.6 %collective-permute-start.3 = (bf16[1,128,320]{1,2,0:T(8,128)(2,1)S(1)}, bf16[1,128,320]{1,2,0:T(8,128)(2,1)S(1)}, u32[]{:S(2)}, u32[]{:S(2)}) collective-permute-start(bf16[1,128,320]{1,2,0:T(8,128)(2,1)S(1)} %get-tuple-element.27), channel_id=1, source_target_pairs={{0,8},{8,16},{16,24},{1,9},{9,17},{17,25},{2,10},{10,18},{18,26},{... | collective-permute-start | bytes 245768 | tf_op jit(solution)/shard_map/ppermute | solution.py:18
  28.5 7.3 %copy-start.2 = (bf16[1,3,128,320]{2,3,1,0:T(8,128)(2,1)S(1)}, bf16[1,3,128,320]{2,3,1,0:T(8,128)(2,1)}, u32[]{:S(2)}) copy-start(bf16[1,3,128,320]{2,3,1,0:T(8,128)(2,1)} %param.9) | copy-start | bytes 737284
  28.5 7.3 %copy-start.11 = (f32[320]{0:T(512)S(1)}, f32[320]{0:T(512)}, u32[]{:S(2)}) copy-start(f32[320]{0:T(512)} %param.12) | copy-start | bytes 3844
  28.5 7.3 %copy-start.13 = (f32[320]{0:T(512)S(1)}, f32[320]{0:T(512)}, u32[]{:S(2)}) copy-start(f32[320]{0:T(512)} %param.11) | copy-start | bytes 3844
  28.5 6.5 %collective-permute-start.4 = (bf16[1,128,320]{1,2,0:T(8,128)(2,1)S(1)}, bf16[1,128,320]{1,2,0:T(8,128)(2,1)S(1)}, u32[]{:S(2)}, u32[]{:S(2)}) collective-permute-start(bf16[1,128,320]{1,2,0:T(8,128)(2,1)S(1)} %get-tuple-element.28), channel_id=1, source_target_pairs={{8,0},{16,8},{24,16},{9,1},{17,9},{25,17},{10,2},{18,10},{26,18},{... | collective-permute-start | bytes 245768 | tf_op jit(solution)/shard_map/ppermute | solution.py:20
  41.0 2.6 %collective-permute-start.7 = (bf16[4,360,320]{1,2,0:T(8,128)(2,1)S(1)}, bf16[4,360,320]{1,2,0:T(8,128)(2,1)S(1)}, u32[]{:S(2)}, u32[]{:S(2)}) collective-permute-start(bf16[4,360,320]{1,2,0:T(8,128)(2,1)S(1)} %copy.48), channel_id=1, source_target_pairs={{0,1},{1,0},{2,3},{3,2},{4,5},{5,4},{6,7},{7,6},{8,9},{9,8},{10,11... | collective-permute-start | bytes 2764808 | tf_op jit(solution)/shard_map/ppermute | solution.py:65
  49.9 10.0 %collective-permute-start.10 = (bf16[360,320]{0,1:T(8,128)(2,1)}, bf16[360,320]{0,1:T(8,128)(2,1)}, u32[]{:S(2)}, u32[]{:S(2)}) collective-permute-start(bf16[360,320]{0,1:T(8,128)(2,1)} %bitcast.121), channel_id=1, source_target_pairs={{0,6},{1,7},{2,4},{3,5},{4,2},{5,3},{6,0},{7,1},{8,14},{9,15},{10,... | collective-permute-start | bytes 691208 | tf_op jit(solution)/shard_map/ppermute | solution.py:78
  54.2 10.3 %collective-permute-start.8 = (bf16[360,320]{0,1:T(8,128)(2,1)}, bf16[360,320]{0,1:T(8,128)(2,1)}, u32[]{:S(2)}, u32[]{:S(2)}) collective-permute-start(bf16[360,320]{0,1:T(8,128)(2,1)} %bitcast.122), channel_id=1, source_target_pairs={{0,2},{1,3},{2,0},{3,1},{4,6},{5,7},{6,4},{7,5},{8,10},{9,11},{10,... | collective-permute-start | bytes 691208 | tf_op jit(solution)/shard_map/ppermute | solution.py:78
  55.6 8.9 %collective-permute-start.9 = (bf16[360,320]{0,1:T(8,128)(2,1)}, bf16[360,320]{0,1:T(8,128)(2,1)S(1)}, u32[]{:S(2)}, u32[]{:S(2)}) collective-permute-start(bf16[360,320]{0,1:T(8,128)(2,1)} %bitcast.123), channel_id=1, source_target_pairs={{0,4},{1,5},{2,6},{3,7},{4,0},{5,1},{6,2},{7,3},{8,12},{9,13},{10,... | collective-permute-start | bytes 691208 | tf_op jit(solution)/shard_map/ppermute | solution.py:78
  65.7 7.4 %collective-permute-start.11 = (bf16[360,320]{0,1:T(8,128)(2,1)S(1)}, bf16[360,320]{0,1:T(8,128)(2,1)S(1)}, u32[]{:S(2)}, u32[]{:S(2)}) collective-permute-start(bf16[360,320]{0,1:T(8,128)(2,1)S(1)} %fusion.38), channel_id=1, source_target_pairs={{0,8},{8,0},{16,24},{24,16},{1,9},{9,1},{17,25},{25,17},{2,10},{10... | collective-permute-start | bytes 691208 | tf_op jit(solution)/shard_map/ppermute | solution.py:91
  86.1 19.4 %copy-start.3 = (f32[360,320]{0,1:T(8,128)S(1)}, f32[360,320]{0,1:T(8,128)}, u32[]{:S(2)}) copy-start(f32[360,320]{0,1:T(8,128)} %param.15) | copy-start | bytes 1382404
  86.2 9.4 %collective-permute-start.12 = (f32[2,32]{1,0:T(2,128)S(1)}, f32[2,32]{1,0:T(2,128)S(1)}, u32[]{:S(2)}, u32[]{:S(2)}) collective-permute-start(f32[2,32]{1,0:T(2,128)S(1)} %pad_maximum_fusion.3), channel_id=1, source_target_pairs={{0,8},{8,16},{16,24},{24,0},{1,9},{9,17},{17,25},{25,1},{2,10},{10... | collective-permute-start | bytes 776 | tf_op jit(solution)/shard_map/ppermute | solution.py:33
  86.5 9.1 %collective-permute-start.13 = (f32[2,32]{1,0:T(2,128)S(1)}, f32[2,32]{1,0:T(2,128)S(1)}, u32[]{:S(2)}, u32[]{:S(2)}) collective-permute-start(f32[2,32]{1,0:T(2,128)S(1)} %pad_maximum_fusion.3), channel_id=1, source_target_pairs={{0,16},{8,24},{16,0},{24,8},{1,17},{9,25},{17,1},{25,9},{2,18},{10... | collective-permute-start | bytes 776 | tf_op jit(solution)/shard_map/ppermute | solution.py:33
  86.8 8.8 %collective-permute-start.14 = (f32[2,32]{1,0:T(2,128)S(1)}, f32[2,32]{1,0:T(2,128)S(1)}, u32[]{:S(2)}, u32[]{:S(2)}) collective-permute-start(f32[2,32]{1,0:T(2,128)S(1)} %pad_maximum_fusion.3), channel_id=1, source_target_pairs={{0,24},{8,0},{16,8},{24,16},{1,25},{9,1},{17,9},{25,17},{2,26},{10... | collective-permute-start | bytes 776 | tf_op jit(solution)/shard_map/ppermute | solution.py:33
  93.6 12.0 %collective-permute-start.15 = (bf16[360,320]{0,1:T(8,128)(2,1)S(1)}, bf16[360,320]{0,1:T(8,128)(2,1)S(1)}, u32[]{:S(2)}, u32[]{:S(2)}) collective-permute-start(bf16[360,320]{0,1:T(8,128)(2,1)S(1)} %convert_add_fusion.1), channel_id=1, source_target_pairs={{0,16},{8,24},{16,0},{24,8},{1,17},{9,25},{17,1},{25,9},{2,18},{10... | collective-permute-start | bytes 691208 | tf_op jit(solution)/shard_map/ppermute | solution.py:91
  (8 other events, 17.5 us)
Sparse Core Ops, SparseCore 0:
  22.3 27.6 all-gather.2

commit v12 on v9

--- a/solution.py
+++ b/solution.py
@@ -167,7 +167,7 @@
     local_first = group_sum(scaled, GROUPS)
     local_second = group_sum(scaled * normed, GROUPS)
     sum_first, sum_second = space_sum((local_first, local_second), "space")
-    grad_piece = with_layout_constraint(grad_piece, Layout(major_to_minor=(1, 0)))
+    grad_piece = row_major(grad_piece)
     first = sum_first / cell_count
     second = sum_second / cell_count
     input_grad = (

time: 111 us -> 117 us (1.054)
  local copies, waits for them, and re-layouts: 16.4 us -> 19.6 us
  waiting for transfers between devices: 26.9 us -> 29.6 us
    ppermute x3, waiting for transfers between devices: 9.13 us -> 12.4 us  [halving_scatter(): lax.ppermute(send.astype(jnp.bfloat16), axis, pairs).astype(jnp.float32)]
    unnamed x36 -> x59, local copies, waits for them, and re-layouts: 7.58 us -> 10.3 us
    ppermute x2, waiting for transfers between devices: 2.1 us -> 0.01 us  [with_halo(): lax.ppermute(head, axis, [((i + 1) % count, i) for i in range(ends)])]
    ppermute x2, waiting for transfers between devices: 7.78 us -> 9.29 us  [replicated_sum(): lax.ppermute(mine, axis, pairs).astype(jnp.float32)]
  transfers between devices with their start and end apart: 17 -> 17, of which waited for: 10 -> 9; matrix products, arithmetic and copies ran while one was open for 18% -> 18% of each run, Pallas kernels for 0% -> 0%
where the time goes in v12:
time: 117 us; the launch traced here: 116 us
  waiting for transfers between devices  29.6 us (25%)
  starting transfers between devices  28.9 us (25%)
  local copies, waits for them, and re-layouts  19.6 us (17%)
  between operations  16 us (14%)
  other arithmetic  12.5 us (11%)
  matrix products  9.46 us (8%)
    ppermute x3, waiting for transfers between devices, halving_scatter(): lax.ppermute(send.astype(jnp.bfloat16), axis, pairs).astype(jnp.float32)  12.4 us
    unnamed x59, local copies, waits for them, and re-layouts  10.3 us
    ppermute x2, waiting for transfers between devices, replicated_sum(): lax.ppermute(mine, axis, pairs).astype(jnp.float32)  9.29 us
    ppermute x6, starting transfers between devices, space_sum(): lax.ppermute(joined, axis, [(i, (i + shift) % count) for i in range(count)])  9.2 us
    ppermute x2, starting transfers between devices, with_halo(): lax.ppermute(tail, axis, [(i, (i + 1) % count) for i in range(ends)])  9.1 us
    ppermute x2, starting transfers between devices, replicated_sum(): lax.ppermute(mine, axis, pairs).astype(jnp.float32)  4.46 us
    dot_general x1, matrix products, local(): upstream = jnp.dot(cot_cols, flipped, preferred_element_type=jnp.float32)  4.41 us
    ppermute x6, waiting for transfers between devices, space_sum(): lax.ppermute(joined, axis, [(i, (i + shift) % count) for i in range(count)])  4.33 us
  transfers between devices with their start and end apart: 17, of which 9 were waited for; matrix products, arithmetic and copies ran while one was open for 18% of the time, Pallas kernels for 0%

profile of v12, /device:TPU:0, one launch (start us, length us, event | category | flops | bytes accessed | tf_op | source)
XLA Modules:
  0.0 116.1 jit_solution(3264229359913313650)
XLA Ops:
  10.2 5.1 %collective-permute-start.2 = (f32[2,32]{1,0:T(2,128)S(1)}, f32[2,32]{1,0:T(2,128)S(1)}, u32[]{:S(2)}, u32[]{:S(2)}) collective-permute-start(f32[2,32]{1,0:T(2,128)S(1)} %pad_maximum_fusion.2), channel_id=1, source_target_pairs={{0,24},{8,0},{16,8},{24,16},{1,25},{9,1},{17,9},{25,17},{2,26},{10... | collective-permute-start | bytes 776 | tf_op jit(solution)/shard_map/ppermute | solution.py:33
  16.6 3.2 %collective-permute-done.1 = f32[2,32]{1,0:T(2,128)S(1)} collective-permute-done((f32[2,32]{1,0:T(2,128)S(1)}, f32[2,32]{1,0:T(2,128)S(1)}, u32[]{:S(2)}, u32[]{:S(2)}) %collective-permute-start.1) | collective-permute-done | bytes 288 | tf_op jit(solution)/shard_map/ppermute | solution.py:33
  21.1 1.3 %multiply_convert_fusion = bf16[3,128,320]{1,2,0:T(8,128)(2,1)S(1)} fusion(bf16[1,3,128,320]{2,3,1,0:T(8,128)(2,1)} %param.9, f32[320]{0:T(512)} %param.12, f32[320]{0:T(512)} %param.11, f32[320]{0:T(512)S(1)} %mul.163, f32[320]{0:T(512)S(1)} %sub.37, f32[3,128]{1,0:T(4,128)S(1)} %get-tuple-element.44), kind=kLoop, calls=%fused_computation.51 | loop fusion | flops 1597440 | bytes 498176 | tf_op jit(solution)/shard_map/convert_element_type | solution.py:132
  23.8 4.6 %collective-permute-start.3 = (bf16[1,128,320]{1,2,0:T(8,128)(2,1)S(1)}, bf16[1,128,320]{1,2,0:T(8,128)(2,1)S(1)}, u32[]{:S(2)}, u32[]{:S(2)}) collective-permute-start(bf16[1,128,320]{1,2,0:T(8,128)(2,1)S(1)} %get-tuple-element.39), channel_id=1, source_target_pairs={{0,8},{8,16},{16,24},{1,9},{9,17},{17,25},{2,10},{10,18},{18,26},{... | collective-permute-start | bytes 245768 | tf_op jit(solution)/shard_map/ppermute | solution.py:18
  32.0 1.5 %fusion.51 = f32[2880,320,1]{1,0,2:T(8,128)S(1)} fusion(bf16[3,128,2880]{1,2,0:T(8,128)(2,1)S(1)} %slice_dynamic-update-slice_fusion, bf16[3,128,320]{1,2,0:T(8,128)(2,1)S(1)} %bitcast_multiply_fusion), kind=kOutput, calls=%fused_computation.95 | convolution fusion | flops 707788800 | bytes 6144000 | tf_op jit(solution)/shard_map/dot_general | solution.py:145
  33.5 2.0 %copy-done = f32[2880,320,1]{1,0,2:T(8,128)} copy-done((f32[2880,320,1]{1,0,2:T(8,128)}, f32[2880,320,1]{1,0,2:T(8,128)S(1)}, u32[]{:S(2)}) %copy-start) | copy-done | bytes 3686424
  36.5 2.5 %collective-permute-done.5 = bf16[4,360,320]{1,2,0:T(8,128)(2,1)S(1)} collective-permute-done((bf16[4,360,320]{1,2,0:T(8,128)(2,1)S(1)}, bf16[4,360,320]{1,2,0:T(8,128)(2,1)S(1)}, u32[]{:S(2)}, u32[]{:S(2)}) %collective-permute-start.5) | collective-permute-done | bytes 921632 | tf_op jit(solution)/shard_map/ppermute | solution.py:65
  39.8 1.8 %bitcast_add_fusion = f32[4,360,320]{2,1,0:T(8,128)S(1)} fusion(bf16[4,360,320]{2,1,0:T(8,128)(2,1)S(1)} %copy.49, f32[4,2,360,320]{3,2,1,0:T(8,128)} %bitcast.113, s32[]{:T(128)S(6)} %select_n.33), kind=kLoop, calls=%fused_computation.3 | loop fusion | flops 921600 | bytes 4608004 | tf_op jit(solution)/shard_map/add | solution.py:66
  42.6 2.4 %collective-permute-start.8 = (bf16[360,320]{1,0:T(8,128)(2,1)}, bf16[360,320]{1,0:T(8,128)(2,1)S(1)}, u32[]{:S(2)}, u32[]{:S(2)}) collective-permute-start(bf16[360,320]{1,0:T(8,128)(2,1)} %get-tuple-element.34), channel_id=1, source_target_pairs={{0,6},{1,7},{2,4},{3,5},{4,2},{5,3},{6,0},{7,1},{8,14},{9,15},{10,... | collective-permute-start | bytes 691208 | tf_op jit(solution)/shard_map/ppermute | solution.py:78
  46.1 7.1 %collective-permute-done.8 = bf16[360,320]{1,0:T(8,128)(2,1)S(1)} collective-permute-done((bf16[360,320]{1,0:T(8,128)(2,1)}, bf16[360,320]{1,0:T(8,128)(2,1)S(1)}, u32[]{:S(2)}, u32[]{:S(2)}) %collective-permute-start.8) | collective-permute-done | bytes 230432 | tf_op jit(solution)/shard_map/ppermute | solution.py:78
  53.2 5.2 %collective-permute-done.7 = bf16[360,320]{1,0:T(8,128)(2,1)} collective-permute-done((bf16[360,320]{1,0:T(8,128)(2,1)}, bf16[360,320]{1,0:T(8,128)(2,1)}, u32[]{:S(2)}, u32[]{:S(2)}) %collective-permute-start.7) | collective-permute-done | bytes 230432 | tf_op jit(solution)/shard_map/ppermute | solution.py:78
  59.7 2.5 %collective-permute-start.9 = (bf16[360,320]{1,0:T(8,128)(2,1)S(1)}, bf16[360,320]{1,0:T(8,128)(2,1)S(1)}, u32[]{:S(2)}, u32[]{:S(2)}) collective-permute-start(bf16[360,320]{1,0:T(8,128)(2,1)S(1)} %fusion.24), channel_id=1, source_target_pairs={{0,8},{8,0},{16,24},{24,16},{1,9},{9,1},{17,25},{25,17},{2,10},{10... | collective-permute-start | bytes 691208 | tf_op jit(solution)/shard_map/ppermute | solution.py:91
  63.6 4.6 %collective-permute-start.10 = (bf16[1,128,320]{1,2,0:T(8,128)(2,1)S(1)}, bf16[1,128,320]{1,2,0:T(8,128)(2,1)S(1)}, u32[]{:S(2)}, u32[]{:S(2)}) collective-permute-start(bf16[1,128,320]{1,2,0:T(8,128)(2,1)S(1)} %get-tuple-element.37), channel_id=1, source_target_pairs={{0,8},{8,16},{16,24},{1,9},{9,17},{17,25},{2,10},{10,18},{18,26},{... | collective-permute-start | bytes 245768 | tf_op jit(solution)/shard_map/ppermute | solution.py:18
  69.2 2.1 %copy.56 = f32[360,320]{1,0:T(8,128)} copy(f32[360,320]{0,1:T(8,128)} %param.14) | data formatting | bytes 921600 | tf_op args[5]
  72.5 3.0 %copy.52 = bf16[8,360,320]{2,1,0:T(8,128)(2,1)S(1)} copy(bf16[8,360,320]{1,2,0:T(8,128)(2,1)} %all-gather.3.cloned.1.call-done) | data formatting | bytes 3686400 | tf_op jit(solution)/shard_map/all_gather | solution.py:122
  76.7 1.4 %copy-done.16 = bf16[3,128,2880]{1,2,0:T(8,128)(2,1)} copy-done((bf16[3,128,2880]{1,2,0:T(8,128)(2,1)}, bf16[3,128,2880]{1,2,0:T(8,128)(2,1)S(1)}, u32[]{:S(2)}) %copy-start.16) | copy-done | bytes 2211864
  78.1 2.5 %copy.54 = bf16[9,320,320]{1,2,0:T(8,128)(2,1)} copy(bf16[9,320,320]{2,1,0:T(8,128)(2,1)S(1)} %bitcast.114) | data formatting | bytes 3686400 | tf_op jit(solution)/shard_map/reshape | solution.py:153
  80.7 4.4 %fusion.48 = (f32[320]{0:T(512)S(1)}, f32[320]{0:T(512)S(1)}, f32[3,128,320]{1,2,0:T(8,128)}) fusion(f32[320]{0:T(512)S(1)} %copy-done.13, f32[320]{0:T(512)S(1)} %copy-done.15, f32[3,128]{1,0:T(4,128)S(1)} %copy-done.11, bf16[1,3,128,320]{2,3,1,0:T(8,128)(2,1)S(1)} %copy-done.3, f32[320]{0:T(512)S(1)} %copy-done.18, f32[320]{0:T(512)S(1)} %copy-done.20, ...), kind=kOutput, calls=%fused_computation.92 | convolution fusion | flops 710245760 | bytes 4801536 | tf_op jit(solution)/shard_map/dot_general | solution.py:163
  85.6 1.7 %collective-permute-start.14 = (f32[2,32]{1,0:T(2,128)S(1)}, f32[2,32]{1,0:T(2,128)S(1)}, u32[]{:S(2)}, u32[]{:S(2)}) collective-permute-start(f32[2,32]{1,0:T(2,128)S(1)} %pad_maximum_fusion.3), channel_id=1, source_target_pairs={{0,24},{8,0},{16,8},{24,16},{1,25},{9,1},{17,9},{25,17},{2,26},{10... | collective-permute-start | bytes 776 | tf_op jit(solution)/shard_map/ppermute | solution.py:33
  88.7 3.5 %fusion.11 = bf16[1,3,128,320]{2,3,1,0:T(8,128)(2,1)} fusion(bf16[3,128,2880]{1,2,0:T(8,128)(2,1)} %copy-done.1, bf16[2880,320]{1,0:T(8,128)(2,1)S(1)} %bitcast.115, f32[3,128]{1,0:T(4,128)S(1)} %copy-done.11), kind=kOutput, calls=%fused_computation.12 | convolution fusion | flops 708034560 | bytes 4302336 | tf_op jit(solution)/shard_map/dot_general | solution.py:151
  92.2 1.9 %collective-permute-start.15 = (bf16[360,320]{1,0:T(8,128)(2,1)S(1)}, bf16[360,320]{1,0:T(8,128)(2,1)S(1)}, u32[]{:S(2)}, u32[]{:S(2)}) collective-permute-start(bf16[360,320]{1,0:T(8,128)(2,1)S(1)} %copy-done.7), channel_id=1, source_target_pairs={{0,16},{8,24},{16,0},{24,8},{1,17},{9,25},{17,1},{25,9},{2,18},{10... | collective-permute-start | bytes 691208 | tf_op jit(solution)/shard_map/ppermute | solution.py:91
  94.5 2.0 %fusion.44 = bf16[1,3,128,320]{2,3,1,0:T(8,128)(2,1)} fusion(f32[320]{0:T(512)S(1)} %mul.180, f32[320]{0:T(512)S(1)} %copy-done.15, f32[3,128]{1,0:T(4,128)S(1)} %copy-done.11, bf16[1,3,128,320]{2,3,1,0:T(8,128)(2,1)S(1)} %copy-done.3, f32[3,128,320]{1,2,0:T(8,128)} %get-tuple-element.45, f32[320]{0:T(512)S(1)} %sub.44, f32[320]{0:T(512)S(1)} %copy-done.13), kind=kLoop, calls=%fused_computation.76 | loop fusion | flops 1351680 | bytes 989696 | tf_op jit(solution)/shard_map/broadcast_in_dim | solution.py:181
  96.5 9.3 %collective-permute-done.15 = bf16[360,320]{1,0:T(8,128)(2,1)S(1)} collective-permute-done((bf16[360,320]{1,0:T(8,128)(2,1)S(1)}, bf16[360,320]{1,0:T(8,128)(2,1)S(1)}, u32[]{:S(2)}, u32[]{:S(2)}) %collective-permute-start.15) | collective-permute-done | bytes 230432 | tf_op jit(solution)/shard_map/ppermute | solution.py:91
  105.8 1.5 %fusion.21 = (f32[360,320]{1,0:T(8,128)S(1)}, f32[360,320]{1,0:T(8,128)S(1)}) fusion(f32[360,320]{1,0:T(8,128)S(1)} %copy-done.6, f32[360,320]{1,0:T(8,128)} %copy.56, bf16[360,320]{1,0:T(8,128)(2,1)S(1)} %collective-permute-done.15, bf16[360,320]{1,0:T(8,128)(2,1)S(1)} %copy-done.7), kind=kLoop, calls=%fused_computation.27 | loop fusion | flops 1612800 | bytes 2304000 | tf_op jit(solution)/shard_map/div | solution.py:180
  (121 shorter events, 23.0 us)
Async XLA Ops:
  7.2 65.3 %all-gather.3.cloned.1.call-start = ((), (), s32[]{:S(2)}) async-start(), calls=%async_computation | async-start | bytes 2211840 | tf_op jit(solution)/shard_map/all_gather | solution.py:122
  8.6 22.5 %copy-start.10 = (f32[3,128]{1,0:T(4,128)}, f32[3,128]{1,0:T(4,128)S(1)}, u32[]{:S(2)}) copy-start(f32[3,128]{1,0:T(4,128)S(1)} %get-tuple-element.44) | copy-start | bytes 4612
  10.2 6.4 %collective-permute-start.2 = (f32[2,32]{1,0:T(2,128)S(1)}, f32[2,32]{1,0:T(2,128)S(1)}, u32[]{:S(2)}, u32[]{:S(2)}) collective-permute-start(f32[2,32]{1,0:T(2,128)S(1)} %pad_maximum_fusion.2), channel_id=1, source_target_pairs={{0,24},{8,0},{16,8},{24,16},{1,25},{9,1},{17,9},{25,17},{2,26},{10... | collective-permute-start | bytes 776 | tf_op jit(solution)/shard_map/ppermute | solution.py:33
  15.3 4.5 %collective-permute-start.1 = (f32[2,32]{1,0:T(2,128)S(1)}, f32[2,32]{1,0:T(2,128)S(1)}, u32[]{:S(2)}, u32[]{:S(2)}) collective-permute-start(f32[2,32]{1,0:T(2,128)S(1)} %pad_maximum_fusion.2), channel_id=1, source_target_pairs={{0,16},{8,24},{16,0},{24,8},{1,17},{9,25},{17,1},{25,9},{2,18},{10... | collective-permute-start | bytes 776 | tf_op jit(solution)/shard_map/ppermute | solution.py:33
  15.3 5.4 %collective-permute-start = (f32[2,32]{1,0:T(2,128)S(1)}, f32[2,32]{1,0:T(2,128)S(1)}, u32[]{:S(2)}, u32[]{:S(2)}) collective-permute-start(f32[2,32]{1,0:T(2,128)S(1)} %pad_maximum_fusion.2), channel_id=1, source_target_pairs={{0,8},{8,16},{16,24},{24,0},{1,9},{9,17},{17,25},{25,1},{2,10},{10... | collective-permute-start | bytes 776 | tf_op jit(solution)/shard_map/ppermute | solution.py:33
  20.9 10.2 %copy-start.12 = (f32[320]{0:T(512)}, f32[320]{0:T(512)S(1)}, u32[]{:S(2)}) copy-start(f32[320]{0:T(512)S(1)} %mul.163) | copy-start | bytes 3844
  21.1 10.0 %copy-start.14 = (f32[320]{0:T(512)}, f32[320]{0:T(512)S(1)}, u32[]{:S(2)}) copy-start(f32[320]{0:T(512)S(1)} %sub.37) | copy-start | bytes 3844
  21.1 10.0 %copy-start.2 = (bf16[1,3,128,320]{2,3,1,0:T(8,128)(2,1)S(1)}, bf16[1,3,128,320]{2,3,1,0:T(8,128)(2,1)}, u32[]{:S(2)}) copy-start(bf16[1,3,128,320]{2,3,1,0:T(8,128)(2,1)} %param.9) | copy-start | bytes 737284
  22.5 6.9 %collective-permute-start.4 = (bf16[1,128,320]{1,2,0:T(8,128)(2,1)S(1)}, bf16[1,128,320]{1,2,0:T(8,128)(2,1)S(1)}, u32[]{:S(2)}, u32[]{:S(2)}) collective-permute-start(bf16[1,128,320]{1,2,0:T(8,128)(2,1)S(1)} %get-tuple-element.40), channel_id=1, source_target_pairs={{8,0},{16,8},{24,16},{9,1},{17,9},{25,17},{10,2},{18,10},{26,18},{... | collective-permute-start | bytes 245768 | tf_op jit(solution)/shard_map/ppermute | solution.py:20
  23.8 6.6 %collective-permute-start.3 = (bf16[1,128,320]{1,2,0:T(8,128)(2,1)S(1)}, bf16[1,128,320]{1,2,0:T(8,128)(2,1)S(1)}, u32[]{:S(2)}, u32[]{:S(2)}) collective-permute-start(bf16[1,128,320]{1,2,0:T(8,128)(2,1)S(1)} %get-tuple-element.39), channel_id=1, source_target_pairs={{0,8},{8,16},{16,24},{1,9},{9,17},{17,25},{2,10},{10,18},{18,26},{... | collective-permute-start | bytes 245768 | tf_op jit(solution)/shard_map/ppermute | solution.py:18
  36.4 2.6 %collective-permute-start.5 = (bf16[4,360,320]{1,2,0:T(8,128)(2,1)S(1)}, bf16[4,360,320]{1,2,0:T(8,128)(2,1)S(1)}, u32[]{:S(2)}, u32[]{:S(2)}) collective-permute-start(bf16[4,360,320]{1,2,0:T(8,128)(2,1)S(1)} %copy.48), channel_id=1, source_target_pairs={{0,1},{1,0},{2,3},{3,2},{4,5},{5,4},{6,7},{7,6},{8,9},{9,8},{10,11... | collective-permute-start | bytes 2764808 | tf_op jit(solution)/shard_map/ppermute | solution.py:65
  41.6 20.7 %copy-start.5 = (bf16[3,128,320]{1,2,0:T(8,128)(2,1)S(1)}, bf16[3,128,320]{1,2,0:T(8,128)(2,1)}, u32[]{:S(2)}) copy-start(bf16[3,128,320]{1,2,0:T(8,128)(2,1)} %copy-done.4) | copy-start | bytes 737284
  41.6 26.5 %copy-start.8 = (f32[360,320]{0,1:T(8,128)S(1)}, f32[360,320]{0,1:T(8,128)}, u32[]{:S(2)}) copy-start(f32[360,320]{0,1:T(8,128)} %param.15) | copy-start | bytes 1382404
  42.6 10.6 %collective-permute-start.8 = (bf16[360,320]{1,0:T(8,128)(2,1)}, bf16[360,320]{1,0:T(8,128)(2,1)S(1)}, u32[]{:S(2)}, u32[]{:S(2)}) collective-permute-start(bf16[360,320]{1,0:T(8,128)(2,1)} %get-tuple-element.34), channel_id=1, source_target_pairs={{0,6},{1,7},{2,4},{3,5},{4,2},{5,3},{6,0},{7,1},{8,14},{9,15},{10,... | collective-permute-start | bytes 691208 | tf_op jit(solution)/shard_map/ppermute | solution.py:78
  45.0 13.4 %collective-permute-start.7 = (bf16[360,320]{1,0:T(8,128)(2,1)}, bf16[360,320]{1,0:T(8,128)(2,1)}, u32[]{:S(2)}, u32[]{:S(2)}) collective-permute-start(bf16[360,320]{1,0:T(8,128)(2,1)} %get-tuple-element.33), channel_id=1, source_target_pairs={{0,4},{1,5},{2,6},{3,7},{4,0},{5,1},{6,2},{7,3},{8,12},{9,13},{10,... | collective-permute-start | bytes 691208 | tf_op jit(solution)/shard_map/ppermute | solution.py:78
  45.5 13.0 %collective-permute-start.6 = (bf16[360,320]{1,0:T(8,128)(2,1)S(1)}, bf16[360,320]{1,0:T(8,128)(2,1)}, u32[]{:S(2)}, u32[]{:S(2)}) collective-permute-start(bf16[360,320]{1,0:T(8,128)(2,1)S(1)} %get-tuple-element.32), channel_id=1, source_target_pairs={{0,2},{1,3},{2,0},{3,1},{4,6},{5,7},{6,4},{7,5},{8,10},{9,11},{10,... | collective-permute-start | bytes 691208 | tf_op jit(solution)/shard_map/ppermute | solution.py:78
  59.7 12.0 %collective-permute-start.9 = (bf16[360,320]{1,0:T(8,128)(2,1)S(1)}, bf16[360,320]{1,0:T(8,128)(2,1)S(1)}, u32[]{:S(2)}, u32[]{:S(2)}) collective-permute-start(bf16[360,320]{1,0:T(8,128)(2,1)S(1)} %fusion.24), channel_id=1, source_target_pairs={{0,8},{8,0},{16,24},{24,16},{1,9},{9,1},{17,25},{25,17},{2,10},{10... | collective-permute-start | bytes 691208 | tf_op jit(solution)/shard_map/ppermute | solution.py:91
  62.3 9.0 %collective-permute-start.11 = (bf16[1,128,320]{1,2,0:T(8,128)(2,1)S(1)}, bf16[1,128,320]{1,2,0:T(8,128)(2,1)S(1)}, u32[]{:S(2)}, u32[]{:S(2)}) collective-permute-start(bf16[1,128,320]{1,2,0:T(8,128)(2,1)S(1)} %get-tuple-element.38), channel_id=1, source_target_pairs={{8,0},{16,8},{24,16},{9,1},{17,9},{25,17},{10,2},{18,10},{26,18},{... | collective-permute-start | bytes 245768 | tf_op jit(solution)/shard_map/ppermute | solution.py:20
  63.6 7.7 %collective-permute-start.10 = (bf16[1,128,320]{1,2,0:T(8,128)(2,1)S(1)}, bf16[1,128,320]{1,2,0:T(8,128)(2,1)S(1)}, u32[]{:S(2)}, u32[]{:S(2)}) collective-permute-start(bf16[1,128,320]{1,2,0:T(8,128)(2,1)S(1)} %get-tuple-element.37), channel_id=1, source_target_pairs={{0,8},{8,16},{16,24},{1,9},{9,17},{17,25},{2,10},{10,18},{18,26},{... | collective-permute-start | bytes 245768 | tf_op jit(solution)/shard_map/ppermute | solution.py:18
  85.6 20.2 %copy-start.6 = (f32[360,320]{1,0:T(8,128)S(1)}, f32[360,320]{1,0:T(8,128)}, u32[]{:S(2)}) copy-start(f32[360,320]{1,0:T(8,128)} %copy.57) | copy-start | bytes 1382404
  85.6 8.5 %collective-permute-start.14 = (f32[2,32]{1,0:T(2,128)S(1)}, f32[2,32]{1,0:T(2,128)S(1)}, u32[]{:S(2)}, u32[]{:S(2)}) collective-permute-start(f32[2,32]{1,0:T(2,128)S(1)} %pad_maximum_fusion.3), channel_id=1, source_target_pairs={{0,24},{8,0},{16,8},{24,16},{1,25},{9,1},{17,9},{25,17},{2,26},{10... | collective-permute-start | bytes 776 | tf_op jit(solution)/shard_map/ppermute | solution.py:33
  87.3 6.8 %collective-permute-start.13 = (f32[2,32]{1,0:T(2,128)S(1)}, f32[2,32]{1,0:T(2,128)S(1)}, u32[]{:S(2)}, u32[]{:S(2)}) collective-permute-start(f32[2,32]{1,0:T(2,128)S(1)} %pad_maximum_fusion.3), channel_id=1, source_target_pairs={{0,16},{8,24},{16,0},{24,8},{1,17},{9,25},{17,1},{25,9},{2,18},{10... | collective-permute-start | bytes 776 | tf_op jit(solution)/shard_map/ppermute | solution.py:33
  88.3 5.8 %collective-permute-start.12 = (f32[2,32]{1,0:T(2,128)S(1)}, f32[2,32]{1,0:T(2,128)S(1)}, u32[]{:S(2)}, u32[]{:S(2)}) collective-permute-start(f32[2,32]{1,0:T(2,128)S(1)} %pad_maximum_fusion.3), channel_id=1, source_target_pairs={{0,8},{8,16},{16,24},{24,0},{1,9},{9,17},{17,25},{25,1},{2,10},{10... | collective-permute-start | bytes 776 | tf_op jit(solution)/shard_map/ppermute | solution.py:33
  92.2 13.6 %collective-permute-start.15 = (bf16[360,320]{1,0:T(8,128)(2,1)S(1)}, bf16[360,320]{1,0:T(8,128)(2,1)S(1)}, u32[]{:S(2)}, u32[]{:S(2)}) collective-permute-start(bf16[360,320]{1,0:T(8,128)(2,1)S(1)} %copy-done.7), channel_id=1, source_target_pairs={{0,16},{8,24},{16,0},{24,8},{1,17},{9,25},{17,1},{25,9},{2,18},{10... | collective-permute-start | bytes 691208 | tf_op jit(solution)/shard_map/ppermute | solution.py:91
  (14 other events, 54.7 us)
Sparse Core Ops, SparseCore 0:
  16.5 27.7 all-gather.2

commit v13 on v9

--- a/solution.py
+++ b/solution.py
@@ -84,14 +84,14 @@
     if count & (count - 1):
         value, companions = lax.optimization_barrier((value, companions))
         return lax.psum(value.astype(jnp.bfloat16), axis).astype(jnp.float32), companions
-    step = 1
-    while step < count:
+    step = count // 2
+    while step:
         mine = value.astype(jnp.bfloat16)
         pairs = [(i, i ^ step) for i in range(count)]
         value = mine.astype(jnp.float32) + lax.ppermute(mine, axis, pairs).astype(jnp.float32)
-        if step == 1:
+        if step * 2 == count:
             value, companions = lax.optimization_barrier((value, companions))
-        step *= 2
+        step //= 2
     return value, companions
 
 

time: 111 us -> 112 us (level)
    ppermute x2, waiting for transfers between devices: 2.1 us -> 0.48 us  [with_halo(): lax.ppermute(head, axis, [((i + 1) % count, i) for i in range(ends)])]
    ppermute x2, waiting for transfers between devices: 1.03 us -> 2.59 us  [with_halo(): lax.ppermute(tail, axis, [(i, (i + 1) % count) for i in range(ends)])]
    ppermute x6, starting transfers between devices: 9.98 us -> 11.3 us  [space_sum(): lax.ppermute(joined, axis, [(i, (i + shift) % count) for i in range(count)])]
  transfers between devices with their start and end apart: 17 -> 17, of which waited for: 10 -> 12; matrix products, arithmetic and copies ran while one was open for 18% -> 17% of each run, Pallas kernels for 0% -> 0%
where the time goes in v13:
time: 112 us; the launch traced here: 111 us
  starting transfers between devices  30 us (27%)
  waiting for transfers between devices  27 us (24%)
  local copies, waits for them, and re-layouts  16.4 us (15%)
  between operations  15.9 us (14%)
  other arithmetic  12.4 us (11%)
  matrix products  9.45 us (8%)
    ppermute x6, starting transfers between devices, space_sum(): lax.ppermute(joined, axis, [(i, (i + shift) % count) for i in range(count)])  11.3 us
    ppermute x3, waiting for transfers between devices, halving_scatter(): lax.ppermute(send.astype(jnp.bfloat16), axis, pairs).astype(jnp.float32)  9.13 us
    ppermute x2, starting transfers between devices, with_halo(): lax.ppermute(tail, axis, [(i, (i + 1) % count) for i in range(ends)])  9.1 us
    ppermute x2, waiting for transfers between devices, replicated_sum(): lax.ppermute(mine, axis, pairs).astype(jnp.float32)  7.91 us
    unnamed x36, local copies, waits for them, and re-layouts  7.58 us
    dot_general x1, matrix products, local(): upstream = jnp.dot(cot_cols, flipped, preferred_element_type=jnp.float32)  4.4 us
    ppermute x6, waiting for transfers between devices, space_sum(): lax.ppermute(joined, axis, [(i, (i + shift) % count) for i in range(count)])  4.33 us
    dot_general x1, matrix products, local(): output = jnp.dot(act_cols, gathered, preferred_element_type=jnp.float32)  3.53 us
  transfers between devices with their start and end apart: 17, of which 12 were waited for; matrix products, arithmetic and copies ran while one was open for 17% of the time, Pallas kernels for 0%

profile of v13, /device:TPU:0, one launch (start us, length us, event | category | flops | bytes accessed | tf_op | source)
XLA Modules:
  0.0 111.0 jit_solution(17007533623039676636)
XLA Ops:
  10.2 5.1 %collective-permute-start.2 = (f32[2,32]{1,0:T(2,128)S(1)}, f32[2,32]{1,0:T(2,128)S(1)}, u32[]{:S(2)}, u32[]{:S(2)}) collective-permute-start(f32[2,32]{1,0:T(2,128)S(1)} %pad_maximum_fusion.2), channel_id=1, source_target_pairs={{0,24},{8,0},{16,8},{24,16},{1,25},{9,1},{17,9},{25,17},{2,26},{10... | collective-permute-start | bytes 776 | tf_op jit(solution)/shard_map/ppermute | solution.py:33
  16.6 3.2 %collective-permute-done.1 = f32[2,32]{1,0:T(2,128)S(1)} collective-permute-done((f32[2,32]{1,0:T(2,128)S(1)}, f32[2,32]{1,0:T(2,128)S(1)}, u32[]{:S(2)}, u32[]{:S(2)}) %collective-permute-start.1) | collective-permute-done | bytes 288 | tf_op jit(solution)/shard_map/ppermute | solution.py:33
  23.8 4.6 %collective-permute-start.3 = (bf16[1,128,320]{1,2,0:T(8,128)(2,1)S(1)}, bf16[1,128,320]{1,2,0:T(8,128)(2,1)S(1)}, u32[]{:S(2)}, u32[]{:S(2)}) collective-permute-start(bf16[1,128,320]{1,2,0:T(8,128)(2,1)S(1)} %get-tuple-element.23), channel_id=1, source_target_pairs={{0,8},{8,16},{16,24},{1,9},{9,17},{17,25},{2,10},{10,18},{18,26},{... | collective-permute-start | bytes 245768 | tf_op jit(solution)/shard_map/ppermute | solution.py:18
  31.9 1.5 %fusion.48 = f32[2880,320,1]{1,0,2:T(8,128)S(1)} fusion(bf16[3,128,2880]{1,2,0:T(8,128)(2,1)S(1)} %slice_dynamic-update-slice_fusion, bf16[3,128,320]{1,2,0:T(8,128)(2,1)S(1)} %bitcast_multiply_fusion), kind=kOutput, calls=%fused_computation.96 | convolution fusion | flops 707788800 | bytes 6144000 | tf_op jit(solution)/shard_map/dot_general | solution.py:145
  33.5 2.0 %copy-done = f32[2880,320,1]{1,0,2:T(8,128)} copy-done((f32[2880,320,1]{1,0,2:T(8,128)}, f32[2880,320,1]{1,0,2:T(8,128)S(1)}, u32[]{:S(2)}) %copy-start) | copy-done | bytes 3686424
  36.4 2.5 %collective-permute-done.5 = bf16[4,360,320]{1,2,0:T(8,128)(2,1)S(1)} collective-permute-done((bf16[4,360,320]{1,2,0:T(8,128)(2,1)S(1)}, bf16[4,360,320]{1,2,0:T(8,128)(2,1)S(1)}, u32[]{:S(2)}, u32[]{:S(2)}) %collective-permute-start.5) | collective-permute-done | bytes 921632 | tf_op jit(solution)/shard_map/ppermute | solution.py:65
  39.7 1.8 %bitcast_add_fusion = f32[4,360,320]{2,1,0:T(8,128)S(1)} fusion(bf16[4,360,320]{2,1,0:T(8,128)(2,1)S(1)} %copy.49, f32[4,2,360,320]{3,2,1,0:T(8,128)} %bitcast.116, s32[]{:T(128)S(6)} %select_n.33), kind=kLoop, calls=%fused_computation.3 | loop fusion | flops 921600 | bytes 4608004 | tf_op jit(solution)/shard_map/add | solution.py:66
  42.5 2.5 %collective-permute-start.8 = (bf16[360,320]{0,1:T(8,128)(2,1)}, bf16[360,320]{0,1:T(8,128)(2,1)S(1)}, u32[]{:S(2)}, u32[]{:S(2)}) collective-permute-start(bf16[360,320]{0,1:T(8,128)(2,1)} %bitcast.100), channel_id=1, source_target_pairs={{0,6},{1,7},{2,4},{3,5},{4,2},{5,3},{6,0},{7,1},{8,14},{9,15},{10,... | collective-permute-start | bytes 691208 | tf_op jit(solution)/shard_map/ppermute | solution.py:78
  48.0 4.5 %collective-permute-done.8 = bf16[360,320]{0,1:T(8,128)(2,1)S(1)} collective-permute-done((bf16[360,320]{0,1:T(8,128)(2,1)}, bf16[360,320]{0,1:T(8,128)(2,1)S(1)}, u32[]{:S(2)}, u32[]{:S(2)}) %collective-permute-start.8) | collective-permute-done | bytes 230432 | tf_op jit(solution)/shard_map/ppermute | solution.py:78
  52.5 4.4 %collective-permute-done.7 = bf16[360,320]{0,1:T(8,128)(2,1)S(1)} collective-permute-done((bf16[360,320]{0,1:T(8,128)(2,1)}, bf16[360,320]{0,1:T(8,128)(2,1)S(1)}, u32[]{:S(2)}, u32[]{:S(2)}) %collective-permute-start.7) | collective-permute-done | bytes 230432 | tf_op jit(solution)/shard_map/ppermute | solution.py:78
  58.2 1.9 %collective-permute-start.9 = (bf16[360,320]{0,1:T(8,128)(2,1)S(1)}, bf16[360,320]{0,1:T(8,128)(2,1)S(1)}, u32[]{:S(2)}, u32[]{:S(2)}) collective-permute-start(bf16[360,320]{0,1:T(8,128)(2,1)S(1)} %fusion.38), channel_id=1, source_target_pairs={{0,16},{8,24},{16,0},{24,8},{1,17},{9,25},{17,1},{25,9},{2,18},{10... | collective-permute-start | bytes 691208 | tf_op jit(solution)/shard_map/ppermute | solution.py:91
  61.4 4.6 %collective-permute-start.10 = (bf16[1,128,320]{1,2,0:T(8,128)(2,1)S(1)}, bf16[1,128,320]{1,2,0:T(8,128)(2,1)S(1)}, u32[]{:S(2)}, u32[]{:S(2)}) collective-permute-start(bf16[1,128,320]{1,2,0:T(8,128)(2,1)S(1)} %get-tuple-element.21), channel_id=1, source_target_pairs={{0,8},{8,16},{16,24},{1,9},{9,17},{17,25},{2,10},{10,18},{18,26},{... | collective-permute-start | bytes 245768 | tf_op jit(solution)/shard_map/ppermute | solution.py:18
  66.4 1.6 %collective-permute-done.10 = bf16[1,128,320]{1,2,0:T(8,128)(2,1)S(1)} collective-permute-done((bf16[1,128,320]{1,2,0:T(8,128)(2,1)S(1)}, bf16[1,128,320]{1,2,0:T(8,128)(2,1)S(1)}, u32[]{:S(2)}, u32[]{:S(2)}) %collective-permute-start.10) | collective-permute-done | bytes 81952 | tf_op jit(solution)/shard_map/ppermute | solution.py:18
  68.4 4.7 %collective-permute-done.9 = bf16[360,320]{0,1:T(8,128)(2,1)S(1)} collective-permute-done((bf16[360,320]{0,1:T(8,128)(2,1)S(1)}, bf16[360,320]{0,1:T(8,128)(2,1)S(1)}, u32[]{:S(2)}, u32[]{:S(2)}) %collective-permute-start.9) | collective-permute-done | bytes 230432 | tf_op jit(solution)/shard_map/ppermute | solution.py:91
  73.2 3.0 %copy.56 = bf16[8,360,320]{2,1,0:T(8,128)(2,1)S(1)} copy(bf16[8,360,320]{1,2,0:T(8,128)(2,1)} %all-gather.3.cloned.1.call-done) | data formatting | bytes 3686400 | tf_op jit(solution)/shard_map/all_gather | solution.py:122
  78.7 2.5 %copy.58 = bf16[9,320,320]{1,2,0:T(8,128)(2,1)} copy(bf16[9,320,320]{2,1,0:T(8,128)(2,1)S(1)} %bitcast.117) | data formatting | bytes 3686400 | tf_op jit(solution)/shard_map/reshape | solution.py:153
  81.2 4.4 %fusion.45 = (f32[320]{0:T(512)S(1)}, f32[320]{0:T(512)S(1)}, f32[3,128,320]{1,2,0:T(8,128)}) fusion(f32[320]{0:T(512)S(1)} %mul.163, f32[320]{0:T(512)S(1)} %sub.37, f32[3,128]{1,0:T(4,128)S(1)} %get-tuple-element.28, bf16[1,3,128,320]{2,3,1,0:T(8,128)(2,1)S(1)} %copy-done.3, f32[320]{0:T(512)S(1)} %copy-done.8, f32[320]{0:T(512)S(1)} %copy-done.9, ...), kind=kOutput, calls=%fused_computation.93 | convolution fusion | flops 710245760 | bytes 4801536 | tf_op jit(solution)/shard_map/dot_general | solution.py:163
  86.1 3.2 %collective-permute-start.14 = (f32[2,32]{1,0:T(2,128)S(1)}, f32[2,32]{1,0:T(2,128)S(1)}, u32[]{:S(2)}, u32[]{:S(2)}) collective-permute-start(f32[2,32]{1,0:T(2,128)S(1)} %pad_maximum_fusion.3), channel_id=1, source_target_pairs={{0,24},{8,0},{16,8},{24,16},{1,25},{9,1},{17,9},{25,17},{2,26},{10... | collective-permute-start | bytes 776 | tf_op jit(solution)/shard_map/ppermute | solution.py:33
  89.5 1.9 %collective-permute-start.12 = (f32[2,32]{1,0:T(2,128)S(1)}, f32[2,32]{1,0:T(2,128)S(1)}, u32[]{:S(2)}, u32[]{:S(2)}) collective-permute-start(f32[2,32]{1,0:T(2,128)S(1)} %pad_maximum_fusion.3), channel_id=1, source_target_pairs={{0,8},{8,16},{16,24},{24,0},{1,9},{9,17},{17,25},{25,1},{2,10},{10... | collective-permute-start | bytes 776 | tf_op jit(solution)/shard_map/ppermute | solution.py:33
  91.3 3.5 %fusion.11 = bf16[1,3,128,320]{2,3,1,0:T(8,128)(2,1)} fusion(bf16[3,128,2880]{1,2,0:T(8,128)(2,1)} %copy-done.1, bf16[2880,320]{1,0:T(8,128)(2,1)S(1)} %bitcast.118, f32[3,128]{1,0:T(4,128)S(1)} %get-tuple-element.28), kind=kOutput, calls=%fused_computation.12 | convolution fusion | flops 708034560 | bytes 4302336 | tf_op jit(solution)/shard_map/dot_general | solution.py:151
  94.8 1.4 %collective-permute-start.15 = (bf16[360,320]{0,1:T(8,128)(2,1)S(1)}, bf16[360,320]{0,1:T(8,128)(2,1)S(1)}, u32[]{:S(2)}, u32[]{:S(2)}) collective-permute-start(bf16[360,320]{0,1:T(8,128)(2,1)S(1)} %convert_add_fusion.1), channel_id=1, source_target_pairs={{0,8},{8,0},{16,24},{24,16},{1,9},{9,1},{17,25},{25,17},{2,10},{10... | collective-permute-start | bytes 691208 | tf_op jit(solution)/shard_map/ppermute | solution.py:91
  96.7 2.0 %fusion.41 = bf16[1,3,128,320]{2,3,1,0:T(8,128)(2,1)} fusion(f32[320]{0:T(512)S(1)} %mul.180, f32[320]{0:T(512)S(1)} %sub.37, f32[3,128]{1,0:T(4,128)S(1)} %get-tuple-element.28, bf16[1,3,128,320]{2,3,1,0:T(8,128)(2,1)S(1)} %copy-done.3, f32[3,128,320]{1,2,0:T(8,128)} %get-tuple-element.29, f32[320]{0:T(512)S(1)} %sub.44, f32[320]{0:T(512)S(1)} %mul.163), kind=kLoop, calls=%fused_computation.73 | loop fusion | flops 1351680 | bytes 989696 | tf_op jit(solution)/shard_map/broadcast_in_dim | solution.py:181
  98.7 3.2 %collective-permute-done.15 = bf16[360,320]{0,1:T(8,128)(2,1)S(1)} collective-permute-done((bf16[360,320]{0,1:T(8,128)(2,1)S(1)}, bf16[360,320]{0,1:T(8,128)(2,1)S(1)}, u32[]{:S(2)}, u32[]{:S(2)}) %collective-permute-start.15) | collective-permute-done | bytes 230432 | tf_op jit(solution)/shard_map/ppermute | solution.py:91
  101.9 2.3 %fusion.35 = (f32[360,320]{0,1:T(8,128)}, f32[360,320]{0,1:T(8,128)}) fusion(f32[360,320]{0,1:T(8,128)S(1)} %copy-done.6, f32[360,320]{0,1:T(8,128)} %param.14, bf16[360,320]{0,1:T(8,128)(2,1)S(1)} %collective-permute-done.15, bf16[360,320]{0,1:T(8,128)(2,1)S(1)} %convert_add_fusion.1), kind=kLoop, calls=%fused_computation.41 | loop fusion | flops 1612800 | bytes 2304000 | tf_op jit(solution)/shard_map/div | solution.py:180
  (100 shorter events, 23.0 us)
Async XLA Ops:
  7.2 66.0 %all-gather.3.cloned.1.call-start = ((), (), s32[]{:S(2)}) async-start(), calls=%async_computation | async-start | bytes 2211840 | tf_op jit(solution)/shard_map/all_gather | solution.py:122
  10.2 6.4 %collective-permute-start.2 = (f32[2,32]{1,0:T(2,128)S(1)}, f32[2,32]{1,0:T(2,128)S(1)}, u32[]{:S(2)}, u32[]{:S(2)}) collective-permute-start(f32[2,32]{1,0:T(2,128)S(1)} %pad_maximum_fusion.2), channel_id=1, source_target_pairs={{0,24},{8,0},{16,8},{24,16},{1,25},{9,1},{17,9},{25,17},{2,26},{10... | collective-permute-start | bytes 776 | tf_op jit(solution)/shard_map/ppermute | solution.py:33
  15.3 4.5 %collective-permute-start.1 = (f32[2,32]{1,0:T(2,128)S(1)}, f32[2,32]{1,0:T(2,128)S(1)}, u32[]{:S(2)}, u32[]{:S(2)}) collective-permute-start(f32[2,32]{1,0:T(2,128)S(1)} %pad_maximum_fusion.2), channel_id=1, source_target_pairs={{0,16},{8,24},{16,0},{24,8},{1,17},{9,25},{17,1},{25,9},{2,18},{10... | collective-permute-start | bytes 776 | tf_op jit(solution)/shard_map/ppermute | solution.py:33
  15.3 5.4 %collective-permute-start = (f32[2,32]{1,0:T(2,128)S(1)}, f32[2,32]{1,0:T(2,128)S(1)}, u32[]{:S(2)}, u32[]{:S(2)}) collective-permute-start(f32[2,32]{1,0:T(2,128)S(1)} %pad_maximum_fusion.2), channel_id=1, source_target_pairs={{0,8},{8,16},{16,24},{24,0},{1,9},{9,17},{17,25},{25,1},{2,10},{10... | collective-permute-start | bytes 776 | tf_op jit(solution)/shard_map/ppermute | solution.py:33
  21.1 10.0 %copy-start.2 = (bf16[1,3,128,320]{2,3,1,0:T(8,128)(2,1)S(1)}, bf16[1,3,128,320]{2,3,1,0:T(8,128)(2,1)}, u32[]{:S(2)}) copy-start(bf16[1,3,128,320]{2,3,1,0:T(8,128)(2,1)} %param.9) | copy-start | bytes 737284
  21.1 10.0 %copy-start.8 = (f32[320]{0:T(512)S(1)}, f32[320]{0:T(512)}, u32[]{:S(2)}) copy-start(f32[320]{0:T(512)} %param.12) | copy-start | bytes 3844
  21.1 10.0 %copy-start.9 = (f32[320]{0:T(512)S(1)}, f32[320]{0:T(512)}, u32[]{:S(2)}) copy-start(f32[320]{0:T(512)} %param.11) | copy-start | bytes 3844
  22.5 6.9 %collective-permute-start.4 = (bf16[1,128,320]{1,2,0:T(8,128)(2,1)S(1)}, bf16[1,128,320]{1,2,0:T(8,128)(2,1)S(1)}, u32[]{:S(2)}, u32[]{:S(2)}) collective-permute-start(bf16[1,128,320]{1,2,0:T(8,128)(2,1)S(1)} %get-tuple-element.24), channel_id=1, source_target_pairs={{8,0},{16,8},{24,16},{9,1},{17,9},{25,17},{10,2},{18,10},{26,18},{... | collective-permute-start | bytes 245768 | tf_op jit(solution)/shard_map/ppermute | solution.py:20
  23.8 6.6 %collective-permute-start.3 = (bf16[1,128,320]{1,2,0:T(8,128)(2,1)S(1)}, bf16[1,128,320]{1,2,0:T(8,128)(2,1)S(1)}, u32[]{:S(2)}, u32[]{:S(2)}) collective-permute-start(bf16[1,128,320]{1,2,0:T(8,128)(2,1)S(1)} %get-tuple-element.23), channel_id=1, source_target_pairs={{0,8},{8,16},{16,24},{1,9},{9,17},{17,25},{2,10},{10,18},{18,26},{... | collective-permute-start | bytes 245768 | tf_op jit(solution)/shard_map/ppermute | solution.py:18
  29.3 2.6 %copy-start.4 = (bf16[3,128,320]{1,2,0:T(8,128)(2,1)}, bf16[3,128,320]{1,2,0:T(8,128)(2,1)S(1)}, u32[]{:S(2)}) copy-start(bf16[3,128,320]{1,2,0:T(8,128)(2,1)S(1)} %bitcast_multiply_fusion) | copy-start | bytes 737284
  36.3 2.6 %collective-permute-start.5 = (bf16[4,360,320]{1,2,0:T(8,128)(2,1)S(1)}, bf16[4,360,320]{1,2,0:T(8,128)(2,1)S(1)}, u32[]{:S(2)}, u32[]{:S(2)}) collective-permute-start(bf16[4,360,320]{1,2,0:T(8,128)(2,1)S(1)} %copy.48), channel_id=1, source_target_pairs={{0,1},{1,0},{2,3},{3,2},{4,5},{5,4},{6,7},{7,6},{8,9},{9,8},{10,11... | collective-permute-start | bytes 2764808 | tf_op jit(solution)/shard_map/ppermute | solution.py:65
  42.5 10.0 %collective-permute-start.8 = (bf16[360,320]{0,1:T(8,128)(2,1)}, bf16[360,320]{0,1:T(8,128)(2,1)S(1)}, u32[]{:S(2)}, u32[]{:S(2)}) collective-permute-start(bf16[360,320]{0,1:T(8,128)(2,1)} %bitcast.100), channel_id=1, source_target_pairs={{0,6},{1,7},{2,4},{3,5},{4,2},{5,3},{6,0},{7,1},{8,14},{9,15},{10,... | collective-permute-start | bytes 691208 | tf_op jit(solution)/shard_map/ppermute | solution.py:78
  45.0 15.0 %copy-start.5 = (bf16[3,128,320]{1,2,0:T(8,128)(2,1)S(1)}, bf16[3,128,320]{1,2,0:T(8,128)(2,1)}, u32[]{:S(2)}) copy-start(bf16[3,128,320]{1,2,0:T(8,128)(2,1)} %copy-done.4) | copy-start | bytes 737284
  45.9 11.0 %collective-permute-start.7 = (bf16[360,320]{0,1:T(8,128)(2,1)}, bf16[360,320]{0,1:T(8,128)(2,1)S(1)}, u32[]{:S(2)}, u32[]{:S(2)}) collective-permute-start(bf16[360,320]{0,1:T(8,128)(2,1)} %bitcast.121), channel_id=1, source_target_pairs={{0,4},{1,5},{2,6},{3,7},{4,0},{5,1},{6,2},{7,3},{8,12},{9,13},{10,... | collective-permute-start | bytes 691208 | tf_op jit(solution)/shard_map/ppermute | solution.py:78
  47.2 9.9 %collective-permute-start.6 = (bf16[360,320]{0,1:T(8,128)(2,1)}, bf16[360,320]{0,1:T(8,128)(2,1)}, u32[]{:S(2)}, u32[]{:S(2)}) collective-permute-start(bf16[360,320]{0,1:T(8,128)(2,1)} %bitcast.102), channel_id=1, source_target_pairs={{0,2},{1,3},{2,0},{3,1},{4,6},{5,7},{6,4},{7,5},{8,10},{9,11},{10,... | collective-permute-start | bytes 691208 | tf_op jit(solution)/shard_map/ppermute | solution.py:78
  58.2 14.9 %collective-permute-start.9 = (bf16[360,320]{0,1:T(8,128)(2,1)S(1)}, bf16[360,320]{0,1:T(8,128)(2,1)S(1)}, u32[]{:S(2)}, u32[]{:S(2)}) collective-permute-start(bf16[360,320]{0,1:T(8,128)(2,1)S(1)} %fusion.38), channel_id=1, source_target_pairs={{0,16},{8,24},{16,0},{24,8},{1,17},{9,25},{17,1},{25,9},{2,18},{10... | collective-permute-start | bytes 691208 | tf_op jit(solution)/shard_map/ppermute | solution.py:91
  60.1 6.3 %collective-permute-start.11 = (bf16[1,128,320]{1,2,0:T(8,128)(2,1)S(1)}, bf16[1,128,320]{1,2,0:T(8,128)(2,1)S(1)}, u32[]{:S(2)}, u32[]{:S(2)}) collective-permute-start(bf16[1,128,320]{1,2,0:T(8,128)(2,1)S(1)} %get-tuple-element.22), channel_id=1, source_target_pairs={{8,0},{16,8},{24,16},{9,1},{17,9},{25,17},{10,2},{18,10},{26,18},{... | collective-permute-start | bytes 245768 | tf_op jit(solution)/shard_map/ppermute | solution.py:20
  61.4 6.6 %collective-permute-start.10 = (bf16[1,128,320]{1,2,0:T(8,128)(2,1)S(1)}, bf16[1,128,320]{1,2,0:T(8,128)(2,1)S(1)}, u32[]{:S(2)}, u32[]{:S(2)}) collective-permute-start(bf16[1,128,320]{1,2,0:T(8,128)(2,1)S(1)} %get-tuple-element.21), channel_id=1, source_target_pairs={{0,8},{8,16},{16,24},{1,9},{9,17},{17,25},{2,10},{10,18},{18,26},{... | collective-permute-start | bytes 245768 | tf_op jit(solution)/shard_map/ppermute | solution.py:18
  78.7 2.5 %copy-start.3 = (bf16[1,3,128,320]{2,3,1,0:T(8,128)(2,1)S(1)}, bf16[1,3,128,320]{2,3,1,0:T(8,128)(2,1)}, u32[]{:S(2)}) copy-start(bf16[1,3,128,320]{2,3,1,0:T(8,128)(2,1)} %param.9) | copy-start | bytes 737284
  86.1 15.8 %copy-start.6 = (f32[360,320]{0,1:T(8,128)S(1)}, f32[360,320]{0,1:T(8,128)}, u32[]{:S(2)}) copy-start(f32[360,320]{0,1:T(8,128)} %param.15) | copy-start | bytes 1382404
  86.1 10.2 %collective-permute-start.14 = (f32[2,32]{1,0:T(2,128)S(1)}, f32[2,32]{1,0:T(2,128)S(1)}, u32[]{:S(2)}, u32[]{:S(2)}) collective-permute-start(f32[2,32]{1,0:T(2,128)S(1)} %pad_maximum_fusion.3), channel_id=1, source_target_pairs={{0,24},{8,0},{16,8},{24,16},{1,25},{9,1},{17,9},{25,17},{2,26},{10... | collective-permute-start | bytes 776 | tf_op jit(solution)/shard_map/ppermute | solution.py:33
  89.3 7.0 %collective-permute-start.13 = (f32[2,32]{1,0:T(2,128)S(1)}, f32[2,32]{1,0:T(2,128)S(1)}, u32[]{:S(2)}, u32[]{:S(2)}) collective-permute-start(f32[2,32]{1,0:T(2,128)S(1)} %pad_maximum_fusion.3), channel_id=1, source_target_pairs={{0,16},{8,24},{16,0},{24,8},{1,17},{9,25},{17,1},{25,9},{2,18},{10... | collective-permute-start | bytes 776 | tf_op jit(solution)/shard_map/ppermute | solution.py:33
  89.5 6.8 %collective-permute-start.12 = (f32[2,32]{1,0:T(2,128)S(1)}, f32[2,32]{1,0:T(2,128)S(1)}, u32[]{:S(2)}, u32[]{:S(2)}) collective-permute-start(f32[2,32]{1,0:T(2,128)S(1)} %pad_maximum_fusion.3), channel_id=1, source_target_pairs={{0,8},{8,16},{16,24},{24,0},{1,9},{9,17},{17,25},{25,1},{2,10},{10... | collective-permute-start | bytes 776 | tf_op jit(solution)/shard_map/ppermute | solution.py:33
  94.8 7.0 %collective-permute-start.15 = (bf16[360,320]{0,1:T(8,128)(2,1)S(1)}, bf16[360,320]{0,1:T(8,128)(2,1)S(1)}, u32[]{:S(2)}, u32[]{:S(2)}) collective-permute-start(bf16[360,320]{0,1:T(8,128)(2,1)S(1)} %convert_add_fusion.1), channel_id=1, source_target_pairs={{0,8},{8,0},{16,24},{24,16},{1,9},{9,1},{17,25},{25,17},{2,10},{10... | collective-permute-start | bytes 691208 | tf_op jit(solution)/shard_map/ppermute | solution.py:91
  (3 other events, 4.9 us)
Sparse Core Ops, SparseCore 0:
  16.5 27.7 all-gather.2

commit v14 on v13

--- a/solution.py
+++ b/solution.py
@@ -64,6 +64,8 @@
         pairs = [(i, i ^ step) for i in range(count)]
         got = lax.ppermute(send.astype(jnp.bfloat16), axis, pairs)
         held = row_major(keep + got.astype(jnp.float32))
+        if step == 1:
+            held, companions = lax.optimization_barrier((held, companions))
         step *= 2
         if step < count <= 4 * step:
             break
@@ -146,8 +148,8 @@
         act_cols, flat_cot, (((0,), (0,)), ((), ())), preferred_element_type=jnp.float32
     )
     weight_terms = row_major(weight_terms)
-    grad_piece, companions = halving_scatter(weight_terms, "dp", (gathered, cot_pad))
-    grad_piece, (gathered, cot_pad) = replicated_sum(grad_piece, "space", companions)
+    grad_piece, cot_pad = halving_scatter(weight_terms, "dp", cot_pad)
+    grad_piece, (gathered, cot_pad) = replicated_sum(grad_piece, "space", (gathered, cot_pad))
     output = jnp.dot(act_cols, gathered, preferred_element_type=jnp.float32)
     block_out = (output.reshape(height_dev, width_dev, channels) * inside).astype(jnp.bfloat16)
     tap_weights = gathered.reshape(9, channels, channels)

time: 112 us -> 120 us (1.071)
  local copies, waits for them, and re-layouts: 16.4 us -> 20.6 us
  waiting for transfers between devices: 27 us -> 29.6 us
  starting transfers between devices: 30 us -> 31.4 us
    ppermute x2, waiting for transfers between devices: 7.91 us -> 13.3 us  [replicated_sum(): lax.ppermute(mine, axis, pairs).astype(jnp.float32)]
    ppermute x2, starting transfers between devices: 3.34 us -> 6.25 us  [replicated_sum(): lax.ppermute(mine, axis, pairs).astype(jnp.float32)]
    unnamed x36 -> x27, local copies, waits for them, and re-layouts: 7.58 us -> 5 us
    ppermute x1, waiting for transfers between devices: 2.51 us -> 0.01 us  [halving_scatter(): got = lax.ppermute(send.astype(jnp.bfloat16), axis, pairs)]
    convert_element_type x0 -> x1, local copies, waits for them, and re-layouts: none -> 2.03 us  [halving_scatter(): send.astype(jnp.bfloat16)]
    dynamic_slice x2, local copies, waits for them, and re-layouts: 0.25 us -> 2.1 us  [halving_scatter(): total = lax.dynamic_index_in_dim(held, own, keepdims=False)]
    ppermute x6, starting transfers between devices: 11.3 us -> 9.49 us  [space_sum(): lax.ppermute(joined, axis, [(i, (i + shift) % count) for i in range(count)])]
    ppermute x1, local copies, waits for them, and re-layouts: 0.73 us -> 2.35 us  [halving_scatter(): got = lax.ppermute(send.astype(jnp.bfloat16), axis, pairs)]
  transfers between devices with their start and end apart: 17 -> 17, of which waited for: 12 -> 11; matrix products, arithmetic and copies ran while one was open for 17% -> 20% of each run, Pallas kernels for 0% -> 0%
where the time goes in v14:
time: 120 us
  starting transfers between devices  31.4 us (26%)
  waiting for transfers between devices  29.6 us (25%)
  local copies, waits for them, and re-layouts  20.6 us (17%)
  between operations  15.8 us (13%)
  other arithmetic  13 us (11%)
  matrix products  9.45 us (8%)
    ppermute x2, waiting for transfers between devices, replicated_sum(): lax.ppermute(mine, axis, pairs).astype(jnp.float32)  13.3 us
    ppermute x6, starting transfers between devices, space_sum(): lax.ppermute(joined, axis, [(i, (i + shift) % count) for i in range(count)])  9.49 us
    ppermute x2, starting transfers between devices, with_halo(): lax.ppermute(tail, axis, [(i, (i + 1) % count) for i in range(ends)])  9.46 us
    ppermute x3, waiting for transfers between devices, halving_scatter(): lax.ppermute(send.astype(jnp.bfloat16), axis, pairs).astype(jnp.float32)  8.56 us
    ppermute x2, starting transfers between devices, replicated_sum(): lax.ppermute(mine, axis, pairs).astype(jnp.float32)  6.25 us
    unnamed x27, local copies, waits for them, and re-layouts  5 us
    dot_general x1, matrix products, local(): upstream = jnp.dot(cot_cols, flipped, preferred_element_type=jnp.float32)  4.4 us
    ppermute x6, waiting for transfers between devices, space_sum(): lax.ppermute(joined, axis, [(i, (i + shift) % count) for i in range(count)])  4.33 us
  transfers between devices with their start and end apart: 17, of which 11 were waited for; matrix products, arithmetic and copies ran while one was open for 20% of the time, Pallas kernels for 0%

profile of v14, /device:TPU:0, one launch (start us, length us, event | category | flops | bytes accessed | tf_op | source)
XLA Modules:
  0.0 119.8 jit_solution(8500427018834849538)
XLA Ops:
  10.2 5.1 %collective-permute-start.2 = (f32[2,32]{1,0:T(2,128)S(1)}, f32[2,32]{1,0:T(2,128)S(1)}, u32[]{:S(2)}, u32[]{:S(2)}) collective-permute-start(f32[2,32]{1,0:T(2,128)S(1)} %pad_maximum_fusion.2), channel_id=1, source_target_pairs={{0,24},{8,0},{16,8},{24,16},{1,25},{9,1},{17,9},{25,17},{2,26},{10... | collective-permute-start | bytes 776 | tf_op jit(solution)/shard_map/ppermute | solution.py:33
  16.6 3.2 %collective-permute-done.1 = f32[2,32]{1,0:T(2,128)S(1)} collective-permute-done((f32[2,32]{1,0:T(2,128)S(1)}, f32[2,32]{1,0:T(2,128)S(1)}, u32[]{:S(2)}, u32[]{:S(2)}) %collective-permute-start.1) | collective-permute-done | bytes 288 | tf_op jit(solution)/shard_map/ppermute | solution.py:33
  23.8 4.6 %collective-permute-start.3 = (bf16[1,128,320]{1,2,0:T(8,128)(2,1)S(1)}, bf16[1,128,320]{1,2,0:T(8,128)(2,1)S(1)}, u32[]{:S(2)}, u32[]{:S(2)}) collective-permute-start(bf16[1,128,320]{1,2,0:T(8,128)(2,1)S(1)} %get-tuple-element.27), channel_id=1, source_target_pairs={{0,8},{8,16},{16,24},{1,9},{9,17},{17,25},{2,10},{10,18},{18,26},{... | collective-permute-start | bytes 245768 | tf_op jit(solution)/shard_map/ppermute | solution.py:18
  31.9 1.5 %fusion.51 = f32[2880,320,1]{1,0,2:T(8,128)S(1)} fusion(bf16[3,128,2880]{1,2,0:T(8,128)(2,1)S(1)} %slice_dynamic-update-slice_fusion, bf16[3,128,320]{1,2,0:T(8,128)(2,1)S(1)} %bitcast_multiply_fusion), kind=kOutput, calls=%fused_computation.96 | convolution fusion | flops 707788800 | bytes 6144000 | tf_op jit(solution)/shard_map/dot_general | solution.py:147
  33.5 2.0 %copy-done = f32[2880,320,1]{1,0,2:T(8,128)} copy-done((f32[2880,320,1]{1,0,2:T(8,128)}, f32[2880,320,1]{1,0,2:T(8,128)S(1)}, u32[]{:S(2)}) %copy-start) | copy-done | bytes 3686424
  37.7 4.9 %collective-permute-start.6 = (bf16[1,128,320]{1,2,0:T(8,128)(2,1)S(1)}, bf16[1,128,320]{1,2,0:T(8,128)(2,1)S(1)}, u32[]{:S(2)}, u32[]{:S(2)}) collective-permute-start(bf16[1,128,320]{1,2,0:T(8,128)(2,1)S(1)} %get-tuple-element.25), channel_id=1, source_target_pairs={{0,8},{8,16},{16,24},{1,9},{9,17},{17,25},{2,10},{10,18},{18,26},{... | collective-permute-start | bytes 245768 | tf_op jit(solution)/shard_map/ppermute | solution.py:18
  45.4 2.4 %copy.49 = bf16[4,360,320]{2,1,0:T(8,128)(2,1)} copy(bf16[4,360,320]{1,2,0:T(8,128)(2,1)} %collective-permute-done.5) | data formatting | bytes 1843200 | tf_op jit(solution)/shard_map/ppermute | solution.py:65
  47.7 2.1 %bitcast_add_fusion = f32[4,360,320]{2,1,0:T(8,128)S(1)} fusion(bf16[4,360,320]{2,1,0:T(8,128)(2,1)} %copy.49, f32[4,2,360,320]{3,2,1,0:T(8,128)} %bitcast.113, s32[]{:T(128)S(6)} %select_n.33), kind=kLoop, calls=%fused_computation.3 | loop fusion | flops 921600 | bytes 4608004 | tf_op jit(solution)/shard_map/add | solution.py:66
  49.9 1.4 %copy.51 = bf16[4,360,320]{1,2,0:T(8,128)(2,1)} copy(f32[4,360,320]{2,1,0:T(8,128)S(1)} %bitcast_add_fusion) | data formatting | bytes 2764800 | tf_op jit(solution)/shard_map/optimization_barrier | solution.py:68
  51.3 2.0 %fusion.39 = (bf16[360,320]{0,1:T(8,128)(2,1)S(1)}, bf16[360,320]{0,1:T(8,128)(2,1)}, bf16[360,320]{0,1:T(8,128)(2,1)}) fusion(bf16[4,360,320]{1,2,0:T(8,128)(2,1)} %copy.51, s32[]{:T(128)S(6)} %select_n.37, s32[]{:T(128)S(6)} %select_n.39, s32[]{:T(128)S(6)} %select_n.38), kind=kLoop, calls=%fused_computation.53 | loop fusion | bytes 1382412 | tf_op jit(solution)/shard_map/convert_element_type | solution.py:80
  53.3 2.5 %collective-permute-start.10 = (bf16[360,320]{0,1:T(8,128)(2,1)}, bf16[360,320]{0,1:T(8,128)(2,1)}, u32[]{:S(2)}, u32[]{:S(2)}) collective-permute-start(bf16[360,320]{0,1:T(8,128)(2,1)} %get-tuple-element.23), channel_id=1, source_target_pairs={{0,6},{1,7},{2,4},{3,5},{4,2},{5,3},{6,0},{7,1},{8,14},{9,15},{10,... | collective-permute-start | bytes 691208 | tf_op jit(solution)/shard_map/ppermute | solution.py:80
  58.9 4.5 %collective-permute-done.10 = bf16[360,320]{0,1:T(8,128)(2,1)} collective-permute-done((bf16[360,320]{0,1:T(8,128)(2,1)}, bf16[360,320]{0,1:T(8,128)(2,1)}, u32[]{:S(2)}, u32[]{:S(2)}) %collective-permute-start.10) | collective-permute-done | bytes 230432 | tf_op jit(solution)/shard_map/ppermute | solution.py:80
  63.4 3.9 %collective-permute-done.9 = bf16[360,320]{0,1:T(8,128)(2,1)} collective-permute-done((bf16[360,320]{0,1:T(8,128)(2,1)}, bf16[360,320]{0,1:T(8,128)(2,1)}, u32[]{:S(2)}, u32[]{:S(2)}) %collective-permute-start.9) | collective-permute-done | bytes 230432 | tf_op jit(solution)/shard_map/ppermute | solution.py:80
  68.8 3.4 %collective-permute-start.11 = (bf16[360,320]{0,1:T(8,128)(2,1)S(1)}, bf16[360,320]{0,1:T(8,128)(2,1)S(1)}, u32[]{:S(2)}, u32[]{:S(2)}) collective-permute-start(bf16[360,320]{0,1:T(8,128)(2,1)S(1)} %fusion.38), channel_id=1, source_target_pairs={{0,16},{8,24},{16,0},{24,8},{1,17},{9,25},{17,1},{25,9},{2,18},{10... | collective-permute-start | bytes 691208 | tf_op jit(solution)/shard_map/ppermute | solution.py:93
  72.2 11.3 %collective-permute-done.11 = bf16[360,320]{0,1:T(8,128)(2,1)S(1)} collective-permute-done((bf16[360,320]{0,1:T(8,128)(2,1)S(1)}, bf16[360,320]{0,1:T(8,128)(2,1)S(1)}, u32[]{:S(2)}, u32[]{:S(2)}) %collective-permute-start.11) | collective-permute-done | bytes 230432 | tf_op jit(solution)/shard_map/ppermute | solution.py:93
  83.6 3.0 %copy.56 = bf16[8,360,320]{2,1,0:T(8,128)(2,1)S(1)} copy(bf16[8,360,320]{1,2,0:T(8,128)(2,1)} %all-gather.3.cloned.1.call-done) | data formatting | bytes 3686400 | tf_op jit(solution)/shard_map/all_gather | solution.py:124
  89.2 2.5 %copy.58 = bf16[9,320,320]{1,2,0:T(8,128)(2,1)} copy(bf16[9,320,320]{2,1,0:T(8,128)(2,1)S(1)} %bitcast.114) | data formatting | bytes 3686400 | tf_op jit(solution)/shard_map/reshape | solution.py:155
  91.6 4.4 %fusion.48 = (f32[320]{0:T(512)S(1)}, f32[320]{0:T(512)S(1)}, f32[3,128,320]{1,2,0:T(8,128)}) fusion(f32[320]{0:T(512)S(1)} %mul.163, f32[320]{0:T(512)S(1)} %sub.37, f32[3,128]{1,0:T(4,128)S(1)} %get-tuple-element.32, bf16[1,3,128,320]{2,3,1,0:T(8,128)(2,1)S(1)} %copy-done.2, f32[320]{0:T(512)S(1)} %copy-done.5, f32[320]{0:T(512)S(1)} %copy-done.6, ...), kind=kOutput, calls=%fused_computation.93 | convolution fusion | flops 710245760 | bytes 4801536 | tf_op jit(solution)/shard_map/dot_general | solution.py:165
  96.5 2.7 %collective-permute-start.14 = (f32[2,32]{1,0:T(2,128)S(1)}, f32[2,32]{1,0:T(2,128)S(1)}, u32[]{:S(2)}, u32[]{:S(2)}) collective-permute-start(f32[2,32]{1,0:T(2,128)S(1)} %pad_maximum_fusion.3), channel_id=1, source_target_pairs={{0,24},{8,0},{16,8},{24,16},{1,25},{9,1},{17,9},{25,17},{2,26},{10... | collective-permute-start | bytes 776 | tf_op jit(solution)/shard_map/ppermute | solution.py:33
  99.9 3.5 %fusion.11 = bf16[1,3,128,320]{2,3,1,0:T(8,128)(2,1)} fusion(bf16[3,128,2880]{1,2,0:T(8,128)(2,1)} %copy-done.1, bf16[2880,320]{1,0:T(8,128)(2,1)S(1)} %bitcast.115, f32[3,128]{1,0:T(4,128)S(1)} %get-tuple-element.32), kind=kOutput, calls=%fused_computation.12 | convolution fusion | flops 708034560 | bytes 4302336 | tf_op jit(solution)/shard_map/dot_general | solution.py:153
  103.4 2.8 %collective-permute-start.15 = (bf16[360,320]{0,1:T(8,128)(2,1)S(1)}, bf16[360,320]{0,1:T(8,128)(2,1)S(1)}, u32[]{:S(2)}, u32[]{:S(2)}) collective-permute-start(bf16[360,320]{0,1:T(8,128)(2,1)S(1)} %convert_add_fusion.1), channel_id=1, source_target_pairs={{0,8},{8,0},{16,24},{24,16},{1,9},{9,1},{17,25},{25,17},{2,10},{10... | collective-permute-start | bytes 691208 | tf_op jit(solution)/shard_map/ppermute | solution.py:93
  106.7 2.0 %fusion.44 = bf16[1,3,128,320]{2,3,1,0:T(8,128)(2,1)} fusion(f32[320]{0:T(512)S(1)} %mul.180, f32[320]{0:T(512)S(1)} %sub.37, f32[3,128]{1,0:T(4,128)S(1)} %get-tuple-element.32, bf16[1,3,128,320]{2,3,1,0:T(8,128)(2,1)S(1)} %copy-done.2, f32[3,128,320]{1,2,0:T(8,128)} %get-tuple-element.33, f32[320]{0:T(512)S(1)} %sub.44, f32[320]{0:T(512)S(1)} %mul.163), kind=kLoop, calls=%fused_computation.76 | loop fusion | flops 1351680 | bytes 989696 | tf_op jit(solution)/shard_map/broadcast_in_dim | solution.py:183
  108.6 2.0 %collective-permute-done.15 = bf16[360,320]{0,1:T(8,128)(2,1)S(1)} collective-permute-done((bf16[360,320]{0,1:T(8,128)(2,1)S(1)}, bf16[360,320]{0,1:T(8,128)(2,1)S(1)}, u32[]{:S(2)}, u32[]{:S(2)}) %collective-permute-start.15) | collective-permute-done | bytes 230432 | tf_op jit(solution)/shard_map/ppermute | solution.py:93
  110.7 2.3 %fusion.35 = (f32[360,320]{0,1:T(8,128)}, f32[360,320]{0,1:T(8,128)}) fusion(f32[360,320]{0,1:T(8,128)S(1)} %copy-done.3, f32[360,320]{0,1:T(8,128)} %param.14, bf16[360,320]{0,1:T(8,128)(2,1)S(1)} %collective-permute-done.15, bf16[360,320]{0,1:T(8,128)(2,1)S(1)} %convert_add_fusion.1), kind=kLoop, calls=%fused_computation.41 | loop fusion | flops 1612800 | bytes 2304000 | tf_op jit(solution)/shard_map/div | solution.py:182
  (92 shorter events, 23.9 us)
Async XLA Ops:
  7.2 76.4 %all-gather.3.cloned.1.call-start = ((), (), s32[]{:S(2)}) async-start(), calls=%async_computation | async-start | bytes 2211840 | tf_op jit(solution)/shard_map/all_gather | solution.py:124
  10.2 6.4 %collective-permute-start.2 = (f32[2,32]{1,0:T(2,128)S(1)}, f32[2,32]{1,0:T(2,128)S(1)}, u32[]{:S(2)}, u32[]{:S(2)}) collective-permute-start(f32[2,32]{1,0:T(2,128)S(1)} %pad_maximum_fusion.2), channel_id=1, source_target_pairs={{0,24},{8,0},{16,8},{24,16},{1,25},{9,1},{17,9},{25,17},{2,26},{10... | collective-permute-start | bytes 776 | tf_op jit(solution)/shard_map/ppermute | solution.py:33
  15.3 4.5 %collective-permute-start.1 = (f32[2,32]{1,0:T(2,128)S(1)}, f32[2,32]{1,0:T(2,128)S(1)}, u32[]{:S(2)}, u32[]{:S(2)}) collective-permute-start(f32[2,32]{1,0:T(2,128)S(1)} %pad_maximum_fusion.2), channel_id=1, source_target_pairs={{0,16},{8,24},{16,0},{24,8},{1,17},{9,25},{17,1},{25,9},{2,18},{10... | collective-permute-start | bytes 776 | tf_op jit(solution)/shard_map/ppermute | solution.py:33
  15.3 5.4 %collective-permute-start = (f32[2,32]{1,0:T(2,128)S(1)}, f32[2,32]{1,0:T(2,128)S(1)}, u32[]{:S(2)}, u32[]{:S(2)}) collective-permute-start(f32[2,32]{1,0:T(2,128)S(1)} %pad_maximum_fusion.2), channel_id=1, source_target_pairs={{0,8},{8,16},{16,24},{24,0},{1,9},{9,17},{17,25},{25,1},{2,10},{10... | collective-permute-start | bytes 776 | tf_op jit(solution)/shard_map/ppermute | solution.py:33
  21.1 10.0 %copy-start.2 = (bf16[1,3,128,320]{2,3,1,0:T(8,128)(2,1)S(1)}, bf16[1,3,128,320]{2,3,1,0:T(8,128)(2,1)}, u32[]{:S(2)}) copy-start(bf16[1,3,128,320]{2,3,1,0:T(8,128)(2,1)} %param.9) | copy-start | bytes 737284
  21.1 10.0 %copy-start.5 = (f32[320]{0:T(512)S(1)}, f32[320]{0:T(512)}, u32[]{:S(2)}) copy-start(f32[320]{0:T(512)} %param.12) | copy-start | bytes 3844
  21.1 10.0 %copy-start.6 = (f32[320]{0:T(512)S(1)}, f32[320]{0:T(512)}, u32[]{:S(2)}) copy-start(f32[320]{0:T(512)} %param.11) | copy-start | bytes 3844
  22.5 6.8 %collective-permute-start.4 = (bf16[1,128,320]{1,2,0:T(8,128)(2,1)S(1)}, bf16[1,128,320]{1,2,0:T(8,128)(2,1)S(1)}, u32[]{:S(2)}, u32[]{:S(2)}) collective-permute-start(bf16[1,128,320]{1,2,0:T(8,128)(2,1)S(1)} %get-tuple-element.28), channel_id=1, source_target_pairs={{8,0},{16,8},{24,16},{9,1},{17,9},{25,17},{10,2},{18,10},{26,18},{... | collective-permute-start | bytes 245768 | tf_op jit(solution)/shard_map/ppermute | solution.py:20
  23.8 6.6 %collective-permute-start.3 = (bf16[1,128,320]{1,2,0:T(8,128)(2,1)S(1)}, bf16[1,128,320]{1,2,0:T(8,128)(2,1)S(1)}, u32[]{:S(2)}, u32[]{:S(2)}) collective-permute-start(bf16[1,128,320]{1,2,0:T(8,128)(2,1)S(1)} %get-tuple-element.27), channel_id=1, source_target_pairs={{0,8},{8,16},{16,24},{1,9},{9,17},{17,25},{2,10},{10,18},{18,26},{... | collective-permute-start | bytes 245768 | tf_op jit(solution)/shard_map/ppermute | solution.py:18
  31.9 1.5 %copy-start.1 = (bf16[3,128,2880]{1,2,0:T(8,128)(2,1)}, bf16[3,128,2880]{1,2,0:T(8,128)(2,1)S(1)}, u32[]{:S(2)}) copy-start(bf16[3,128,2880]{1,2,0:T(8,128)(2,1)S(1)} %slice_dynamic-update-slice_fusion) | copy-start | bytes 6635524
  33.5 2.0 %copy-start = (f32[2880,320,1]{1,0,2:T(8,128)}, f32[2880,320,1]{1,0,2:T(8,128)S(1)}, u32[]{:S(2)}) copy-start(f32[2880,320,1]{1,0,2:T(8,128)S(1)} %fusion.51) | copy-start | bytes 11059204
  36.3 9.0 %collective-permute-start.5 = (bf16[4,360,320]{1,2,0:T(8,128)(2,1)S(1)}, bf16[4,360,320]{1,2,0:T(8,128)(2,1)}, u32[]{:S(2)}, u32[]{:S(2)}) collective-permute-start(bf16[4,360,320]{1,2,0:T(8,128)(2,1)S(1)} %copy.48), channel_id=1, source_target_pairs={{0,1},{1,0},{2,3},{3,2},{4,5},{5,4},{6,7},{7,6},{8,9},{9,8},{10,11... | collective-permute-start | bytes 2764808 | tf_op jit(solution)/shard_map/ppermute | solution.py:65
  36.4 7.4 %collective-permute-start.7 = (bf16[1,128,320]{1,2,0:T(8,128)(2,1)S(1)}, bf16[1,128,320]{1,2,0:T(8,128)(2,1)S(1)}, u32[]{:S(2)}, u32[]{:S(2)}) collective-permute-start(bf16[1,128,320]{1,2,0:T(8,128)(2,1)S(1)} %get-tuple-element.26), channel_id=1, source_target_pairs={{8,0},{16,8},{24,16},{9,1},{17,9},{25,17},{10,2},{18,10},{26,18},{... | collective-permute-start | bytes 245768 | tf_op jit(solution)/shard_map/ppermute | solution.py:20
  37.7 7.3 %collective-permute-start.6 = (bf16[1,128,320]{1,2,0:T(8,128)(2,1)S(1)}, bf16[1,128,320]{1,2,0:T(8,128)(2,1)S(1)}, u32[]{:S(2)}, u32[]{:S(2)}) collective-permute-start(bf16[1,128,320]{1,2,0:T(8,128)(2,1)S(1)} %get-tuple-element.25), channel_id=1, source_target_pairs={{0,8},{8,16},{16,24},{1,9},{9,17},{17,25},{2,10},{10,18},{18,26},{... | collective-permute-start | bytes 245768 | tf_op jit(solution)/shard_map/ppermute | solution.py:18
  53.3 10.1 %collective-permute-start.10 = (bf16[360,320]{0,1:T(8,128)(2,1)}, bf16[360,320]{0,1:T(8,128)(2,1)}, u32[]{:S(2)}, u32[]{:S(2)}) collective-permute-start(bf16[360,320]{0,1:T(8,128)(2,1)} %get-tuple-element.23), channel_id=1, source_target_pairs={{0,6},{1,7},{2,4},{3,5},{4,2},{5,3},{6,0},{7,1},{8,14},{9,15},{10,... | collective-permute-start | bytes 691208 | tf_op jit(solution)/shard_map/ppermute | solution.py:80
  55.8 11.6 %collective-permute-start.9 = (bf16[360,320]{0,1:T(8,128)(2,1)}, bf16[360,320]{0,1:T(8,128)(2,1)}, u32[]{:S(2)}, u32[]{:S(2)}) collective-permute-start(bf16[360,320]{0,1:T(8,128)(2,1)} %get-tuple-element.24), channel_id=1, source_target_pairs={{0,4},{1,5},{2,6},{3,7},{4,0},{5,1},{6,2},{7,3},{8,12},{9,13},{10,... | collective-permute-start | bytes 691208 | tf_op jit(solution)/shard_map/ppermute | solution.py:80
  56.3 11.2 %collective-permute-start.8 = (bf16[360,320]{0,1:T(8,128)(2,1)S(1)}, bf16[360,320]{0,1:T(8,128)(2,1)}, u32[]{:S(2)}, u32[]{:S(2)}) collective-permute-start(bf16[360,320]{0,1:T(8,128)(2,1)S(1)} %get-tuple-element.22), channel_id=1, source_target_pairs={{0,2},{1,3},{2,0},{3,1},{4,6},{5,7},{6,4},{7,5},{8,10},{9,11},{10,... | collective-permute-start | bytes 691208 | tf_op jit(solution)/shard_map/ppermute | solution.py:80
  68.8 14.7 %collective-permute-start.11 = (bf16[360,320]{0,1:T(8,128)(2,1)S(1)}, bf16[360,320]{0,1:T(8,128)(2,1)S(1)}, u32[]{:S(2)}, u32[]{:S(2)}) collective-permute-start(bf16[360,320]{0,1:T(8,128)(2,1)S(1)} %fusion.38), channel_id=1, source_target_pairs={{0,16},{8,24},{16,0},{24,8},{1,17},{9,25},{17,1},{25,9},{2,18},{10... | collective-permute-start | bytes 691208 | tf_op jit(solution)/shard_map/ppermute | solution.py:93
  87.8 1.4 %copy-start.4 = (bf16[3,128,2880]{1,2,0:T(8,128)(2,1)}, bf16[3,128,2880]{1,2,0:T(8,128)(2,1)S(1)}, u32[]{:S(2)}) copy-start(bf16[3,128,2880]{1,2,0:T(8,128)(2,1)S(1)} %slice_dynamic-update-slice_fusion.6) | copy-start | bytes 6635524
  96.5 14.2 %copy-start.3 = (f32[360,320]{0,1:T(8,128)S(1)}, f32[360,320]{0,1:T(8,128)}, u32[]{:S(2)}) copy-start(f32[360,320]{0,1:T(8,128)} %param.15) | copy-start | bytes 1382404
  96.5 9.8 %collective-permute-start.14 = (f32[2,32]{1,0:T(2,128)S(1)}, f32[2,32]{1,0:T(2,128)S(1)}, u32[]{:S(2)}, u32[]{:S(2)}) collective-permute-start(f32[2,32]{1,0:T(2,128)S(1)} %pad_maximum_fusion.3), channel_id=1, source_target_pairs={{0,24},{8,0},{16,8},{24,16},{1,25},{9,1},{17,9},{25,17},{2,26},{10... | collective-permute-start | bytes 776 | tf_op jit(solution)/shard_map/ppermute | solution.py:33
  99.2 7.0 %collective-permute-start.13 = (f32[2,32]{1,0:T(2,128)S(1)}, f32[2,32]{1,0:T(2,128)S(1)}, u32[]{:S(2)}, u32[]{:S(2)}) collective-permute-start(f32[2,32]{1,0:T(2,128)S(1)} %pad_maximum_fusion.3), channel_id=1, source_target_pairs={{0,16},{8,24},{16,0},{24,8},{1,17},{9,25},{17,1},{25,9},{2,18},{10... | collective-permute-start | bytes 776 | tf_op jit(solution)/shard_map/ppermute | solution.py:33
  99.2 7.0 %collective-permute-start.12 = (f32[2,32]{1,0:T(2,128)S(1)}, f32[2,32]{1,0:T(2,128)S(1)}, u32[]{:S(2)}, u32[]{:S(2)}) collective-permute-start(f32[2,32]{1,0:T(2,128)S(1)} %pad_maximum_fusion.3), channel_id=1, source_target_pairs={{0,8},{8,16},{16,24},{24,0},{1,9},{9,17},{17,25},{25,1},{2,10},{10... | collective-permute-start | bytes 776 | tf_op jit(solution)/shard_map/ppermute | solution.py:33
  103.4 7.3 %collective-permute-start.15 = (bf16[360,320]{0,1:T(8,128)(2,1)S(1)}, bf16[360,320]{0,1:T(8,128)(2,1)S(1)}, u32[]{:S(2)}, u32[]{:S(2)}) collective-permute-start(bf16[360,320]{0,1:T(8,128)(2,1)S(1)} %convert_add_fusion.1), channel_id=1, source_target_pairs={{0,8},{8,0},{16,24},{24,16},{1,9},{9,1},{17,25},{25,17},{2,10},{10... | collective-permute-start | bytes 691208 | tf_op jit(solution)/shard_map/ppermute | solution.py:93
Sparse Core Ops, SparseCore 0:
  16.5 27.7 all-gather.2

commit v15 on v9

--- a/solution.py
+++ b/solution.py
@@ -63,7 +63,7 @@
         send = row_major(lax.dynamic_index_in_dim(paired, 1 - bit, axis=1, keepdims=False))
         pairs = [(i, i ^ step) for i in range(count)]
         got = lax.ppermute(send.astype(jnp.bfloat16), axis, pairs)
-        held = row_major(keep + got.astype(jnp.float32))
+        held = row_major(keep.astype(jnp.float32) + got.astype(jnp.float32))
         step *= 2
         if step < count <= 4 * step:
             break
@@ -144,7 +144,7 @@
     flat_cot = masked.reshape(-1, channels)
     weight_terms = lax.dot_general(
         act_cols, flat_cot, (((0,), (0,)), ((), ())), preferred_element_type=jnp.float32
-    )
+    ).astype(jnp.bfloat16)
     weight_terms = row_major(weight_terms)
     grad_piece, companions = halving_scatter(weight_terms, "dp", (gathered, cot_pad))
     grad_piece, (gathered, cot_pad) = replicated_sum(grad_piece, "space", companions)

time: 111 us -> 109 us (0.982)
  other arithmetic: 12.4 us -> 9.88 us
    unnamed x36, local copies, waits for them, and re-layouts: 7.58 us -> 4.89 us
    add x1, other arithmetic: 1.83 us -> 0.22 us  [halving_scatter(): held = row_major(keep.astype(jnp.float32) + got.astype(jnp.float32))]
    another operation x0 -> x1, local copies, waits for them, and re-layouts: none -> 1.39 us  [row_major(): with_layout_constraint(value, Layout(major_to_minor=tuple(range(value.ndi...]
  transfers between devices with their start and end apart: 17 -> 17, of which waited for: 10 -> 11; matrix products, arithmetic and copies ran while one was open for 18% -> 16% of each run, Pallas kernels for 0% -> 0%
where the time goes in v15:
time: 109 us
  starting transfers between devices  30.1 us (28%)
  waiting for transfers between devices  27.2 us (25%)
  local copies, waits for them, and re-layouts  16.3 us (15%)
  between operations  15.8 us (14%)
  other arithmetic  9.88 us (9%)
  matrix products  9.47 us (9%)
    ppermute x6, starting transfers between devices, space_sum(): lax.ppermute(joined, axis, [(i, (i + shift) % count) for i in range(count)])  10.4 us
    ppermute x3, waiting for transfers between devices, halving_scatter(): lax.ppermute(send.astype(jnp.bfloat16), axis, pairs).astype(jnp.float32)  9.32 us
    ppermute x2, starting transfers between devices, with_halo(): lax.ppermute(tail, axis, [(i, (i + 1) % count) for i in range(ends)])  9.1 us
    ppermute x2, waiting for transfers between devices, replicated_sum(): lax.ppermute(mine, axis, pairs).astype(jnp.float32)  7.44 us
    unnamed x36, local copies, waits for them, and re-layouts  4.89 us
    dot_general x1, matrix products, local(): upstream = jnp.dot(cot_cols, flipped, preferred_element_type=jnp.float32)  4.4 us
    ppermute x6, waiting for transfers between devices, space_sum(): lax.ppermute(joined, axis, [(i, (i + shift) % count) for i in range(count)])  4.33 us
    ppermute x2, starting transfers between devices, replicated_sum(): lax.ppermute(mine, axis, pairs).astype(jnp.float32)  4.3 us
  transfers between devices with their start and end apart: 17, of which 11 were waited for; matrix products, arithmetic and copies ran while one was open for 16% of the time, Pallas kernels for 0%

profile of v15, /device:TPU:0, one launch (start us, length us, event | category | flops | bytes accessed | tf_op | source)
XLA Modules:
  0.0 108.7 jit_solution(8678140589697739668)
XLA Ops:
  10.2 5.1 %collective-permute-start.2 = (f32[2,32]{1,0:T(2,128)S(1)}, f32[2,32]{1,0:T(2,128)S(1)}, u32[]{:S(2)}, u32[]{:S(2)}) collective-permute-start(f32[2,32]{1,0:T(2,128)S(1)} %pad_maximum_fusion.2), channel_id=1, source_target_pairs={{0,24},{8,0},{16,8},{24,16},{1,25},{9,1},{17,9},{25,17},{2,26},{10... | collective-permute-start | bytes 776 | tf_op jit(solution)/shard_map/ppermute | solution.py:33
  16.6 3.2 %collective-permute-done.1 = f32[2,32]{1,0:T(2,128)S(1)} collective-permute-done((f32[2,32]{1,0:T(2,128)S(1)}, f32[2,32]{1,0:T(2,128)S(1)}, u32[]{:S(2)}, u32[]{:S(2)}) %collective-permute-start.1) | collective-permute-done | bytes 288 | tf_op jit(solution)/shard_map/ppermute | solution.py:33
  23.8 4.6 %collective-permute-start.3 = (bf16[1,128,320]{1,2,0:T(8,128)(2,1)S(1)}, bf16[1,128,320]{1,2,0:T(8,128)(2,1)S(1)}, u32[]{:S(2)}, u32[]{:S(2)}) collective-permute-start(bf16[1,128,320]{1,2,0:T(8,128)(2,1)S(1)} %get-tuple-element.23), channel_id=1, source_target_pairs={{0,8},{8,16},{16,24},{1,9},{9,17},{17,25},{2,10},{10,18},{18,26},{... | collective-permute-start | bytes 245768 | tf_op jit(solution)/shard_map/ppermute | solution.py:18
  31.9 1.5 %fusion = bf16[2880,320]{1,0:T(8,128)(2,1)S(1)} fusion(bf16[3,128,2880]{1,2,0:T(8,128)(2,1)S(1)} %slice_dynamic-update-slice_fusion, bf16[3,128,320]{1,2,0:T(8,128)(2,1)S(1)} %bitcast_multiply_fusion), kind=kOutput, calls=%fused_computation.1 | convolution fusion | flops 708710400 | bytes 4300800 | tf_op jit(solution)/shard_map/dot_general | solution.py:145
  33.6 1.4 %copy.34 = bf16[4,360,320]{1,2,0:T(8,128)(2,1)} copy(bf16[4,360,320]{2,1,0:T(8,128)(2,1)S(1)} %dynamic-slice_bitcast_fusion) | data formatting | bytes 1843200 | tf_op jit(solution)/shard_map/layout_constraint | solution.py:42
  35.0 3.0 %collective-permute-done.5 = bf16[4,360,320]{1,2,0:T(8,128)(2,1)} collective-permute-done((bf16[4,360,320]{1,2,0:T(8,128)(2,1)}, bf16[4,360,320]{1,2,0:T(8,128)(2,1)}, u32[]{:S(2)}, u32[]{:S(2)}) %collective-permute-start.5) | collective-permute-done | bytes 921632 | tf_op jit(solution)/shard_map/ppermute | solution.py:65
  38.0 1.6 %copy.35 = bf16[4,360,320]{2,1,0:T(8,128)(2,1)S(1)} copy(bf16[4,360,320]{1,2,0:T(8,128)(2,1)} %collective-permute-done.5) | data formatting | bytes 1843200 | tf_op jit(solution)/shard_map/ppermute | solution.py:65
  39.9 1.3 %copy-done.1 = f32[4,360,320]{2,1,0:T(8,128)} copy-done((f32[4,360,320]{2,1,0:T(8,128)}, f32[4,360,320]{2,1,0:T(8,128)S(1)}, u32[]{:S(2)}) %copy-start.1) | copy-done | bytes 1843224
  41.5 2.7 %collective-permute-start.8 = (bf16[360,320]{0,1:T(8,128)(2,1)S(1)}, bf16[360,320]{0,1:T(8,128)(2,1)S(1)}, u32[]{:S(2)}, u32[]{:S(2)}) collective-permute-start(bf16[360,320]{0,1:T(8,128)(2,1)S(1)} %bitcast.123), channel_id=1, source_target_pairs={{0,6},{1,7},{2,4},{3,5},{4,2},{5,3},{6,0},{7,1},{8,14},{9,15},{10,... | collective-permute-start | bytes 691208 | tf_op jit(solution)/shard_map/ppermute | solution.py:78
  46.9 4.4 %collective-permute-done.8 = bf16[360,320]{0,1:T(8,128)(2,1)S(1)} collective-permute-done((bf16[360,320]{0,1:T(8,128)(2,1)S(1)}, bf16[360,320]{0,1:T(8,128)(2,1)S(1)}, u32[]{:S(2)}, u32[]{:S(2)}) %collective-permute-start.8) | collective-permute-done | bytes 230432 | tf_op jit(solution)/shard_map/ppermute | solution.py:78
  51.3 4.6 %collective-permute-done.7 = bf16[360,320]{0,1:T(8,128)(2,1)S(1)} collective-permute-done((bf16[360,320]{0,1:T(8,128)(2,1)S(1)}, bf16[360,320]{0,1:T(8,128)(2,1)S(1)}, u32[]{:S(2)}, u32[]{:S(2)}) %collective-permute-start.7) | collective-permute-done | bytes 230432 | tf_op jit(solution)/shard_map/ppermute | solution.py:78
  56.3 2.0 %collective-permute-start.9 = (bf16[360,320]{0,1:T(8,128)(2,1)S(1)}, bf16[360,320]{0,1:T(8,128)(2,1)S(1)}, u32[]{:S(2)}, u32[]{:S(2)}) collective-permute-start(bf16[360,320]{0,1:T(8,128)(2,1)S(1)} %fusion.39), channel_id=1, source_target_pairs={{0,8},{8,0},{16,24},{24,16},{1,9},{9,1},{17,25},{25,17},{2,10},{10... | collective-permute-start | bytes 691208 | tf_op jit(solution)/shard_map/ppermute | solution.py:91
  59.7 4.6 %collective-permute-start.10 = (bf16[1,128,320]{1,2,0:T(8,128)(2,1)S(1)}, bf16[1,128,320]{1,2,0:T(8,128)(2,1)S(1)}, u32[]{:S(2)}, u32[]{:S(2)}) collective-permute-start(bf16[1,128,320]{1,2,0:T(8,128)(2,1)S(1)} %get-tuple-element.21), channel_id=1, source_target_pairs={{0,8},{8,16},{16,24},{1,9},{9,17},{17,25},{2,10},{10,18},{18,26},{... | collective-permute-start | bytes 245768 | tf_op jit(solution)/shard_map/ppermute | solution.py:18
  64.2 1.9 %collective-permute-done.11 = bf16[1,128,320]{1,2,0:T(8,128)(2,1)S(1)} collective-permute-done((bf16[1,128,320]{1,2,0:T(8,128)(2,1)S(1)}, bf16[1,128,320]{1,2,0:T(8,128)(2,1)S(1)}, u32[]{:S(2)}, u32[]{:S(2)}) %collective-permute-start.11) | collective-permute-done | bytes 81952 | tf_op jit(solution)/shard_map/ppermute | solution.py:20
  66.8 3.0 %copy.42 = bf16[8,360,320]{2,1,0:T(8,128)(2,1)S(1)} copy(bf16[8,360,320]{1,2,0:T(8,128)(2,1)} %all-gather.3.cloned.1.call-done) | data formatting | bytes 3686400 | tf_op jit(solution)/shard_map/all_gather | solution.py:122
  71.0 1.3 %copy-done.7 = bf16[3,128,2880]{1,2,0:T(8,128)(2,1)} copy-done((bf16[3,128,2880]{1,2,0:T(8,128)(2,1)}, bf16[3,128,2880]{1,2,0:T(8,128)(2,1)S(1)}, u32[]{:S(2)}) %copy-start.7) | copy-done | bytes 2211864
  72.3 2.5 %copy.44 = bf16[9,320,320]{1,2,0:T(8,128)(2,1)} copy(bf16[9,320,320]{2,1,0:T(8,128)(2,1)S(1)} %bitcast.119) | data formatting | bytes 3686400 | tf_op jit(solution)/shard_map/reshape | solution.py:153
  74.8 4.4 %fusion.46 = (f32[320]{0:T(512)S(1)}, f32[320]{0:T(512)S(1)}, f32[3,128,320]{1,2,0:T(8,128)}) fusion(f32[320]{0:T(512)S(1)} %mul.163, f32[320]{0:T(512)S(1)} %sub.37, f32[3,128]{1,0:T(4,128)S(1)} %get-tuple-element.28, bf16[1,3,128,320]{2,3,1,0:T(8,128)(2,1)S(1)} %copy-done.3, f32[320]{0:T(512)S(1)} %copy-done.8, f32[320]{0:T(512)S(1)} %copy-done.9, ...), kind=kOutput, calls=%fused_computation.95 | convolution fusion | flops 710245760 | bytes 4801536 | tf_op jit(solution)/shard_map/dot_general | solution.py:163
  79.7 3.6 %collective-permute-start.14 = (f32[2,32]{1,0:T(2,128)S(1)}, f32[2,32]{1,0:T(2,128)S(1)}, u32[]{:S(2)}, u32[]{:S(2)}) collective-permute-start(f32[2,32]{1,0:T(2,128)S(1)} %pad_maximum_fusion.3), channel_id=1, source_target_pairs={{0,24},{8,0},{16,8},{24,16},{1,25},{9,1},{17,9},{25,17},{2,26},{10... | collective-permute-start | bytes 776 | tf_op jit(solution)/shard_map/ppermute | solution.py:33
  84.0 3.5 %fusion.12 = bf16[1,3,128,320]{2,3,1,0:T(8,128)(2,1)} fusion(bf16[3,128,2880]{1,2,0:T(8,128)(2,1)} %copy-done, bf16[2880,320]{1,0:T(8,128)(2,1)S(1)} %bitcast.120, f32[3,128]{1,0:T(4,128)S(1)} %get-tuple-element.28), kind=kOutput, calls=%fused_computation.13 | convolution fusion | flops 708034560 | bytes 4302336 | tf_op jit(solution)/shard_map/dot_general | solution.py:151
  87.5 2.3 %collective-permute-start.15 = (bf16[360,320]{0,1:T(8,128)(2,1)S(1)}, bf16[360,320]{0,1:T(8,128)(2,1)S(1)}, u32[]{:S(2)}, u32[]{:S(2)}) collective-permute-start(bf16[360,320]{0,1:T(8,128)(2,1)S(1)} %convert_add_fusion.2), channel_id=1, source_target_pairs={{0,16},{8,24},{16,0},{24,8},{1,17},{9,25},{17,1},{25,9},{2,18},{10... | collective-permute-start | bytes 691208 | tf_op jit(solution)/shard_map/ppermute | solution.py:91
  90.2 2.0 %fusion.42 = bf16[1,3,128,320]{2,3,1,0:T(8,128)(2,1)} fusion(f32[320]{0:T(512)S(1)} %mul.180, f32[320]{0:T(512)S(1)} %sub.37, f32[3,128]{1,0:T(4,128)S(1)} %get-tuple-element.28, bf16[1,3,128,320]{2,3,1,0:T(8,128)(2,1)S(1)} %copy-done.3, f32[3,128,320]{1,2,0:T(8,128)} %get-tuple-element.29, f32[320]{0:T(512)S(1)} %sub.44, f32[320]{0:T(512)S(1)} %mul.163), kind=kLoop, calls=%fused_computation.75 | loop fusion | flops 1351680 | bytes 989696 | tf_op jit(solution)/shard_map/broadcast_in_dim | solution.py:181
  92.2 7.4 %collective-permute-done.15 = bf16[360,320]{0,1:T(8,128)(2,1)S(1)} collective-permute-done((bf16[360,320]{0,1:T(8,128)(2,1)S(1)}, bf16[360,320]{0,1:T(8,128)(2,1)S(1)}, u32[]{:S(2)}, u32[]{:S(2)}) %collective-permute-start.15) | collective-permute-done | bytes 230432 | tf_op jit(solution)/shard_map/ppermute | solution.py:91
  99.6 2.3 %fusion.36 = (f32[360,320]{0,1:T(8,128)}, f32[360,320]{0,1:T(8,128)}) fusion(f32[360,320]{0,1:T(8,128)S(1)} %copy-done.6, f32[360,320]{0,1:T(8,128)} %param.14, bf16[360,320]{0,1:T(8,128)(2,1)S(1)} %collective-permute-done.15, bf16[360,320]{0,1:T(8,128)(2,1)S(1)} %convert_add_fusion.2), kind=kLoop, calls=%fused_computation.43 | loop fusion | flops 1612800 | bytes 2304000 | tf_op jit(solution)/shard_map/div | solution.py:180
  (100 shorter events, 18.7 us)
Async XLA Ops:
  7.2 59.6 %all-gather.3.cloned.1.call-start = ((), (), s32[]{:S(2)}) async-start(), calls=%async_computation | async-start | bytes 2211840 | tf_op jit(solution)/shard_map/all_gather | solution.py:122
  10.2 6.4 %collective-permute-start.2 = (f32[2,32]{1,0:T(2,128)S(1)}, f32[2,32]{1,0:T(2,128)S(1)}, u32[]{:S(2)}, u32[]{:S(2)}) collective-permute-start(f32[2,32]{1,0:T(2,128)S(1)} %pad_maximum_fusion.2), channel_id=1, source_target_pairs={{0,24},{8,0},{16,8},{24,16},{1,25},{9,1},{17,9},{25,17},{2,26},{10... | collective-permute-start | bytes 776 | tf_op jit(solution)/shard_map/ppermute | solution.py:33
  15.3 4.5 %collective-permute-start.1 = (f32[2,32]{1,0:T(2,128)S(1)}, f32[2,32]{1,0:T(2,128)S(1)}, u32[]{:S(2)}, u32[]{:S(2)}) collective-permute-start(f32[2,32]{1,0:T(2,128)S(1)} %pad_maximum_fusion.2), channel_id=1, source_target_pairs={{0,16},{8,24},{16,0},{24,8},{1,17},{9,25},{17,1},{25,9},{2,18},{10... | collective-permute-start | bytes 776 | tf_op jit(solution)/shard_map/ppermute | solution.py:33
  15.3 5.4 %collective-permute-start = (f32[2,32]{1,0:T(2,128)S(1)}, f32[2,32]{1,0:T(2,128)S(1)}, u32[]{:S(2)}, u32[]{:S(2)}) collective-permute-start(f32[2,32]{1,0:T(2,128)S(1)} %pad_maximum_fusion.2), channel_id=1, source_target_pairs={{0,8},{8,16},{16,24},{24,0},{1,9},{9,17},{17,25},{25,1},{2,10},{10... | collective-permute-start | bytes 776 | tf_op jit(solution)/shard_map/ppermute | solution.py:33
  21.1 10.0 %copy-start.2 = (bf16[1,3,128,320]{2,3,1,0:T(8,128)(2,1)S(1)}, bf16[1,3,128,320]{2,3,1,0:T(8,128)(2,1)}, u32[]{:S(2)}) copy-start(bf16[1,3,128,320]{2,3,1,0:T(8,128)(2,1)} %param.9) | copy-start | bytes 737284
  21.1 10.0 %copy-start.8 = (f32[320]{0:T(512)S(1)}, f32[320]{0:T(512)}, u32[]{:S(2)}) copy-start(f32[320]{0:T(512)} %param.12) | copy-start | bytes 3844
  21.1 10.0 %copy-start.9 = (f32[320]{0:T(512)S(1)}, f32[320]{0:T(512)}, u32[]{:S(2)}) copy-start(f32[320]{0:T(512)} %param.11) | copy-start | bytes 3844
  22.5 6.9 %collective-permute-start.4 = (bf16[1,128,320]{1,2,0:T(8,128)(2,1)S(1)}, bf16[1,128,320]{1,2,0:T(8,128)(2,1)S(1)}, u32[]{:S(2)}, u32[]{:S(2)}) collective-permute-start(bf16[1,128,320]{1,2,0:T(8,128)(2,1)S(1)} %get-tuple-element.24), channel_id=1, source_target_pairs={{8,0},{16,8},{24,16},{9,1},{17,9},{25,17},{10,2},{18,10},{26,18},{... | collective-permute-start | bytes 245768 | tf_op jit(solution)/shard_map/ppermute | solution.py:20
  23.8 6.6 %collective-permute-start.3 = (bf16[1,128,320]{1,2,0:T(8,128)(2,1)S(1)}, bf16[1,128,320]{1,2,0:T(8,128)(2,1)S(1)}, u32[]{:S(2)}, u32[]{:S(2)}) collective-permute-start(bf16[1,128,320]{1,2,0:T(8,128)(2,1)S(1)} %get-tuple-element.23), channel_id=1, source_target_pairs={{0,8},{8,16},{16,24},{1,9},{9,17},{17,25},{2,10},{10,18},{18,26},{... | collective-permute-start | bytes 245768 | tf_op jit(solution)/shard_map/ppermute | solution.py:18
  29.3 2.6 %copy-start.4 = (bf16[3,128,320]{1,2,0:T(8,128)(2,1)}, bf16[3,128,320]{1,2,0:T(8,128)(2,1)S(1)}, u32[]{:S(2)}) copy-start(bf16[3,128,320]{1,2,0:T(8,128)(2,1)S(1)} %bitcast_multiply_fusion) | copy-start | bytes 737284
  35.0 3.0 %collective-permute-start.5 = (bf16[4,360,320]{1,2,0:T(8,128)(2,1)}, bf16[4,360,320]{1,2,0:T(8,128)(2,1)}, u32[]{:S(2)}, u32[]{:S(2)}) collective-permute-start(bf16[4,360,320]{1,2,0:T(8,128)(2,1)} %copy.34), channel_id=1, source_target_pairs={{0,1},{1,0},{2,3},{3,2},{4,5},{5,4},{6,7},{7,6},{8,9},{9,8},{10,11... | collective-permute-start | bytes 2764808 | tf_op jit(solution)/shard_map/ppermute | solution.py:65
  41.5 9.8 %collective-permute-start.8 = (bf16[360,320]{0,1:T(8,128)(2,1)S(1)}, bf16[360,320]{0,1:T(8,128)(2,1)S(1)}, u32[]{:S(2)}, u32[]{:S(2)}) collective-permute-start(bf16[360,320]{0,1:T(8,128)(2,1)S(1)} %bitcast.123), channel_id=1, source_target_pairs={{0,6},{1,7},{2,4},{3,5},{4,2},{5,3},{6,0},{7,1},{8,14},{9,15},{10,... | collective-permute-start | bytes 691208 | tf_op jit(solution)/shard_map/ppermute | solution.py:78
  44.2 14.2 %copy-start.5 = (bf16[3,128,320]{1,2,0:T(8,128)(2,1)S(1)}, bf16[3,128,320]{1,2,0:T(8,128)(2,1)}, u32[]{:S(2)}) copy-start(bf16[3,128,320]{1,2,0:T(8,128)(2,1)} %copy-done.4) | copy-start | bytes 737284
  44.4 11.5 %collective-permute-start.7 = (bf16[360,320]{0,1:T(8,128)(2,1)S(1)}, bf16[360,320]{0,1:T(8,128)(2,1)S(1)}, u32[]{:S(2)}, u32[]{:S(2)}) collective-permute-start(bf16[360,320]{0,1:T(8,128)(2,1)S(1)} %bitcast.124), channel_id=1, source_target_pairs={{0,4},{1,5},{2,6},{3,7},{4,0},{5,1},{6,2},{7,3},{8,12},{9,13},{10,... | collective-permute-start | bytes 691208 | tf_op jit(solution)/shard_map/ppermute | solution.py:78
  45.2 11.0 %collective-permute-start.6 = (bf16[360,320]{0,1:T(8,128)(2,1)S(1)}, bf16[360,320]{0,1:T(8,128)(2,1)S(1)}, u32[]{:S(2)}, u32[]{:S(2)}) collective-permute-start(bf16[360,320]{0,1:T(8,128)(2,1)S(1)} %bitcast.125), channel_id=1, source_target_pairs={{0,2},{1,3},{2,0},{3,1},{4,6},{5,7},{6,4},{7,5},{8,10},{9,11},{10,... | collective-permute-start | bytes 691208 | tf_op jit(solution)/shard_map/ppermute | solution.py:78
  56.3 10.3 %collective-permute-start.9 = (bf16[360,320]{0,1:T(8,128)(2,1)S(1)}, bf16[360,320]{0,1:T(8,128)(2,1)S(1)}, u32[]{:S(2)}, u32[]{:S(2)}) collective-permute-start(bf16[360,320]{0,1:T(8,128)(2,1)S(1)} %fusion.39), channel_id=1, source_target_pairs={{0,8},{8,0},{16,24},{24,16},{1,9},{9,1},{17,25},{25,17},{2,10},{10... | collective-permute-start | bytes 691208 | tf_op jit(solution)/shard_map/ppermute | solution.py:91
  58.4 7.8 %collective-permute-start.11 = (bf16[1,128,320]{1,2,0:T(8,128)(2,1)S(1)}, bf16[1,128,320]{1,2,0:T(8,128)(2,1)S(1)}, u32[]{:S(2)}, u32[]{:S(2)}) collective-permute-start(bf16[1,128,320]{1,2,0:T(8,128)(2,1)S(1)} %get-tuple-element.22), channel_id=1, source_target_pairs={{8,0},{16,8},{24,16},{9,1},{17,9},{25,17},{10,2},{18,10},{26,18},{... | collective-permute-start | bytes 245768 | tf_op jit(solution)/shard_map/ppermute | solution.py:20
  59.7 6.6 %collective-permute-start.10 = (bf16[1,128,320]{1,2,0:T(8,128)(2,1)S(1)}, bf16[1,128,320]{1,2,0:T(8,128)(2,1)S(1)}, u32[]{:S(2)}, u32[]{:S(2)}) collective-permute-start(bf16[1,128,320]{1,2,0:T(8,128)(2,1)S(1)} %get-tuple-element.21), channel_id=1, source_target_pairs={{0,8},{8,16},{16,24},{1,9},{9,17},{17,25},{2,10},{10,18},{18,26},{... | collective-permute-start | bytes 245768 | tf_op jit(solution)/shard_map/ppermute | solution.py:18
  72.3 2.5 %copy-start.3 = (bf16[1,3,128,320]{2,3,1,0:T(8,128)(2,1)S(1)}, bf16[1,3,128,320]{2,3,1,0:T(8,128)(2,1)}, u32[]{:S(2)}) copy-start(bf16[1,3,128,320]{2,3,1,0:T(8,128)(2,1)} %param.9) | copy-start | bytes 737284
  79.7 19.9 %copy-start.6 = (f32[360,320]{0,1:T(8,128)S(1)}, f32[360,320]{0,1:T(8,128)}, u32[]{:S(2)}) copy-start(f32[360,320]{0,1:T(8,128)} %param.15) | copy-start | bytes 1382404
  79.7 10.1 %collective-permute-start.14 = (f32[2,32]{1,0:T(2,128)S(1)}, f32[2,32]{1,0:T(2,128)S(1)}, u32[]{:S(2)}, u32[]{:S(2)}) collective-permute-start(f32[2,32]{1,0:T(2,128)S(1)} %pad_maximum_fusion.3), channel_id=1, source_target_pairs={{0,24},{8,0},{16,8},{24,16},{1,25},{9,1},{17,9},{25,17},{2,26},{10... | collective-permute-start | bytes 776 | tf_op jit(solution)/shard_map/ppermute | solution.py:33
  83.3 6.5 %collective-permute-start.13 = (f32[2,32]{1,0:T(2,128)S(1)}, f32[2,32]{1,0:T(2,128)S(1)}, u32[]{:S(2)}, u32[]{:S(2)}) collective-permute-start(f32[2,32]{1,0:T(2,128)S(1)} %pad_maximum_fusion.3), channel_id=1, source_target_pairs={{0,16},{8,24},{16,0},{24,8},{1,17},{9,25},{17,1},{25,9},{2,18},{10... | collective-permute-start | bytes 776 | tf_op jit(solution)/shard_map/ppermute | solution.py:33
  83.6 6.2 %collective-permute-start.12 = (f32[2,32]{1,0:T(2,128)S(1)}, f32[2,32]{1,0:T(2,128)S(1)}, u32[]{:S(2)}, u32[]{:S(2)}) collective-permute-start(f32[2,32]{1,0:T(2,128)S(1)} %pad_maximum_fusion.3), channel_id=1, source_target_pairs={{0,8},{8,16},{16,24},{24,0},{1,9},{9,17},{17,25},{25,1},{2,10},{10... | collective-permute-start | bytes 776 | tf_op jit(solution)/shard_map/ppermute | solution.py:33
  87.5 12.1 %collective-permute-start.15 = (bf16[360,320]{0,1:T(8,128)(2,1)S(1)}, bf16[360,320]{0,1:T(8,128)(2,1)S(1)}, u32[]{:S(2)}, u32[]{:S(2)}) collective-permute-start(bf16[360,320]{0,1:T(8,128)(2,1)S(1)} %convert_add_fusion.2), channel_id=1, source_target_pairs={{0,16},{8,24},{16,0},{24,8},{1,17},{9,25},{17,1},{25,9},{2,18},{10... | collective-permute-start | bytes 691208 | tf_op jit(solution)/shard_map/ppermute | solution.py:91
  (3 other events, 4.2 us)
Sparse Core Ops, SparseCore 0:
  16.5 27.7 all-gather.2

commit v16 on v15

--- a/solution.py
+++ b/solution.py
@@ -63,15 +63,15 @@
         send = row_major(lax.dynamic_index_in_dim(paired, 1 - bit, axis=1, keepdims=False))
         pairs = [(i, i ^ step) for i in range(count)]
         got = lax.ppermute(send.astype(jnp.bfloat16), axis, pairs)
-        held = row_major(keep.astype(jnp.float32) + got.astype(jnp.float32))
+        held = row_major((keep.astype(jnp.float32) + got.astype(jnp.float32)).astype(jnp.bfloat16))
         step *= 2
         if step < count <= 4 * step:
             break
     if step == count:
-        return held[0], companions
+        return held[0].astype(jnp.float32), companions
     spots = count // step
     own = index // step
-    total = lax.dynamic_index_in_dim(held, own, keepdims=False)
+    total = lax.dynamic_index_in_dim(held, own, keepdims=False).astype(jnp.float32)
     for shift in range(1, spots):
         send = lax.dynamic_index_in_dim(held, own ^ shift, keepdims=False)
         pairs = [(i, i ^ (shift * step)) for i in range(count)]

time: 109 us -> 108 us (level)
  local copies, waits for them, and re-layouts: 16.3 us -> 13.8 us
  waiting for transfers between devices: 27.2 us -> 28.3 us
    unnamed x36 -> x32, local copies, waits for them, and re-layouts: 4.89 us -> 3.16 us
    dynamic_slice x2 -> x1, local copies, waits for them, and re-layouts: 1.3 us -> 0.12 us  [halving_scatter(): lax.dynamic_index_in_dim(held, own, keepdims=False).astype(jnp.float32)]
    ppermute x3, waiting for transfers between devices: 9.32 us -> 10.4 us  [halving_scatter(): lax.ppermute(send.astype(jnp.bfloat16), axis, pairs).astype(jnp.float32)]
  transfers between devices with their start and end apart: 17 -> 17, of which waited for: 11 -> 11; matrix products, arithmetic and copies ran while one was open for 16% -> 15% of each run, Pallas kernels for 0% -> 0%
where the time goes in v16:
time: 108 us; the launch traced here: 107 us
  starting transfers between devices  30.1 us (28%)
  waiting for transfers between devices  28.3 us (26%)
  between operations  15.8 us (15%)
  local copies, waits for them, and re-layouts  13.8 us (13%)
  other arithmetic  9.96 us (9%)
  matrix products  9.47 us (9%)
    ppermute x3, waiting for transfers between devices, halving_scatter(): lax.ppermute(send.astype(jnp.bfloat16), axis, pairs).astype(jnp.float32)  10.4 us
    ppermute x6, starting transfers between devices, space_sum(): lax.ppermute(joined, axis, [(i, (i + shift) % count) for i in range(count)])  10.4 us
    ppermute x2, starting transfers between devices, with_halo(): lax.ppermute(tail, axis, [(i, (i + 1) % count) for i in range(ends)])  9.1 us
    ppermute x2, waiting for transfers between devices, replicated_sum(): lax.ppermute(mine, axis, pairs).astype(jnp.float32)  7.41 us
    dot_general x1, matrix products, local(): upstream = jnp.dot(cot_cols, flipped, preferred_element_type=jnp.float32)  4.4 us
    ppermute x6, waiting for transfers between devices, space_sum(): lax.ppermute(joined, axis, [(i, (i + shift) % count) for i in range(count)])  4.33 us
    ppermute x2, starting transfers between devices, replicated_sum(): lax.ppermute(mine, axis, pairs).astype(jnp.float32)  4.28 us
    ppermute x3, starting transfers between devices, halving_scatter(): lax.ppermute(send.astype(jnp.bfloat16), axis, pairs).astype(jnp.float32)  3.68 us
  transfers between devices with their start and end apart: 17, of which 11 were waited for; matrix products, arithmetic and copies ran while one was open for 15% of the time, Pallas kernels for 0%

profile of v16, /device:TPU:0, one launch (start us, length us, event | category | flops | bytes accessed | tf_op | source)
XLA Modules:
  0.0 107.5 jit_solution(17002661390113809983)
XLA Ops:
  10.2 5.1 %collective-permute-start.2 = (f32[2,32]{1,0:T(2,128)S(1)}, f32[2,32]{1,0:T(2,128)S(1)}, u32[]{:S(2)}, u32[]{:S(2)}) collective-permute-start(f32[2,32]{1,0:T(2,128)S(1)} %pad_maximum_fusion.2), channel_id=1, source_target_pairs={{0,24},{8,0},{16,8},{24,16},{1,25},{9,1},{17,9},{25,17},{2,26},{10... | collective-permute-start | bytes 776 | tf_op jit(solution)/shard_map/ppermute | solution.py:33
  16.6 3.2 %collective-permute-done.1 = f32[2,32]{1,0:T(2,128)S(1)} collective-permute-done((f32[2,32]{1,0:T(2,128)S(1)}, f32[2,32]{1,0:T(2,128)S(1)}, u32[]{:S(2)}, u32[]{:S(2)}) %collective-permute-start.1) | collective-permute-done | bytes 288 | tf_op jit(solution)/shard_map/ppermute | solution.py:33
  21.1 1.3 %multiply_convert_fusion = bf16[3,128,320]{1,2,0:T(8,128)(2,1)S(1)} fusion(bf16[1,3,128,320]{2,3,1,0:T(8,128)(2,1)} %param.9, f32[320]{0:T(512)} %param.12, f32[320]{0:T(512)} %param.11, f32[320]{0:T(512)S(1)} %mul.163, f32[320]{0:T(512)S(1)} %sub.37, f32[3,128]{1,0:T(4,128)S(1)} %get-tuple-element.29), kind=kLoop, calls=%fused_computation.50 | loop fusion | flops 1597440 | bytes 498176 | tf_op jit(solution)/shard_map/convert_element_type | solution.py:132
  23.8 4.6 %collective-permute-start.3 = (bf16[1,128,320]{1,2,0:T(8,128)(2,1)S(1)}, bf16[1,128,320]{1,2,0:T(8,128)(2,1)S(1)}, u32[]{:S(2)}, u32[]{:S(2)}) collective-permute-start(bf16[1,128,320]{1,2,0:T(8,128)(2,1)S(1)} %get-tuple-element.24), channel_id=1, source_target_pairs={{0,8},{8,16},{16,24},{1,9},{9,17},{17,25},{2,10},{10,18},{18,26},{... | collective-permute-start | bytes 245768 | tf_op jit(solution)/shard_map/ppermute | solution.py:18
  31.9 1.5 %fusion = bf16[2880,320]{1,0:T(8,128)(2,1)S(1)} fusion(bf16[3,128,2880]{1,2,0:T(8,128)(2,1)S(1)} %slice_dynamic-update-slice_fusion, bf16[3,128,320]{1,2,0:T(8,128)(2,1)S(1)} %bitcast_multiply_fusion), kind=kOutput, calls=%fused_computation.1 | convolution fusion | flops 708710400 | bytes 4300800 | tf_op jit(solution)/shard_map/dot_general | solution.py:145
  33.6 1.4 %copy.34 = bf16[4,360,320]{1,2,0:T(8,128)(2,1)} copy(bf16[4,360,320]{2,1,0:T(8,128)(2,1)S(1)} %dynamic-slice_bitcast_fusion) | data formatting | bytes 1843200 | tf_op jit(solution)/shard_map/layout_constraint | solution.py:42
  35.0 3.0 %collective-permute-done.5 = bf16[4,360,320]{1,2,0:T(8,128)(2,1)} collective-permute-done((bf16[4,360,320]{1,2,0:T(8,128)(2,1)}, bf16[4,360,320]{1,2,0:T(8,128)(2,1)}, u32[]{:S(2)}, u32[]{:S(2)}) %collective-permute-start.5) | collective-permute-done | bytes 921632 | tf_op jit(solution)/shard_map/ppermute | solution.py:65
  38.0 1.6 %copy.35 = bf16[4,360,320]{2,1,0:T(8,128)(2,1)S(1)} copy(bf16[4,360,320]{1,2,0:T(8,128)(2,1)} %collective-permute-done.5) | data formatting | bytes 1843200 | tf_op jit(solution)/shard_map/ppermute | solution.py:65
  40.3 2.7 %collective-permute-start.8 = (bf16[360,320]{0,1:T(8,128)(2,1)S(1)}, bf16[360,320]{0,1:T(8,128)(2,1)S(1)}, u32[]{:S(2)}, u32[]{:S(2)}) collective-permute-start(bf16[360,320]{0,1:T(8,128)(2,1)S(1)} %bitcast.112), channel_id=1, source_target_pairs={{0,6},{1,7},{2,4},{3,5},{4,2},{5,3},{6,0},{7,1},{8,14},{9,15},{10,... | collective-permute-start | bytes 691208 | tf_op jit(solution)/shard_map/ppermute | solution.py:78
  44.5 5.5 %collective-permute-done.8 = bf16[360,320]{0,1:T(8,128)(2,1)S(1)} collective-permute-done((bf16[360,320]{0,1:T(8,128)(2,1)S(1)}, bf16[360,320]{0,1:T(8,128)(2,1)S(1)}, u32[]{:S(2)}, u32[]{:S(2)}) %collective-permute-start.8) | collective-permute-done | bytes 230432 | tf_op jit(solution)/shard_map/ppermute | solution.py:78
  50.1 4.6 %collective-permute-done.7 = bf16[360,320]{0,1:T(8,128)(2,1)S(1)} collective-permute-done((bf16[360,320]{0,1:T(8,128)(2,1)S(1)}, bf16[360,320]{0,1:T(8,128)(2,1)S(1)}, u32[]{:S(2)}, u32[]{:S(2)}) %collective-permute-start.7) | collective-permute-done | bytes 230432 | tf_op jit(solution)/shard_map/ppermute | solution.py:78
  55.1 2.0 %collective-permute-start.9 = (bf16[360,320]{0,1:T(8,128)(2,1)S(1)}, bf16[360,320]{0,1:T(8,128)(2,1)S(1)}, u32[]{:S(2)}, u32[]{:S(2)}) collective-permute-start(bf16[360,320]{0,1:T(8,128)(2,1)S(1)} %fusion.39), channel_id=1, source_target_pairs={{0,8},{8,0},{16,24},{24,16},{1,9},{9,1},{17,25},{25,17},{2,10},{10... | collective-permute-start | bytes 691208 | tf_op jit(solution)/shard_map/ppermute | solution.py:91
  58.4 4.6 %collective-permute-start.10 = (bf16[1,128,320]{1,2,0:T(8,128)(2,1)S(1)}, bf16[1,128,320]{1,2,0:T(8,128)(2,1)S(1)}, u32[]{:S(2)}, u32[]{:S(2)}) collective-permute-start(bf16[1,128,320]{1,2,0:T(8,128)(2,1)S(1)} %get-tuple-element.22), channel_id=1, source_target_pairs={{0,8},{8,16},{16,24},{1,9},{9,17},{17,25},{2,10},{10,18},{18,26},{... | collective-permute-start | bytes 245768 | tf_op jit(solution)/shard_map/ppermute | solution.py:18
  63.0 1.9 %collective-permute-done.11 = bf16[1,128,320]{1,2,0:T(8,128)(2,1)S(1)} collective-permute-done((bf16[1,128,320]{1,2,0:T(8,128)(2,1)S(1)}, bf16[1,128,320]{1,2,0:T(8,128)(2,1)S(1)}, u32[]{:S(2)}, u32[]{:S(2)}) %collective-permute-start.11) | collective-permute-done | bytes 81952 | tf_op jit(solution)/shard_map/ppermute | solution.py:20
  65.5 3.0 %copy.42 = bf16[8,360,320]{2,1,0:T(8,128)(2,1)S(1)} copy(bf16[8,360,320]{1,2,0:T(8,128)(2,1)} %all-gather.3.cloned.1.call-done) | data formatting | bytes 3686400 | tf_op jit(solution)/shard_map/all_gather | solution.py:122
  69.7 1.3 %copy-done.6 = bf16[3,128,2880]{1,2,0:T(8,128)(2,1)} copy-done((bf16[3,128,2880]{1,2,0:T(8,128)(2,1)}, bf16[3,128,2880]{1,2,0:T(8,128)(2,1)S(1)}, u32[]{:S(2)}) %copy-start.6) | copy-done | bytes 2211864
  71.1 2.5 %copy.44 = bf16[9,320,320]{1,2,0:T(8,128)(2,1)} copy(bf16[9,320,320]{2,1,0:T(8,128)(2,1)S(1)} %bitcast.108) | data formatting | bytes 3686400 | tf_op jit(solution)/shard_map/reshape | solution.py:153
  73.5 4.4 %fusion.46 = (f32[320]{0:T(512)S(1)}, f32[320]{0:T(512)S(1)}, f32[3,128,320]{1,2,0:T(8,128)}) fusion(f32[320]{0:T(512)S(1)} %mul.163, f32[320]{0:T(512)S(1)} %sub.37, f32[3,128]{1,0:T(4,128)S(1)} %get-tuple-element.29, bf16[1,3,128,320]{2,3,1,0:T(8,128)(2,1)S(1)} %copy-done.2, f32[320]{0:T(512)S(1)} %copy-done.7, f32[320]{0:T(512)S(1)} %copy-done.8, ...), kind=kOutput, calls=%fused_computation.92 | convolution fusion | flops 710245760 | bytes 4801536 | tf_op jit(solution)/shard_map/dot_general | solution.py:163
  78.4 3.7 %collective-permute-start.14 = (f32[2,32]{1,0:T(2,128)S(1)}, f32[2,32]{1,0:T(2,128)S(1)}, u32[]{:S(2)}, u32[]{:S(2)}) collective-permute-start(f32[2,32]{1,0:T(2,128)S(1)} %pad_maximum_fusion.3), channel_id=1, source_target_pairs={{0,24},{8,0},{16,8},{24,16},{1,25},{9,1},{17,9},{25,17},{2,26},{10... | collective-permute-start | bytes 776 | tf_op jit(solution)/shard_map/ppermute | solution.py:33
  82.7 3.5 %fusion.12 = bf16[1,3,128,320]{2,3,1,0:T(8,128)(2,1)} fusion(bf16[3,128,2880]{1,2,0:T(8,128)(2,1)} %copy-done, bf16[2880,320]{1,0:T(8,128)(2,1)S(1)} %bitcast.109, f32[3,128]{1,0:T(4,128)S(1)} %get-tuple-element.29), kind=kOutput, calls=%fused_computation.13 | convolution fusion | flops 708034560 | bytes 4302336 | tf_op jit(solution)/shard_map/dot_general | solution.py:151
  86.2 2.3 %collective-permute-start.15 = (bf16[360,320]{0,1:T(8,128)(2,1)S(1)}, bf16[360,320]{0,1:T(8,128)(2,1)S(1)}, u32[]{:S(2)}, u32[]{:S(2)}) collective-permute-start(bf16[360,320]{0,1:T(8,128)(2,1)S(1)} %convert_add_fusion.2), channel_id=1, source_target_pairs={{0,16},{8,24},{16,0},{24,8},{1,17},{9,25},{17,1},{25,9},{2,18},{10... | collective-permute-start | bytes 691208 | tf_op jit(solution)/shard_map/ppermute | solution.py:91
  88.9 2.0 %fusion.42 = bf16[1,3,128,320]{2,3,1,0:T(8,128)(2,1)} fusion(f32[320]{0:T(512)S(1)} %mul.180, f32[320]{0:T(512)S(1)} %sub.37, f32[3,128]{1,0:T(4,128)S(1)} %get-tuple-element.29, bf16[1,3,128,320]{2,3,1,0:T(8,128)(2,1)S(1)} %copy-done.2, f32[3,128,320]{1,2,0:T(8,128)} %get-tuple-element.30, f32[320]{0:T(512)S(1)} %sub.44, f32[320]{0:T(512)S(1)} %mul.163), kind=kLoop, calls=%fused_computation.72 | loop fusion | flops 1351680 | bytes 989696 | tf_op jit(solution)/shard_map/broadcast_in_dim | solution.py:181
  90.9 7.4 %collective-permute-done.15 = bf16[360,320]{0,1:T(8,128)(2,1)S(1)} collective-permute-done((bf16[360,320]{0,1:T(8,128)(2,1)S(1)}, bf16[360,320]{0,1:T(8,128)(2,1)S(1)}, u32[]{:S(2)}, u32[]{:S(2)}) %collective-permute-start.15) | collective-permute-done | bytes 230432 | tf_op jit(solution)/shard_map/ppermute | solution.py:91
  98.3 2.3 %fusion.36 = (f32[360,320]{0,1:T(8,128)}, f32[360,320]{0,1:T(8,128)}) fusion(f32[360,320]{0,1:T(8,128)S(1)} %copy-done.5, f32[360,320]{0,1:T(8,128)} %param.14, bf16[360,320]{0,1:T(8,128)(2,1)S(1)} %collective-permute-done.15, bf16[360,320]{0,1:T(8,128)(2,1)S(1)} %convert_add_fusion.2), kind=kLoop, calls=%fused_computation.43 | loop fusion | flops 1612800 | bytes 2304000 | tf_op jit(solution)/shard_map/div | solution.py:180
  (97 shorter events, 16.3 us)
Async XLA Ops:
  7.2 58.3 %all-gather.3.cloned.1.call-start = ((), (), s32[]{:S(2)}) async-start(), calls=%async_computation | async-start | bytes 2211840 | tf_op jit(solution)/shard_map/all_gather | solution.py:122
  10.2 6.4 %collective-permute-start.2 = (f32[2,32]{1,0:T(2,128)S(1)}, f32[2,32]{1,0:T(2,128)S(1)}, u32[]{:S(2)}, u32[]{:S(2)}) collective-permute-start(f32[2,32]{1,0:T(2,128)S(1)} %pad_maximum_fusion.2), channel_id=1, source_target_pairs={{0,24},{8,0},{16,8},{24,16},{1,25},{9,1},{17,9},{25,17},{2,26},{10... | collective-permute-start | bytes 776 | tf_op jit(solution)/shard_map/ppermute | solution.py:33
  15.3 4.5 %collective-permute-start.1 = (f32[2,32]{1,0:T(2,128)S(1)}, f32[2,32]{1,0:T(2,128)S(1)}, u32[]{:S(2)}, u32[]{:S(2)}) collective-permute-start(f32[2,32]{1,0:T(2,128)S(1)} %pad_maximum_fusion.2), channel_id=1, source_target_pairs={{0,16},{8,24},{16,0},{24,8},{1,17},{9,25},{17,1},{25,9},{2,18},{10... | collective-permute-start | bytes 776 | tf_op jit(solution)/shard_map/ppermute | solution.py:33
  15.3 5.4 %collective-permute-start = (f32[2,32]{1,0:T(2,128)S(1)}, f32[2,32]{1,0:T(2,128)S(1)}, u32[]{:S(2)}, u32[]{:S(2)}) collective-permute-start(f32[2,32]{1,0:T(2,128)S(1)} %pad_maximum_fusion.2), channel_id=1, source_target_pairs={{0,8},{8,16},{16,24},{24,0},{1,9},{9,17},{17,25},{25,1},{2,10},{10... | collective-permute-start | bytes 776 | tf_op jit(solution)/shard_map/ppermute | solution.py:33
  21.1 10.0 %copy-start.1 = (bf16[1,3,128,320]{2,3,1,0:T(8,128)(2,1)S(1)}, bf16[1,3,128,320]{2,3,1,0:T(8,128)(2,1)}, u32[]{:S(2)}) copy-start(bf16[1,3,128,320]{2,3,1,0:T(8,128)(2,1)} %param.9) | copy-start | bytes 737284
  21.1 10.0 %copy-start.7 = (f32[320]{0:T(512)S(1)}, f32[320]{0:T(512)}, u32[]{:S(2)}) copy-start(f32[320]{0:T(512)} %param.12) | copy-start | bytes 3844
  21.1 10.0 %copy-start.8 = (f32[320]{0:T(512)S(1)}, f32[320]{0:T(512)}, u32[]{:S(2)}) copy-start(f32[320]{0:T(512)} %param.11) | copy-start | bytes 3844
  22.5 6.9 %collective-permute-start.4 = (bf16[1,128,320]{1,2,0:T(8,128)(2,1)S(1)}, bf16[1,128,320]{1,2,0:T(8,128)(2,1)S(1)}, u32[]{:S(2)}, u32[]{:S(2)}) collective-permute-start(bf16[1,128,320]{1,2,0:T(8,128)(2,1)S(1)} %get-tuple-element.25), channel_id=1, source_target_pairs={{8,0},{16,8},{24,16},{9,1},{17,9},{25,17},{10,2},{18,10},{26,18},{... | collective-permute-start | bytes 245768 | tf_op jit(solution)/shard_map/ppermute | solution.py:20
  23.8 6.6 %collective-permute-start.3 = (bf16[1,128,320]{1,2,0:T(8,128)(2,1)S(1)}, bf16[1,128,320]{1,2,0:T(8,128)(2,1)S(1)}, u32[]{:S(2)}, u32[]{:S(2)}) collective-permute-start(bf16[1,128,320]{1,2,0:T(8,128)(2,1)S(1)} %get-tuple-element.24), channel_id=1, source_target_pairs={{0,8},{8,16},{16,24},{1,9},{9,17},{17,25},{2,10},{10,18},{18,26},{... | collective-permute-start | bytes 245768 | tf_op jit(solution)/shard_map/ppermute | solution.py:18
  29.3 2.6 %copy-start.3 = (bf16[3,128,320]{1,2,0:T(8,128)(2,1)}, bf16[3,128,320]{1,2,0:T(8,128)(2,1)S(1)}, u32[]{:S(2)}) copy-start(bf16[3,128,320]{1,2,0:T(8,128)(2,1)S(1)} %bitcast_multiply_fusion) | copy-start | bytes 737284
  35.0 3.0 %collective-permute-start.5 = (bf16[4,360,320]{1,2,0:T(8,128)(2,1)}, bf16[4,360,320]{1,2,0:T(8,128)(2,1)}, u32[]{:S(2)}, u32[]{:S(2)}) collective-permute-start(bf16[4,360,320]{1,2,0:T(8,128)(2,1)} %copy.34), channel_id=1, source_target_pairs={{0,1},{1,0},{2,3},{3,2},{4,5},{5,4},{6,7},{7,6},{8,9},{9,8},{10,11... | collective-permute-start | bytes 2764808 | tf_op jit(solution)/shard_map/ppermute | solution.py:65
  40.1 17.0 %copy-start.4 = (bf16[3,128,320]{1,2,0:T(8,128)(2,1)S(1)}, bf16[3,128,320]{1,2,0:T(8,128)(2,1)}, u32[]{:S(2)}) copy-start(bf16[3,128,320]{1,2,0:T(8,128)(2,1)} %copy-done.3) | copy-start | bytes 737284
  40.3 9.8 %collective-permute-start.8 = (bf16[360,320]{0,1:T(8,128)(2,1)S(1)}, bf16[360,320]{0,1:T(8,128)(2,1)S(1)}, u32[]{:S(2)}, u32[]{:S(2)}) collective-permute-start(bf16[360,320]{0,1:T(8,128)(2,1)S(1)} %bitcast.112), channel_id=1, source_target_pairs={{0,6},{1,7},{2,4},{3,5},{4,2},{5,3},{6,0},{7,1},{8,14},{9,15},{10,... | collective-permute-start | bytes 691208 | tf_op jit(solution)/shard_map/ppermute | solution.py:78
  43.2 11.5 %collective-permute-start.7 = (bf16[360,320]{0,1:T(8,128)(2,1)S(1)}, bf16[360,320]{0,1:T(8,128)(2,1)S(1)}, u32[]{:S(2)}, u32[]{:S(2)}) collective-permute-start(bf16[360,320]{0,1:T(8,128)(2,1)S(1)} %bitcast.113), channel_id=1, source_target_pairs={{0,4},{1,5},{2,6},{3,7},{4,0},{5,1},{6,2},{7,3},{8,12},{9,13},{10,... | collective-permute-start | bytes 691208 | tf_op jit(solution)/shard_map/ppermute | solution.py:78
  44.0 11.0 %collective-permute-start.6 = (bf16[360,320]{0,1:T(8,128)(2,1)S(1)}, bf16[360,320]{0,1:T(8,128)(2,1)S(1)}, u32[]{:S(2)}, u32[]{:S(2)}) collective-permute-start(bf16[360,320]{0,1:T(8,128)(2,1)S(1)} %bitcast.114), channel_id=1, source_target_pairs={{0,2},{1,3},{2,0},{3,1},{4,6},{5,7},{6,4},{7,5},{8,10},{9,11},{10,... | collective-permute-start | bytes 691208 | tf_op jit(solution)/shard_map/ppermute | solution.py:78
  55.1 10.3 %collective-permute-start.9 = (bf16[360,320]{0,1:T(8,128)(2,1)S(1)}, bf16[360,320]{0,1:T(8,128)(2,1)S(1)}, u32[]{:S(2)}, u32[]{:S(2)}) collective-permute-start(bf16[360,320]{0,1:T(8,128)(2,1)S(1)} %fusion.39), channel_id=1, source_target_pairs={{0,8},{8,0},{16,24},{24,16},{1,9},{9,1},{17,25},{25,17},{2,10},{10... | collective-permute-start | bytes 691208 | tf_op jit(solution)/shard_map/ppermute | solution.py:91
  57.1 7.8 %collective-permute-start.11 = (bf16[1,128,320]{1,2,0:T(8,128)(2,1)S(1)}, bf16[1,128,320]{1,2,0:T(8,128)(2,1)S(1)}, u32[]{:S(2)}, u32[]{:S(2)}) collective-permute-start(bf16[1,128,320]{1,2,0:T(8,128)(2,1)S(1)} %get-tuple-element.23), channel_id=1, source_target_pairs={{8,0},{16,8},{24,16},{9,1},{17,9},{25,17},{10,2},{18,10},{26,18},{... | collective-permute-start | bytes 245768 | tf_op jit(solution)/shard_map/ppermute | solution.py:20
  58.4 6.6 %collective-permute-start.10 = (bf16[1,128,320]{1,2,0:T(8,128)(2,1)S(1)}, bf16[1,128,320]{1,2,0:T(8,128)(2,1)S(1)}, u32[]{:S(2)}, u32[]{:S(2)}) collective-permute-start(bf16[1,128,320]{1,2,0:T(8,128)(2,1)S(1)} %get-tuple-element.22), channel_id=1, source_target_pairs={{0,8},{8,16},{16,24},{1,9},{9,17},{17,25},{2,10},{10,18},{18,26},{... | collective-permute-start | bytes 245768 | tf_op jit(solution)/shard_map/ppermute | solution.py:18
  71.1 2.5 %copy-start.2 = (bf16[1,3,128,320]{2,3,1,0:T(8,128)(2,1)S(1)}, bf16[1,3,128,320]{2,3,1,0:T(8,128)(2,1)}, u32[]{:S(2)}) copy-start(bf16[1,3,128,320]{2,3,1,0:T(8,128)(2,1)} %param.9) | copy-start | bytes 737284
  78.4 19.9 %copy-start.5 = (f32[360,320]{0,1:T(8,128)S(1)}, f32[360,320]{0,1:T(8,128)}, u32[]{:S(2)}) copy-start(f32[360,320]{0,1:T(8,128)} %param.15) | copy-start | bytes 1382404
  78.4 10.1 %collective-permute-start.14 = (f32[2,32]{1,0:T(2,128)S(1)}, f32[2,32]{1,0:T(2,128)S(1)}, u32[]{:S(2)}, u32[]{:S(2)}) collective-permute-start(f32[2,32]{1,0:T(2,128)S(1)} %pad_maximum_fusion.3), channel_id=1, source_target_pairs={{0,24},{8,0},{16,8},{24,16},{1,25},{9,1},{17,9},{25,17},{2,26},{10... | collective-permute-start | bytes 776 | tf_op jit(solution)/shard_map/ppermute | solution.py:33
  82.1 6.5 %collective-permute-start.13 = (f32[2,32]{1,0:T(2,128)S(1)}, f32[2,32]{1,0:T(2,128)S(1)}, u32[]{:S(2)}, u32[]{:S(2)}) collective-permute-start(f32[2,32]{1,0:T(2,128)S(1)} %pad_maximum_fusion.3), channel_id=1, source_target_pairs={{0,16},{8,24},{16,0},{24,8},{1,17},{9,25},{17,1},{25,9},{2,18},{10... | collective-permute-start | bytes 776 | tf_op jit(solution)/shard_map/ppermute | solution.py:33
  82.3 6.2 %collective-permute-start.12 = (f32[2,32]{1,0:T(2,128)S(1)}, f32[2,32]{1,0:T(2,128)S(1)}, u32[]{:S(2)}, u32[]{:S(2)}) collective-permute-start(f32[2,32]{1,0:T(2,128)S(1)} %pad_maximum_fusion.3), channel_id=1, source_target_pairs={{0,8},{8,16},{16,24},{24,0},{1,9},{9,17},{17,25},{25,1},{2,10},{10... | collective-permute-start | bytes 776 | tf_op jit(solution)/shard_map/ppermute | solution.py:33
  86.2 12.1 %collective-permute-start.15 = (bf16[360,320]{0,1:T(8,128)(2,1)S(1)}, bf16[360,320]{0,1:T(8,128)(2,1)S(1)}, u32[]{:S(2)}, u32[]{:S(2)}) collective-permute-start(bf16[360,320]{0,1:T(8,128)(2,1)S(1)} %convert_add_fusion.2), channel_id=1, source_target_pairs={{0,16},{8,24},{16,0},{24,8},{1,17},{9,25},{17,1},{25,9},{2,18},{10... | collective-permute-start | bytes 691208 | tf_op jit(solution)/shard_map/ppermute | solution.py:91
  (2 other events, 2.9 us)
Sparse Core Ops, SparseCore 0:
  16.5 27.7 all-gather.2

commit v17 on v16

--- a/solution.py
+++ b/solution.py
@@ -59,11 +59,11 @@
     while step < count:
         bit = (index // step) % 2
         paired = held.reshape(-1, 2, rows, channels)
-        keep = row_major(lax.dynamic_index_in_dim(paired, bit, axis=1, keepdims=False))
-        send = row_major(lax.dynamic_index_in_dim(paired, 1 - bit, axis=1, keepdims=False))
+        keep = lax.dynamic_index_in_dim(paired, bit, axis=1, keepdims=False)
+        send = lax.dynamic_index_in_dim(paired, 1 - bit, axis=1, keepdims=False)
         pairs = [(i, i ^ step) for i in range(count)]
         got = lax.ppermute(send.astype(jnp.bfloat16), axis, pairs)
-        held = row_major((keep.astype(jnp.float32) + got.astype(jnp.float32)).astype(jnp.bfloat16))
+        held = (keep.astype(jnp.float32) + got.astype(jnp.float32)).astype(jnp.bfloat16)
         step *= 2
         if step < count <= 4 * step:
             break

time: 108 us -> 107 us (level)
  local copies, waits for them, and re-layouts: 13.8 us -> 12.3 us
  other arithmetic: 9.96 us -> 11.1 us
    ppermute x1 -> x0, local copies, waits for them, and re-layouts: 1.64 us -> none  [halving_scatter(): got = lax.ppermute(send.astype(jnp.bfloat16), axis, pairs)]
    another operation x1 -> x0, local copies, waits for them, and re-layouts: 1.37 us -> none  [row_major(): with_layout_constraint(value, Layout(major_to_minor=tuple(range(value.ndi...]
    convert_element_type x1, other arithmetic: 0.29 us -> 1.45 us  [halving_scatter(): (keep.astype(jnp.float32) + got.astype(jnp.float32)).astype(jnp.bfloat16)]
    unnamed x32 -> x26, local copies, waits for them, and re-layouts: 3.16 us -> 3.68 us
where the time goes in v17:
time: 107 us
  starting transfers between devices  30.1 us (28%)
  waiting for transfers between devices  28.2 us (26%)
  between operations  15.8 us (15%)
  local copies, waits for them, and re-layouts  12.3 us (11%)
  other arithmetic  11.1 us (10%)
  matrix products  9.47 us (9%)
    ppermute x3, waiting for transfers between devices, halving_scatter(): lax.ppermute(send.astype(jnp.bfloat16), axis, pairs).astype(jnp.float32)  11.1 us
    ppermute x6, starting transfers between devices, space_sum(): lax.ppermute(joined, axis, [(i, (i + shift) % count) for i in range(count)])  10.4 us
    ppermute x2, starting transfers between devices, with_halo(): lax.ppermute(tail, axis, [(i, (i + 1) % count) for i in range(ends)])  9.1 us
    ppermute x2, waiting for transfers between devices, replicated_sum(): lax.ppermute(mine, axis, pairs).astype(jnp.float32)  7.5 us
    dot_general x1, matrix products, local(): upstream = jnp.dot(cot_cols, flipped, preferred_element_type=jnp.float32)  4.4 us
    ppermute x2, starting transfers between devices, replicated_sum(): lax.ppermute(mine, axis, pairs).astype(jnp.float32)  4.39 us
    ppermute x6, waiting for transfers between devices, space_sum(): lax.ppermute(joined, axis, [(i, (i + shift) % count) for i in range(count)])  4.33 us
    unnamed x26, local copies, waits for them, and re-layouts  3.68 us
  transfers between devices with their start and end apart: 17, of which 11 were waited for; matrix products, arithmetic and copies ran while one was open for 15% of the time, Pallas kernels for 0%

profile of v17, /device:TPU:0, one launch (start us, length us, event | category | flops | bytes accessed | tf_op | source)
XLA Modules:
  0.0 107.0 jit_solution(7647071468730449884)
XLA Ops:
  10.2 5.1 %collective-permute-start.2 = (f32[2,32]{1,0:T(2,128)S(1)}, f32[2,32]{1,0:T(2,128)S(1)}, u32[]{:S(2)}, u32[]{:S(2)}) collective-permute-start(f32[2,32]{1,0:T(2,128)S(1)} %pad_maximum_fusion.2), channel_id=1, source_target_pairs={{0,24},{8,0},{16,8},{24,16},{1,25},{9,1},{17,9},{25,17},{2,26},{10... | collective-permute-start | bytes 776 | tf_op jit(solution)/shard_map/ppermute | solution.py:33
  16.6 3.2 %collective-permute-done.1 = f32[2,32]{1,0:T(2,128)S(1)} collective-permute-done((f32[2,32]{1,0:T(2,128)S(1)}, f32[2,32]{1,0:T(2,128)S(1)}, u32[]{:S(2)}, u32[]{:S(2)}) %collective-permute-start.1) | collective-permute-done | bytes 288 | tf_op jit(solution)/shard_map/ppermute | solution.py:33
  21.1 1.3 %multiply_convert_fusion = bf16[3,128,320]{1,2,0:T(8,128)(2,1)S(1)} fusion(bf16[1,3,128,320]{2,3,1,0:T(8,128)(2,1)} %param.9, f32[320]{0:T(512)} %param.12, f32[320]{0:T(512)} %param.11, f32[320]{0:T(512)S(1)} %mul.163, f32[320]{0:T(512)S(1)} %sub.37, f32[3,128]{1,0:T(4,128)S(1)} %get-tuple-element.30), kind=kLoop, calls=%fused_computation.50 | loop fusion | flops 1597440 | bytes 498176 | tf_op jit(solution)/shard_map/convert_element_type | solution.py:132
  23.8 4.6 %collective-permute-start.3 = (bf16[1,128,320]{1,2,0:T(8,128)(2,1)S(1)}, bf16[1,128,320]{1,2,0:T(8,128)(2,1)S(1)}, u32[]{:S(2)}, u32[]{:S(2)}) collective-permute-start(bf16[1,128,320]{1,2,0:T(8,128)(2,1)S(1)} %get-tuple-element.25), channel_id=1, source_target_pairs={{0,8},{8,16},{16,24},{1,9},{9,17},{17,25},{2,10},{10,18},{18,26},{... | collective-permute-start | bytes 245768 | tf_op jit(solution)/shard_map/ppermute | solution.py:18
  31.9 1.5 %fusion = bf16[2880,320]{1,0:T(8,128)(2,1)S(1)} fusion(bf16[3,128,2880]{1,2,0:T(8,128)(2,1)S(1)} %slice_dynamic-update-slice_fusion, bf16[3,128,320]{1,2,0:T(8,128)(2,1)S(1)} %bitcast_multiply_fusion), kind=kOutput, calls=%fused_computation.1 | convolution fusion | flops 708710400 | bytes 4300800 | tf_op jit(solution)/shard_map/dot_general | solution.py:145
  33.7 1.4 %copy.25 = bf16[4,1,360,320]{2,3,0,1:T(8,128)(2,1)} copy(bf16[4,1,360,320]{3,2,1,0:T(8,128)(2,1)S(1)} %get-tuple-element.19) | data formatting | bytes 1843200 | tf_op jit(solution)/shard_map/jit(dynamic_index_in_dim)/dynamic_slice | solution.py:63
  35.8 2.2 %collective-permute-done.5 = bf16[4,360,320]{1,2,0:T(8,128)(2,1)} collective-permute-done((bf16[4,360,320]{1,2,0:T(8,128)(2,1)}, bf16[4,360,320]{1,2,0:T(8,128)(2,1)}, u32[]{:S(2)}, u32[]{:S(2)}) %collective-permute-start.5) | collective-permute-done | bytes 921632 | tf_op jit(solution)/shard_map/ppermute | solution.py:65
  38.0 1.4 %fusion.3 = bf16[4,360,320]{1,2,0:T(8,128)(2,1)S(1)} fusion(bf16[4,360,320]{1,2,0:T(8,128)(2,1)} %collective-permute-done.5, bf16[4,1,360,320]{2,3,0,1:T(8,128)(2,1)S(1)} %copy.39), kind=kLoop, calls=%fused_computation.7 | loop fusion | flops 1843200 | bytes 2764800 | tf_op jit(solution)/shard_map/convert_element_type | solution.py:66
  39.6 2.7 %collective-permute-start.8 = (bf16[360,320]{0,1:T(8,128)(2,1)S(1)}, bf16[360,320]{0,1:T(8,128)(2,1)S(1)}, u32[]{:S(2)}, u32[]{:S(2)}) collective-permute-start(bf16[360,320]{0,1:T(8,128)(2,1)S(1)} %get-tuple-element.21), channel_id=1, source_target_pairs={{0,6},{1,7},{2,4},{3,5},{4,2},{5,3},{6,0},{7,1},{8,14},{9,15},{10,... | collective-permute-start | bytes 691208 | tf_op jit(solution)/shard_map/ppermute | solution.py:78
  43.1 6.2 %collective-permute-done.8 = bf16[360,320]{0,1:T(8,128)(2,1)S(1)} collective-permute-done((bf16[360,320]{0,1:T(8,128)(2,1)S(1)}, bf16[360,320]{0,1:T(8,128)(2,1)S(1)}, u32[]{:S(2)}, u32[]{:S(2)}) %collective-permute-start.8) | collective-permute-done | bytes 230432 | tf_op jit(solution)/shard_map/ppermute | solution.py:78
  49.4 4.8 %collective-permute-done.7 = bf16[360,320]{0,1:T(8,128)(2,1)S(1)} collective-permute-done((bf16[360,320]{0,1:T(8,128)(2,1)S(1)}, bf16[360,320]{0,1:T(8,128)(2,1)S(1)}, u32[]{:S(2)}, u32[]{:S(2)}) %collective-permute-start.7) | collective-permute-done | bytes 230432 | tf_op jit(solution)/shard_map/ppermute | solution.py:78
  54.4 2.1 %collective-permute-start.9 = (bf16[360,320]{0,1:T(8,128)(2,1)S(1)}, bf16[360,320]{0,1:T(8,128)(2,1)S(1)}, u32[]{:S(2)}, u32[]{:S(2)}) collective-permute-start(bf16[360,320]{0,1:T(8,128)(2,1)S(1)} %fusion.40), channel_id=1, source_target_pairs={{0,8},{8,0},{16,24},{24,16},{1,9},{9,1},{17,25},{25,17},{2,10},{10... | collective-permute-start | bytes 691208 | tf_op jit(solution)/shard_map/ppermute | solution.py:91
  57.8 4.6 %collective-permute-start.10 = (bf16[1,128,320]{1,2,0:T(8,128)(2,1)S(1)}, bf16[1,128,320]{1,2,0:T(8,128)(2,1)S(1)}, u32[]{:S(2)}, u32[]{:S(2)}) collective-permute-start(bf16[1,128,320]{1,2,0:T(8,128)(2,1)S(1)} %get-tuple-element.23), channel_id=1, source_target_pairs={{0,8},{8,16},{16,24},{1,9},{9,17},{17,25},{2,10},{10,18},{18,26},{... | collective-permute-start | bytes 245768 | tf_op jit(solution)/shard_map/ppermute | solution.py:18
  62.3 1.9 %collective-permute-done.11 = bf16[1,128,320]{1,2,0:T(8,128)(2,1)S(1)} collective-permute-done((bf16[1,128,320]{1,2,0:T(8,128)(2,1)S(1)}, bf16[1,128,320]{1,2,0:T(8,128)(2,1)S(1)}, u32[]{:S(2)}, u32[]{:S(2)}) %collective-permute-start.11) | collective-permute-done | bytes 81952 | tf_op jit(solution)/shard_map/ppermute | solution.py:20
  64.9 3.0 %copy.28 = bf16[8,360,320]{2,1,0:T(8,128)(2,1)S(1)} copy(bf16[8,360,320]{1,2,0:T(8,128)(2,1)} %all-gather.3.cloned.1.call-done) | data formatting | bytes 3686400 | tf_op jit(solution)/shard_map/all_gather | solution.py:122
  69.1 1.3 %copy-done.3 = bf16[3,128,2880]{1,2,0:T(8,128)(2,1)} copy-done((bf16[3,128,2880]{1,2,0:T(8,128)(2,1)}, bf16[3,128,2880]{1,2,0:T(8,128)(2,1)S(1)}, u32[]{:S(2)}) %copy-start.3) | copy-done | bytes 2211864
  70.4 2.5 %copy.30 = bf16[9,320,320]{1,2,0:T(8,128)(2,1)} copy(bf16[9,320,320]{2,1,0:T(8,128)(2,1)S(1)} %bitcast.106) | data formatting | bytes 3686400 | tf_op jit(solution)/shard_map/reshape | solution.py:153
  72.9 4.4 %fusion.47 = (f32[320]{0:T(512)S(1)}, f32[320]{0:T(512)S(1)}, f32[3,128,320]{1,2,0:T(8,128)}) fusion(f32[320]{0:T(512)S(1)} %mul.163, f32[320]{0:T(512)S(1)} %sub.37, f32[3,128]{1,0:T(4,128)S(1)} %get-tuple-element.30, bf16[1,3,128,320]{2,3,1,0:T(8,128)(2,1)S(1)} %copy-done.1, f32[320]{0:T(512)S(1)} %copy-done.4, f32[320]{0:T(512)S(1)} %copy-done.5, ...), kind=kOutput, calls=%fused_computation.93 | convolution fusion | flops 710245760 | bytes 4801536 | tf_op jit(solution)/shard_map/dot_general | solution.py:163
  77.8 3.7 %collective-permute-start.14 = (f32[2,32]{1,0:T(2,128)S(1)}, f32[2,32]{1,0:T(2,128)S(1)}, u32[]{:S(2)}, u32[]{:S(2)}) collective-permute-start(f32[2,32]{1,0:T(2,128)S(1)} %pad_maximum_fusion.3), channel_id=1, source_target_pairs={{0,24},{8,0},{16,8},{24,16},{1,25},{9,1},{17,9},{25,17},{2,26},{10... | collective-permute-start | bytes 776 | tf_op jit(solution)/shard_map/ppermute | solution.py:33
  82.1 3.5 %fusion.13 = bf16[1,3,128,320]{2,3,1,0:T(8,128)(2,1)} fusion(bf16[3,128,2880]{1,2,0:T(8,128)(2,1)} %copy-done, bf16[2880,320]{1,0:T(8,128)(2,1)S(1)} %bitcast.107, f32[3,128]{1,0:T(4,128)S(1)} %get-tuple-element.30), kind=kOutput, calls=%fused_computation.14 | convolution fusion | flops 708034560 | bytes 4302336 | tf_op jit(solution)/shard_map/dot_general | solution.py:151
  85.6 2.3 %collective-permute-start.15 = (bf16[360,320]{0,1:T(8,128)(2,1)S(1)}, bf16[360,320]{0,1:T(8,128)(2,1)S(1)}, u32[]{:S(2)}, u32[]{:S(2)}) collective-permute-start(bf16[360,320]{0,1:T(8,128)(2,1)S(1)} %convert_add_fusion.3), channel_id=1, source_target_pairs={{0,16},{8,24},{16,0},{24,8},{1,17},{9,25},{17,1},{25,9},{2,18},{10... | collective-permute-start | bytes 691208 | tf_op jit(solution)/shard_map/ppermute | solution.py:91
  88.3 2.0 %fusion.43 = bf16[1,3,128,320]{2,3,1,0:T(8,128)(2,1)} fusion(f32[320]{0:T(512)S(1)} %mul.180, f32[320]{0:T(512)S(1)} %sub.37, f32[3,128]{1,0:T(4,128)S(1)} %get-tuple-element.30, bf16[1,3,128,320]{2,3,1,0:T(8,128)(2,1)S(1)} %copy-done.1, f32[3,128,320]{1,2,0:T(8,128)} %get-tuple-element.31, f32[320]{0:T(512)S(1)} %sub.44, f32[320]{0:T(512)S(1)} %mul.163), kind=kLoop, calls=%fused_computation.75 | loop fusion | flops 1351680 | bytes 989696 | tf_op jit(solution)/shard_map/broadcast_in_dim | solution.py:181
  90.3 7.5 %collective-permute-done.15 = bf16[360,320]{0,1:T(8,128)(2,1)S(1)} collective-permute-done((bf16[360,320]{0,1:T(8,128)(2,1)S(1)}, bf16[360,320]{0,1:T(8,128)(2,1)S(1)}, u32[]{:S(2)}, u32[]{:S(2)}) %collective-permute-start.15) | collective-permute-done | bytes 230432 | tf_op jit(solution)/shard_map/ppermute | solution.py:91
  97.8 2.3 %fusion.37 = (f32[360,320]{0,1:T(8,128)}, f32[360,320]{0,1:T(8,128)}) fusion(f32[360,320]{0,1:T(8,128)S(1)} %copy-done.2, f32[360,320]{0,1:T(8,128)} %param.14, bf16[360,320]{0,1:T(8,128)(2,1)S(1)} %collective-permute-done.15, bf16[360,320]{0,1:T(8,128)(2,1)S(1)} %convert_add_fusion.3), kind=kLoop, calls=%fused_computation.43 | loop fusion | flops 1612800 | bytes 2304000 | tf_op jit(solution)/shard_map/div | solution.py:180
  (87 shorter events, 15.7 us)
Async XLA Ops:
  7.2 57.7 %all-gather.3.cloned.1.call-start = ((), (), s32[]{:S(2)}) async-start(), calls=%async_computation | async-start | bytes 2211840 | tf_op jit(solution)/shard_map/all_gather | solution.py:122
  10.2 6.4 %collective-permute-start.2 = (f32[2,32]{1,0:T(2,128)S(1)}, f32[2,32]{1,0:T(2,128)S(1)}, u32[]{:S(2)}, u32[]{:S(2)}) collective-permute-start(f32[2,32]{1,0:T(2,128)S(1)} %pad_maximum_fusion.2), channel_id=1, source_target_pairs={{0,24},{8,0},{16,8},{24,16},{1,25},{9,1},{17,9},{25,17},{2,26},{10... | collective-permute-start | bytes 776 | tf_op jit(solution)/shard_map/ppermute | solution.py:33
  15.3 4.5 %collective-permute-start.1 = (f32[2,32]{1,0:T(2,128)S(1)}, f32[2,32]{1,0:T(2,128)S(1)}, u32[]{:S(2)}, u32[]{:S(2)}) collective-permute-start(f32[2,32]{1,0:T(2,128)S(1)} %pad_maximum_fusion.2), channel_id=1, source_target_pairs={{0,16},{8,24},{16,0},{24,8},{1,17},{9,25},{17,1},{25,9},{2,18},{10... | collective-permute-start | bytes 776 | tf_op jit(solution)/shard_map/ppermute | solution.py:33
  15.3 5.4 %collective-permute-start = (f32[2,32]{1,0:T(2,128)S(1)}, f32[2,32]{1,0:T(2,128)S(1)}, u32[]{:S(2)}, u32[]{:S(2)}) collective-permute-start(f32[2,32]{1,0:T(2,128)S(1)} %pad_maximum_fusion.2), channel_id=1, source_target_pairs={{0,8},{8,16},{16,24},{24,0},{1,9},{9,17},{17,25},{25,1},{2,10},{10... | collective-permute-start | bytes 776 | tf_op jit(solution)/shard_map/ppermute | solution.py:33
  21.1 10.0 %copy-start.1 = (bf16[1,3,128,320]{2,3,1,0:T(8,128)(2,1)S(1)}, bf16[1,3,128,320]{2,3,1,0:T(8,128)(2,1)}, u32[]{:S(2)}) copy-start(bf16[1,3,128,320]{2,3,1,0:T(8,128)(2,1)} %param.9) | copy-start | bytes 737284
  21.1 10.0 %copy-start.4 = (f32[320]{0:T(512)S(1)}, f32[320]{0:T(512)}, u32[]{:S(2)}) copy-start(f32[320]{0:T(512)} %param.12) | copy-start | bytes 3844
  21.1 10.0 %copy-start.5 = (f32[320]{0:T(512)S(1)}, f32[320]{0:T(512)}, u32[]{:S(2)}) copy-start(f32[320]{0:T(512)} %param.11) | copy-start | bytes 3844
  22.5 6.9 %collective-permute-start.4 = (bf16[1,128,320]{1,2,0:T(8,128)(2,1)S(1)}, bf16[1,128,320]{1,2,0:T(8,128)(2,1)S(1)}, u32[]{:S(2)}, u32[]{:S(2)}) collective-permute-start(bf16[1,128,320]{1,2,0:T(8,128)(2,1)S(1)} %get-tuple-element.26), channel_id=1, source_target_pairs={{8,0},{16,8},{24,16},{9,1},{17,9},{25,17},{10,2},{18,10},{26,18},{... | collective-permute-start | bytes 245768 | tf_op jit(solution)/shard_map/ppermute | solution.py:20
  23.8 6.6 %collective-permute-start.3 = (bf16[1,128,320]{1,2,0:T(8,128)(2,1)S(1)}, bf16[1,128,320]{1,2,0:T(8,128)(2,1)S(1)}, u32[]{:S(2)}, u32[]{:S(2)}) collective-permute-start(bf16[1,128,320]{1,2,0:T(8,128)(2,1)S(1)} %get-tuple-element.25), channel_id=1, source_target_pairs={{0,8},{8,16},{16,24},{1,9},{9,17},{17,25},{2,10},{10,18},{18,26},{... | collective-permute-start | bytes 245768 | tf_op jit(solution)/shard_map/ppermute | solution.py:18
  31.9 1.6 %copy-start = (bf16[3,128,2880]{1,2,0:T(8,128)(2,1)}, bf16[3,128,2880]{1,2,0:T(8,128)(2,1)S(1)}, u32[]{:S(2)}) copy-start(bf16[3,128,2880]{1,2,0:T(8,128)(2,1)S(1)} %slice_dynamic-update-slice_fusion) | copy-start | bytes 6635524
  35.1 2.9 %collective-permute-start.5 = (bf16[4,360,320]{1,2,0:T(8,128)(2,1)}, bf16[4,360,320]{1,2,0:T(8,128)(2,1)}, u32[]{:S(2)}, u32[]{:S(2)}) collective-permute-start(bf16[4,360,320]{1,2,0:T(8,128)(2,1)} %bitcast.109), channel_id=1, source_target_pairs={{0,1},{1,0},{2,3},{3,2},{4,5},{5,4},{6,7},{7,6},{8,9},{9,8},{10,11... | collective-permute-start | bytes 2764808 | tf_op jit(solution)/shard_map/ppermute | solution.py:65
  39.6 9.8 %collective-permute-start.8 = (bf16[360,320]{0,1:T(8,128)(2,1)S(1)}, bf16[360,320]{0,1:T(8,128)(2,1)S(1)}, u32[]{:S(2)}, u32[]{:S(2)}) collective-permute-start(bf16[360,320]{0,1:T(8,128)(2,1)S(1)} %get-tuple-element.21), channel_id=1, source_target_pairs={{0,6},{1,7},{2,4},{3,5},{4,2},{5,3},{6,0},{7,1},{8,14},{9,15},{10,... | collective-permute-start | bytes 691208 | tf_op jit(solution)/shard_map/ppermute | solution.py:78
  42.2 11.9 %collective-permute-start.7 = (bf16[360,320]{0,1:T(8,128)(2,1)S(1)}, bf16[360,320]{0,1:T(8,128)(2,1)S(1)}, u32[]{:S(2)}, u32[]{:S(2)}) collective-permute-start(bf16[360,320]{0,1:T(8,128)(2,1)S(1)} %get-tuple-element.22), channel_id=1, source_target_pairs={{0,4},{1,5},{2,6},{3,7},{4,0},{5,1},{6,2},{7,3},{8,12},{9,13},{10,... | collective-permute-start | bytes 691208 | tf_op jit(solution)/shard_map/ppermute | solution.py:78
  42.8 11.5 %collective-permute-start.6 = (bf16[360,320]{0,1:T(8,128)(2,1)S(1)}, bf16[360,320]{0,1:T(8,128)(2,1)S(1)}, u32[]{:S(2)}, u32[]{:S(2)}) collective-permute-start(bf16[360,320]{0,1:T(8,128)(2,1)S(1)} %get-tuple-element.20), channel_id=1, source_target_pairs={{0,2},{1,3},{2,0},{3,1},{4,6},{5,7},{6,4},{7,5},{8,10},{9,11},{10,... | collective-permute-start | bytes 691208 | tf_op jit(solution)/shard_map/ppermute | solution.py:78
  54.4 10.4 %collective-permute-start.9 = (bf16[360,320]{0,1:T(8,128)(2,1)S(1)}, bf16[360,320]{0,1:T(8,128)(2,1)S(1)}, u32[]{:S(2)}, u32[]{:S(2)}) collective-permute-start(bf16[360,320]{0,1:T(8,128)(2,1)S(1)} %fusion.40), channel_id=1, source_target_pairs={{0,8},{8,0},{16,24},{24,16},{1,9},{9,1},{17,25},{25,17},{2,10},{10... | collective-permute-start | bytes 691208 | tf_op jit(solution)/shard_map/ppermute | solution.py:91
  56.5 7.8 %collective-permute-start.11 = (bf16[1,128,320]{1,2,0:T(8,128)(2,1)S(1)}, bf16[1,128,320]{1,2,0:T(8,128)(2,1)S(1)}, u32[]{:S(2)}, u32[]{:S(2)}) collective-permute-start(bf16[1,128,320]{1,2,0:T(8,128)(2,1)S(1)} %get-tuple-element.24), channel_id=1, source_target_pairs={{8,0},{16,8},{24,16},{9,1},{17,9},{25,17},{10,2},{18,10},{26,18},{... | collective-permute-start | bytes 245768 | tf_op jit(solution)/shard_map/ppermute | solution.py:20
  57.8 6.6 %collective-permute-start.10 = (bf16[1,128,320]{1,2,0:T(8,128)(2,1)S(1)}, bf16[1,128,320]{1,2,0:T(8,128)(2,1)S(1)}, u32[]{:S(2)}, u32[]{:S(2)}) collective-permute-start(bf16[1,128,320]{1,2,0:T(8,128)(2,1)S(1)} %get-tuple-element.23), channel_id=1, source_target_pairs={{0,8},{8,16},{16,24},{1,9},{9,17},{17,25},{2,10},{10,18},{18,26},{... | collective-permute-start | bytes 245768 | tf_op jit(solution)/shard_map/ppermute | solution.py:18
  69.1 1.3 %copy-start.3 = (bf16[3,128,2880]{1,2,0:T(8,128)(2,1)}, bf16[3,128,2880]{1,2,0:T(8,128)(2,1)S(1)}, u32[]{:S(2)}) copy-start(bf16[3,128,2880]{1,2,0:T(8,128)(2,1)S(1)} %slice_dynamic-update-slice_fusion.6) | copy-start | bytes 6635524
  77.8 20.0 %copy-start.2 = (f32[360,320]{0,1:T(8,128)S(1)}, f32[360,320]{0,1:T(8,128)}, u32[]{:S(2)}) copy-start(f32[360,320]{0,1:T(8,128)} %param.15) | copy-start | bytes 1382404
  77.8 10.1 %collective-permute-start.14 = (f32[2,32]{1,0:T(2,128)S(1)}, f32[2,32]{1,0:T(2,128)S(1)}, u32[]{:S(2)}, u32[]{:S(2)}) collective-permute-start(f32[2,32]{1,0:T(2,128)S(1)} %pad_maximum_fusion.3), channel_id=1, source_target_pairs={{0,24},{8,0},{16,8},{24,16},{1,25},{9,1},{17,9},{25,17},{2,26},{10... | collective-permute-start | bytes 776 | tf_op jit(solution)/shard_map/ppermute | solution.py:33
  81.5 6.5 %collective-permute-start.13 = (f32[2,32]{1,0:T(2,128)S(1)}, f32[2,32]{1,0:T(2,128)S(1)}, u32[]{:S(2)}, u32[]{:S(2)}) collective-permute-start(f32[2,32]{1,0:T(2,128)S(1)} %pad_maximum_fusion.3), channel_id=1, source_target_pairs={{0,16},{8,24},{16,0},{24,8},{1,17},{9,25},{17,1},{25,9},{2,18},{10... | collective-permute-start | bytes 776 | tf_op jit(solution)/shard_map/ppermute | solution.py:33
  81.7 6.2 %collective-permute-start.12 = (f32[2,32]{1,0:T(2,128)S(1)}, f32[2,32]{1,0:T(2,128)S(1)}, u32[]{:S(2)}, u32[]{:S(2)}) collective-permute-start(f32[2,32]{1,0:T(2,128)S(1)} %pad_maximum_fusion.3), channel_id=1, source_target_pairs={{0,8},{8,16},{16,24},{24,0},{1,9},{9,17},{17,25},{25,1},{2,10},{10... | collective-permute-start | bytes 776 | tf_op jit(solution)/shard_map/ppermute | solution.py:33
  85.6 12.2 %collective-permute-start.15 = (bf16[360,320]{0,1:T(8,128)(2,1)S(1)}, bf16[360,320]{0,1:T(8,128)(2,1)S(1)}, u32[]{:S(2)}, u32[]{:S(2)}) collective-permute-start(bf16[360,320]{0,1:T(8,128)(2,1)S(1)} %convert_add_fusion.3), channel_id=1, source_target_pairs={{0,16},{8,24},{16,0},{24,8},{1,17},{9,25},{17,1},{25,9},{2,18},{10... | collective-permute-start | bytes 691208 | tf_op jit(solution)/shard_map/ppermute | solution.py:91
Sparse Core Ops, SparseCore 0:
  16.5 27.7 all-gather.2

commit v18 on v17

--- a/solution.py
+++ b/solution.py
@@ -159,8 +159,12 @@
         ],
         axis=-1,
     ).reshape(height_dev * width_dev, 9 * channels)
-    flipped = tap_weights.transpose(0, 2, 1).reshape(9 * channels, channels)
-    upstream = jnp.dot(cot_cols, flipped, preferred_element_type=jnp.float32)
+    upstream = lax.dot_general(
+        cot_cols.reshape(-1, 9, channels),
+        tap_weights,
+        (((1, 2), (0, 2)), ((), ())),
+        preferred_element_type=jnp.float32,
+    )
     gate_sig = jax.nn.sigmoid(before)
     silu_slope = gate_sig * (1.0 + before * (1.0 - gate_sig))
     scaled = upstream.reshape(height_dev, width_dev, channels) * silu_slope * inside * norm_gain

time: 107 us -> 107 us (level)
  matrix products: 9.47 us -> 7 us
  other arithmetic: 11.1 us -> 12.6 us
  local copies, waits for them, and re-layouts: 12.3 us -> 13.6 us
    reshape x1 -> x0, local copies, waits for them, and re-layouts: 2.49 us -> none  [local(): tap_weights = gathered.reshape(9, channels, channels)]
    dot_general x1, matrix products: 4.4 us -> 1.95 us  [local(): lax.dot_general(cot_cols.reshape(-1, 9, channels), tap_weights, (((1, 2),...]
    convert_element_type x1, other arithmetic: 0.13 us -> 1.31 us  [replicated_sum(): mine = value.astype(jnp.bfloat16)]
    all_gather x1, local copies, waits for them, and re-layouts: 2.97 us -> 4.06 us  [local(): lax.all_gather(row_major(weight), 'dp', axis=0, tiled=True)]
    dynamic_slice x1, local copies, waits for them, and re-layouts: 1.39 us -> 2.47 us  [halving_scatter(): send = lax.dynamic_index_in_dim(paired, 1 - bit, axis=1, keepdims=False)]
    unnamed x26 -> x30, local copies, waits for them, and re-layouts: 3.68 us -> 3.54 us
  transfers between devices with their start and end apart: 17 -> 17, of which waited for: 11 -> 10; matrix products, arithmetic and copies ran while one was open for 15% -> 20% of each run, Pallas kernels for 0% -> 0%
where the time goes in v18:
time: 107 us; the launch traced here: 106 us
  starting transfers between devices  29.6 us (28%)
  waiting for transfers between devices  27.6 us (26%)
  between operations  15.8 us (15%)
  local copies, waits for them, and re-layouts  13.6 us (13%)
  other arithmetic  12.6 us (12%)
  matrix products  7 us (7%)
    ppermute x3, waiting for transfers between devices, halving_scatter(): lax.ppermute(send.astype(jnp.bfloat16), axis, pairs).astype(jnp.float32)  11 us
    ppermute x6, starting transfers between devices, space_sum(): lax.ppermute(joined, axis, [(i, (i + shift) % count) for i in range(count)])  10 us
    ppermute x2, starting transfers between devices, with_halo(): lax.ppermute(tail, axis, [(i, (i + 1) % count) for i in range(ends)])  9.1 us
    ppermute x2, waiting for transfers between devices, replicated_sum(): lax.ppermute(mine, axis, pairs).astype(jnp.float32)  7.6 us
    ppermute x2, starting transfers between devices, replicated_sum(): lax.ppermute(mine, axis, pairs).astype(jnp.float32)  4.35 us
    ppermute x6, waiting for transfers between devices, space_sum(): lax.ppermute(joined, axis, [(i, (i + shift) % count) for i in range(count)])  4.33 us
    all_gather x1, local copies, waits for them, and re-layouts, local(): lax.all_gather(row_major(weight), 'dp', axis=0, tiled=True)  4.06 us
    unnamed x30, local copies, waits for them, and re-layouts  3.54 us
  transfers between devices with their start and end apart: 17, of which 10 were waited for; matrix products, arithmetic and copies ran while one was open for 20% of the time, Pallas kernels for 0%

profile of v18, /device:TPU:0, one launch (start us, length us, event | category | flops | bytes accessed | tf_op | source)
XLA Modules:
  0.0 106.1 jit_solution(2824813401083790925)
XLA Ops:
  10.2 5.1 %collective-permute-start.2 = (f32[2,32]{1,0:T(2,128)S(1)}, f32[2,32]{1,0:T(2,128)S(1)}, u32[]{:S(2)}, u32[]{:S(2)}) collective-permute-start(f32[2,32]{1,0:T(2,128)S(1)} %pad_maximum_fusion.2), channel_id=1, source_target_pairs={{0,24},{8,0},{16,8},{24,16},{1,25},{9,1},{17,9},{25,17},{2,26},{10... | collective-permute-start | bytes 776 | tf_op jit(solution)/shard_map/ppermute | solution.py:33
  16.6 3.2 %collective-permute-done.1 = f32[2,32]{1,0:T(2,128)S(1)} collective-permute-done((f32[2,32]{1,0:T(2,128)S(1)}, f32[2,32]{1,0:T(2,128)S(1)}, u32[]{:S(2)}, u32[]{:S(2)}) %collective-permute-start.1) | collective-permute-done | bytes 288 | tf_op jit(solution)/shard_map/ppermute | solution.py:33
  21.1 1.3 %multiply_convert_fusion = bf16[3,128,320]{1,2,0:T(8,128)(2,1)S(1)} fusion(bf16[1,3,128,320]{2,3,1,0:T(8,128)(2,1)} %param.9, f32[320]{0:T(512)} %param.12, f32[320]{0:T(512)} %param.11, f32[320]{0:T(512)S(1)} %mul.163, f32[320]{0:T(512)S(1)} %sub.37, f32[3,128]{1,0:T(4,128)S(1)} %get-tuple-element.30), kind=kLoop, calls=%fused_computation.51 | loop fusion | flops 1597440 | bytes 498176 | tf_op jit(solution)/shard_map/convert_element_type | solution.py:132
  23.8 4.6 %collective-permute-start.3 = (bf16[1,128,320]{1,2,0:T(8,128)(2,1)S(1)}, bf16[1,128,320]{1,2,0:T(8,128)(2,1)S(1)}, u32[]{:S(2)}, u32[]{:S(2)}) collective-permute-start(bf16[1,128,320]{1,2,0:T(8,128)(2,1)S(1)} %get-tuple-element.25), channel_id=1, source_target_pairs={{0,8},{8,16},{16,24},{1,9},{9,17},{17,25},{2,10},{10,18},{18,26},{... | collective-permute-start | bytes 245768 | tf_op jit(solution)/shard_map/ppermute | solution.py:18
  31.9 1.5 %fusion = bf16[2880,320]{1,0:T(8,128)(2,1)S(1)} fusion(bf16[3,128,2880]{1,2,0:T(8,128)(2,1)S(1)} %slice_dynamic-update-slice_fusion, bf16[3,128,320]{1,2,0:T(8,128)(2,1)S(1)} %bitcast_multiply_fusion), kind=kOutput, calls=%fused_computation.1 | convolution fusion | flops 708710400 | bytes 4300800 | tf_op jit(solution)/shard_map/dot_general | solution.py:145
  34.7 2.5 %copy.22 = bf16[4,1,360,320]{2,3,0,1:T(8,128)(2,1)} copy(bf16[4,1,360,320]{3,2,1,0:T(8,128)(2,1)} %get-tuple-element.19) | data formatting | bytes 1843200 | tf_op jit(solution)/shard_map/jit(dynamic_index_in_dim)/dynamic_slice | solution.py:63
  37.2 1.4 %copy.33 = bf16[4,1,360,320]{2,3,0,1:T(8,128)(2,1)} copy(bf16[4,1,360,320]{3,2,1,0:T(8,128)(2,1)S(1)} %get-tuple-element.18) | data formatting | bytes 1843200
  38.5 1.5 %collective-permute-done.5 = bf16[4,360,320]{1,2,0:T(8,128)(2,1)} collective-permute-done((bf16[4,360,320]{1,2,0:T(8,128)(2,1)}, bf16[4,360,320]{1,2,0:T(8,128)(2,1)}, u32[]{:S(2)}, u32[]{:S(2)}) %collective-permute-start.5) | collective-permute-done | bytes 921632 | tf_op jit(solution)/shard_map/ppermute | solution.py:65
  40.1 1.7 %fusion.3 = bf16[4,360,320]{1,2,0:T(8,128)(2,1)S(1)} fusion(bf16[4,360,320]{1,2,0:T(8,128)(2,1)} %collective-permute-done.5, bf16[4,1,360,320]{2,3,0,1:T(8,128)(2,1)} %copy.33), kind=kLoop, calls=%fused_computation.7 | loop fusion | flops 1843200 | bytes 2764800 | tf_op jit(solution)/shard_map/convert_element_type | solution.py:66
  42.7 2.4 %collective-permute-start.8 = (bf16[360,320]{0,1:T(8,128)(2,1)}, bf16[360,320]{0,1:T(8,128)(2,1)}, u32[]{:S(2)}, u32[]{:S(2)}) collective-permute-start(bf16[360,320]{0,1:T(8,128)(2,1)} %get-tuple-element.21), channel_id=1, source_target_pairs={{0,6},{1,7},{2,4},{3,5},{4,2},{5,3},{6,0},{7,1},{8,14},{9,15},{10,... | collective-permute-start | bytes 691208 | tf_op jit(solution)/shard_map/ppermute | solution.py:78
  46.2 6.6 %collective-permute-done.8 = bf16[360,320]{0,1:T(8,128)(2,1)} collective-permute-done((bf16[360,320]{0,1:T(8,128)(2,1)}, bf16[360,320]{0,1:T(8,128)(2,1)}, u32[]{:S(2)}, u32[]{:S(2)}) %collective-permute-start.8) | collective-permute-done | bytes 230432 | tf_op jit(solution)/shard_map/ppermute | solution.py:78
  52.8 4.4 %collective-permute-done.7 = bf16[360,320]{0,1:T(8,128)(2,1)} collective-permute-done((bf16[360,320]{0,1:T(8,128)(2,1)}, bf16[360,320]{0,1:T(8,128)(2,1)}, u32[]{:S(2)}, u32[]{:S(2)}) %collective-permute-start.7) | collective-permute-done | bytes 230432 | tf_op jit(solution)/shard_map/ppermute | solution.py:78
  57.2 1.3 %fusion.41 = bf16[360,320]{0,1:T(8,128)(2,1)S(1)} fusion(bf16[360,320]{0,1:T(8,128)(2,1)} %collective-permute-done.8, bf16[360,320]{0,1:T(8,128)(2,1)} %collective-permute-done.7, bf16[360,320]{0,1:T(8,128)(2,1)} %collective-permute-done.6, bf16[4,360,320]{1,2,0:T(8,128)(2,1)S(1)} %fusion.3, s32[]{:T(128)S(6)} %select_n.36), kind=kLoop, calls=%fused_computation.48 | loop fusion | flops 921600 | bytes 1152004 | tf_op jit(solution)/shard_map/convert_element_type | solution.py:89
  58.5 2.4 %collective-permute-start.9 = (bf16[360,320]{0,1:T(8,128)(2,1)S(1)}, bf16[360,320]{0,1:T(8,128)(2,1)S(1)}, u32[]{:S(2)}, u32[]{:S(2)}) collective-permute-start(bf16[360,320]{0,1:T(8,128)(2,1)S(1)} %fusion.41), channel_id=1, source_target_pairs={{0,8},{8,0},{16,24},{24,16},{1,9},{9,1},{17,25},{25,17},{2,10},{10... | collective-permute-start | bytes 691208 | tf_op jit(solution)/shard_map/ppermute | solution.py:91
  62.2 4.6 %collective-permute-start.10 = (bf16[1,128,320]{1,2,0:T(8,128)(2,1)S(1)}, bf16[1,128,320]{1,2,0:T(8,128)(2,1)S(1)}, u32[]{:S(2)}, u32[]{:S(2)}) collective-permute-start(bf16[1,128,320]{1,2,0:T(8,128)(2,1)S(1)} %get-tuple-element.23), channel_id=1, source_target_pairs={{0,8},{8,16},{16,24},{1,9},{9,17},{17,25},{2,10},{10,18},{18,26},{... | collective-permute-start | bytes 245768 | tf_op jit(solution)/shard_map/ppermute | solution.py:18
  66.7 1.9 %collective-permute-done.11 = bf16[1,128,320]{1,2,0:T(8,128)(2,1)S(1)} collective-permute-done((bf16[1,128,320]{1,2,0:T(8,128)(2,1)S(1)}, bf16[1,128,320]{1,2,0:T(8,128)(2,1)S(1)}, u32[]{:S(2)}, u32[]{:S(2)}) %collective-permute-start.11) | collective-permute-done | bytes 81952 | tf_op jit(solution)/shard_map/ppermute | solution.py:20
  69.3 4.1 %copy.25 = bf16[8,360,320]{2,1,0:T(8,128)(2,1)} copy(bf16[8,360,320]{1,2,0:T(8,128)(2,1)} %all-gather.3.cloned.1.call-done) | data formatting | bytes 3686400 | tf_op jit(solution)/shard_map/all_gather | solution.py:122
  75.1 2.0 %fusion.48 = (f32[320]{0:T(512)S(1)}, f32[320]{0:T(512)S(1)}, f32[3,128,320]{1,2,0:T(8,128)}) fusion(f32[320]{0:T(512)S(1)} %mul.163, f32[320]{0:T(512)S(1)} %sub.37, f32[3,128]{1,0:T(4,128)S(1)} %get-tuple-element.30, bf16[1,3,128,320]{2,3,1,0:T(8,128)(2,1)S(1)} %copy-done.1, f32[320]{0:T(512)S(1)} %copy-done.6, f32[320]{0:T(512)S(1)} %copy-done.7, ...), kind=kOutput, calls=%fused_computation.94 | convolution fusion | flops 710245760 | bytes 4801536 | tf_op jit(solution)/shard_map/dot_general | solution.py:162
  77.5 3.0 %collective-permute-start.14 = (f32[2,32]{1,0:T(2,128)S(1)}, f32[2,32]{1,0:T(2,128)S(1)}, u32[]{:S(2)}, u32[]{:S(2)}) collective-permute-start(f32[2,32]{1,0:T(2,128)S(1)} %pad_maximum_fusion.3), channel_id=1, source_target_pairs={{0,24},{8,0},{16,8},{24,16},{1,25},{9,1},{17,9},{25,17},{2,26},{10... | collective-permute-start | bytes 776 | tf_op jit(solution)/shard_map/ppermute | solution.py:33
  81.5 3.5 %fusion.14 = bf16[1,3,128,320]{2,3,1,0:T(8,128)(2,1)} fusion(bf16[3,128,2880]{1,2,0:T(8,128)(2,1)S(1)} %slice_dynamic-update-slice_fusion, bf16[2880,320]{1,0:T(8,128)(2,1)} %bitcast.113, f32[3,128]{1,0:T(4,128)S(1)} %get-tuple-element.30), kind=kOutput, calls=%fused_computation.15 | convolution fusion | flops 708034560 | bytes 4302336 | tf_op jit(solution)/shard_map/dot_general | solution.py:151
  85.0 2.0 %collective-permute-start.15 = (bf16[360,320]{0,1:T(8,128)(2,1)S(1)}, bf16[360,320]{0,1:T(8,128)(2,1)S(1)}, u32[]{:S(2)}, u32[]{:S(2)}) collective-permute-start(bf16[360,320]{0,1:T(8,128)(2,1)S(1)} %convert_add_fusion.3), channel_id=1, source_target_pairs={{0,16},{8,24},{16,0},{24,8},{1,17},{9,25},{17,1},{25,9},{2,18},{10... | collective-permute-start | bytes 691208 | tf_op jit(solution)/shard_map/ppermute | solution.py:91
  87.4 2.0 %fusion.44 = bf16[1,3,128,320]{2,3,1,0:T(8,128)(2,1)} fusion(f32[320]{0:T(512)S(1)} %mul.180, f32[320]{0:T(512)S(1)} %sub.37, f32[3,128]{1,0:T(4,128)S(1)} %get-tuple-element.30, bf16[1,3,128,320]{2,3,1,0:T(8,128)(2,1)S(1)} %copy-done.1, f32[3,128,320]{1,2,0:T(8,128)} %get-tuple-element.31, f32[320]{0:T(512)S(1)} %sub.44, f32[320]{0:T(512)S(1)} %mul.163), kind=kLoop, calls=%fused_computation.76 | loop fusion | flops 1351680 | bytes 989696 | tf_op jit(solution)/shard_map/broadcast_in_dim | solution.py:185
  89.4 7.6 %collective-permute-done.15 = bf16[360,320]{0,1:T(8,128)(2,1)S(1)} collective-permute-done((bf16[360,320]{0,1:T(8,128)(2,1)S(1)}, bf16[360,320]{0,1:T(8,128)(2,1)S(1)}, u32[]{:S(2)}, u32[]{:S(2)}) %collective-permute-start.15) | collective-permute-done | bytes 230432 | tf_op jit(solution)/shard_map/ppermute | solution.py:91
  97.0 2.3 %fusion.38 = (f32[360,320]{0,1:T(8,128)}, f32[360,320]{0,1:T(8,128)}) fusion(f32[360,320]{0,1:T(8,128)S(1)} %copy-done.5, f32[360,320]{0,1:T(8,128)} %param.14, bf16[360,320]{0,1:T(8,128)(2,1)S(1)} %collective-permute-done.15, bf16[360,320]{0,1:T(8,128)(2,1)S(1)} %convert_add_fusion.3), kind=kLoop, calls=%fused_computation.44 | loop fusion | flops 1612800 | bytes 2304000 | tf_op jit(solution)/shard_map/div | solution.py:184
  (90 shorter events, 17.7 us)
Async XLA Ops:
  7.2 62.1 %all-gather.3.cloned.1.call-start = ((), (), s32[]{:S(2)}) async-start(), calls=%async_computation | async-start | bytes 2211840 | tf_op jit(solution)/shard_map/all_gather | solution.py:122
  10.2 6.4 %collective-permute-start.2 = (f32[2,32]{1,0:T(2,128)S(1)}, f32[2,32]{1,0:T(2,128)S(1)}, u32[]{:S(2)}, u32[]{:S(2)}) collective-permute-start(f32[2,32]{1,0:T(2,128)S(1)} %pad_maximum_fusion.2), channel_id=1, source_target_pairs={{0,24},{8,0},{16,8},{24,16},{1,25},{9,1},{17,9},{25,17},{2,26},{10... | collective-permute-start | bytes 776 | tf_op jit(solution)/shard_map/ppermute | solution.py:33
  15.3 4.5 %collective-permute-start.1 = (f32[2,32]{1,0:T(2,128)S(1)}, f32[2,32]{1,0:T(2,128)S(1)}, u32[]{:S(2)}, u32[]{:S(2)}) collective-permute-start(f32[2,32]{1,0:T(2,128)S(1)} %pad_maximum_fusion.2), channel_id=1, source_target_pairs={{0,16},{8,24},{16,0},{24,8},{1,17},{9,25},{17,1},{25,9},{2,18},{10... | collective-permute-start | bytes 776 | tf_op jit(solution)/shard_map/ppermute | solution.py:33
  15.3 5.4 %collective-permute-start = (f32[2,32]{1,0:T(2,128)S(1)}, f32[2,32]{1,0:T(2,128)S(1)}, u32[]{:S(2)}, u32[]{:S(2)}) collective-permute-start(f32[2,32]{1,0:T(2,128)S(1)} %pad_maximum_fusion.2), channel_id=1, source_target_pairs={{0,8},{8,16},{16,24},{24,0},{1,9},{9,17},{17,25},{25,1},{2,10},{10... | collective-permute-start | bytes 776 | tf_op jit(solution)/shard_map/ppermute | solution.py:33
  21.1 10.0 %copy-start = (bf16[1,3,128,320]{2,3,1,0:T(8,128)(2,1)S(1)}, bf16[1,3,128,320]{2,3,1,0:T(8,128)(2,1)}, u32[]{:S(2)}) copy-start(bf16[1,3,128,320]{2,3,1,0:T(8,128)(2,1)} %param.9) | copy-start | bytes 737284
  21.1 10.0 %copy-start.6 = (f32[320]{0:T(512)S(1)}, f32[320]{0:T(512)}, u32[]{:S(2)}) copy-start(f32[320]{0:T(512)} %param.12) | copy-start | bytes 3844
  21.1 10.0 %copy-start.7 = (f32[320]{0:T(512)S(1)}, f32[320]{0:T(512)}, u32[]{:S(2)}) copy-start(f32[320]{0:T(512)} %param.11) | copy-start | bytes 3844
  22.5 6.9 %collective-permute-start.4 = (bf16[1,128,320]{1,2,0:T(8,128)(2,1)S(1)}, bf16[1,128,320]{1,2,0:T(8,128)(2,1)S(1)}, u32[]{:S(2)}, u32[]{:S(2)}) collective-permute-start(bf16[1,128,320]{1,2,0:T(8,128)(2,1)S(1)} %get-tuple-element.26), channel_id=1, source_target_pairs={{8,0},{16,8},{24,16},{9,1},{17,9},{25,17},{10,2},{18,10},{26,18},{... | collective-permute-start | bytes 245768 | tf_op jit(solution)/shard_map/ppermute | solution.py:20
  23.8 6.6 %collective-permute-start.3 = (bf16[1,128,320]{1,2,0:T(8,128)(2,1)S(1)}, bf16[1,128,320]{1,2,0:T(8,128)(2,1)S(1)}, u32[]{:S(2)}, u32[]{:S(2)}) collective-permute-start(bf16[1,128,320]{1,2,0:T(8,128)(2,1)S(1)} %get-tuple-element.25), channel_id=1, source_target_pairs={{0,8},{8,16},{16,24},{1,9},{9,17},{17,25},{2,10},{10,18},{18,26},{... | collective-permute-start | bytes 245768 | tf_op jit(solution)/shard_map/ppermute | solution.py:18
  29.3 2.6 %copy-start.2 = (bf16[3,128,320]{1,2,0:T(8,128)(2,1)}, bf16[3,128,320]{1,2,0:T(8,128)(2,1)S(1)}, u32[]{:S(2)}) copy-start(bf16[3,128,320]{1,2,0:T(8,128)(2,1)S(1)} %bitcast_multiply_fusion) | copy-start | bytes 737284
  37.2 2.9 %collective-permute-start.5 = (bf16[4,360,320]{1,2,0:T(8,128)(2,1)}, bf16[4,360,320]{1,2,0:T(8,128)(2,1)}, u32[]{:S(2)}, u32[]{:S(2)}) collective-permute-start(bf16[4,360,320]{1,2,0:T(8,128)(2,1)} %bitcast.115), channel_id=1, source_target_pairs={{0,1},{1,0},{2,3},{3,2},{4,5},{5,4},{6,7},{7,6},{8,9},{9,8},{10,11... | collective-permute-start | bytes 2764808 | tf_op jit(solution)/shard_map/ppermute | solution.py:65
  38.5 22.3 %copy-start.3 = (bf16[3,128,320]{1,2,0:T(8,128)(2,1)S(1)}, bf16[3,128,320]{1,2,0:T(8,128)(2,1)}, u32[]{:S(2)}) copy-start(bf16[3,128,320]{1,2,0:T(8,128)(2,1)} %copy-done.2) | copy-start | bytes 737284
  42.7 10.1 %collective-permute-start.8 = (bf16[360,320]{0,1:T(8,128)(2,1)}, bf16[360,320]{0,1:T(8,128)(2,1)}, u32[]{:S(2)}, u32[]{:S(2)}) collective-permute-start(bf16[360,320]{0,1:T(8,128)(2,1)} %get-tuple-element.21), channel_id=1, source_target_pairs={{0,6},{1,7},{2,4},{3,5},{4,2},{5,3},{6,0},{7,1},{8,14},{9,15},{10,... | collective-permute-start | bytes 691208 | tf_op jit(solution)/shard_map/ppermute | solution.py:78
  45.1 12.1 %collective-permute-start.7 = (bf16[360,320]{0,1:T(8,128)(2,1)}, bf16[360,320]{0,1:T(8,128)(2,1)}, u32[]{:S(2)}, u32[]{:S(2)}) collective-permute-start(bf16[360,320]{0,1:T(8,128)(2,1)} %get-tuple-element.22), channel_id=1, source_target_pairs={{0,4},{1,5},{2,6},{3,7},{4,0},{5,1},{6,2},{7,3},{8,12},{9,13},{10,... | collective-permute-start | bytes 691208 | tf_op jit(solution)/shard_map/ppermute | solution.py:78
  45.5 11.7 %collective-permute-start.6 = (bf16[360,320]{0,1:T(8,128)(2,1)}, bf16[360,320]{0,1:T(8,128)(2,1)}, u32[]{:S(2)}, u32[]{:S(2)}) collective-permute-start(bf16[360,320]{0,1:T(8,128)(2,1)} %get-tuple-element.20), channel_id=1, source_target_pairs={{0,2},{1,3},{2,0},{3,1},{4,6},{5,7},{6,4},{7,5},{8,10},{9,11},{10,... | collective-permute-start | bytes 691208 | tf_op jit(solution)/shard_map/ppermute | solution.py:78
  58.5 10.7 %collective-permute-start.9 = (bf16[360,320]{0,1:T(8,128)(2,1)S(1)}, bf16[360,320]{0,1:T(8,128)(2,1)S(1)}, u32[]{:S(2)}, u32[]{:S(2)}) collective-permute-start(bf16[360,320]{0,1:T(8,128)(2,1)S(1)} %fusion.41), channel_id=1, source_target_pairs={{0,8},{8,0},{16,24},{24,16},{1,9},{9,1},{17,25},{25,17},{2,10},{10... | collective-permute-start | bytes 691208 | tf_op jit(solution)/shard_map/ppermute | solution.py:91
  60.9 7.8 %collective-permute-start.11 = (bf16[1,128,320]{1,2,0:T(8,128)(2,1)S(1)}, bf16[1,128,320]{1,2,0:T(8,128)(2,1)S(1)}, u32[]{:S(2)}, u32[]{:S(2)}) collective-permute-start(bf16[1,128,320]{1,2,0:T(8,128)(2,1)S(1)} %get-tuple-element.24), channel_id=1, source_target_pairs={{8,0},{16,8},{24,16},{9,1},{17,9},{25,17},{10,2},{18,10},{26,18},{... | collective-permute-start | bytes 245768 | tf_op jit(solution)/shard_map/ppermute | solution.py:20
  62.2 6.6 %collective-permute-start.10 = (bf16[1,128,320]{1,2,0:T(8,128)(2,1)S(1)}, bf16[1,128,320]{1,2,0:T(8,128)(2,1)S(1)}, u32[]{:S(2)}, u32[]{:S(2)}) collective-permute-start(bf16[1,128,320]{1,2,0:T(8,128)(2,1)S(1)} %get-tuple-element.23), channel_id=1, source_target_pairs={{0,8},{8,16},{16,24},{1,9},{9,17},{17,25},{2,10},{10,18},{18,26},{... | collective-permute-start | bytes 245768 | tf_op jit(solution)/shard_map/ppermute | solution.py:18
  73.3 1.8 %copy-start.4 = (bf16[8,360,320]{2,1,0:T(8,128)(2,1)S(1)}, bf16[8,360,320]{2,1,0:T(8,128)(2,1)}, u32[]{:S(2)}) copy-start(bf16[8,360,320]{2,1,0:T(8,128)(2,1)} %copy.25) | copy-start | bytes 5529604
  77.5 19.5 %copy-start.5 = (f32[360,320]{0,1:T(8,128)S(1)}, f32[360,320]{0,1:T(8,128)}, u32[]{:S(2)}) copy-start(f32[360,320]{0,1:T(8,128)} %param.15) | copy-start | bytes 1382404
  77.5 9.5 %collective-permute-start.14 = (f32[2,32]{1,0:T(2,128)S(1)}, f32[2,32]{1,0:T(2,128)S(1)}, u32[]{:S(2)}, u32[]{:S(2)}) collective-permute-start(f32[2,32]{1,0:T(2,128)S(1)} %pad_maximum_fusion.3), channel_id=1, source_target_pairs={{0,24},{8,0},{16,8},{24,16},{1,25},{9,1},{17,9},{25,17},{2,26},{10... | collective-permute-start | bytes 776 | tf_op jit(solution)/shard_map/ppermute | solution.py:33
  80.5 6.5 %collective-permute-start.13 = (f32[2,32]{1,0:T(2,128)S(1)}, f32[2,32]{1,0:T(2,128)S(1)}, u32[]{:S(2)}, u32[]{:S(2)}) collective-permute-start(f32[2,32]{1,0:T(2,128)S(1)} %pad_maximum_fusion.3), channel_id=1, source_target_pairs={{0,16},{8,24},{16,0},{24,8},{1,17},{9,25},{17,1},{25,9},{2,18},{10... | collective-permute-start | bytes 776 | tf_op jit(solution)/shard_map/ppermute | solution.py:33
  81.4 5.6 %collective-permute-start.12 = (f32[2,32]{1,0:T(2,128)S(1)}, f32[2,32]{1,0:T(2,128)S(1)}, u32[]{:S(2)}, u32[]{:S(2)}) collective-permute-start(f32[2,32]{1,0:T(2,128)S(1)} %pad_maximum_fusion.3), channel_id=1, source_target_pairs={{0,8},{8,16},{16,24},{24,0},{1,9},{9,17},{17,25},{25,1},{2,10},{10... | collective-permute-start | bytes 776 | tf_op jit(solution)/shard_map/ppermute | solution.py:33
  85.0 12.0 %collective-permute-start.15 = (bf16[360,320]{0,1:T(8,128)(2,1)S(1)}, bf16[360,320]{0,1:T(8,128)(2,1)S(1)}, u32[]{:S(2)}, u32[]{:S(2)}) collective-permute-start(bf16[360,320]{0,1:T(8,128)(2,1)S(1)} %convert_add_fusion.3), channel_id=1, source_target_pairs={{0,16},{8,24},{16,0},{24,8},{1,17},{9,25},{17,1},{25,9},{2,18},{10... | collective-permute-start | bytes 691208 | tf_op jit(solution)/shard_map/ppermute | solution.py:91
  (1 other events, 1.2 us)
Sparse Core Ops, SparseCore 0:
  16.5 27.7 all-gather.2

commit v19 on v18

--- a/solution.py
+++ b/solution.py
@@ -71,7 +71,8 @@
         return held[0].astype(jnp.float32), companions
     spots = count // step
     own = index // step
-    total = lax.dynamic_index_in_dim(held, own, keepdims=False).astype(jnp.float32)
+    tied, companions = lax.optimization_barrier((held, companions))
+    total = lax.dynamic_index_in_dim(tied, own, keepdims=False).astype(jnp.float32)
     for shift in range(1, spots):
         send = lax.dynamic_index_in_dim(held, own ^ shift, keepdims=False)
         pairs = [(i, i ^ (shift * step)) for i in range(count)]
@@ -146,8 +147,8 @@
         act_cols, flat_cot, (((0,), (0,)), ((), ())), preferred_element_type=jnp.float32
     ).astype(jnp.bfloat16)
     weight_terms = row_major(weight_terms)
-    grad_piece, companions = halving_scatter(weight_terms, "dp", (gathered, cot_pad))
-    grad_piece, (gathered, cot_pad) = replicated_sum(grad_piece, "space", companions)
+    grad_piece, gathered = halving_scatter(weight_terms, "dp", gathered)
+    grad_piece, (gathered, cot_pad) = replicated_sum(grad_piece, "space", (gathered, cot_pad))
     output = jnp.dot(act_cols, gathered, preferred_element_type=jnp.float32)
     block_out = (output.reshape(height_dev, width_dev, channels) * inside).astype(jnp.bfloat16)
     tap_weights = gathered.reshape(9, channels, channels)

time: 107 us -> 103 us (0.963)
  waiting for transfers between devices: 27.6 us -> 23.4 us
    ppermute x3, waiting for transfers between devices: 11 us -> 6.91 us  [halving_scatter(): lax.ppermute(send.astype(jnp.bfloat16), axis, pairs).astype(jnp.float32)]
  transfers between devices with their start and end apart: 17 -> 17, of which waited for: 10 -> 10; matrix products, arithmetic and copies ran while one was open for 20% -> 23% of each run, Pallas kernels for 0% -> 0%
where the time goes in v19:
time: 103 us; the launch traced here: 102 us
  starting transfers between devices  29.6 us (29%)
  waiting for transfers between devices  23.4 us (23%)
  between operations  15.8 us (15%)
  local copies, waits for them, and re-layouts  13.6 us (13%)
  other arithmetic  12.6 us (12%)
  matrix products  7 us (7%)
    ppermute x6, starting transfers between devices, space_sum(): lax.ppermute(joined, axis, [(i, (i + shift) % count) for i in range(count)])  10 us
    ppermute x2, starting transfers between devices, with_halo(): lax.ppermute(tail, axis, [(i, (i + 1) % count) for i in range(ends)])  9.1 us
    ppermute x2, waiting for transfers between devices, replicated_sum(): lax.ppermute(mine, axis, pairs).astype(jnp.float32)  7.6 us
    ppermute x3, waiting for transfers between devices, halving_scatter(): lax.ppermute(send.astype(jnp.bfloat16), axis, pairs).astype(jnp.float32)  6.91 us
    ppermute x2, starting transfers between devices, replicated_sum(): lax.ppermute(mine, axis, pairs).astype(jnp.float32)  4.35 us
    ppermute x6, waiting for transfers between devices, space_sum(): lax.ppermute(joined, axis, [(i, (i + shift) % count) for i in range(count)])  4.33 us
    all_gather x1, local copies, waits for them, and re-layouts, local(): lax.all_gather(row_major(weight), 'dp', axis=0, tiled=True)  4.1 us
    unnamed x30, local copies, waits for them, and re-layouts  3.53 us
  transfers between devices with their start and end apart: 17, of which 10 were waited for; matrix products, arithmetic and copies ran while one was open for 23% of the time, Pallas kernels for 0%

profile of v19, /device:TPU:0, one launch (start us, length us, event | category | flops | bytes accessed | tf_op | source)
XLA Modules:
  0.0 102.0 jit_solution(4039586151169453565)
XLA Ops:
  10.2 5.1 %collective-permute-start.2 = (f32[2,32]{1,0:T(2,128)S(1)}, f32[2,32]{1,0:T(2,128)S(1)}, u32[]{:S(2)}, u32[]{:S(2)}) collective-permute-start(f32[2,32]{1,0:T(2,128)S(1)} %pad_maximum_fusion.2), channel_id=1, source_target_pairs={{0,24},{8,0},{16,8},{24,16},{1,25},{9,1},{17,9},{25,17},{2,26},{10... | collective-permute-start | bytes 776 | tf_op jit(solution)/shard_map/ppermute | solution.py:33
  16.6 3.2 %collective-permute-done.1 = f32[2,32]{1,0:T(2,128)S(1)} collective-permute-done((f32[2,32]{1,0:T(2,128)S(1)}, f32[2,32]{1,0:T(2,128)S(1)}, u32[]{:S(2)}, u32[]{:S(2)}) %collective-permute-start.1) | collective-permute-done | bytes 288 | tf_op jit(solution)/shard_map/ppermute | solution.py:33
  21.1 1.3 %multiply_convert_fusion = bf16[3,128,320]{1,2,0:T(8,128)(2,1)S(1)} fusion(bf16[1,3,128,320]{2,3,1,0:T(8,128)(2,1)} %param.9, f32[320]{0:T(512)} %param.12, f32[320]{0:T(512)} %param.11, f32[320]{0:T(512)S(1)} %mul.163, f32[320]{0:T(512)S(1)} %sub.37, f32[3,128]{1,0:T(4,128)S(1)} %get-tuple-element.34), kind=kLoop, calls=%fused_computation.51 | loop fusion | flops 1597440 | bytes 498176 | tf_op jit(solution)/shard_map/convert_element_type | solution.py:133
  23.8 4.6 %collective-permute-start.3 = (bf16[1,128,320]{1,2,0:T(8,128)(2,1)S(1)}, bf16[1,128,320]{1,2,0:T(8,128)(2,1)S(1)}, u32[]{:S(2)}, u32[]{:S(2)}) collective-permute-start(bf16[1,128,320]{1,2,0:T(8,128)(2,1)S(1)} %get-tuple-element.29), channel_id=1, source_target_pairs={{0,8},{8,16},{16,24},{1,9},{9,17},{17,25},{2,10},{10,18},{18,26},{... | collective-permute-start | bytes 245768 | tf_op jit(solution)/shard_map/ppermute | solution.py:18
  31.9 1.5 %fusion = bf16[2880,320]{1,0:T(8,128)(2,1)S(1)} fusion(bf16[3,128,2880]{1,2,0:T(8,128)(2,1)S(1)} %slice_dynamic-update-slice_fusion, bf16[3,128,320]{1,2,0:T(8,128)(2,1)S(1)} %bitcast_multiply_fusion), kind=kOutput, calls=%fused_computation.1 | convolution fusion | flops 708710400 | bytes 4300800 | tf_op jit(solution)/shard_map/dot_general | solution.py:146
  34.7 2.5 %copy.22 = bf16[4,1,360,320]{2,3,0,1:T(8,128)(2,1)} copy(bf16[4,1,360,320]{3,2,1,0:T(8,128)(2,1)} %get-tuple-element.23) | data formatting | bytes 1843200 | tf_op jit(solution)/shard_map/jit(dynamic_index_in_dim)/dynamic_slice | solution.py:63
  37.2 1.4 %copy.33 = bf16[4,1,360,320]{2,3,0,1:T(8,128)(2,1)} copy(bf16[4,1,360,320]{3,2,1,0:T(8,128)(2,1)S(1)} %get-tuple-element.22) | data formatting | bytes 1843200
  38.5 1.5 %collective-permute-done.5 = bf16[4,360,320]{1,2,0:T(8,128)(2,1)} collective-permute-done((bf16[4,360,320]{1,2,0:T(8,128)(2,1)}, bf16[4,360,320]{1,2,0:T(8,128)(2,1)}, u32[]{:S(2)}, u32[]{:S(2)}) %collective-permute-start.5) | collective-permute-done | bytes 921632 | tf_op jit(solution)/shard_map/ppermute | solution.py:65
  40.1 1.7 %fusion.3 = bf16[4,360,320]{1,2,0:T(8,128)(2,1)S(1)} fusion(bf16[4,360,320]{1,2,0:T(8,128)(2,1)} %collective-permute-done.5, bf16[4,1,360,320]{2,3,0,1:T(8,128)(2,1)} %copy.33), kind=kLoop, calls=%fused_computation.7 | loop fusion | flops 1843200 | bytes 2764800 | tf_op jit(solution)/shard_map/convert_element_type | solution.py:66
  42.7 2.4 %collective-permute-start.8 = (bf16[360,320]{0,1:T(8,128)(2,1)}, bf16[360,320]{0,1:T(8,128)(2,1)}, u32[]{:S(2)}, u32[]{:S(2)}) collective-permute-start(bf16[360,320]{0,1:T(8,128)(2,1)} %get-tuple-element.25), channel_id=1, source_target_pairs={{0,6},{1,7},{2,4},{3,5},{4,2},{5,3},{6,0},{7,1},{8,14},{9,15},{10,... | collective-permute-start | bytes 691208 | tf_op jit(solution)/shard_map/ppermute | solution.py:79
  46.2 4.1 %copy.25 = bf16[8,360,320]{2,1,0:T(8,128)(2,1)} copy(bf16[8,360,320]{1,2,0:T(8,128)(2,1)} %all-gather.3.cloned.1.call-done) | data formatting | bytes 3686400 | tf_op jit(solution)/shard_map/all_gather | solution.py:123
  50.3 2.5 %collective-permute-done.8 = bf16[360,320]{0,1:T(8,128)(2,1)} collective-permute-done((bf16[360,320]{0,1:T(8,128)(2,1)}, bf16[360,320]{0,1:T(8,128)(2,1)}, u32[]{:S(2)}, u32[]{:S(2)}) %collective-permute-start.8) | collective-permute-done | bytes 230432 | tf_op jit(solution)/shard_map/ppermute | solution.py:79
  52.8 4.4 %collective-permute-done.7 = bf16[360,320]{0,1:T(8,128)(2,1)} collective-permute-done((bf16[360,320]{0,1:T(8,128)(2,1)}, bf16[360,320]{0,1:T(8,128)(2,1)}, u32[]{:S(2)}, u32[]{:S(2)}) %collective-permute-start.7) | collective-permute-done | bytes 230432 | tf_op jit(solution)/shard_map/ppermute | solution.py:79
  57.2 1.3 %fusion.41 = bf16[360,320]{0,1:T(8,128)(2,1)S(1)} fusion(bf16[360,320]{0,1:T(8,128)(2,1)} %collective-permute-done.8, bf16[360,320]{0,1:T(8,128)(2,1)} %collective-permute-done.7, bf16[360,320]{0,1:T(8,128)(2,1)} %collective-permute-done.6, bf16[4,360,320]{1,2,0:T(8,128)(2,1)S(1)} %fusion.3, s32[]{:T(128)S(6)} %select_n.36), kind=kLoop, calls=%fused_computation.48 | loop fusion | flops 921600 | bytes 1152004 | tf_op jit(solution)/shard_map/convert_element_type | solution.py:90
  58.5 2.4 %collective-permute-start.9 = (bf16[360,320]{0,1:T(8,128)(2,1)S(1)}, bf16[360,320]{0,1:T(8,128)(2,1)S(1)}, u32[]{:S(2)}, u32[]{:S(2)}) collective-permute-start(bf16[360,320]{0,1:T(8,128)(2,1)S(1)} %fusion.41), channel_id=1, source_target_pairs={{0,8},{8,0},{16,24},{24,16},{1,9},{9,1},{17,25},{25,17},{2,10},{10... | collective-permute-start | bytes 691208 | tf_op jit(solution)/shard_map/ppermute | solution.py:92
  62.2 4.6 %collective-permute-start.10 = (bf16[1,128,320]{1,2,0:T(8,128)(2,1)S(1)}, bf16[1,128,320]{1,2,0:T(8,128)(2,1)S(1)}, u32[]{:S(2)}, u32[]{:S(2)}) collective-permute-start(bf16[1,128,320]{1,2,0:T(8,128)(2,1)S(1)} %get-tuple-element.27), channel_id=1, source_target_pairs={{0,8},{8,16},{16,24},{1,9},{9,17},{17,25},{2,10},{10,18},{18,26},{... | collective-permute-start | bytes 245768 | tf_op jit(solution)/shard_map/ppermute | solution.py:18
  66.7 1.9 %collective-permute-done.11 = bf16[1,128,320]{1,2,0:T(8,128)(2,1)S(1)} collective-permute-done((bf16[1,128,320]{1,2,0:T(8,128)(2,1)S(1)}, bf16[1,128,320]{1,2,0:T(8,128)(2,1)S(1)}, u32[]{:S(2)}, u32[]{:S(2)}) %collective-permute-start.11) | collective-permute-done | bytes 81952 | tf_op jit(solution)/shard_map/ppermute | solution.py:20
  71.0 1.9 %fusion.48 = (f32[320]{0:T(512)S(1)}, f32[320]{0:T(512)S(1)}, f32[3,128,320]{1,2,0:T(8,128)}) fusion(f32[320]{0:T(512)S(1)} %mul.163, f32[320]{0:T(512)S(1)} %sub.37, f32[3,128]{1,0:T(4,128)S(1)} %get-tuple-element.34, bf16[1,3,128,320]{2,3,1,0:T(8,128)(2,1)S(1)} %copy-done.1, f32[320]{0:T(512)S(1)} %copy-done.6, f32[320]{0:T(512)S(1)} %copy-done.7, ...), kind=kOutput, calls=%fused_computation.94 | convolution fusion | flops 710245760 | bytes 4801536 | tf_op jit(solution)/shard_map/dot_general | solution.py:163
  73.5 3.0 %collective-permute-start.14 = (f32[2,32]{1,0:T(2,128)S(1)}, f32[2,32]{1,0:T(2,128)S(1)}, u32[]{:S(2)}, u32[]{:S(2)}) collective-permute-start(f32[2,32]{1,0:T(2,128)S(1)} %pad_maximum_fusion.3), channel_id=1, source_target_pairs={{0,24},{8,0},{16,8},{24,16},{1,25},{9,1},{17,9},{25,17},{2,26},{10... | collective-permute-start | bytes 776 | tf_op jit(solution)/shard_map/ppermute | solution.py:33
  77.4 3.5 %fusion.14 = bf16[1,3,128,320]{2,3,1,0:T(8,128)(2,1)} fusion(bf16[3,128,2880]{1,2,0:T(8,128)(2,1)S(1)} %slice_dynamic-update-slice_fusion, bf16[2880,320]{1,0:T(8,128)(2,1)} %bitcast.113, f32[3,128]{1,0:T(4,128)S(1)} %get-tuple-element.34), kind=kOutput, calls=%fused_computation.15 | convolution fusion | flops 708034560 | bytes 4302336 | tf_op jit(solution)/shard_map/dot_general | solution.py:152
  80.9 2.0 %collective-permute-start.15 = (bf16[360,320]{0,1:T(8,128)(2,1)S(1)}, bf16[360,320]{0,1:T(8,128)(2,1)S(1)}, u32[]{:S(2)}, u32[]{:S(2)}) collective-permute-start(bf16[360,320]{0,1:T(8,128)(2,1)S(1)} %convert_add_fusion.3), channel_id=1, source_target_pairs={{0,16},{8,24},{16,0},{24,8},{1,17},{9,25},{17,1},{25,9},{2,18},{10... | collective-permute-start | bytes 691208 | tf_op jit(solution)/shard_map/ppermute | solution.py:92
  83.3 2.0 %fusion.44 = bf16[1,3,128,320]{2,3,1,0:T(8,128)(2,1)} fusion(f32[320]{0:T(512)S(1)} %mul.180, f32[320]{0:T(512)S(1)} %sub.37, f32[3,128]{1,0:T(4,128)S(1)} %get-tuple-element.34, bf16[1,3,128,320]{2,3,1,0:T(8,128)(2,1)S(1)} %copy-done.1, f32[3,128,320]{1,2,0:T(8,128)} %get-tuple-element.35, f32[320]{0:T(512)S(1)} %sub.44, f32[320]{0:T(512)S(1)} %mul.163), kind=kLoop, calls=%fused_computation.76 | loop fusion | flops 1351680 | bytes 989696 | tf_op jit(solution)/shard_map/broadcast_in_dim | solution.py:186
  85.3 7.6 %collective-permute-done.15 = bf16[360,320]{0,1:T(8,128)(2,1)S(1)} collective-permute-done((bf16[360,320]{0,1:T(8,128)(2,1)S(1)}, bf16[360,320]{0,1:T(8,128)(2,1)S(1)}, u32[]{:S(2)}, u32[]{:S(2)}) %collective-permute-start.15) | collective-permute-done | bytes 230432 | tf_op jit(solution)/shard_map/ppermute | solution.py:92
  92.9 2.3 %fusion.38 = (f32[360,320]{0,1:T(8,128)}, f32[360,320]{0,1:T(8,128)}) fusion(f32[360,320]{0,1:T(8,128)S(1)} %copy-done.5, f32[360,320]{0,1:T(8,128)} %param.14, bf16[360,320]{0,1:T(8,128)(2,1)S(1)} %collective-permute-done.15, bf16[360,320]{0,1:T(8,128)(2,1)S(1)} %convert_add_fusion.3), kind=kLoop, calls=%fused_computation.44 | loop fusion | flops 1612800 | bytes 2304000 | tf_op jit(solution)/shard_map/div | solution.py:185
  (90 shorter events, 17.7 us)
Async XLA Ops:
  7.2 39.0 %all-gather.3.cloned.1.call-start = ((), (), s32[]{:S(2)}) async-start(), calls=%async_computation | async-start | bytes 2211840 | tf_op jit(solution)/shard_map/all_gather | solution.py:123
  10.2 6.4 %collective-permute-start.2 = (f32[2,32]{1,0:T(2,128)S(1)}, f32[2,32]{1,0:T(2,128)S(1)}, u32[]{:S(2)}, u32[]{:S(2)}) collective-permute-start(f32[2,32]{1,0:T(2,128)S(1)} %pad_maximum_fusion.2), channel_id=1, source_target_pairs={{0,24},{8,0},{16,8},{24,16},{1,25},{9,1},{17,9},{25,17},{2,26},{10... | collective-permute-start | bytes 776 | tf_op jit(solution)/shard_map/ppermute | solution.py:33
  15.3 4.5 %collective-permute-start.1 = (f32[2,32]{1,0:T(2,128)S(1)}, f32[2,32]{1,0:T(2,128)S(1)}, u32[]{:S(2)}, u32[]{:S(2)}) collective-permute-start(f32[2,32]{1,0:T(2,128)S(1)} %pad_maximum_fusion.2), channel_id=1, source_target_pairs={{0,16},{8,24},{16,0},{24,8},{1,17},{9,25},{17,1},{25,9},{2,18},{10... | collective-permute-start | bytes 776 | tf_op jit(solution)/shard_map/ppermute | solution.py:33
  15.3 5.4 %collective-permute-start = (f32[2,32]{1,0:T(2,128)S(1)}, f32[2,32]{1,0:T(2,128)S(1)}, u32[]{:S(2)}, u32[]{:S(2)}) collective-permute-start(f32[2,32]{1,0:T(2,128)S(1)} %pad_maximum_fusion.2), channel_id=1, source_target_pairs={{0,8},{8,16},{16,24},{24,0},{1,9},{9,17},{17,25},{25,1},{2,10},{10... | collective-permute-start | bytes 776 | tf_op jit(solution)/shard_map/ppermute | solution.py:33
  21.1 10.0 %copy-start = (bf16[1,3,128,320]{2,3,1,0:T(8,128)(2,1)S(1)}, bf16[1,3,128,320]{2,3,1,0:T(8,128)(2,1)}, u32[]{:S(2)}) copy-start(bf16[1,3,128,320]{2,3,1,0:T(8,128)(2,1)} %param.9) | copy-start | bytes 737284
  21.1 10.0 %copy-start.6 = (f32[320]{0:T(512)S(1)}, f32[320]{0:T(512)}, u32[]{:S(2)}) copy-start(f32[320]{0:T(512)} %param.12) | copy-start | bytes 3844
  21.1 10.0 %copy-start.7 = (f32[320]{0:T(512)S(1)}, f32[320]{0:T(512)}, u32[]{:S(2)}) copy-start(f32[320]{0:T(512)} %param.11) | copy-start | bytes 3844
  22.5 6.9 %collective-permute-start.4 = (bf16[1,128,320]{1,2,0:T(8,128)(2,1)S(1)}, bf16[1,128,320]{1,2,0:T(8,128)(2,1)S(1)}, u32[]{:S(2)}, u32[]{:S(2)}) collective-permute-start(bf16[1,128,320]{1,2,0:T(8,128)(2,1)S(1)} %get-tuple-element.30), channel_id=1, source_target_pairs={{8,0},{16,8},{24,16},{9,1},{17,9},{25,17},{10,2},{18,10},{26,18},{... | collective-permute-start | bytes 245768 | tf_op jit(solution)/shard_map/ppermute | solution.py:20
  23.8 6.6 %collective-permute-start.3 = (bf16[1,128,320]{1,2,0:T(8,128)(2,1)S(1)}, bf16[1,128,320]{1,2,0:T(8,128)(2,1)S(1)}, u32[]{:S(2)}, u32[]{:S(2)}) collective-permute-start(bf16[1,128,320]{1,2,0:T(8,128)(2,1)S(1)} %get-tuple-element.29), channel_id=1, source_target_pairs={{0,8},{8,16},{16,24},{1,9},{9,17},{17,25},{2,10},{10,18},{18,26},{... | collective-permute-start | bytes 245768 | tf_op jit(solution)/shard_map/ppermute | solution.py:18
  29.3 2.6 %copy-start.2 = (bf16[3,128,320]{1,2,0:T(8,128)(2,1)}, bf16[3,128,320]{1,2,0:T(8,128)(2,1)S(1)}, u32[]{:S(2)}) copy-start(bf16[3,128,320]{1,2,0:T(8,128)(2,1)S(1)} %bitcast_multiply_fusion) | copy-start | bytes 737284
  37.2 2.9 %collective-permute-start.5 = (bf16[4,360,320]{1,2,0:T(8,128)(2,1)}, bf16[4,360,320]{1,2,0:T(8,128)(2,1)}, u32[]{:S(2)}, u32[]{:S(2)}) collective-permute-start(bf16[4,360,320]{1,2,0:T(8,128)(2,1)} %bitcast.115), channel_id=1, source_target_pairs={{0,1},{1,0},{2,3},{3,2},{4,5},{5,4},{6,7},{7,6},{8,9},{9,8},{10,11... | collective-permute-start | bytes 2764808 | tf_op jit(solution)/shard_map/ppermute | solution.py:65
  42.7 10.1 %collective-permute-start.8 = (bf16[360,320]{0,1:T(8,128)(2,1)}, bf16[360,320]{0,1:T(8,128)(2,1)}, u32[]{:S(2)}, u32[]{:S(2)}) collective-permute-start(bf16[360,320]{0,1:T(8,128)(2,1)} %get-tuple-element.25), channel_id=1, source_target_pairs={{0,6},{1,7},{2,4},{3,5},{4,2},{5,3},{6,0},{7,1},{8,14},{9,15},{10,... | collective-permute-start | bytes 691208 | tf_op jit(solution)/shard_map/ppermute | solution.py:79
  45.1 12.1 %collective-permute-start.7 = (bf16[360,320]{0,1:T(8,128)(2,1)}, bf16[360,320]{0,1:T(8,128)(2,1)}, u32[]{:S(2)}, u32[]{:S(2)}) collective-permute-start(bf16[360,320]{0,1:T(8,128)(2,1)} %get-tuple-element.26), channel_id=1, source_target_pairs={{0,4},{1,5},{2,6},{3,7},{4,0},{5,1},{6,2},{7,3},{8,12},{9,13},{10,... | collective-permute-start | bytes 691208 | tf_op jit(solution)/shard_map/ppermute | solution.py:79
  45.5 11.7 %collective-permute-start.6 = (bf16[360,320]{0,1:T(8,128)(2,1)}, bf16[360,320]{0,1:T(8,128)(2,1)}, u32[]{:S(2)}, u32[]{:S(2)}) collective-permute-start(bf16[360,320]{0,1:T(8,128)(2,1)} %get-tuple-element.24), channel_id=1, source_target_pairs={{0,2},{1,3},{2,0},{3,1},{4,6},{5,7},{6,4},{7,5},{8,10},{9,11},{10,... | collective-permute-start | bytes 691208 | tf_op jit(solution)/shard_map/ppermute | solution.py:79
  46.2 14.7 %copy-start.3 = (bf16[3,128,320]{1,2,0:T(8,128)(2,1)S(1)}, bf16[3,128,320]{1,2,0:T(8,128)(2,1)}, u32[]{:S(2)}) copy-start(bf16[3,128,320]{1,2,0:T(8,128)(2,1)} %copy-done.2) | copy-start | bytes 737284
  58.5 10.7 %collective-permute-start.9 = (bf16[360,320]{0,1:T(8,128)(2,1)S(1)}, bf16[360,320]{0,1:T(8,128)(2,1)S(1)}, u32[]{:S(2)}, u32[]{:S(2)}) collective-permute-start(bf16[360,320]{0,1:T(8,128)(2,1)S(1)} %fusion.41), channel_id=1, source_target_pairs={{0,8},{8,0},{16,24},{24,16},{1,9},{9,1},{17,25},{25,17},{2,10},{10... | collective-permute-start | bytes 691208 | tf_op jit(solution)/shard_map/ppermute | solution.py:92
  60.9 7.8 %collective-permute-start.11 = (bf16[1,128,320]{1,2,0:T(8,128)(2,1)S(1)}, bf16[1,128,320]{1,2,0:T(8,128)(2,1)S(1)}, u32[]{:S(2)}, u32[]{:S(2)}) collective-permute-start(bf16[1,128,320]{1,2,0:T(8,128)(2,1)S(1)} %get-tuple-element.28), channel_id=1, source_target_pairs={{8,0},{16,8},{24,16},{9,1},{17,9},{25,17},{10,2},{18,10},{26,18},{... | collective-permute-start | bytes 245768 | tf_op jit(solution)/shard_map/ppermute | solution.py:20
  62.2 6.6 %collective-permute-start.10 = (bf16[1,128,320]{1,2,0:T(8,128)(2,1)S(1)}, bf16[1,128,320]{1,2,0:T(8,128)(2,1)S(1)}, u32[]{:S(2)}, u32[]{:S(2)}) collective-permute-start(bf16[1,128,320]{1,2,0:T(8,128)(2,1)S(1)} %get-tuple-element.27), channel_id=1, source_target_pairs={{0,8},{8,16},{16,24},{1,9},{9,17},{17,25},{2,10},{10,18},{18,26},{... | collective-permute-start | bytes 245768 | tf_op jit(solution)/shard_map/ppermute | solution.py:18
  69.3 1.8 %copy-start.4 = (bf16[8,360,320]{2,1,0:T(8,128)(2,1)S(1)}, bf16[8,360,320]{2,1,0:T(8,128)(2,1)}, u32[]{:S(2)}) copy-start(bf16[8,360,320]{2,1,0:T(8,128)(2,1)} %copy.25) | copy-start | bytes 5529604
  73.4 19.4 %copy-start.5 = (f32[360,320]{0,1:T(8,128)S(1)}, f32[360,320]{0,1:T(8,128)}, u32[]{:S(2)}) copy-start(f32[360,320]{0,1:T(8,128)} %param.15) | copy-start | bytes 1382404
  73.5 9.5 %collective-permute-start.14 = (f32[2,32]{1,0:T(2,128)S(1)}, f32[2,32]{1,0:T(2,128)S(1)}, u32[]{:S(2)}, u32[]{:S(2)}) collective-permute-start(f32[2,32]{1,0:T(2,128)S(1)} %pad_maximum_fusion.3), channel_id=1, source_target_pairs={{0,24},{8,0},{16,8},{24,16},{1,25},{9,1},{17,9},{25,17},{2,26},{10... | collective-permute-start | bytes 776 | tf_op jit(solution)/shard_map/ppermute | solution.py:33
  76.5 6.5 %collective-permute-start.13 = (f32[2,32]{1,0:T(2,128)S(1)}, f32[2,32]{1,0:T(2,128)S(1)}, u32[]{:S(2)}, u32[]{:S(2)}) collective-permute-start(f32[2,32]{1,0:T(2,128)S(1)} %pad_maximum_fusion.3), channel_id=1, source_target_pairs={{0,16},{8,24},{16,0},{24,8},{1,17},{9,25},{17,1},{25,9},{2,18},{10... | collective-permute-start | bytes 776 | tf_op jit(solution)/shard_map/ppermute | solution.py:33
  77.4 5.6 %collective-permute-start.12 = (f32[2,32]{1,0:T(2,128)S(1)}, f32[2,32]{1,0:T(2,128)S(1)}, u32[]{:S(2)}, u32[]{:S(2)}) collective-permute-start(f32[2,32]{1,0:T(2,128)S(1)} %pad_maximum_fusion.3), channel_id=1, source_target_pairs={{0,8},{8,16},{16,24},{24,0},{1,9},{9,17},{17,25},{25,1},{2,10},{10... | collective-permute-start | bytes 776 | tf_op jit(solution)/shard_map/ppermute | solution.py:33
  80.9 12.0 %collective-permute-start.15 = (bf16[360,320]{0,1:T(8,128)(2,1)S(1)}, bf16[360,320]{0,1:T(8,128)(2,1)S(1)}, u32[]{:S(2)}, u32[]{:S(2)}) collective-permute-start(bf16[360,320]{0,1:T(8,128)(2,1)S(1)} %convert_add_fusion.3), channel_id=1, source_target_pairs={{0,16},{8,24},{16,0},{24,8},{1,17},{9,25},{17,1},{25,9},{2,18},{10... | collective-permute-start | bytes 691208 | tf_op jit(solution)/shard_map/ppermute | solution.py:92
  (1 other events, 1.2 us)
Sparse Core Ops, SparseCore 0:
  16.5 27.7 all-gather.2

commit v20 on v19

--- a/solution.py
+++ b/solution.py
@@ -147,10 +147,10 @@
         act_cols, flat_cot, (((0,), (0,)), ((), ())), preferred_element_type=jnp.float32
     ).astype(jnp.bfloat16)
     weight_terms = row_major(weight_terms)
-    grad_piece, gathered = halving_scatter(weight_terms, "dp", gathered)
-    grad_piece, (gathered, cot_pad) = replicated_sum(grad_piece, "space", (gathered, cot_pad))
     output = jnp.dot(act_cols, gathered, preferred_element_type=jnp.float32)
     block_out = (output.reshape(height_dev, width_dev, channels) * inside).astype(jnp.bfloat16)
+    grad_piece, (gathered, block_out) = halving_scatter(weight_terms, "dp", (gathered, block_out))
+    grad_piece, (gathered, cot_pad) = replicated_sum(grad_piece, "space", (gathered, cot_pad))
     tap_weights = gathered.reshape(9, channels, channels)
     cot_cols = jnp.concatenate(
         [

time: 103 us -> 97.4 us (0.946)
  waiting for transfers between devices: 23.4 us -> 21 us
  other arithmetic: 12.6 us -> 10.5 us
    ppermute x6, waiting for transfers between devices: 4.33 us -> 7.91 us  [space_sum(): lax.ppermute(joined, axis, [(i, (i + shift) % count) for i in range(count)])]
    ppermute x3, waiting for transfers between devices: 6.91 us -> 3.38 us  [halving_scatter(): lax.ppermute(send.astype(jnp.bfloat16), axis, pairs).astype(jnp.float32)]
    ppermute x2, waiting for transfers between devices: 7.6 us -> 5.1 us  [replicated_sum(): lax.ppermute(mine, axis, pairs).astype(jnp.float32)]
    unnamed x30 -> x32, local copies, waits for them, and re-layouts: 3.53 us -> 3.53 us
where the time goes in v20:
time: 97.4 us; the launch traced here: 96.9 us
  starting transfers between devices  29.6 us (30%)
  waiting for transfers between devices  21 us (22%)
  between operations  15.8 us (16%)
  local copies, waits for them, and re-layouts  13.5 us (14%)
  other arithmetic  10.5 us (11%)
  matrix products  6.41 us (7%)
    ppermute x6, starting transfers between devices, space_sum(): lax.ppermute(joined, axis, [(i, (i + shift) % count) for i in range(count)])  10 us
    ppermute x2, starting transfers between devices, with_halo(): lax.ppermute(tail, axis, [(i, (i + 1) % count) for i in range(ends)])  9.1 us
    ppermute x6, waiting for transfers between devices, space_sum(): lax.ppermute(joined, axis, [(i, (i + shift) % count) for i in range(count)])  7.91 us
    ppermute x2, waiting for transfers between devices, replicated_sum(): lax.ppermute(mine, axis, pairs).astype(jnp.float32)  5.1 us
    ppermute x2, starting transfers between devices, replicated_sum(): lax.ppermute(mine, axis, pairs).astype(jnp.float32)  4.35 us
    all_gather x1, local copies, waits for them, and re-layouts, local(): lax.all_gather(row_major(weight), 'dp', axis=0, tiled=True)  4.05 us
    dot_general x1, matrix products, local(): output = jnp.dot(act_cols, gathered, preferred_element_type=jnp.float32)  3.57 us
    unnamed x32, local copies, waits for them, and re-layouts  3.53 us
  transfers between devices with their start and end apart: 17, of which 10 were waited for; matrix products, arithmetic and copies ran while one was open for 23% of the time, Pallas kernels for 0%

profile of v20, /device:TPU:0, one launch (start us, length us, event | category | flops | bytes accessed | tf_op | source)
XLA Modules:
  0.0 96.9 jit_solution(12992926665619240118)
XLA Ops:
  10.2 5.1 %collective-permute-start.2 = (f32[2,32]{1,0:T(2,128)S(1)}, f32[2,32]{1,0:T(2,128)S(1)}, u32[]{:S(2)}, u32[]{:S(2)}) collective-permute-start(f32[2,32]{1,0:T(2,128)S(1)} %pad_maximum_fusion.2), channel_id=1, source_target_pairs={{0,24},{8,0},{16,8},{24,16},{1,25},{9,1},{17,9},{25,17},{2,26},{10... | collective-permute-start | bytes 776 | tf_op jit(solution)/shard_map/ppermute | solution.py:33
  16.6 3.2 %collective-permute-done.1 = f32[2,32]{1,0:T(2,128)S(1)} collective-permute-done((f32[2,32]{1,0:T(2,128)S(1)}, f32[2,32]{1,0:T(2,128)S(1)}, u32[]{:S(2)}, u32[]{:S(2)}) %collective-permute-start.1) | collective-permute-done | bytes 288 | tf_op jit(solution)/shard_map/ppermute | solution.py:33
  21.1 1.3 %multiply_convert_fusion = bf16[3,128,320]{1,2,0:T(8,128)(2,1)S(1)} fusion(bf16[1,3,128,320]{2,3,1,0:T(8,128)(2,1)} %param.9, f32[320]{0:T(512)} %param.12, f32[320]{0:T(512)} %param.11, f32[320]{0:T(512)S(1)} %mul.163, f32[320]{0:T(512)S(1)} %sub.37, f32[3,128]{1,0:T(4,128)S(1)} %get-tuple-element.36), kind=kLoop, calls=%fused_computation.48 | loop fusion | flops 1597440 | bytes 498176 | tf_op jit(solution)/shard_map/convert_element_type | solution.py:133
  22.5 1.3 %collective-permute-start.4 = (bf16[1,128,320]{1,2,0:T(8,128)(2,1)S(1)}, bf16[1,128,320]{1,2,0:T(8,128)(2,1)S(1)}, u32[]{:S(2)}, u32[]{:S(2)}) collective-permute-start(bf16[1,128,320]{1,2,0:T(8,128)(2,1)S(1)} %get-tuple-element.32), channel_id=1, source_target_pairs={{8,0},{16,8},{24,16},{9,1},{17,9},{25,17},{10,2},{18,10},{26,18},{... | collective-permute-start | bytes 245768 | tf_op jit(solution)/shard_map/ppermute | solution.py:20
  23.8 4.6 %collective-permute-start.3 = (bf16[1,128,320]{1,2,0:T(8,128)(2,1)S(1)}, bf16[1,128,320]{1,2,0:T(8,128)(2,1)S(1)}, u32[]{:S(2)}, u32[]{:S(2)}) collective-permute-start(bf16[1,128,320]{1,2,0:T(8,128)(2,1)S(1)} %get-tuple-element.31), channel_id=1, source_target_pairs={{0,8},{8,16},{16,24},{1,9},{9,17},{17,25},{2,10},{10,18},{18,26},{... | collective-permute-start | bytes 245768 | tf_op jit(solution)/shard_map/ppermute | solution.py:18
  31.9 1.5 %fusion = bf16[2880,320]{1,0:T(8,128)(2,1)S(1)} fusion(bf16[3,128,2880]{1,2,0:T(8,128)(2,1)S(1)} %slice_dynamic-update-slice_fusion, bf16[3,128,320]{1,2,0:T(8,128)(2,1)S(1)} %bitcast_multiply_fusion), kind=kOutput, calls=%fused_computation.1 | convolution fusion | flops 708710400 | bytes 4300800 | tf_op jit(solution)/shard_map/dot_general | solution.py:146
  34.7 2.5 %copy.20 = bf16[4,1,360,320]{2,3,0,1:T(8,128)(2,1)} copy(bf16[4,1,360,320]{3,2,1,0:T(8,128)(2,1)} %get-tuple-element.25) | data formatting | bytes 1843200 | tf_op jit(solution)/shard_map/jit(dynamic_index_in_dim)/dynamic_slice | solution.py:63
  37.2 1.4 %copy.28 = bf16[4,1,360,320]{2,3,0,1:T(8,128)(2,1)} copy(bf16[4,1,360,320]{3,2,1,0:T(8,128)(2,1)S(1)} %get-tuple-element.24) | data formatting | bytes 1843200
  38.5 1.5 %collective-permute-done.5 = bf16[4,360,320]{1,2,0:T(8,128)(2,1)} collective-permute-done((bf16[4,360,320]{1,2,0:T(8,128)(2,1)}, bf16[4,360,320]{1,2,0:T(8,128)(2,1)}, u32[]{:S(2)}, u32[]{:S(2)}) %collective-permute-start.5) | collective-permute-done | bytes 921632 | tf_op jit(solution)/shard_map/ppermute | solution.py:65
  40.1 1.7 %fusion.1 = bf16[4,360,320]{1,2,0:T(8,128)(2,1)S(1)} fusion(bf16[4,360,320]{1,2,0:T(8,128)(2,1)} %collective-permute-done.5, bf16[4,1,360,320]{2,3,0,1:T(8,128)(2,1)} %copy.28), kind=kLoop, calls=%fused_computation.5 | loop fusion | flops 1843200 | bytes 2764800 | tf_op jit(solution)/shard_map/convert_element_type | solution.py:66
  42.7 2.3 %collective-permute-start.8 = (bf16[360,320]{0,1:T(8,128)(2,1)}, bf16[360,320]{0,1:T(8,128)(2,1)}, u32[]{:S(2)}, u32[]{:S(2)}) collective-permute-start(bf16[360,320]{0,1:T(8,128)(2,1)} %get-tuple-element.27), channel_id=1, source_target_pairs={{0,6},{1,7},{2,4},{3,5},{4,2},{5,3},{6,0},{7,1},{8,14},{9,15},{10,... | collective-permute-start | bytes 691208 | tf_op jit(solution)/shard_map/ppermute | solution.py:79
  46.2 4.1 %copy.23 = bf16[8,360,320]{2,1,0:T(8,128)(2,1)} copy(bf16[8,360,320]{1,2,0:T(8,128)(2,1)} %all-gather.3.cloned.1.call-done) | data formatting | bytes 3686400 | tf_op jit(solution)/shard_map/all_gather | solution.py:123
  50.2 3.6 %fusion.6 = bf16[3,128,320]{1,2,0:T(8,128)(2,1)} fusion(bf16[3,128,2880]{1,2,0:T(8,128)(2,1)S(1)} %slice_dynamic-update-slice_fusion, bf16[2880,320,1]{1,0,2:T(8,128)(2,1)} %bitcast.106, f32[3,128]{1,0:T(4,128)S(1)} %get-tuple-element.36), kind=kOutput, calls=%fused_computation.12 | convolution fusion | flops 708034560 | bytes 4302336 | tf_op jit(solution)/shard_map/dot_general | solution.py:150
  53.8 3.4 %collective-permute-done.7 = bf16[360,320]{0,1:T(8,128)(2,1)} collective-permute-done((bf16[360,320]{0,1:T(8,128)(2,1)}, bf16[360,320]{0,1:T(8,128)(2,1)}, u32[]{:S(2)}, u32[]{:S(2)}) %collective-permute-start.7) | collective-permute-done | bytes 230432 | tf_op jit(solution)/shard_map/ppermute | solution.py:79
  57.2 1.3 %fusion.31 = bf16[360,320]{0,1:T(8,128)(2,1)S(1)} fusion(bf16[360,320]{0,1:T(8,128)(2,1)} %collective-permute-done.8, bf16[360,320]{0,1:T(8,128)(2,1)} %collective-permute-done.7, bf16[360,320]{0,1:T(8,128)(2,1)} %collective-permute-done.6, bf16[4,360,320]{1,2,0:T(8,128)(2,1)S(1)} %fusion.1, s32[]{:T(128)S(6)} %select_n.36), kind=kLoop, calls=%fused_computation.45 | loop fusion | flops 921600 | bytes 1152004 | tf_op jit(solution)/shard_map/convert_element_type | solution.py:90
  58.5 2.4 %collective-permute-start.9 = (bf16[360,320]{0,1:T(8,128)(2,1)S(1)}, bf16[360,320]{0,1:T(8,128)(2,1)S(1)}, u32[]{:S(2)}, u32[]{:S(2)}) collective-permute-start(bf16[360,320]{0,1:T(8,128)(2,1)S(1)} %fusion.31), channel_id=1, source_target_pairs={{0,8},{8,0},{16,24},{24,16},{1,9},{9,1},{17,25},{25,17},{2,10},{10... | collective-permute-start | bytes 691208 | tf_op jit(solution)/shard_map/ppermute | solution.py:92
  60.8 1.3 %collective-permute-start.11 = (bf16[1,128,320]{1,2,0:T(8,128)(2,1)S(1)}, bf16[1,128,320]{1,2,0:T(8,128)(2,1)S(1)}, u32[]{:S(2)}, u32[]{:S(2)}) collective-permute-start(bf16[1,128,320]{1,2,0:T(8,128)(2,1)S(1)} %get-tuple-element.30), channel_id=1, source_target_pairs={{8,0},{16,8},{24,16},{9,1},{17,9},{25,17},{10,2},{18,10},{26,18},{... | collective-permute-start | bytes 245768 | tf_op jit(solution)/shard_map/ppermute | solution.py:20
  62.1 4.6 %collective-permute-start.10 = (bf16[1,128,320]{1,2,0:T(8,128)(2,1)S(1)}, bf16[1,128,320]{1,2,0:T(8,128)(2,1)S(1)}, u32[]{:S(2)}, u32[]{:S(2)}) collective-permute-start(bf16[1,128,320]{1,2,0:T(8,128)(2,1)S(1)} %get-tuple-element.29), channel_id=1, source_target_pairs={{0,8},{8,16},{16,24},{1,9},{9,17},{17,25},{2,10},{10,18},{18,26},{... | collective-permute-start | bytes 245768 | tf_op jit(solution)/shard_map/ppermute | solution.py:18
  66.7 1.9 %collective-permute-done.11 = bf16[1,128,320]{1,2,0:T(8,128)(2,1)S(1)} collective-permute-done((bf16[1,128,320]{1,2,0:T(8,128)(2,1)S(1)}, bf16[1,128,320]{1,2,0:T(8,128)(2,1)S(1)}, u32[]{:S(2)}, u32[]{:S(2)}) %collective-permute-start.11) | collective-permute-done | bytes 81952 | tf_op jit(solution)/shard_map/ppermute | solution.py:20
  71.0 1.3 %fusion.38 = (f32[320]{0:T(512)S(1)}, f32[320]{0:T(512)S(1)}, f32[3,128,320]{1,2,0:T(8,128)S(1)}) fusion(f32[320]{0:T(512)S(1)} %mul.163, f32[320]{0:T(512)S(1)} %sub.37, f32[3,128]{1,0:T(4,128)S(1)} %get-tuple-element.36, bf16[1,3,128,320]{2,3,1,0:T(8,128)(2,1)S(1)} %copy-done.1, f32[320]{0:T(512)S(1)} %copy-done.7, f32[320]{0:T(512)S(1)} %copy-done.8, ...), kind=kOutput, calls=%fused_computation.91 | convolution fusion | flops 710245760 | bytes 4801536 | tf_op jit(solution)/shard_map/dot_general | solution.py:163
  72.8 3.0 %collective-permute-start.14 = (f32[2,32]{1,0:T(2,128)S(1)}, f32[2,32]{1,0:T(2,128)S(1)}, u32[]{:S(2)}, u32[]{:S(2)}) collective-permute-start(f32[2,32]{1,0:T(2,128)S(1)} %pad_maximum_fusion.3), channel_id=1, source_target_pairs={{0,24},{8,0},{16,8},{24,16},{1,25},{9,1},{17,9},{25,17},{2,26},{10... | collective-permute-start | bytes 776 | tf_op jit(solution)/shard_map/ppermute | solution.py:33
  76.7 2.0 %collective-permute-start.15 = (bf16[360,320]{0,1:T(8,128)(2,1)S(1)}, bf16[360,320]{0,1:T(8,128)(2,1)S(1)}, u32[]{:S(2)}, u32[]{:S(2)}) collective-permute-start(bf16[360,320]{0,1:T(8,128)(2,1)S(1)} %convert_add_fusion.3), channel_id=1, source_target_pairs={{0,16},{8,24},{16,0},{24,8},{1,17},{9,25},{17,1},{25,9},{2,18},{10... | collective-permute-start | bytes 691208 | tf_op jit(solution)/shard_map/ppermute | solution.py:92
  78.7 3.6 %collective-permute-done.13 = f32[2,32]{1,0:T(2,128)S(1)} collective-permute-done((f32[2,32]{1,0:T(2,128)S(1)}, f32[2,32]{1,0:T(2,128)S(1)}, u32[]{:S(2)}, u32[]{:S(2)}) %collective-permute-start.13) | collective-permute-done | bytes 288 | tf_op jit(solution)/shard_map/ppermute | solution.py:33
  83.6 5.1 %collective-permute-done.15 = bf16[360,320]{0,1:T(8,128)(2,1)S(1)} collective-permute-done((bf16[360,320]{0,1:T(8,128)(2,1)S(1)}, bf16[360,320]{0,1:T(8,128)(2,1)S(1)}, u32[]{:S(2)}, u32[]{:S(2)}) %collective-permute-start.15) | collective-permute-done | bytes 230432 | tf_op jit(solution)/shard_map/ppermute | solution.py:92
  (92 shorter events, 17.3 us)
Async XLA Ops:
  7.2 39.0 %all-gather.3.cloned.1.call-start = ((), (), s32[]{:S(2)}) async-start(), calls=%async_computation | async-start | bytes 2211840 | tf_op jit(solution)/shard_map/all_gather | solution.py:123
  10.2 6.4 %collective-permute-start.2 = (f32[2,32]{1,0:T(2,128)S(1)}, f32[2,32]{1,0:T(2,128)S(1)}, u32[]{:S(2)}, u32[]{:S(2)}) collective-permute-start(f32[2,32]{1,0:T(2,128)S(1)} %pad_maximum_fusion.2), channel_id=1, source_target_pairs={{0,24},{8,0},{16,8},{24,16},{1,25},{9,1},{17,9},{25,17},{2,26},{10... | collective-permute-start | bytes 776 | tf_op jit(solution)/shard_map/ppermute | solution.py:33
  15.3 4.5 %collective-permute-start.1 = (f32[2,32]{1,0:T(2,128)S(1)}, f32[2,32]{1,0:T(2,128)S(1)}, u32[]{:S(2)}, u32[]{:S(2)}) collective-permute-start(f32[2,32]{1,0:T(2,128)S(1)} %pad_maximum_fusion.2), channel_id=1, source_target_pairs={{0,16},{8,24},{16,0},{24,8},{1,17},{9,25},{17,1},{25,9},{2,18},{10... | collective-permute-start | bytes 776 | tf_op jit(solution)/shard_map/ppermute | solution.py:33
  15.3 5.4 %collective-permute-start = (f32[2,32]{1,0:T(2,128)S(1)}, f32[2,32]{1,0:T(2,128)S(1)}, u32[]{:S(2)}, u32[]{:S(2)}) collective-permute-start(f32[2,32]{1,0:T(2,128)S(1)} %pad_maximum_fusion.2), channel_id=1, source_target_pairs={{0,8},{8,16},{16,24},{24,0},{1,9},{9,17},{17,25},{25,1},{2,10},{10... | collective-permute-start | bytes 776 | tf_op jit(solution)/shard_map/ppermute | solution.py:33
  21.1 10.0 %copy-start = (bf16[1,3,128,320]{2,3,1,0:T(8,128)(2,1)S(1)}, bf16[1,3,128,320]{2,3,1,0:T(8,128)(2,1)}, u32[]{:S(2)}) copy-start(bf16[1,3,128,320]{2,3,1,0:T(8,128)(2,1)} %param.9) | copy-start | bytes 737284
  21.1 10.0 %copy-start.7 = (f32[320]{0:T(512)S(1)}, f32[320]{0:T(512)}, u32[]{:S(2)}) copy-start(f32[320]{0:T(512)} %param.12) | copy-start | bytes 3844
  21.1 10.0 %copy-start.8 = (f32[320]{0:T(512)S(1)}, f32[320]{0:T(512)}, u32[]{:S(2)}) copy-start(f32[320]{0:T(512)} %param.11) | copy-start | bytes 3844
  22.5 6.9 %collective-permute-start.4 = (bf16[1,128,320]{1,2,0:T(8,128)(2,1)S(1)}, bf16[1,128,320]{1,2,0:T(8,128)(2,1)S(1)}, u32[]{:S(2)}, u32[]{:S(2)}) collective-permute-start(bf16[1,128,320]{1,2,0:T(8,128)(2,1)S(1)} %get-tuple-element.32), channel_id=1, source_target_pairs={{8,0},{16,8},{24,16},{9,1},{17,9},{25,17},{10,2},{18,10},{26,18},{... | collective-permute-start | bytes 245768 | tf_op jit(solution)/shard_map/ppermute | solution.py:20
  23.8 6.6 %collective-permute-start.3 = (bf16[1,128,320]{1,2,0:T(8,128)(2,1)S(1)}, bf16[1,128,320]{1,2,0:T(8,128)(2,1)S(1)}, u32[]{:S(2)}, u32[]{:S(2)}) collective-permute-start(bf16[1,128,320]{1,2,0:T(8,128)(2,1)S(1)} %get-tuple-element.31), channel_id=1, source_target_pairs={{0,8},{8,16},{16,24},{1,9},{9,17},{17,25},{2,10},{10,18},{18,26},{... | collective-permute-start | bytes 245768 | tf_op jit(solution)/shard_map/ppermute | solution.py:18
  29.3 2.6 %copy-start.2 = (bf16[3,128,320]{1,2,0:T(8,128)(2,1)}, bf16[3,128,320]{1,2,0:T(8,128)(2,1)S(1)}, u32[]{:S(2)}) copy-start(bf16[3,128,320]{1,2,0:T(8,128)(2,1)S(1)} %bitcast_multiply_fusion) | copy-start | bytes 737284
  37.1 2.9 %collective-permute-start.5 = (bf16[4,360,320]{1,2,0:T(8,128)(2,1)}, bf16[4,360,320]{1,2,0:T(8,128)(2,1)}, u32[]{:S(2)}, u32[]{:S(2)}) collective-permute-start(bf16[4,360,320]{1,2,0:T(8,128)(2,1)} %bitcast.108), channel_id=1, source_target_pairs={{0,1},{1,0},{2,3},{3,2},{4,5},{5,4},{6,7},{7,6},{8,9},{9,8},{10,11... | collective-permute-start | bytes 2764808 | tf_op jit(solution)/shard_map/ppermute | solution.py:65
  42.7 11.1 %collective-permute-start.8 = (bf16[360,320]{0,1:T(8,128)(2,1)}, bf16[360,320]{0,1:T(8,128)(2,1)}, u32[]{:S(2)}, u32[]{:S(2)}) collective-permute-start(bf16[360,320]{0,1:T(8,128)(2,1)} %get-tuple-element.27), channel_id=1, source_target_pairs={{0,6},{1,7},{2,4},{3,5},{4,2},{5,3},{6,0},{7,1},{8,14},{9,15},{10,... | collective-permute-start | bytes 691208 | tf_op jit(solution)/shard_map/ppermute | solution.py:79
  45.0 12.2 %collective-permute-start.7 = (bf16[360,320]{0,1:T(8,128)(2,1)}, bf16[360,320]{0,1:T(8,128)(2,1)}, u32[]{:S(2)}, u32[]{:S(2)}) collective-permute-start(bf16[360,320]{0,1:T(8,128)(2,1)} %get-tuple-element.28), channel_id=1, source_target_pairs={{0,4},{1,5},{2,6},{3,7},{4,0},{5,1},{6,2},{7,3},{8,12},{9,13},{10,... | collective-permute-start | bytes 691208 | tf_op jit(solution)/shard_map/ppermute | solution.py:79
  45.5 11.7 %collective-permute-start.6 = (bf16[360,320]{0,1:T(8,128)(2,1)S(1)}, bf16[360,320]{0,1:T(8,128)(2,1)}, u32[]{:S(2)}, u32[]{:S(2)}) collective-permute-start(bf16[360,320]{0,1:T(8,128)(2,1)S(1)} %get-tuple-element.26), channel_id=1, source_target_pairs={{0,2},{1,3},{2,0},{3,1},{4,6},{5,7},{6,4},{7,5},{8,10},{9,11},{10,... | collective-permute-start | bytes 691208 | tf_op jit(solution)/shard_map/ppermute | solution.py:79
  50.2 10.6 %copy-start.3 = (bf16[3,128,320]{1,2,0:T(8,128)(2,1)S(1)}, bf16[3,128,320]{1,2,0:T(8,128)(2,1)}, u32[]{:S(2)}) copy-start(bf16[3,128,320]{1,2,0:T(8,128)(2,1)} %copy-done.2) | copy-start | bytes 737284
  58.5 10.7 %collective-permute-start.9 = (bf16[360,320]{0,1:T(8,128)(2,1)S(1)}, bf16[360,320]{0,1:T(8,128)(2,1)S(1)}, u32[]{:S(2)}, u32[]{:S(2)}) collective-permute-start(bf16[360,320]{0,1:T(8,128)(2,1)S(1)} %fusion.31), channel_id=1, source_target_pairs={{0,8},{8,0},{16,24},{24,16},{1,9},{9,1},{17,25},{25,17},{2,10},{10... | collective-permute-start | bytes 691208 | tf_op jit(solution)/shard_map/ppermute | solution.py:92
  60.8 7.8 %collective-permute-start.11 = (bf16[1,128,320]{1,2,0:T(8,128)(2,1)S(1)}, bf16[1,128,320]{1,2,0:T(8,128)(2,1)S(1)}, u32[]{:S(2)}, u32[]{:S(2)}) collective-permute-start(bf16[1,128,320]{1,2,0:T(8,128)(2,1)S(1)} %get-tuple-element.30), channel_id=1, source_target_pairs={{8,0},{16,8},{24,16},{9,1},{17,9},{25,17},{10,2},{18,10},{26,18},{... | collective-permute-start | bytes 245768 | tf_op jit(solution)/shard_map/ppermute | solution.py:20
  62.1 6.6 %collective-permute-start.10 = (bf16[1,128,320]{1,2,0:T(8,128)(2,1)S(1)}, bf16[1,128,320]{1,2,0:T(8,128)(2,1)S(1)}, u32[]{:S(2)}, u32[]{:S(2)}) collective-permute-start(bf16[1,128,320]{1,2,0:T(8,128)(2,1)S(1)} %get-tuple-element.29), channel_id=1, source_target_pairs={{0,8},{8,16},{16,24},{1,9},{9,17},{17,25},{2,10},{10,18},{18,26},{... | collective-permute-start | bytes 245768 | tf_op jit(solution)/shard_map/ppermute | solution.py:18
  71.0 17.7 %copy-start.5 = (f32[360,320]{0,1:T(8,128)S(1)}, f32[360,320]{0,1:T(8,128)}, u32[]{:S(2)}) copy-start(f32[360,320]{0,1:T(8,128)} %param.15) | copy-start | bytes 1382404
  71.0 17.7 %copy-start.6 = (f32[360,320]{0,1:T(8,128)S(1)}, f32[360,320]{0,1:T(8,128)}, u32[]{:S(2)}) copy-start(f32[360,320]{0,1:T(8,128)} %param.14) | copy-start | bytes 1382404
  72.8 5.9 %collective-permute-start.14 = (f32[2,32]{1,0:T(2,128)S(1)}, f32[2,32]{1,0:T(2,128)S(1)}, u32[]{:S(2)}, u32[]{:S(2)}) collective-permute-start(f32[2,32]{1,0:T(2,128)S(1)} %pad_maximum_fusion.3), channel_id=1, source_target_pairs={{0,24},{8,0},{16,8},{24,16},{1,25},{9,1},{17,9},{25,17},{2,26},{10... | collective-permute-start | bytes 776 | tf_op jit(solution)/shard_map/ppermute | solution.py:33
  75.8 6.5 %collective-permute-start.13 = (f32[2,32]{1,0:T(2,128)S(1)}, f32[2,32]{1,0:T(2,128)S(1)}, u32[]{:S(2)}, u32[]{:S(2)}) collective-permute-start(f32[2,32]{1,0:T(2,128)S(1)} %pad_maximum_fusion.3), channel_id=1, source_target_pairs={{0,16},{8,24},{16,0},{24,8},{1,17},{9,25},{17,1},{25,9},{2,18},{10... | collective-permute-start | bytes 776 | tf_op jit(solution)/shard_map/ppermute | solution.py:33
  76.7 5.6 %collective-permute-start.12 = (f32[2,32]{1,0:T(2,128)S(1)}, f32[2,32]{1,0:T(2,128)S(1)}, u32[]{:S(2)}, u32[]{:S(2)}) collective-permute-start(f32[2,32]{1,0:T(2,128)S(1)} %pad_maximum_fusion.3), channel_id=1, source_target_pairs={{0,8},{8,16},{16,24},{24,0},{1,9},{9,17},{17,25},{25,1},{2,10},{10... | collective-permute-start | bytes 776 | tf_op jit(solution)/shard_map/ppermute | solution.py:33
  76.7 12.0 %collective-permute-start.15 = (bf16[360,320]{0,1:T(8,128)(2,1)S(1)}, bf16[360,320]{0,1:T(8,128)(2,1)S(1)}, u32[]{:S(2)}, u32[]{:S(2)}) collective-permute-start(bf16[360,320]{0,1:T(8,128)(2,1)S(1)} %convert_add_fusion.3), channel_id=1, source_target_pairs={{0,16},{8,24},{16,0},{24,8},{1,17},{9,25},{17,1},{25,9},{2,18},{10... | collective-permute-start | bytes 691208 | tf_op jit(solution)/shard_map/ppermute | solution.py:92
  (2 other events, 3.0 us)
Sparse Core Ops, SparseCore 0:
  16.5 27.7 all-gather.2

commit v21 on v20

--- a/solution.py
+++ b/solution.py
@@ -150,7 +150,6 @@
     output = jnp.dot(act_cols, gathered, preferred_element_type=jnp.float32)
     block_out = (output.reshape(height_dev, width_dev, channels) * inside).astype(jnp.bfloat16)
     grad_piece, (gathered, block_out) = halving_scatter(weight_terms, "dp", (gathered, block_out))
-    grad_piece, (gathered, cot_pad) = replicated_sum(grad_piece, "space", (gathered, cot_pad))
     tap_weights = gathered.reshape(9, channels, channels)
     cot_cols = jnp.concatenate(
         [
@@ -166,6 +165,7 @@
         (((1, 2), (0, 2)), ((), ())),
         preferred_element_type=jnp.float32,
     )
+    grad_piece, upstream = replicated_sum(grad_piece, "space", upstream)
     gate_sig = jax.nn.sigmoid(before)
     silu_slope = gate_sig * (1.0 + before * (1.0 - gate_sig))
     scaled = upstream.reshape(height_dev, width_dev, channels) * silu_slope * inside * norm_gain

time: 97.4 us -> 117 us (1.20)
  local copies, waits for them, and re-layouts: 13.5 us -> 33.8 us
  waiting for transfers between devices: 21 us -> 18.8 us
    concatenate x1 -> x2, local copies, waits for them, and re-layouts: 0.06 us -> 13.3 us  [local(): jnp.concatenate([cot_pad[2 - row_off:2 - row_off + height_dev, 2 - col_of...]
    ppermute x2, waiting for transfers between devices: 5.1 us -> 12.4 us  [replicated_sum(): lax.ppermute(mine, axis, pairs).astype(jnp.float32)]
    ppermute x6, waiting for transfers between devices: 7.91 us -> 2.63 us  [space_sum(): lax.ppermute(joined, axis, [(i, (i + shift) % count) for i in range(count)])]
    another operation x0 -> x1, local copies, waits for them, and re-layouts: none -> 3.51 us  [local(): cot_cols.reshape(-1, 9, channels)]
    convert_element_type x0 -> x2, local copies, waits for them, and re-layouts: none -> 2.13 us  [local(): values = latent.astype(jnp.float32) * inside]
    unnamed x32 -> x35, local copies, waits for them, and re-layouts: 3.53 us -> 5.45 us
    ppermute x2, waiting for transfers between devices: 1.92 us -> 0.01 us  [with_halo(): lax.ppermute(head, axis, [((i + 1) % count, i) for i in range(ends)])]
    unnamed x3 -> x6, other arithmetic: 0.41 us -> 1.94 us
  transfers between devices with their start and end apart: 17 -> 17, of which waited for: 10 -> 6; matrix products, arithmetic and copies ran while one was open for 23% -> 38% of each run, Pallas kernels for 0% -> 0%
where the time goes in v21:
time: 117 us; the launch traced here: 116 us
  local copies, waits for them, and re-layouts  33.8 us (29%)
  starting transfers between devices  30 us (26%)
  waiting for transfers between devices  18.8 us (16%)
  between operations  15.9 us (14%)
  other arithmetic  11.6 us (10%)
  matrix products  6.36 us (5%)
    concatenate x2, local copies, waits for them, and re-layouts, local(): jnp.concatenate([cot_pad[2 - row_off:2 - row_off + height_dev, 2 - col_of...  13.3 us
    ppermute x2, waiting for transfers between devices, replicated_sum(): lax.ppermute(mine, axis, pairs).astype(jnp.float32)  12.4 us
    ppermute x6, starting transfers between devices, space_sum(): lax.ppermute(joined, axis, [(i, (i + shift) % count) for i in range(count)])  11.4 us
    ppermute x2, starting transfers between devices, with_halo(): lax.ppermute(tail, axis, [(i, (i + 1) % count) for i in range(ends)])  9.56 us
    unnamed x35, local copies, waits for them, and re-layouts  5.45 us
    all_gather x1, local copies, waits for them, and re-layouts, local(): lax.all_gather(row_major(weight), 'dp', axis=0, tiled=True)  4.05 us
    ppermute x3, waiting for transfers between devices, halving_scatter(): lax.ppermute(send.astype(jnp.bfloat16), axis, pairs).astype(jnp.float32)  3.71 us
    dot_general x1, matrix products, local(): output = jnp.dot(act_cols, gathered, preferred_element_type=jnp.float32)  3.68 us
  transfers between devices with their start and end apart: 17, of which 6 were waited for; matrix products, arithmetic and copies ran while one was open for 38% of the time, Pallas kernels for 0%

profile of v21, /device:TPU:0, one launch (start us, length us, event | category | flops | bytes accessed | tf_op | source)
XLA Modules:
  0.0 116.5 jit_solution(711115332169681736)
XLA Ops:
  10.3 5.1 %collective-permute-start.2 = (f32[2,32]{1,0:T(2,128)S(1)}, f32[2,32]{1,0:T(2,128)S(1)}, u32[]{:S(2)}, u32[]{:S(2)}) collective-permute-start(f32[2,32]{1,0:T(2,128)S(1)} %pad_maximum_fusion.4), channel_id=1, source_target_pairs={{0,24},{8,0},{16,8},{24,16},{1,25},{9,1},{17,9},{25,17},{2,26},{10... | collective-permute-start | bytes 776 | tf_op jit(solution)/shard_map/ppermute | solution.py:33
  17.5 1.3 %collective-permute-start.11 = (bf16[1,128,320]{1,2,0:T(8,128)(2,1)S(1)}, bf16[1,128,320]{1,2,0:T(8,128)(2,1)S(1)}, u32[]{:S(2)}, u32[]{:S(2)}) collective-permute-start(bf16[1,128,320]{1,2,0:T(8,128)(2,1)S(1)} %get-tuple-element.28), channel_id=1, source_target_pairs={{8,0},{16,8},{24,16},{9,1},{17,9},{25,17},{10,2},{18,10},{26,18},{... | collective-permute-start | bytes 245768 | tf_op jit(solution)/shard_map/ppermute | solution.py:20
  18.8 5.0 %collective-permute-start.10 = (bf16[1,128,320]{1,2,0:T(8,128)(2,1)S(1)}, bf16[1,128,320]{1,2,0:T(8,128)(2,1)S(1)}, u32[]{:S(2)}, u32[]{:S(2)}) collective-permute-start(bf16[1,128,320]{1,2,0:T(8,128)(2,1)S(1)} %get-tuple-element.27), channel_id=1, source_target_pairs={{0,8},{8,16},{16,24},{1,9},{9,17},{17,25},{2,10},{10,18},{18,26},{... | collective-permute-start | bytes 245768 | tf_op jit(solution)/shard_map/ppermute | solution.py:18
  26.8 1.3 %collective-permute-start.4 = (bf16[1,128,320]{1,2,0:T(8,128)(2,1)S(1)}, bf16[1,128,320]{1,2,0:T(8,128)(2,1)S(1)}, u32[]{:S(2)}, u32[]{:S(2)}) collective-permute-start(bf16[1,128,320]{1,2,0:T(8,128)(2,1)S(1)} %get-tuple-element.30), channel_id=1, source_target_pairs={{8,0},{16,8},{24,16},{9,1},{17,9},{25,17},{10,2},{18,10},{26,18},{... | collective-permute-start | bytes 245768 | tf_op jit(solution)/shard_map/ppermute | solution.py:20
  28.1 4.6 %collective-permute-start.3 = (bf16[1,128,320]{1,2,0:T(8,128)(2,1)S(1)}, bf16[1,128,320]{1,2,0:T(8,128)(2,1)S(1)}, u32[]{:S(2)}, u32[]{:S(2)}) collective-permute-start(bf16[1,128,320]{1,2,0:T(8,128)(2,1)S(1)} %get-tuple-element.29), channel_id=1, source_target_pairs={{0,8},{8,16},{16,24},{1,9},{9,17},{17,25},{2,10},{10,18},{18,26},{... | collective-permute-start | bytes 245768 | tf_op jit(solution)/shard_map/ppermute | solution.py:18
  33.5 1.3 %copy-done.3 = bf16[3,128,2880]{1,2,0:T(8,128)(2,1)} copy-done((bf16[3,128,2880]{1,2,0:T(8,128)(2,1)}, bf16[3,128,2880]{1,2,0:T(8,128)(2,1)S(1)}, u32[]{:S(2)}) %copy-start.3) | copy-done | bytes 2211864
  36.4 1.5 %fusion = bf16[2880,320]{1,0:T(8,128)(2,1)S(1)} fusion(bf16[3,128,2880]{1,2,0:T(8,128)(2,1)S(1)} %slice_dynamic-update-slice_fusion.6, bf16[3,128,320]{1,2,0:T(8,128)(2,1)S(1)} %bitcast_multiply_fusion.1), kind=kOutput, calls=%fused_computation.1 | convolution fusion | flops 708710400 | bytes 4300800 | tf_op jit(solution)/shard_map/dot_general | solution.py:146
  37.9 1.3 %constant_dynamic-slice_fusion.1 = (bf16[4,1,360,320]{3,2,1,0:T(8,128)(2,1)}, bf16[4,1,360,320]{3,2,1,0:T(8,128)(2,1)S(1)}) fusion(bf16[4,2,360,320]{3,2,1,0:T(8,128)(2,1)S(1)} %bitcast.85, s32[]{:T(128)S(6)} %select_n.33, s32[]{:T(128)S(6)} %select_n.34), kind=kLoop, calls=%fused_computation.70 | loop fusion | bytes 3686408 | tf_op jit(solution)/shard_map/jit(dynamic_index_in_dim)/dynamic_slice | solution.py:62
  39.2 1.4 %copy.26 = bf16[4,1,360,320]{2,3,0,1:T(8,128)(2,1)} copy(bf16[4,1,360,320]{3,2,1,0:T(8,128)(2,1)S(1)} %get-tuple-element.23) | data formatting | bytes 1843200 | tf_op jit(solution)/shard_map/jit(dynamic_index_in_dim)/dynamic_slice | solution.py:63
  44.5 12.6 %copy.30 = bf16[3,128,2880]{1,0,2:T(4,128)(2,1)S(1)} copy(bf16[3,128,2880]{1,2,0:T(8,128)(2,1)} %slice_dynamic-update-slice_fusion) | data formatting | bytes 4423680 | tf_op jit(solution)/shard_map/concatenate | solution.py:154
  57.0 3.5 %reshape_reshape.7 = bf16[384,9,320]{0,2,1:T(8,128)(2,1)} reshape(bf16[3,128,2880]{1,0,2:T(4,128)(2,1)S(1)} %copy.30) | data formatting | bytes 4423680 | tf_op jit(solution)/shard_map/reshape;reshape | solution.py:163
  60.5 1.6 %copy.38 = bf16[4,1,360,320]{2,3,0,1:T(8,128)(2,1)S(1)} copy(bf16[4,1,360,320]{3,2,1,0:T(8,128)(2,1)} %get-tuple-element.22) | data formatting | bytes 1843200
  62.2 1.4 %fusion.1 = bf16[4,360,320]{1,2,0:T(8,128)(2,1)S(1)} fusion(bf16[4,360,320]{1,2,0:T(8,128)(2,1)} %collective-permute-done.5, bf16[4,1,360,320]{2,3,0,1:T(8,128)(2,1)S(1)} %copy.38), kind=kLoop, calls=%fused_computation.5 | loop fusion | flops 1843200 | bytes 2764800 | tf_op jit(solution)/shard_map/convert_element_type | solution.py:66
  64.5 2.4 %collective-permute-start.8 = (bf16[360,320]{0,1:T(8,128)(2,1)}, bf16[360,320]{0,1:T(8,128)(2,1)}, u32[]{:S(2)}, u32[]{:S(2)}) collective-permute-start(bf16[360,320]{0,1:T(8,128)(2,1)} %get-tuple-element.25), channel_id=1, source_target_pairs={{0,6},{1,7},{2,4},{3,5},{4,2},{5,3},{6,0},{7,1},{8,14},{9,15},{10,... | collective-permute-start | bytes 691208 | tf_op jit(solution)/shard_map/ppermute | solution.py:79
  68.0 4.1 %copy.29 = bf16[8,360,320]{2,1,0:T(8,128)(2,1)} copy(bf16[8,360,320]{1,2,0:T(8,128)(2,1)} %all-gather.3.cloned.1.call-done) | data formatting | bytes 3686400 | tf_op jit(solution)/shard_map/all_gather | solution.py:123
  72.1 3.7 %fusion.3 = bf16[3,128,320]{1,2,0:T(8,128)(2,1)} fusion(bf16[3,128,2880]{1,2,0:T(8,128)(2,1)S(1)} %copy-done.1, bf16[2880,320,1]{1,0,2:T(8,128)(2,1)} %bitcast.88, f32[3,128]{1,0:T(4,128)S(1)} %get-tuple-element.34), kind=kOutput, calls=%fused_computation.9 | convolution fusion | flops 708034560 | bytes 4302336 | tf_op jit(solution)/shard_map/dot_general | solution.py:150
  75.8 3.6 %collective-permute-done.7 = bf16[360,320]{0,1:T(8,128)(2,1)} collective-permute-done((bf16[360,320]{0,1:T(8,128)(2,1)}, bf16[360,320]{0,1:T(8,128)(2,1)}, u32[]{:S(2)}, u32[]{:S(2)}) %collective-permute-start.7) | collective-permute-done | bytes 230432 | tf_op jit(solution)/shard_map/ppermute | solution.py:79
  79.5 1.3 %fusion.12 = bf16[360,320]{0,1:T(8,128)(2,1)S(1)} fusion(bf16[360,320]{0,1:T(8,128)(2,1)} %collective-permute-done.8, bf16[360,320]{0,1:T(8,128)(2,1)} %collective-permute-done.7, bf16[360,320]{0,1:T(8,128)(2,1)} %collective-permute-done.6, bf16[4,360,320]{1,2,0:T(8,128)(2,1)S(1)} %fusion.1, s32[]{:T(128)S(6)} %select_n.36), kind=kLoop, calls=%fused_computation.24 | loop fusion | flops 921600 | bytes 1152004 | tf_op jit(solution)/shard_map/convert_element_type | solution.py:90
  80.8 2.3 %collective-permute-start.9 = (bf16[360,320]{0,1:T(8,128)(2,1)S(1)}, bf16[360,320]{0,1:T(8,128)(2,1)S(1)}, u32[]{:S(2)}, u32[]{:S(2)}) collective-permute-start(bf16[360,320]{0,1:T(8,128)(2,1)S(1)} %fusion.12), channel_id=1, source_target_pairs={{0,8},{8,0},{16,24},{24,16},{1,9},{9,1},{17,25},{25,17},{2,10},{10... | collective-permute-start | bytes 691208 | tf_op jit(solution)/shard_map/ppermute | solution.py:92
  84.3 4.9 %collective-permute-done.9 = bf16[360,320]{0,1:T(8,128)(2,1)S(1)} collective-permute-done((bf16[360,320]{0,1:T(8,128)(2,1)S(1)}, bf16[360,320]{0,1:T(8,128)(2,1)S(1)}, u32[]{:S(2)}, u32[]{:S(2)}) %collective-permute-start.9) | collective-permute-done | bytes 230432 | tf_op jit(solution)/shard_map/ppermute | solution.py:92
  90.5 3.0 %collective-permute-start.14 = (f32[2,32]{1,0:T(2,128)S(1)}, f32[2,32]{1,0:T(2,128)S(1)}, u32[]{:S(2)}, u32[]{:S(2)}) collective-permute-start(f32[2,32]{1,0:T(2,128)S(1)} %pad_maximum_fusion.5), channel_id=1, source_target_pairs={{0,24},{8,0},{16,8},{24,16},{1,25},{9,1},{17,9},{25,17},{2,26},{10... | collective-permute-start | bytes 776 | tf_op jit(solution)/shard_map/ppermute | solution.py:33
  93.8 1.9 %collective-permute-start.12 = (f32[2,32]{1,0:T(2,128)S(1)}, f32[2,32]{1,0:T(2,128)S(1)}, u32[]{:S(2)}, u32[]{:S(2)}) collective-permute-start(f32[2,32]{1,0:T(2,128)S(1)} %pad_maximum_fusion.5), channel_id=1, source_target_pairs={{0,8},{8,16},{16,24},{24,0},{1,9},{9,17},{17,25},{25,1},{2,10},{10... | collective-permute-start | bytes 776 | tf_op jit(solution)/shard_map/ppermute | solution.py:33
  97.9 1.3 %collective-permute-done.12 = f32[2,32]{1,0:T(2,128)S(1)} collective-permute-done((f32[2,32]{1,0:T(2,128)S(1)}, f32[2,32]{1,0:T(2,128)S(1)}, u32[]{:S(2)}, u32[]{:S(2)}) %collective-permute-start.12) | collective-permute-done | bytes 288 | tf_op jit(solution)/shard_map/ppermute | solution.py:33
  100.8 7.5 %collective-permute-done.15 = bf16[360,320]{0,1:T(8,128)(2,1)S(1)} collective-permute-done((bf16[360,320]{0,1:T(8,128)(2,1)S(1)}, bf16[360,320]{0,1:T(8,128)(2,1)S(1)}, u32[]{:S(2)}, u32[]{:S(2)}) %collective-permute-start.15) | collective-permute-done | bytes 230432 | tf_op jit(solution)/shard_map/ppermute | solution.py:92
  (106 shorter events, 22.6 us)
Async XLA Ops:
  7.2 19.3 %copy-start.2 = (bf16[1,3,128,320]{2,3,1,0:T(8,128)(2,1)S(1)}, bf16[1,3,128,320]{2,3,1,0:T(8,128)(2,1)}, u32[]{:S(2)}) copy-start(bf16[1,3,128,320]{2,3,1,0:T(8,128)(2,1)} %param.9) | copy-start | bytes 737284
  7.2 19.3 %copy-start.10 = (f32[320]{0:T(512)S(1)}, f32[320]{0:T(512)}, u32[]{:S(2)}) copy-start(f32[320]{0:T(512)} %param.12) | copy-start | bytes 3844
  7.2 19.3 %copy-start.11 = (f32[320]{0:T(512)S(1)}, f32[320]{0:T(512)}, u32[]{:S(2)}) copy-start(f32[320]{0:T(512)} %param.11) | copy-start | bytes 3844
  7.2 60.8 %all-gather.3.cloned.1.call-start = ((), (), s32[]{:S(2)}) async-start(), calls=%async_computation | async-start | bytes 2211840 | tf_op jit(solution)/shard_map/all_gather | solution.py:123
  10.3 15.7 %collective-permute-start.2 = (f32[2,32]{1,0:T(2,128)S(1)}, f32[2,32]{1,0:T(2,128)S(1)}, u32[]{:S(2)}, u32[]{:S(2)}) collective-permute-start(f32[2,32]{1,0:T(2,128)S(1)} %pad_maximum_fusion.4), channel_id=1, source_target_pairs={{0,24},{8,0},{16,8},{24,16},{1,25},{9,1},{17,9},{25,17},{2,26},{10... | collective-permute-start | bytes 776 | tf_op jit(solution)/shard_map/ppermute | solution.py:33
  15.4 10.6 %collective-permute-start.1 = (f32[2,32]{1,0:T(2,128)S(1)}, f32[2,32]{1,0:T(2,128)S(1)}, u32[]{:S(2)}, u32[]{:S(2)}) collective-permute-start(f32[2,32]{1,0:T(2,128)S(1)} %pad_maximum_fusion.4), channel_id=1, source_target_pairs={{0,16},{8,24},{16,0},{24,8},{1,17},{9,25},{17,1},{25,9},{2,18},{10... | collective-permute-start | bytes 776 | tf_op jit(solution)/shard_map/ppermute | solution.py:33
  15.4 10.6 %collective-permute-start = (f32[2,32]{1,0:T(2,128)S(1)}, f32[2,32]{1,0:T(2,128)S(1)}, u32[]{:S(2)}, u32[]{:S(2)}) collective-permute-start(f32[2,32]{1,0:T(2,128)S(1)} %pad_maximum_fusion.4), channel_id=1, source_target_pairs={{0,8},{8,16},{16,24},{24,0},{1,9},{9,17},{17,25},{25,1},{2,10},{10... | collective-permute-start | bytes 776 | tf_op jit(solution)/shard_map/ppermute | solution.py:33
  17.5 15.2 %collective-permute-start.11 = (bf16[1,128,320]{1,2,0:T(8,128)(2,1)S(1)}, bf16[1,128,320]{1,2,0:T(8,128)(2,1)S(1)}, u32[]{:S(2)}, u32[]{:S(2)}) collective-permute-start(bf16[1,128,320]{1,2,0:T(8,128)(2,1)S(1)} %get-tuple-element.28), channel_id=1, source_target_pairs={{8,0},{16,8},{24,16},{9,1},{17,9},{25,17},{10,2},{18,10},{26,18},{... | collective-permute-start | bytes 245768 | tf_op jit(solution)/shard_map/ppermute | solution.py:20
  18.8 13.9 %collective-permute-start.10 = (bf16[1,128,320]{1,2,0:T(8,128)(2,1)S(1)}, bf16[1,128,320]{1,2,0:T(8,128)(2,1)S(1)}, u32[]{:S(2)}, u32[]{:S(2)}) collective-permute-start(bf16[1,128,320]{1,2,0:T(8,128)(2,1)S(1)} %get-tuple-element.27), channel_id=1, source_target_pairs={{0,8},{8,16},{16,24},{1,9},{9,17},{17,25},{2,10},{10,18},{18,26},{... | collective-permute-start | bytes 245768 | tf_op jit(solution)/shard_map/ppermute | solution.py:18
  26.8 6.7 %collective-permute-start.4 = (bf16[1,128,320]{1,2,0:T(8,128)(2,1)S(1)}, bf16[1,128,320]{1,2,0:T(8,128)(2,1)S(1)}, u32[]{:S(2)}, u32[]{:S(2)}) collective-permute-start(bf16[1,128,320]{1,2,0:T(8,128)(2,1)S(1)} %get-tuple-element.30), channel_id=1, source_target_pairs={{8,0},{16,8},{24,16},{9,1},{17,9},{25,17},{10,2},{18,10},{26,18},{... | collective-permute-start | bytes 245768 | tf_op jit(solution)/shard_map/ppermute | solution.py:20
  28.1 6.7 %collective-permute-start.3 = (bf16[1,128,320]{1,2,0:T(8,128)(2,1)S(1)}, bf16[1,128,320]{1,2,0:T(8,128)(2,1)S(1)}, u32[]{:S(2)}, u32[]{:S(2)}) collective-permute-start(bf16[1,128,320]{1,2,0:T(8,128)(2,1)S(1)} %get-tuple-element.29), channel_id=1, source_target_pairs={{0,8},{8,16},{16,24},{1,9},{9,17},{17,25},{2,10},{10,18},{18,26},{... | collective-permute-start | bytes 245768 | tf_op jit(solution)/shard_map/ppermute | solution.py:18
  40.6 21.6 %collective-permute-start.5 = (bf16[4,360,320]{1,2,0:T(8,128)(2,1)}, bf16[4,360,320]{1,2,0:T(8,128)(2,1)}, u32[]{:S(2)}, u32[]{:S(2)}) collective-permute-start(bf16[4,360,320]{1,2,0:T(8,128)(2,1)} %bitcast.11), channel_id=1, source_target_pairs={{0,1},{1,0},{2,3},{3,2},{4,5},{5,4},{6,7},{7,6},{8,9},{9,8},{10,11... | collective-permute-start | bytes 2764808 | tf_op jit(solution)/shard_map/ppermute | solution.py:65
  64.5 11.2 %collective-permute-start.8 = (bf16[360,320]{0,1:T(8,128)(2,1)}, bf16[360,320]{0,1:T(8,128)(2,1)}, u32[]{:S(2)}, u32[]{:S(2)}) collective-permute-start(bf16[360,320]{0,1:T(8,128)(2,1)} %get-tuple-element.25), channel_id=1, source_target_pairs={{0,6},{1,7},{2,4},{3,5},{4,2},{5,3},{6,0},{7,1},{8,14},{9,15},{10,... | collective-permute-start | bytes 691208 | tf_op jit(solution)/shard_map/ppermute | solution.py:79
  67.0 12.4 %collective-permute-start.7 = (bf16[360,320]{0,1:T(8,128)(2,1)}, bf16[360,320]{0,1:T(8,128)(2,1)}, u32[]{:S(2)}, u32[]{:S(2)}) collective-permute-start(bf16[360,320]{0,1:T(8,128)(2,1)} %get-tuple-element.26), channel_id=1, source_target_pairs={{0,4},{1,5},{2,6},{3,7},{4,0},{5,1},{6,2},{7,3},{8,12},{9,13},{10,... | collective-permute-start | bytes 691208 | tf_op jit(solution)/shard_map/ppermute | solution.py:79
  67.5 12.0 %collective-permute-start.6 = (bf16[360,320]{0,1:T(8,128)(2,1)}, bf16[360,320]{0,1:T(8,128)(2,1)}, u32[]{:S(2)}, u32[]{:S(2)}) collective-permute-start(bf16[360,320]{0,1:T(8,128)(2,1)} %get-tuple-element.24), channel_id=1, source_target_pairs={{0,2},{1,3},{2,0},{3,1},{4,6},{5,7},{6,4},{7,5},{8,10},{9,11},{10,... | collective-permute-start | bytes 691208 | tf_op jit(solution)/shard_map/ppermute | solution.py:79
  72.1 11.0 %copy-start.4 = (bf16[384,9,320]{0,2,1:T(8,128)(2,1)S(1)}, bf16[384,9,320]{0,2,1:T(8,128)(2,1)}, u32[]{:S(2)}) copy-start(bf16[384,9,320]{0,2,1:T(8,128)(2,1)} %reshape_reshape.7) | copy-start | bytes 6635524
  72.1 11.0 %copy-start.5 = (bf16[8,360,320]{2,1,0:T(8,128)(2,1)S(1)}, bf16[8,360,320]{2,1,0:T(8,128)(2,1)}, u32[]{:S(2)}) copy-start(bf16[8,360,320]{2,1,0:T(8,128)(2,1)} %copy.29) | copy-start | bytes 5529604
  80.8 8.4 %collective-permute-start.9 = (bf16[360,320]{0,1:T(8,128)(2,1)S(1)}, bf16[360,320]{0,1:T(8,128)(2,1)S(1)}, u32[]{:S(2)}, u32[]{:S(2)}) collective-permute-start(bf16[360,320]{0,1:T(8,128)(2,1)S(1)} %fusion.12), channel_id=1, source_target_pairs={{0,8},{8,0},{16,24},{24,16},{1,9},{9,1},{17,25},{25,17},{2,10},{10... | collective-permute-start | bytes 691208 | tf_op jit(solution)/shard_map/ppermute | solution.py:92
  89.2 19.1 %copy-start.8 = (f32[360,320]{0,1:T(8,128)S(1)}, f32[360,320]{0,1:T(8,128)}, u32[]{:S(2)}) copy-start(f32[360,320]{0,1:T(8,128)} %param.15) | copy-start | bytes 1382404
  89.2 19.1 %copy-start.9 = (f32[360,320]{0,1:T(8,128)S(1)}, f32[360,320]{0,1:T(8,128)}, u32[]{:S(2)}) copy-start(f32[360,320]{0,1:T(8,128)} %param.14) | copy-start | bytes 1382404
  90.5 6.2 %collective-permute-start.14 = (f32[2,32]{1,0:T(2,128)S(1)}, f32[2,32]{1,0:T(2,128)S(1)}, u32[]{:S(2)}, u32[]{:S(2)}) collective-permute-start(f32[2,32]{1,0:T(2,128)S(1)} %pad_maximum_fusion.5), channel_id=1, source_target_pairs={{0,24},{8,0},{16,8},{24,16},{1,25},{9,1},{17,9},{25,17},{2,26},{10... | collective-permute-start | bytes 776 | tf_op jit(solution)/shard_map/ppermute | solution.py:33
  93.4 4.5 %collective-permute-start.13 = (f32[2,32]{1,0:T(2,128)S(1)}, f32[2,32]{1,0:T(2,128)S(1)}, u32[]{:S(2)}, u32[]{:S(2)}) collective-permute-start(f32[2,32]{1,0:T(2,128)S(1)} %pad_maximum_fusion.5), channel_id=1, source_target_pairs={{0,16},{8,24},{16,0},{24,8},{1,17},{9,25},{17,1},{25,9},{2,18},{10... | collective-permute-start | bytes 776 | tf_op jit(solution)/shard_map/ppermute | solution.py:33
  93.8 5.5 %collective-permute-start.12 = (f32[2,32]{1,0:T(2,128)S(1)}, f32[2,32]{1,0:T(2,128)S(1)}, u32[]{:S(2)}, u32[]{:S(2)}) collective-permute-start(f32[2,32]{1,0:T(2,128)S(1)} %pad_maximum_fusion.5), channel_id=1, source_target_pairs={{0,8},{8,16},{16,24},{24,0},{1,9},{9,17},{17,25},{25,1},{2,10},{10... | collective-permute-start | bytes 776 | tf_op jit(solution)/shard_map/ppermute | solution.py:33
  96.0 12.4 %collective-permute-start.15 = (bf16[360,320]{0,1:T(8,128)(2,1)S(1)}, bf16[360,320]{0,1:T(8,128)(2,1)S(1)}, u32[]{:S(2)}, u32[]{:S(2)}) collective-permute-start(bf16[360,320]{0,1:T(8,128)(2,1)S(1)} %convert_add_fusion.3), channel_id=1, source_target_pairs={{0,16},{8,24},{16,0},{24,8},{1,17},{9,25},{17,1},{25,9},{2,18},{10... | collective-permute-start | bytes 691208 | tf_op jit(solution)/shard_map/ppermute | solution.py:92
  (5 other events, 19.6 us)
Sparse Core Ops, SparseCore 0:
  16.6 27.7 all-gather.2
